TPU v7x, 256 devices: a whole 4x4x8 slice. The times are simulated.
256 devices in a mesh: row: 16 (over x_hi, y, core), col: 16 (over z, x_lo).
Axes of the slice: x: 4 (x_hi: 2, x_lo: 2; x = x_hi * 2 + x_lo), y: 4, z: 8, core: 2. Of those that a mesh axis runs over, the one named last changes fastest.
Arguments:
- stem: bfloat16 [16, 16, 1, 512, 2, 512], P('row', 'col'), may hold values from -6 to 6
- branch: bfloat16 [16, 4, 2, 512, 512], P('row', None, None, None, 'col'), may hold values from -0.1875 to 0.1875
Outputs:
- amplitudes: bfloat16 [16, 16, 1, 512, 2, 512], P('row', 'col')
All inputs are finite; a program needn't handle non-finite values.
Results may differ from a plain program's by a relative error of at most 0.0075.
Values may be sent and summed in bfloat16 or wider, within the bound.
No kernel may reach another device: no remote copies, remote signals or barrier semaphores. Data moves between devices by JAX's collectives and lax.ppermute only.
A program may use at most 64 MiB of HBM per device.

v0:
```python
import jax
import jax.numpy as jnp
from jax import lax
from jax.sharding import PartitionSpec as P


def right_piece(block, piece):
    width = piece.shape[2]
    items = block.shape[0]
    order_size = block.shape[1]
    flat = block.reshape(items * order_size, 2 * width)
    real_t = piece[0].T
    imag_t = piece[1].T
    weight = jnp.block([[real_t, imag_t], [-imag_t, real_t]])
    product = jnp.dot(flat, weight, preferred_element_type=jnp.float32)
    return product.reshape(items, order_size, 2, order_size)


def left_piece(block, piece):
    rows_out = piece.shape[1]
    real_in = block[:, :, 0, :]
    imag_in = block[:, :, 1, :]
    real_w = piece[0]
    imag_w = piece[1]
    weight_real = jnp.concatenate([real_w, imag_w], axis=0)
    weight_imag = jnp.concatenate([-imag_w, real_w], axis=0)
    product = jnp.einsum("xi,eij->exj", weight_real, real_in, preferred_element_type=jnp.float32)
    product = product + jnp.einsum(
        "xi,eij->exj", weight_imag, imag_in, preferred_element_type=jnp.float32
    )
    return jnp.stack([product[:, :rows_out, :], product[:, rows_out:, :]], axis=2)


def shards(stem, branch):
    slab_count = stem.shape[2]
    order_size = stem.shape[3]
    row_count = lax.axis_size("row")
    share = order_size // row_count
    own_columns = branch[0]
    whole = lax.all_gather(own_columns, "col", axis=3, tiled=True)

    def apply_right(block, build_id):
        return right_piece(block, whole[build_id])

    def apply_left(block, build_id):
        return left_piece(block, whole[build_id])

    block = stem[0, 0]
    half_first = apply_right(block, 1).astype(jnp.bfloat16)
    step_first = apply_left(half_first, 0).astype(jnp.bfloat16)
    outgoing = step_first.reshape(slab_count, row_count, share, 2, order_size)
    moved = lax.all_to_all(outgoing, "row", split_axis=1, concat_axis=1, tiled=True)
    items = moved.shape[0]
    flat = moved.reshape(items, order_size, 2, order_size)
    half_second = apply_right(flat, 3).astype(jnp.bfloat16)
    step_second = apply_left(half_second, 2).astype(jnp.bfloat16)
    leaving = step_second.reshape(slab_count, order_size, 2, row_count, share)
    arrived = lax.all_to_all(leaving, "row", split_axis=3, concat_axis=3, tiled=True)
    return arrived.reshape(1, 1, slab_count, order_size, 2, order_size)


def solution(mesh):
    placed = (P("row", "col", None, None, None, None), P("row", None, None, None, "col"))
    return jax.shard_map(
        shards,
        mesh=mesh,
        in_specs=placed,
        out_specs=P("row", "col", None, None, None, None),
        check_vma=False,
    )
```

profile of v0, /device:TPU:1, one launch (start us, length us, event | category | flops | bytes accessed | tf_op | source)
XLA Modules:
  0.0 182.5 jit_solution(8665607085128221393)
XLA Ops:
  6.5 0.0 all-gather.3.cloned.1.call-start
  6.5 0.7 all-gather.3.cloned.1.call-update
  7.3 1.5 copy.20
  8.7 100.9 %all-gather.3.cloned.1.call-done = bf16[1,4,2,512,512]{3,4,2,1,0:T(8,128)(2,1)} async-done(((bf16[1,4,2,512,32]{3,4,2,1,0:T(8,128)(2,1)}), bf16[1,4,2,512,512]{3,4,2,1,0:T(8,128)(2,1)}) %all-gather.3.cloned.1.call-update) | async-done | bytes 4194320 | tf_op jit(solution)/shard_map/all_gather | solution.py:40
  109.6 2.2 %fusion.36 = (bf16[512,512]{0,1:T(8,128)(2,1)}, bf16[512,512]{0,1:T(8,128)(2,1)S(1)}) fusion(bf16[4,2,512,512]{2,3,1,0:T(8,128)(2,1)} %bitcast.76), kind=kLoop, calls=%fused_computation.52 | loop fusion | flops 524288 | bytes 2097152 | tf_op jit(solution)/shard_map/neg | solution.py:26
  111.8 2.1 %fusion.35 = (bf16[512,512]{1,0:T(8,128)(2,1)}, bf16[512,512]{1,0:T(8,128)(2,1)S(1)}) fusion(bf16[4,2,512,512]{2,3,1,0:T(8,128)(2,1)} %bitcast.77), kind=kLoop, calls=%fused_computation.51 | loop fusion | flops 524288 | bytes 2097152 | tf_op jit(solution)/shard_map/neg | solution.py:14
  113.9 0.0 copy-done
  113.9 1.5 slice_bitcast_fusion.6
  115.4 1.3 fusion.8
  116.7 0.7 fusion.14
  117.4 0.7 fusion.12
  118.1 0.1 fusion.38
  118.2 0.2 copy.11
  118.4 0.2 copy.12
  118.7 0.1 pad_maximum_fusion
  118.8 1.0 copy.13
  119.8 9.4 %all-to-all-start = ((bf16[1,16,32,2,512]{4,2,3,0,1:T(8,128)(2,1)}), bf16[1,16,32,2,512]{4,2,3,0,1:T(8,128)(2,1)S(1)}, u32[]{:S(2)}, u32[]{:S(2)}) async-start(bf16[1,16,32,2,512]{4,2,3,0,1:T(8,128)(2,1)} %copy.13), calls=%async_computation | async-start | bytes 2097152 | tf_op jit(solution)/shard_map/all_to_all | solution.py:52
  129.2 1.8 maximum_bitcast_fusion
  131.0 2.6 %copy.15 = bf16[1024,1024]{1,0:T(8,128)(2,1)} copy(bf16[1024,1024]{0,1:T(8,128)(2,1)S(1)} %maximum_bitcast_fusion) | data formatting | bytes 4194304 | tf_op jit(solution)/shard_map/dot_general | solution.py:15
  133.6 12.7 %all-to-all-done = bf16[1,16,32,2,512]{4,2,3,0,1:T(8,128)(2,1)S(1)} async-done(((bf16[1,16,32,2,512]{4,2,3,0,1:T(8,128)(2,1)}), bf16[1,16,32,2,512]{4,2,3,0,1:T(8,128)(2,1)S(1)}, u32[]{:S(2)}, u32[]{:S(2)}) %all-to-all-start) | async-done | bytes 1048608 | tf_op jit(solution)/shard_map/all_to_all | solution.py:52
  146.3 1.1 copy.14
  147.3 0.8 reshape.153
  148.1 0.0 copy-start.1
  148.1 3.0 %fusion.11 = bf16[1,512,2,512]{3,1,2,0:T(8,128)(2,1)S(1)} fusion(bf16[512,1024,1]{1,0,2:T(8,128)(2,1)S(1)} %reshape.153, bf16[2,512,1024]{2,1,0:T(8,128)(2,1)} %bitcast.80), kind=kOutput, calls=%fused_computation.13 | convolution fusion | flops 1074266112 | bytes 4194304 | tf_op jit(solution)/shard_map/dot_general | solution.py:15
  151.1 0.7 fusion.21
  151.9 0.3 copy-done.2
  152.2 0.7 fusion.13
  152.9 0.1 fusion.37
  153.0 0.1 pad_maximum_fusion.1
  153.1 20.3 %all_to_all.10 = bf16[1,512,2,16,32]{1,4,2,0,3:T(8,128)(2,1)S(1)} all-to-all(bf16[1,512,2,16,32]{1,4,2,0,3:T(8,128)(2,1)S(1)} %pad_maximum_fusion.1), channel_id=1, replica_groups=mesh['row'=16,'col'=16] {'row'}, dimensions={3} | all-to-all | bytes 2097152 | tf_op jit(solution)/shard_map/all_to_all | solution.py:58
  173.4 0.1 copy.18
  173.5 2.1 %copy.19 = bf16[1,1,1,512,2,512]{5,4,3,2,1,0:T(2,128)(2,1)} copy(bf16[1,1,1,512,2,512]{3,5,4,2,1,0:T(8,128)(2,1)S(1)} %bitcast.79) | data formatting | bytes 2097152 | tf_op jit(solution)/shard_map/reshape | solution.py:59
  (5 shorter events, 0.0 us)
Async XLA Ops:
  6.5 103.1 %all-gather.3.cloned.1.call-start = ((), (), s32[]{:S(2)}) async-start(), calls=%async_computation.2 | async-start | bytes 4456448 | tf_op jit(solution)/shard_map/all_gather | solution.py:40
  109.6 4.3 %copy-start = (bf16[1,4,2,512,512]{3,4,2,1,0:T(8,128)(2,1)S(1)}, bf16[1,4,2,512,512]{3,4,2,1,0:T(8,128)(2,1)}, u32[]{:S(2)}) copy-start(bf16[1,4,2,512,512]{3,4,2,1,0:T(8,128)(2,1)} %all-gather.3.cloned.1.call-done) | copy-start | bytes 12582916
  119.8 26.4 %all-to-all-start = ((bf16[1,16,32,2,512]{4,2,3,0,1:T(8,128)(2,1)}), bf16[1,16,32,2,512]{4,2,3,0,1:T(8,128)(2,1)S(1)}, u32[]{:S(2)}, u32[]{:S(2)}) async-start(bf16[1,16,32,2,512]{4,2,3,0,1:T(8,128)(2,1)} %copy.13), calls=%async_computation | async-start | bytes 2097152 | tf_op jit(solution)/shard_map/all_to_all | solution.py:52
  148.1 3.0 %copy-start.1 = (bf16[512,512]{0,1:T(8,128)(2,1)S(1)}, bf16[512,512]{0,1:T(8,128)(2,1)}, u32[]{:S(2)}) copy-start(bf16[512,512]{0,1:T(8,128)(2,1)} %get-tuple-element.9) | copy-start | bytes 1572868
  148.1 3.0 %copy-start.3 = (bf16[512,512]{0,1:T(8,128)(2,1)S(1)}, bf16[512,512]{0,1:T(8,128)(2,1)}, u32[]{:S(2)}) copy-start(bf16[512,512]{0,1:T(8,128)(2,1)} %get-tuple-element.8) | copy-start | bytes 1572868
  151.1 1.0 copy-start.2
Sparse Core Ops, SparseCore 0:
  9.1 100.4 all-gather.2
where the time goes:
time: 183 us; the launch traced here: 182 us
  waiting for transfers between devices  114 us (62%)
  blocking collectives  20.3 us (11%)
  between operations  13.5 us (7%)
  local copies, waits for them, and re-layouts  11.6 us (6%)
  starting transfers between devices  9.37 us (5%)
  matrix products  7.15 us (4%)
  other arithmetic  6.25 us (3%)
    all_gather x1, waiting for transfers between devices, shards(): whole = lax.all_gather(own_columns, 'col', axis=3, tiled=True)  101 us
    all_to_all x1, blocking collectives, shards(): lax.all_to_all(leaving, 'row', split_axis=3, concat_axis=3, tiled=True)  20.3 us
    all_to_all x1, waiting for transfers between devices, shards(): lax.all_to_all(outgoing, 'row', split_axis=1, concat_axis=1, tiled=True)  12.7 us
    all_to_all x1, starting transfers between devices, shards(): lax.all_to_all(outgoing, 'row', split_axis=1, concat_axis=1, tiled=True)  9.37 us
    dot_general x2, matrix products, right_piece(): product = jnp.dot(flat, weight, preferred_element_type=jnp.float32)  4.26 us
  transfers between devices with their start and end apart: 2, of which 2 were waited for; matrix products, arithmetic and copies ran while one was open for 3% of the time, Pallas kernels for 0%

commit v1 on v0

v1 whole, which is shorter than its diff:
```python
import jax
import jax.numpy as jnp
from jax import lax
from jax.sharding import Mesh
from jax.sharding import PartitionSpec as P


def right_piece(block, piece_t):
    items = block.shape[0]
    order_size = block.shape[1]
    flat = block.reshape(items * order_size, 2 * order_size)
    real_t = piece_t[0]
    imag_t = piece_t[1]
    weight = jnp.block([[real_t, imag_t], [-imag_t, real_t]])
    product = jnp.dot(flat, weight, preferred_element_type=jnp.float32)
    return product.reshape(items, order_size, 2, order_size)


def left_piece(block, piece_t):
    rows_out = piece_t.shape[2]
    real_in = block[:, :, 0, :]
    imag_in = block[:, :, 1, :]
    real_w = piece_t[0]
    imag_w = piece_t[1]
    weight_real = jnp.concatenate([real_w, imag_w], axis=1)
    weight_imag = jnp.concatenate([-imag_w, real_w], axis=1)
    product = jnp.einsum("ix,eij->exj", weight_real, real_in, preferred_element_type=jnp.float32)
    product = product + jnp.einsum(
        "ix,eij->exj", weight_imag, imag_in, preferred_element_type=jnp.float32
    )
    return jnp.stack([product[:, :rows_out, :], product[:, rows_out:, :]], axis=2)


def shift(x, axis, n, d):
    return lax.ppermute(x, axis, [(i, (i + d) % n) for i in range(n)])


def ring_gather(t):
    nz = lax.axis_size("cz")
    nx = lax.axis_size("cx")
    z = lax.axis_index("cz")
    x = lax.axis_index("cx")
    nb, comps, width, cols = t.shape
    other = shift(t, "cx", nx, 1)
    first = jnp.where(x == 0, t, other)
    second = jnp.where(x == 0, other, t)
    pair = jnp.stack([first, second], axis=2)
    buf = jnp.zeros((nb, comps, nz, nx, width, cols), t.dtype)
    buf = lax.dynamic_update_slice(buf, pair[:, :, None], (0, 0, z, 0, 0, 0))
    forward = nz // 2
    backward = nz - 1 - forward
    cur_f = pair
    cur_b = pair
    for k in range(1, forward + 1):
        if k == forward and nz % 2 == 0 and width % 2 == 0:
            half = width // 2
            a = shift(cur_f[:, :, :, :half], "cz", nz, 1)
            b = shift(cur_b[:, :, :, half:], "cz", nz, -1)
            piece = jnp.concatenate([a, b], axis=3)
            buf = lax.dynamic_update_slice(buf, piece[:, :, None], (0, 0, (z - k) % nz, 0, 0, 0))
            break
        cur_f = shift(cur_f, "cz", nz, 1)
        buf = lax.dynamic_update_slice(buf, cur_f[:, :, None], (0, 0, (z - k) % nz, 0, 0, 0))
        if k <= backward:
            cur_b = shift(cur_b, "cz", nz, -1)
            buf = lax.dynamic_update_slice(buf, cur_b[:, :, None], (0, 0, (z + k) % nz, 0, 0, 0))
    return buf.reshape(nb, comps, nz * nx * width, cols)


def shards(stem, branch):
    slab_count = stem.shape[2]
    order_size = stem.shape[3]
    row_count = lax.axis_size("row")
    share = order_size // row_count
    own_t = jnp.swapaxes(branch[0], -1, -2)
    first_t = ring_gather(own_t[:2])
    second_t = ring_gather(own_t[2:])

    block = stem[0, 0]
    half_first = right_piece(block, first_t[1]).astype(jnp.bfloat16)
    step_first = left_piece(half_first, first_t[0]).astype(jnp.bfloat16)
    outgoing = step_first.reshape(slab_count, row_count, share, 2, order_size)
    moved = lax.all_to_all(outgoing, "row", split_axis=1, concat_axis=1, tiled=True)
    items = moved.shape[0]
    flat = moved.reshape(items, order_size, 2, order_size)
    half_second = right_piece(flat, second_t[1]).astype(jnp.bfloat16)
    step_second = left_piece(half_second, second_t[0]).astype(jnp.bfloat16)
    leaving = step_second.reshape(slab_count, order_size, 2, row_count, share)
    arrived = lax.all_to_all(leaving, "row", split_axis=3, concat_axis=3, tiled=True)
    return arrived.reshape(1, 1, slab_count, order_size, 2, order_size)


def solution(mesh):
    n_col = mesh.shape["col"]
    split = Mesh(mesh.devices.reshape(mesh.shape["row"], n_col // 2, 2), ("row", "cz", "cx"))
    cols = ("cz", "cx")
    placed = (P("row", cols, None, None, None, None), P("row", None, None, None, cols))
    return jax.shard_map(
        shards,
        mesh=split,
        in_specs=placed,
        out_specs=P("row", cols, None, None, None, None),
        check_vma=False,
    )
```

time: 183 us -> 119 us (0.65)
  waiting for transfers between devices: 114 us -> 30.9 us
  starting transfers between devices: 9.37 us -> 41.2 us
  between operations: 13.5 us -> 0.47 us
  local copies, waits for them, and re-layouts: 11.6 us -> 15.5 us
  other arithmetic: 6.25 us -> 3.02 us
    all_gather x1 -> x0, waiting for transfers between devices: 101 us -> none  [shards(): whole = lax.all_gather(own_columns, 'col', axis=3, tiled=True)]
    ppermute x0 -> x18, starting transfers between devices: none -> 29.4 us  [shift(): return lax.ppermute(x, axis, [(i, (i + d) % n) for i in range(n)])]
    ppermute x0 -> x18, waiting for transfers between devices: none -> 19 us  [shift(): return lax.ppermute(x, axis, [(i, (i + d) % n) for i in range(n)])]
    all_to_all x1, starting transfers between devices: 9.37 us -> 11.8 us  [shards(): lax.all_to_all(outgoing, 'row', split_axis=1, concat_axis=1, tiled=True)]
    slice x0 -> x7, local copies, waits for them, and re-layouts: none -> 2.39 us  [the longest x2 1.36 us: right_piece(): imag_t = piece_t[1]]
    neg x1 -> x2, other arithmetic: 2.06 us -> 0.14 us  [right_piece(): weight = jnp.block([[real_t, imag_t], [-imag_t, real_t]])]
    slice x3, local copies, waits for them, and re-layouts: 0.35 us -> 2.18 us  [left_piece(): product[:, :rows_out, :]]
  transfers between devices with their start and end apart: 2 -> 19, of which waited for: 2 -> 9; matrix products, arithmetic and copies ran while one was open for 3% -> 6% of each run, Pallas kernels for 0% -> 0%
where the time goes in v1:
time: 119 us
  starting transfers between devices  41.2 us (35%)
  waiting for transfers between devices  30.9 us (26%)
  blocking collectives  20.3 us (17%)
  local copies, waits for them, and re-layouts  15.5 us (13%)
  matrix products  7.16 us (6%)
  other arithmetic  3.02 us (3%)
    ppermute x18, starting transfers between devices, shift(): return lax.ppermute(x, axis, [(i, (i + d) % n) for i in range(n)])  29.4 us
    all_to_all x1, blocking collectives, shards(): lax.all_to_all(leaving, 'row', split_axis=3, concat_axis=3, tiled=True)  20.3 us
    ppermute x18, waiting for transfers between devices, shift(): return lax.ppermute(x, axis, [(i, (i + d) % n) for i in range(n)])  19 us
    all_to_all x1, waiting for transfers between devices, shards(): lax.all_to_all(outgoing, 'row', split_axis=1, concat_axis=1, tiled=True)  11.9 us
    all_to_all x1, starting transfers between devices, shards(): lax.all_to_all(outgoing, 'row', split_axis=1, concat_axis=1, tiled=True)  11.8 us
    dot_general x2, matrix products, right_piece(): product = jnp.dot(flat, weight, preferred_element_type=jnp.float32)  4.27 us
    dot_general x1, local copies, waits for them, and re-layouts, right_piece(): product = jnp.dot(flat, weight, preferred_element_type=jnp.float32)  2.59 us
  transfers between devices with their start and end apart: 19, of which 9 were waited for; matrix products, arithmetic and copies ran while one was open for 6% of the time, Pallas kernels for 0%

profile of v1, /device:TPU:1, one launch (start us, length us, event | category | flops | bytes accessed | tf_op | source)
XLA Modules:
  0.0 118.6 jit_solution(418216245868426602)
XLA Ops:
  1.0 2.1 %collective-permute-start = (bf16[2,2,32,512]{3,2,1,0:T(8,128)(2,1)S(1)}, bf16[2,2,32,512]{3,2,1,0:T(8,128)(2,1)S(1)}, u32[]{:S(2)}, u32[]{:S(2)}) collective-permute-start(bf16[2,2,32,512]{3,2,1,0:T(8,128)(2,1)S(1)} %slice.116), channel_id=1, source_target_pairs={{0,1},{1,0},{2,3},{3,2},{4,5},{5,4},{6,7},{7,6},{8,9},{9,8},{10,11... | collective-permute-start | bytes 393224 | tf_op jit(solution)/shard_map/ppermute | solution.py:35
  3.1 1.5 %copy.55 = bf16[64,8,2,512]{3,1,2,0:T(8,128)(2,1)S(1)} copy(bf16[64,8,2,512]{3,2,1,0:T(2,128)(2,1)} %bitcast.140) | data formatting | bytes 2097152
  5.5 2.5 %collective-permute-start.1 = (bf16[2,2,2,32,512]{4,3,1,0,2:T(8,128)(2,1)S(1)}, bf16[2,2,2,32,512]{4,3,1,0,2:T(8,128)(2,1)S(1)}, u32[]{:S(2)}, u32[]{:S(2)}) collective-permute-start(bf16[2,2,2,32,512]{4,3,1,0,2:T(8,128)(2,1)S(1)} %get-tuple-element.21), channel_id=1, source_target_pairs={{0,2},{2,4},{4,6},{6,8},{8,10},{10,12},{12,14},{14,0},{1,3},{3,5},... | collective-permute-start | bytes 786440 | tf_op jit(solution)/shard_map/ppermute | solution.py:35
  8.1 4.0 %collective-permute-start.2 = (bf16[2,2,2,32,512]{4,3,1,0,2:T(8,128)(2,1)S(1)}, bf16[2,2,2,32,512]{4,3,1,0,2:T(8,128)(2,1)S(1)}, u32[]{:S(2)}, u32[]{:S(2)}) collective-permute-start(bf16[2,2,2,32,512]{4,3,1,0,2:T(8,128)(2,1)S(1)} %get-tuple-element.21), channel_id=1, source_target_pairs={{0,14},{2,0},{4,2},{6,4},{8,6},{10,8},{12,10},{14,12},{1,15},{3,1}... | collective-permute-start | bytes 786440 | tf_op jit(solution)/shard_map/ppermute | solution.py:35
  12.1 1.2 %collective-permute-start.9 = (bf16[2,2,32,512]{3,2,1,0:T(8,128)(2,1)S(1)}, bf16[2,2,32,512]{3,2,1,0:T(8,128)(2,1)S(1)}, u32[]{:S(2)}, u32[]{:S(2)}) collective-permute-start(bf16[2,2,32,512]{3,2,1,0:T(8,128)(2,1)S(1)} %get-tuple-element.23), channel_id=1, source_target_pairs={{0,1},{1,0},{2,3},{3,2},{4,5},{5,4},{6,7},{7,6},{8,9},{9,8},{10,11... | collective-permute-start | bytes 393224 | tf_op jit(solution)/shard_map/ppermute | solution.py:35
  13.6 2.6 %collective-permute-done.9 = bf16[2,2,32,512]{3,2,1,0:T(8,128)(2,1)S(1)} collective-permute-done((bf16[2,2,32,512]{3,2,1,0:T(8,128)(2,1)S(1)}, bf16[2,2,32,512]{3,2,1,0:T(8,128)(2,1)S(1)}, u32[]{:S(2)}, u32[]{:S(2)}) %collective-permute-start.9) | collective-permute-done | bytes 131104 | tf_op jit(solution)/shard_map/ppermute | solution.py:35
  16.4 2.7 %collective-permute-start.11 = (bf16[2,2,2,32,512]{4,3,2,1,0:T(8,128)(2,1)S(1)}, bf16[2,2,2,32,512]{4,3,2,1,0:T(8,128)(2,1)S(1)}, u32[]{:S(2)}, u32[]{:S(2)}) collective-permute-start(bf16[2,2,2,32,512]{4,3,2,1,0:T(8,128)(2,1)S(1)} %pad_maximum_fusion.3), channel_id=1, source_target_pairs={{0,14},{2,0},{4,2},{6,4},{8,6},{10,8},{12,10},{14,12},{1,15},{3,1}... | collective-permute-start | bytes 786440 | tf_op jit(solution)/shard_map/ppermute | solution.py:35
  19.4 2.7 %collective-permute-start.4 = (bf16[2,2,2,32,512]{4,3,1,0,2:T(8,128)(2,1)S(1)}, bf16[2,2,2,32,512]{4,3,1,0,2:T(8,128)(2,1)S(1)}, u32[]{:S(2)}, u32[]{:S(2)}) collective-permute-start(bf16[2,2,2,32,512]{4,3,1,0,2:T(8,128)(2,1)S(1)} %collective-permute-done.2), channel_id=1, source_target_pairs={{0,14},{2,0},{4,2},{6,4},{8,6},{10,8},{12,10},{14,12},{1,15},{3,1}... | collective-permute-start | bytes 786440 | tf_op jit(solution)/shard_map/ppermute | solution.py:35
  22.8 2.7 %collective-permute-start.13 = (bf16[2,2,2,32,512]{4,3,2,1,0:T(8,128)(2,1)S(1)}, bf16[2,2,2,32,512]{4,3,2,1,0:T(8,128)(2,1)S(1)}, u32[]{:S(2)}, u32[]{:S(2)}) collective-permute-start(bf16[2,2,2,32,512]{4,3,2,1,0:T(8,128)(2,1)S(1)} %collective-permute-done.11), channel_id=1, source_target_pairs={{0,14},{2,0},{4,2},{6,4},{8,6},{10,8},{12,10},{14,12},{1,15},{3,1}... | collective-permute-start | bytes 786440 | tf_op jit(solution)/shard_map/ppermute | solution.py:35
  25.6 3.3 %collective-permute-done.3 = bf16[2,2,2,32,512]{4,3,1,0,2:T(8,128)(2,1)S(1)} collective-permute-done((bf16[2,2,2,32,512]{4,3,1,0,2:T(8,128)(2,1)S(1)}, bf16[2,2,2,32,512]{4,3,1,0,2:T(8,128)(2,1)S(1)}, u32[]{:S(2)}, u32[]{:S(2)}) %collective-permute-start.3) | collective-permute-done | bytes 262176 | tf_op jit(solution)/shard_map/ppermute | solution.py:35
  28.9 2.7 %collective-permute-start.6 = (bf16[2,2,2,32,512]{4,3,1,0,2:T(8,128)(2,1)S(1)}, bf16[2,2,2,32,512]{4,3,1,0,2:T(8,128)(2,1)S(1)}, u32[]{:S(2)}, u32[]{:S(2)}) collective-permute-start(bf16[2,2,2,32,512]{4,3,1,0,2:T(8,128)(2,1)S(1)} %collective-permute-done.4), channel_id=1, source_target_pairs={{0,14},{2,0},{4,2},{6,4},{8,6},{10,8},{12,10},{14,12},{1,15},{3,1}... | collective-permute-start | bytes 786440 | tf_op jit(solution)/shard_map/ppermute | solution.py:35
  31.6 2.9 %collective-permute-done.12 = bf16[2,2,2,32,512]{4,3,2,1,0:T(8,128)(2,1)S(1)} collective-permute-done((bf16[2,2,2,32,512]{4,3,2,1,0:T(8,128)(2,1)S(1)}, bf16[2,2,2,32,512]{4,3,2,1,0:T(8,128)(2,1)S(1)}, u32[]{:S(2)}, u32[]{:S(2)}) %collective-permute-start.12) | collective-permute-done | bytes 262176 | tf_op jit(solution)/shard_map/ppermute | solution.py:35
  34.5 2.7 %collective-permute-start.15 = (bf16[2,2,2,32,512]{4,3,2,1,0:T(8,128)(2,1)S(1)}, bf16[2,2,2,32,512]{4,3,2,1,0:T(8,128)(2,1)S(1)}, u32[]{:S(2)}, u32[]{:S(2)}) collective-permute-start(bf16[2,2,2,32,512]{4,3,2,1,0:T(8,128)(2,1)S(1)} %collective-permute-done.13), channel_id=1, source_target_pairs={{0,14},{2,0},{4,2},{6,4},{8,6},{10,8},{12,10},{14,12},{1,15},{3,1}... | collective-permute-start | bytes 786440 | tf_op jit(solution)/shard_map/ppermute | solution.py:35
  37.3 2.8 %collective-permute-done.5 = bf16[2,2,2,32,512]{4,3,1,0,2:T(8,128)(2,1)S(1)} collective-permute-done((bf16[2,2,2,32,512]{4,3,1,0,2:T(8,128)(2,1)S(1)}, bf16[2,2,2,32,512]{4,3,1,0,2:T(8,128)(2,1)S(1)}, u32[]{:S(2)}, u32[]{:S(2)}) %collective-permute-start.5) | collective-permute-done | bytes 262176 | tf_op jit(solution)/shard_map/ppermute | solution.py:35
  40.2 2.9 %collective-permute-start.8 = (bf16[2,2,2,16,512]{4,3,1,0,2:T(8,128)(2,1)S(1)}, bf16[2,2,2,16,512]{4,3,1,0,2:T(8,128)(2,1)S(1)}, u32[]{:S(2)}, u32[]{:S(2)}) collective-permute-start(bf16[2,2,2,16,512]{4,3,1,0,2:T(8,128)(2,1)S(1)} %slice.118), channel_id=1, source_target_pairs={{0,14},{2,0},{4,2},{6,4},{8,6},{10,8},{12,10},{14,12},{1,15},{3,1}... | collective-permute-start | bytes 393224 | tf_op jit(solution)/shard_map/ppermute | solution.py:35
  43.2 2.5 %collective-permute-done.14 = bf16[2,2,2,32,512]{4,3,2,1,0:T(8,128)(2,1)S(1)} collective-permute-done((bf16[2,2,2,32,512]{4,3,2,1,0:T(8,128)(2,1)S(1)}, bf16[2,2,2,32,512]{4,3,2,1,0:T(8,128)(2,1)S(1)}, u32[]{:S(2)}, u32[]{:S(2)}) %collective-permute-start.14) | collective-permute-done | bytes 262176 | tf_op jit(solution)/shard_map/ppermute | solution.py:35
  45.9 2.7 %collective-permute-start.17 = (bf16[2,2,2,16,512]{4,3,2,1,0:T(8,128)(2,1)S(1)}, bf16[2,2,2,16,512]{4,3,2,1,0:T(8,128)(2,1)S(1)}, u32[]{:S(2)}, u32[]{:S(2)}) collective-permute-start(bf16[2,2,2,16,512]{4,3,2,1,0:T(8,128)(2,1)S(1)} %slice.129), channel_id=1, source_target_pairs={{0,14},{2,0},{4,2},{6,4},{8,6},{10,8},{12,10},{14,12},{1,15},{3,1}... | collective-permute-start | bytes 393224 | tf_op jit(solution)/shard_map/ppermute | solution.py:35
  48.7 3.4 %collective-permute-done.16 = bf16[2,2,2,16,512]{4,3,2,1,0:T(8,128)(2,1)S(1)} collective-permute-done((bf16[2,2,2,16,512]{4,3,2,1,0:T(8,128)(2,1)S(1)}, bf16[2,2,2,16,512]{4,3,2,1,0:T(8,128)(2,1)S(1)}, u32[]{:S(2)}, u32[]{:S(2)}) %collective-permute-start.16) | collective-permute-done | bytes 131104 | tf_op jit(solution)/shard_map/ppermute | solution.py:35
  52.5 1.3 %fusion.8 = bf16[1024,512]{1,0:T(8,128)(2,1)S(1)} fusion(bf16[512,1024]{1,0:T(8,128)(2,1)S(1)} %bitcast.141, bf16[512,512]{1,0:T(8,128)(2,1)S(1)} %bitcast.145, bf16[512,512]{1,0:T(8,128)(2,1)S(1)} %bitcast_negate_fusion.3, bf16[512,512]{1,0:T(8,128)(2,1)S(1)} %bitcast.137), kind=kOutput, calls=%fused_computation.11 | convolution fusion | flops 1082654720 | bytes 3670016 | tf_op jit(solution)/shard_map/dot_general | solution.py:15
  56.1 1.3 %copy.38 = bf16[1,512,512]{2,1,0:T(8,128)(2,1)S(1)} copy(bf16[1,512,512]{1,2,0:T(8,128)(2,1)} %get-tuple-element.15) | data formatting | bytes 1048576 | tf_op jit(solution)/shard_map/slice | solution.py:31
  57.4 1.0 copy.39
  58.4 1.1 pad_maximum_fusion
  59.6 1.0 copy.40
  60.6 11.8 %all-to-all-start = ((bf16[1,16,32,2,512]{4,2,3,0,1:T(8,128)(2,1)}), bf16[1,16,32,2,512]{4,2,3,0,1:T(8,128)(2,1)S(1)}, u32[]{:S(2)}, u32[]{:S(2)}) async-start(bf16[1,16,32,2,512]{4,2,3,0,1:T(8,128)(2,1)} %copy.40), calls=%async_computation | async-start | bytes 2097152 | tf_op jit(solution)/shard_map/all_to_all | solution.py:83
  72.4 1.1 fusion.35
  73.9 2.6 %copy.50 = bf16[1024,1024]{1,0:T(8,128)(2,1)} copy(bf16[1024,1024]{0,1:T(8,128)(2,1)S(1)} %maximum_bitcast_fusion) | data formatting | bytes 4194304 | tf_op jit(solution)/shard_map/dot_general | solution.py:15
  76.5 1.1 bitcast_negate_fusion
  77.6 11.9 %all-to-all-done = bf16[1,16,32,2,512]{4,2,3,0,1:T(8,128)(2,1)S(1)} async-done(((bf16[1,16,32,2,512]{4,2,3,0,1:T(8,128)(2,1)}), bf16[1,16,32,2,512]{4,2,3,0,1:T(8,128)(2,1)S(1)}, u32[]{:S(2)}, u32[]{:S(2)}) %all-to-all-start) | async-done | bytes 1048608 | tf_op jit(solution)/shard_map/all_to_all | solution.py:83
  89.5 1.1 copy.41
  91.4 3.0 %fusion.11 = bf16[1,512,2,512]{3,1,2,0:T(8,128)(2,1)S(1)} fusion(bf16[512,1024,1]{1,0,2:T(8,128)(2,1)S(1)} %reshape.162, bf16[2,512,1024]{2,1,0:T(8,128)(2,1)} %bitcast.128), kind=kOutput, calls=%fused_computation.13 | convolution fusion | flops 1074266112 | bytes 4194304 | tf_op jit(solution)/shard_map/dot_general | solution.py:15
  96.0 20.3 %all_to_all.10 = bf16[1,512,2,16,32]{1,4,2,0,3:T(8,128)(2,1)S(1)} all-to-all(bf16[1,512,2,16,32]{1,4,2,0,3:T(8,128)(2,1)S(1)} %pad_maximum_fusion.1), channel_id=1, replica_groups=mesh['row'=16,'cz'=8,'cx'=2] {'row'}, dimensions={3} | all-to-all | bytes 2097152 | tf_op jit(solution)/shard_map/all_to_all | solution.py:89
  116.5 2.1 %copy.54 = bf16[1,1,1,512,2,512]{5,4,3,2,1,0:T(2,128)(2,1)} copy(bf16[1,1,1,512,2,512]{3,5,4,2,1,0:T(8,128)(2,1)S(1)} %bitcast.127) | data formatting | bytes 2097152 | tf_op jit(solution)/shard_map/reshape | solution.py:90
  (65 shorter events, 9.4 us)
Async XLA Ops:
  0.0 5.5 %copy-start.2 = (bf16[1,4,2,512,32]{3,4,2,1,0:T(8,128)(2,1)S(1)}, bf16[1,4,2,512,32]{3,4,2,1,0:T(8,128)(2,1)}, u32[]{:S(2)}) copy-start(bf16[1,4,2,512,32]{3,4,2,1,0:T(8,128)(2,1)} %param.3) | copy-start | bytes 786436
  1.0 4.5 %collective-permute-start = (bf16[2,2,32,512]{3,2,1,0:T(8,128)(2,1)S(1)}, bf16[2,2,32,512]{3,2,1,0:T(8,128)(2,1)S(1)}, u32[]{:S(2)}, u32[]{:S(2)}) collective-permute-start(bf16[2,2,32,512]{3,2,1,0:T(8,128)(2,1)S(1)} %slice.116), channel_id=1, source_target_pairs={{0,1},{1,0},{2,3},{3,2},{4,5},{5,4},{6,7},{7,6},{8,9},{9,8},{10,11... | collective-permute-start | bytes 393224 | tf_op jit(solution)/shard_map/ppermute | solution.py:35
  5.5 13.8 %collective-permute-start.1 = (bf16[2,2,2,32,512]{4,3,1,0,2:T(8,128)(2,1)S(1)}, bf16[2,2,2,32,512]{4,3,1,0,2:T(8,128)(2,1)S(1)}, u32[]{:S(2)}, u32[]{:S(2)}) collective-permute-start(bf16[2,2,2,32,512]{4,3,1,0,2:T(8,128)(2,1)S(1)} %get-tuple-element.21), channel_id=1, source_target_pairs={{0,2},{2,4},{4,6},{6,8},{8,10},{10,12},{12,14},{14,0},{1,3},{3,5},... | collective-permute-start | bytes 786440 | tf_op jit(solution)/shard_map/ppermute | solution.py:35
  8.1 11.3 %collective-permute-start.2 = (bf16[2,2,2,32,512]{4,3,1,0,2:T(8,128)(2,1)S(1)}, bf16[2,2,2,32,512]{4,3,1,0,2:T(8,128)(2,1)S(1)}, u32[]{:S(2)}, u32[]{:S(2)}) collective-permute-start(bf16[2,2,2,32,512]{4,3,1,0,2:T(8,128)(2,1)S(1)} %get-tuple-element.21), channel_id=1, source_target_pairs={{0,14},{2,0},{4,2},{6,4},{8,6},{10,8},{12,10},{14,12},{1,15},{3,1}... | collective-permute-start | bytes 786440 | tf_op jit(solution)/shard_map/ppermute | solution.py:35
  12.1 4.1 %collective-permute-start.9 = (bf16[2,2,32,512]{3,2,1,0:T(8,128)(2,1)S(1)}, bf16[2,2,32,512]{3,2,1,0:T(8,128)(2,1)S(1)}, u32[]{:S(2)}, u32[]{:S(2)}) collective-permute-start(bf16[2,2,32,512]{3,2,1,0:T(8,128)(2,1)S(1)} %get-tuple-element.23), channel_id=1, source_target_pairs={{0,1},{1,0},{2,3},{3,2},{4,5},{5,4},{6,7},{7,6},{8,9},{9,8},{10,11... | collective-permute-start | bytes 393224 | tf_op jit(solution)/shard_map/ppermute | solution.py:35
  16.3 6.5 %collective-permute-start.10 = (bf16[2,2,2,32,512]{4,3,2,1,0:T(8,128)(2,1)S(1)}, bf16[2,2,2,32,512]{4,3,2,1,0:T(8,128)(2,1)S(1)}, u32[]{:S(2)}, u32[]{:S(2)}) collective-permute-start(bf16[2,2,2,32,512]{4,3,2,1,0:T(8,128)(2,1)S(1)} %pad_maximum_fusion.3), channel_id=1, source_target_pairs={{0,2},{2,4},{4,6},{6,8},{8,10},{10,12},{12,14},{14,0},{1,3},{3,5},... | collective-permute-start | bytes 786440 | tf_op jit(solution)/shard_map/ppermute | solution.py:35
  16.4 6.5 %collective-permute-start.11 = (bf16[2,2,2,32,512]{4,3,2,1,0:T(8,128)(2,1)S(1)}, bf16[2,2,2,32,512]{4,3,2,1,0:T(8,128)(2,1)S(1)}, u32[]{:S(2)}, u32[]{:S(2)}) collective-permute-start(bf16[2,2,2,32,512]{4,3,2,1,0:T(8,128)(2,1)S(1)} %pad_maximum_fusion.3), channel_id=1, source_target_pairs={{0,14},{2,0},{4,2},{6,4},{8,6},{10,8},{12,10},{14,12},{1,15},{3,1}... | collective-permute-start | bytes 786440 | tf_op jit(solution)/shard_map/ppermute | solution.py:35
  19.3 9.5 %collective-permute-start.3 = (bf16[2,2,2,32,512]{4,3,1,0,2:T(8,128)(2,1)S(1)}, bf16[2,2,2,32,512]{4,3,1,0,2:T(8,128)(2,1)S(1)}, u32[]{:S(2)}, u32[]{:S(2)}) collective-permute-start(bf16[2,2,2,32,512]{4,3,1,0,2:T(8,128)(2,1)S(1)} %collective-permute-done.1), channel_id=1, source_target_pairs={{0,2},{2,4},{4,6},{6,8},{8,10},{10,12},{12,14},{14,0},{1,3},{3,5},... | collective-permute-start | bytes 786440 | tf_op jit(solution)/shard_map/ppermute | solution.py:35
  19.4 9.4 %collective-permute-start.4 = (bf16[2,2,2,32,512]{4,3,1,0,2:T(8,128)(2,1)S(1)}, bf16[2,2,2,32,512]{4,3,1,0,2:T(8,128)(2,1)S(1)}, u32[]{:S(2)}, u32[]{:S(2)}) collective-permute-start(bf16[2,2,2,32,512]{4,3,1,0,2:T(8,128)(2,1)S(1)} %collective-permute-done.2), channel_id=1, source_target_pairs={{0,14},{2,0},{4,2},{6,4},{8,6},{10,8},{12,10},{14,12},{1,15},{3,1}... | collective-permute-start | bytes 786440 | tf_op jit(solution)/shard_map/ppermute | solution.py:35
  22.8 11.7 %collective-permute-start.12 = (bf16[2,2,2,32,512]{4,3,2,1,0:T(8,128)(2,1)S(1)}, bf16[2,2,2,32,512]{4,3,2,1,0:T(8,128)(2,1)S(1)}, u32[]{:S(2)}, u32[]{:S(2)}) collective-permute-start(bf16[2,2,2,32,512]{4,3,2,1,0:T(8,128)(2,1)S(1)} %collective-permute-done.10), channel_id=1, source_target_pairs={{0,2},{2,4},{4,6},{6,8},{8,10},{10,12},{12,14},{14,0},{1,3},{3,5},... | collective-permute-start | bytes 786440 | tf_op jit(solution)/shard_map/ppermute | solution.py:35
  22.8 11.7 %collective-permute-start.13 = (bf16[2,2,2,32,512]{4,3,2,1,0:T(8,128)(2,1)S(1)}, bf16[2,2,2,32,512]{4,3,2,1,0:T(8,128)(2,1)S(1)}, u32[]{:S(2)}, u32[]{:S(2)}) collective-permute-start(bf16[2,2,2,32,512]{4,3,2,1,0:T(8,128)(2,1)S(1)} %collective-permute-done.11), channel_id=1, source_target_pairs={{0,14},{2,0},{4,2},{6,4},{8,6},{10,8},{12,10},{14,12},{1,15},{3,1}... | collective-permute-start | bytes 786440 | tf_op jit(solution)/shard_map/ppermute | solution.py:35
  28.9 11.2 %collective-permute-start.5 = (bf16[2,2,2,32,512]{4,3,1,0,2:T(8,128)(2,1)S(1)}, bf16[2,2,2,32,512]{4,3,1,0,2:T(8,128)(2,1)S(1)}, u32[]{:S(2)}, u32[]{:S(2)}) collective-permute-start(bf16[2,2,2,32,512]{4,3,1,0,2:T(8,128)(2,1)S(1)} %collective-permute-done.3), channel_id=1, source_target_pairs={{0,2},{2,4},{4,6},{6,8},{8,10},{10,12},{12,14},{14,0},{1,3},{3,5},... | collective-permute-start | bytes 786440 | tf_op jit(solution)/shard_map/ppermute | solution.py:35
  28.9 11.3 %collective-permute-start.6 = (bf16[2,2,2,32,512]{4,3,1,0,2:T(8,128)(2,1)S(1)}, bf16[2,2,2,32,512]{4,3,1,0,2:T(8,128)(2,1)S(1)}, u32[]{:S(2)}, u32[]{:S(2)}) collective-permute-start(bf16[2,2,2,32,512]{4,3,1,0,2:T(8,128)(2,1)S(1)} %collective-permute-done.4), channel_id=1, source_target_pairs={{0,14},{2,0},{4,2},{6,4},{8,6},{10,8},{12,10},{14,12},{1,15},{3,1}... | collective-permute-start | bytes 786440 | tf_op jit(solution)/shard_map/ppermute | solution.py:35
  34.5 11.2 %collective-permute-start.14 = (bf16[2,2,2,32,512]{4,3,2,1,0:T(8,128)(2,1)S(1)}, bf16[2,2,2,32,512]{4,3,2,1,0:T(8,128)(2,1)S(1)}, u32[]{:S(2)}, u32[]{:S(2)}) collective-permute-start(bf16[2,2,2,32,512]{4,3,2,1,0:T(8,128)(2,1)S(1)} %collective-permute-done.12), channel_id=1, source_target_pairs={{0,2},{2,4},{4,6},{6,8},{8,10},{10,12},{12,14},{14,0},{1,3},{3,5},... | collective-permute-start | bytes 786440 | tf_op jit(solution)/shard_map/ppermute | solution.py:35
  34.5 11.3 %collective-permute-start.15 = (bf16[2,2,2,32,512]{4,3,2,1,0:T(8,128)(2,1)S(1)}, bf16[2,2,2,32,512]{4,3,2,1,0:T(8,128)(2,1)S(1)}, u32[]{:S(2)}, u32[]{:S(2)}) collective-permute-start(bf16[2,2,2,32,512]{4,3,2,1,0:T(8,128)(2,1)S(1)} %collective-permute-done.13), channel_id=1, source_target_pairs={{0,14},{2,0},{4,2},{6,4},{8,6},{10,8},{12,10},{14,12},{1,15},{3,1}... | collective-permute-start | bytes 786440 | tf_op jit(solution)/shard_map/ppermute | solution.py:35
  40.1 8.5 %collective-permute-start.7 = (bf16[2,2,2,16,512]{4,3,1,0,2:T(8,128)(2,1)S(1)}, bf16[2,2,2,16,512]{4,3,1,0,2:T(8,128)(2,1)S(1)}, u32[]{:S(2)}, u32[]{:S(2)}) collective-permute-start(bf16[2,2,2,16,512]{4,3,1,0,2:T(8,128)(2,1)S(1)} %slice.117), channel_id=1, source_target_pairs={{0,2},{2,4},{4,6},{6,8},{8,10},{10,12},{12,14},{14,0},{1,3},{3,5},... | collective-permute-start | bytes 393224 | tf_op jit(solution)/shard_map/ppermute | solution.py:35
  40.2 8.4 %collective-permute-start.8 = (bf16[2,2,2,16,512]{4,3,1,0,2:T(8,128)(2,1)S(1)}, bf16[2,2,2,16,512]{4,3,1,0,2:T(8,128)(2,1)S(1)}, u32[]{:S(2)}, u32[]{:S(2)}) collective-permute-start(bf16[2,2,2,16,512]{4,3,1,0,2:T(8,128)(2,1)S(1)} %slice.118), channel_id=1, source_target_pairs={{0,14},{2,0},{4,2},{6,4},{8,6},{10,8},{12,10},{14,12},{1,15},{3,1}... | collective-permute-start | bytes 393224 | tf_op jit(solution)/shard_map/ppermute | solution.py:35
  45.7 6.4 %collective-permute-start.16 = (bf16[2,2,2,16,512]{4,3,2,1,0:T(8,128)(2,1)S(1)}, bf16[2,2,2,16,512]{4,3,2,1,0:T(8,128)(2,1)S(1)}, u32[]{:S(2)}, u32[]{:S(2)}) collective-permute-start(bf16[2,2,2,16,512]{4,3,2,1,0:T(8,128)(2,1)S(1)} %slice.128), channel_id=1, source_target_pairs={{0,2},{2,4},{4,6},{6,8},{8,10},{10,12},{12,14},{14,0},{1,3},{3,5},... | collective-permute-start | bytes 393224 | tf_op jit(solution)/shard_map/ppermute | solution.py:35
  45.9 6.2 %collective-permute-start.17 = (bf16[2,2,2,16,512]{4,3,2,1,0:T(8,128)(2,1)S(1)}, bf16[2,2,2,16,512]{4,3,2,1,0:T(8,128)(2,1)S(1)}, u32[]{:S(2)}, u32[]{:S(2)}) collective-permute-start(bf16[2,2,2,16,512]{4,3,2,1,0:T(8,128)(2,1)S(1)} %slice.129), channel_id=1, source_target_pairs={{0,14},{2,0},{4,2},{6,4},{8,6},{10,8},{12,10},{14,12},{1,15},{3,1}... | collective-permute-start | bytes 393224 | tf_op jit(solution)/shard_map/ppermute | solution.py:35
  60.6 28.9 %all-to-all-start = ((bf16[1,16,32,2,512]{4,2,3,0,1:T(8,128)(2,1)}), bf16[1,16,32,2,512]{4,2,3,0,1:T(8,128)(2,1)S(1)}, u32[]{:S(2)}, u32[]{:S(2)}) async-start(bf16[1,16,32,2,512]{4,2,3,0,1:T(8,128)(2,1)} %copy.40), calls=%async_computation | async-start | bytes 2097152 | tf_op jit(solution)/shard_map/all_to_all | solution.py:83
  91.3 3.0 %copy-start = (bf16[1,1,8,2,32,512]{5,4,3,2,1,0:T(8,128)(2,1)S(1)}, bf16[1,1,8,2,32,512]{5,4,3,2,1,0:T(8,128)(2,1)}, u32[]{:S(2)}) copy-start(bf16[1,1,8,2,32,512]{5,4,3,2,1,0:T(8,128)(2,1)} %get-tuple-element.7) | copy-start | bytes 1572868
  91.3 3.0 %copy-start.1 = (bf16[1,1,8,2,32,512]{5,4,3,2,1,0:T(8,128)(2,1)S(1)}, bf16[1,1,8,2,32,512]{5,4,3,2,1,0:T(8,128)(2,1)}, u32[]{:S(2)}) copy-start(bf16[1,1,8,2,32,512]{5,4,3,2,1,0:T(8,128)(2,1)} %get-tuple-element.6) | copy-start | bytes 1572868

commit v2 on v1

--- a/solution.py
+++ b/solution.py
@@ -74,7 +74,8 @@
     share = order_size // row_count
     own_t = jnp.swapaxes(branch[0], -1, -2)
     first_t = ring_gather(own_t[:2])
-    second_t = ring_gather(own_t[2:])
+    later, first_t = lax.optimization_barrier((own_t[2:], first_t))
+    second_t = ring_gather(later)
 
     block = stem[0, 0]
     half_first = right_piece(block, first_t[1]).astype(jnp.bfloat16)

time: 119 us -> 127 us (1.067)
  blocking collectives: 20.3 us -> 26.6 us
  starting transfers between devices: 41.2 us -> 44 us
  waiting for transfers between devices: 30.9 us -> 28.8 us
    all_to_all x1, waiting for transfers between devices: 11.9 us -> 0.01 us  [shards(): lax.all_to_all(outgoing, 'row', split_axis=1, concat_axis=1, tiled=True)]
    ppermute x18, waiting for transfers between devices: 19 us -> 28.8 us  [shift(): return lax.ppermute(x, axis, [(i, (i + d) % n) for i in range(n)])]
    all_to_all x1, blocking collectives: 20.3 us -> 26.6 us  [shards(): lax.all_to_all(leaving, 'row', split_axis=3, concat_axis=3, tiled=True)]
    all_to_all x1, starting transfers between devices: 11.8 us -> 13.8 us  [shards(): lax.all_to_all(outgoing, 'row', split_axis=1, concat_axis=1, tiled=True)]
    slice x3, local copies, waits for them, and re-layouts: 2.18 us -> 0.35 us  [left_piece(): product[:, :rows_out, :]]
    another operation x1, local copies, waits for them, and re-layouts: 0.76 us -> 2.56 us  [right_piece(): flat = block.reshape(items * order_size, 2 * order_size)]
    another operation x4, other arithmetic: 0.12 us -> 1.79 us  [ring_gather(): pair = jnp.stack([first, second], axis=2)]
  transfers between devices with their start and end apart: 19 -> 19, of which waited for: 9 -> 9; matrix products, arithmetic and copies ran while one was open for 6% -> 10% of each run, Pallas kernels for 0% -> 0%
where the time goes in v2:
time: 127 us; the launch traced here: 126 us
  starting transfers between devices  44 us (35%)
  waiting for transfers between devices  28.8 us (23%)
  blocking collectives  26.6 us (21%)
  local copies, waits for them, and re-layouts  16.6 us (13%)
  matrix products  7.45 us (6%)
  other arithmetic  2.57 us (2%)
    ppermute x18, starting transfers between devices, shift(): return lax.ppermute(x, axis, [(i, (i + d) % n) for i in range(n)])  30.2 us
    ppermute x18, waiting for transfers between devices, shift(): return lax.ppermute(x, axis, [(i, (i + d) % n) for i in range(n)])  28.8 us
    all_to_all x1, blocking collectives, shards(): lax.all_to_all(leaving, 'row', split_axis=3, concat_axis=3, tiled=True)  26.6 us
    all_to_all x1, starting transfers between devices, shards(): lax.all_to_all(outgoing, 'row', split_axis=1, concat_axis=1, tiled=True)  13.8 us
    dot_general x2, matrix products, right_piece(): product = jnp.dot(flat, weight, preferred_element_type=jnp.float32)  4.55 us
    dot_general x1, local copies, waits for them, and re-layouts, right_piece(): product = jnp.dot(flat, weight, preferred_element_type=jnp.float32)  2.59 us
    another operation x1, local copies, waits for them, and re-layouts, right_piece(): flat = block.reshape(items * order_size, 2 * order_size)  2.56 us
  transfers between devices with their start and end apart: 19, of which 9 were waited for; matrix products, arithmetic and copies ran while one was open for 10% of the time, Pallas kernels for 0%

profile of v2, /device:TPU:1, one launch (start us, length us, event | category | flops | bytes accessed | tf_op | source)
XLA Modules:
  0.0 126.4 jit_solution(16622802515583069896)
XLA Ops:
  0.0 1.0 slice.115
  1.0 2.1 %collective-permute-start = (bf16[2,2,32,512]{3,2,1,0:T(8,128)(2,1)S(1)}, bf16[2,2,32,512]{3,2,1,0:T(8,128)(2,1)S(1)}, u32[]{:S(2)}, u32[]{:S(2)}) collective-permute-start(bf16[2,2,32,512]{3,2,1,0:T(8,128)(2,1)S(1)} %slice.115), channel_id=1, source_target_pairs={{0,1},{1,0},{2,3},{3,2},{4,5},{5,4},{6,7},{7,6},{8,9},{9,8},{10,11... | collective-permute-start | bytes 393224 | tf_op jit(solution)/shard_map/ppermute | solution.py:35
  3.1 2.4 %collective-permute-done = bf16[2,2,32,512]{3,2,1,0:T(8,128)(2,1)S(1)} collective-permute-done((bf16[2,2,32,512]{3,2,1,0:T(8,128)(2,1)S(1)}, bf16[2,2,32,512]{3,2,1,0:T(8,128)(2,1)S(1)}, u32[]{:S(2)}, u32[]{:S(2)}) %collective-permute-start) | collective-permute-done | bytes 131104 | tf_op jit(solution)/shard_map/ppermute | solution.py:35
  5.5 1.0 select_bitcast_fusion.3
  6.5 2.5 %collective-permute-start.1 = (bf16[2,2,2,32,512]{4,3,2,1,0:T(8,128)(2,1)S(1)}, bf16[2,2,2,32,512]{4,3,2,1,0:T(8,128)(2,1)S(1)}, u32[]{:S(2)}, u32[]{:S(2)}) collective-permute-start(bf16[2,2,2,32,512]{4,3,2,1,0:T(8,128)(2,1)S(1)} %pad_maximum_fusion.2), channel_id=1, source_target_pairs={{0,2},{2,4},{4,6},{6,8},{8,10},{10,12},{12,14},{14,0},{1,3},{3,5},... | collective-permute-start | bytes 786440 | tf_op jit(solution)/shard_map/ppermute | solution.py:35
  9.0 4.0 %collective-permute-start.2 = (bf16[2,2,2,32,512]{4,3,2,1,0:T(8,128)(2,1)S(1)}, bf16[2,2,2,32,512]{4,3,2,1,0:T(8,128)(2,1)S(1)}, u32[]{:S(2)}, u32[]{:S(2)}) collective-permute-start(bf16[2,2,2,32,512]{4,3,2,1,0:T(8,128)(2,1)S(1)} %pad_maximum_fusion.2), channel_id=1, source_target_pairs={{0,14},{2,0},{4,2},{6,4},{8,6},{10,8},{12,10},{14,12},{1,15},{3,1}... | collective-permute-start | bytes 786440 | tf_op jit(solution)/shard_map/ppermute | solution.py:35
  13.6 4.5 %collective-permute-done.1 = bf16[2,2,2,32,512]{4,3,2,1,0:T(8,128)(2,1)S(1)} collective-permute-done((bf16[2,2,2,32,512]{4,3,2,1,0:T(8,128)(2,1)S(1)}, bf16[2,2,2,32,512]{4,3,2,1,0:T(8,128)(2,1)S(1)}, u32[]{:S(2)}, u32[]{:S(2)}) %collective-permute-start.1) | collective-permute-done | bytes 262176 | tf_op jit(solution)/shard_map/ppermute | solution.py:35
  18.1 2.7 %collective-permute-start.4 = (bf16[2,2,2,32,512]{4,3,2,1,0:T(8,128)(2,1)S(1)}, bf16[2,2,2,32,512]{4,3,2,1,0:T(8,128)(2,1)S(1)}, u32[]{:S(2)}, u32[]{:S(2)}) collective-permute-start(bf16[2,2,2,32,512]{4,3,2,1,0:T(8,128)(2,1)S(1)} %collective-permute-done.2), channel_id=1, source_target_pairs={{0,14},{2,0},{4,2},{6,4},{8,6},{10,8},{12,10},{14,12},{1,15},{3,1}... | collective-permute-start | bytes 786440 | tf_op jit(solution)/shard_map/ppermute | solution.py:35
  20.9 4.2 %collective-permute-done.3 = bf16[2,2,2,32,512]{4,3,2,1,0:T(8,128)(2,1)S(1)} collective-permute-done((bf16[2,2,2,32,512]{4,3,2,1,0:T(8,128)(2,1)S(1)}, bf16[2,2,2,32,512]{4,3,2,1,0:T(8,128)(2,1)S(1)}, u32[]{:S(2)}, u32[]{:S(2)}) %collective-permute-start.3) | collective-permute-done | bytes 262176 | tf_op jit(solution)/shard_map/ppermute | solution.py:35
  25.1 2.7 %collective-permute-start.6 = (bf16[2,2,2,32,512]{4,3,2,1,0:T(8,128)(2,1)S(1)}, bf16[2,2,2,32,512]{4,3,2,1,0:T(8,128)(2,1)S(1)}, u32[]{:S(2)}, u32[]{:S(2)}) collective-permute-start(bf16[2,2,2,32,512]{4,3,2,1,0:T(8,128)(2,1)S(1)} %collective-permute-done.4), channel_id=1, source_target_pairs={{0,14},{2,0},{4,2},{6,4},{8,6},{10,8},{12,10},{14,12},{1,15},{3,1}... | collective-permute-start | bytes 786440 | tf_op jit(solution)/shard_map/ppermute | solution.py:35
  27.8 3.3 %collective-permute-done.6 = bf16[2,2,2,32,512]{4,3,2,1,0:T(8,128)(2,1)S(1)} collective-permute-done((bf16[2,2,2,32,512]{4,3,2,1,0:T(8,128)(2,1)S(1)}, bf16[2,2,2,32,512]{4,3,2,1,0:T(8,128)(2,1)S(1)}, u32[]{:S(2)}, u32[]{:S(2)}) %collective-permute-start.6) | collective-permute-done | bytes 262176 | tf_op jit(solution)/shard_map/ppermute | solution.py:35
  31.1 3.2 %collective-permute-start.8 = (bf16[2,2,2,16,512]{4,3,2,1,0:T(8,128)(2,1)S(1)}, bf16[2,2,2,16,512]{4,3,2,1,0:T(8,128)(2,1)S(1)}, u32[]{:S(2)}, u32[]{:S(2)}) collective-permute-start(bf16[2,2,2,16,512]{4,3,2,1,0:T(8,128)(2,1)S(1)} %slice.117), channel_id=1, source_target_pairs={{0,14},{2,0},{4,2},{6,4},{8,6},{10,8},{12,10},{14,12},{1,15},{3,1}... | collective-permute-start | bytes 393224 | tf_op jit(solution)/shard_map/ppermute | solution.py:35
  34.5 1.8 %collective-permute-done.8 = bf16[2,2,2,16,512]{4,3,2,1,0:T(8,128)(2,1)S(1)} collective-permute-done((bf16[2,2,2,16,512]{4,3,2,1,0:T(8,128)(2,1)S(1)}, bf16[2,2,2,16,512]{4,3,2,1,0:T(8,128)(2,1)S(1)}, u32[]{:S(2)}, u32[]{:S(2)}) %collective-permute-start.8) | collective-permute-done | bytes 131104 | tf_op jit(solution)/shard_map/ppermute | solution.py:35
  36.3 3.2 %collective-permute-done.7 = bf16[2,2,2,16,512]{4,3,2,1,0:T(8,128)(2,1)S(1)} collective-permute-done((bf16[2,2,2,16,512]{4,3,2,1,0:T(8,128)(2,1)S(1)}, bf16[2,2,2,16,512]{4,3,2,1,0:T(8,128)(2,1)S(1)}, u32[]{:S(2)}, u32[]{:S(2)}) %collective-permute-start.7) | collective-permute-done | bytes 131104 | tf_op jit(solution)/shard_map/ppermute | solution.py:35
  39.7 1.3 %collective-permute-start.9 = (bf16[2,2,32,512]{3,2,1,0:T(8,128)(2,1)S(1)}, bf16[2,2,32,512]{3,2,1,0:T(8,128)(2,1)S(1)}, u32[]{:S(2)}, u32[]{:S(2)}) collective-permute-start(bf16[2,2,32,512]{3,2,1,0:T(8,128)(2,1)S(1)} %get-tuple-element.8), channel_id=1, source_target_pairs={{0,1},{1,0},{2,3},{3,2},{4,5},{5,4},{6,7},{7,6},{8,9},{9,8},{10,11... | collective-permute-start | bytes 393224 | tf_op jit(solution)/shard_map/ppermute | solution.py:35
  41.0 1.3 %fusion.8 = bf16[1024,512]{1,0:T(8,128)(2,1)S(1)} fusion(bf16[512,1024]{1,0:T(8,128)(2,1)S(1)} %bitcast.146, bf16[512,512]{1,0:T(8,128)(2,1)S(1)} %get-tuple-element.18, bf16[512,512]{1,0:T(8,128)(2,1)S(1)} %get-tuple-element.14, bf16[512,512]{1,0:T(8,128)(2,1)S(1)} %get-tuple-element.15), kind=kOutput, calls=%fused_computation.11 | convolution fusion | flops 1082654720 | bytes 3670016 | tf_op jit(solution)/shard_map/dot_general | solution.py:15
  45.0 2.7 %collective-permute-start.11 = (bf16[2,2,2,32,512]{4,3,1,0,2:T(8,128)(2,1)}, bf16[2,2,2,32,512]{4,3,1,0,2:T(8,128)(2,1)}, u32[]{:S(2)}, u32[]{:S(2)}) collective-permute-start(bf16[2,2,2,32,512]{4,3,1,0,2:T(8,128)(2,1)} %get-tuple-element.25), channel_id=1, source_target_pairs={{0,14},{2,0},{4,2},{6,4},{8,6},{10,8},{12,10},{14,12},{1,15},{3,1}... | collective-permute-start | bytes 786440 | tf_op jit(solution)/shard_map/ppermute | solution.py:35
  47.8 1.0 copy.38
  48.8 13.8 %all-to-all-start = ((bf16[1,16,32,2,512]{4,2,3,0,1:T(8,128)(2,1)}), bf16[1,16,32,2,512]{4,2,3,0,1:T(8,128)(2,1)S(1)}, u32[]{:S(2)}, u32[]{:S(2)}) async-start(bf16[1,16,32,2,512]{4,2,3,0,1:T(8,128)(2,1)} %copy.38), calls=%async_computation | async-start | bytes 2097152 | tf_op jit(solution)/shard_map/all_to_all | solution.py:84
  63.0 2.7 %collective-permute-start.13 = (bf16[2,2,2,32,512]{4,3,1,0,2:T(8,128)(2,1)}, bf16[2,2,2,32,512]{4,3,1,0,2:T(8,128)(2,1)S(1)}, u32[]{:S(2)}, u32[]{:S(2)}) collective-permute-start(bf16[2,2,2,32,512]{4,3,1,0,2:T(8,128)(2,1)} %collective-permute-done.11), channel_id=1, source_target_pairs={{0,14},{2,0},{4,2},{6,4},{8,6},{10,8},{12,10},{14,12},{1,15},{3,1}... | collective-permute-start | bytes 786440 | tf_op jit(solution)/shard_map/ppermute | solution.py:35
  65.7 1.0 copy_dynamic-update-slice_fusion.6
  66.7 1.0 copy_dynamic-update-slice_fusion.5
  67.7 4.5 %collective-permute-done.12 = bf16[2,2,2,32,512]{4,3,1,0,2:T(8,128)(2,1)S(1)} collective-permute-done((bf16[2,2,2,32,512]{4,3,1,0,2:T(8,128)(2,1)}, bf16[2,2,2,32,512]{4,3,1,0,2:T(8,128)(2,1)S(1)}, u32[]{:S(2)}, u32[]{:S(2)}) %collective-permute-start.12) | collective-permute-done | bytes 262176 | tf_op jit(solution)/shard_map/ppermute | solution.py:35
  72.2 2.7 %collective-permute-start.15 = (bf16[2,2,2,32,512]{4,3,1,0,2:T(8,128)(2,1)S(1)}, bf16[2,2,2,32,512]{4,3,1,0,2:T(8,128)(2,1)S(1)}, u32[]{:S(2)}, u32[]{:S(2)}) collective-permute-start(bf16[2,2,2,32,512]{4,3,1,0,2:T(8,128)(2,1)S(1)} %collective-permute-done.13), channel_id=1, source_target_pairs={{0,14},{2,0},{4,2},{6,4},{8,6},{10,8},{12,10},{14,12},{1,15},{3,1}... | collective-permute-start | bytes 786440 | tf_op jit(solution)/shard_map/ppermute | solution.py:35
  74.9 4.4 %collective-permute-done.15 = bf16[2,2,2,32,512]{4,3,1,0,2:T(8,128)(2,1)S(1)} collective-permute-done((bf16[2,2,2,32,512]{4,3,1,0,2:T(8,128)(2,1)S(1)}, bf16[2,2,2,32,512]{4,3,1,0,2:T(8,128)(2,1)S(1)}, u32[]{:S(2)}, u32[]{:S(2)}) %collective-permute-start.15) | collective-permute-done | bytes 262176 | tf_op jit(solution)/shard_map/ppermute | solution.py:35
  79.3 3.5 %collective-permute-start.17 = (bf16[2,2,2,16,512]{4,3,1,0,2:T(8,128)(2,1)S(1)}, bf16[2,2,2,16,512]{4,3,1,0,2:T(8,128)(2,1)S(1)}, u32[]{:S(2)}, u32[]{:S(2)}) collective-permute-start(bf16[2,2,2,16,512]{4,3,1,0,2:T(8,128)(2,1)S(1)} %slice.123), channel_id=1, source_target_pairs={{0,14},{2,0},{4,2},{6,4},{8,6},{10,8},{12,10},{14,12},{1,15},{3,1}... | collective-permute-start | bytes 393224 | tf_op jit(solution)/shard_map/ppermute | solution.py:35
  83.6 2.1 %copy.39 = bf16[1,16,32,2,512]{4,3,2,1,0:T(2,128)(2,1)} copy(bf16[1,16,32,2,512]{4,2,3,0,1:T(8,128)(2,1)S(1)} %all-to-all-done) | data formatting | bytes 2097152 | tf_op jit(solution)/shard_map/all_to_all | solution.py:84
  85.6 2.6 %reshape.161 = bf16[512,1024,1]{1,0,2:T(8,128)(2,1)} reshape(bf16[1,16,32,2,512]{4,3,2,1,0:T(2,128)(2,1)} %copy.39) | data formatting | bytes 2097152 | tf_op jit(solution)/shard_map/reshape;reshape | solution.py:11
  90.0 2.6 %copy.48 = bf16[1024,1024]{1,0:T(8,128)(2,1)} copy(bf16[1024,1024]{0,1:T(8,128)(2,1)S(1)} %maximum_bitcast_fusion) | data formatting | bytes 4194304 | tf_op jit(solution)/shard_map/dot_general | solution.py:15
  92.6 3.2 %fusion.11 = bf16[1,512,2,512]{3,1,2,0:T(8,128)(2,1)S(1)} fusion(bf16[512,1024,1]{1,0,2:T(8,128)(2,1)} %reshape.161, bf16[2,512,1024]{2,1,0:T(8,128)(2,1)} %bitcast.134), kind=kOutput, calls=%fused_computation.13 | convolution fusion | flops 1074266112 | bytes 4194304 | tf_op jit(solution)/shard_map/dot_general | solution.py:15
  97.6 26.6 %all_to_all.10 = bf16[1,512,2,16,32]{1,4,2,0,3:T(8,128)(2,1)S(1)} all-to-all(bf16[1,512,2,16,32]{1,4,2,0,3:T(8,128)(2,1)S(1)} %pad_maximum_fusion.1), channel_id=1, replica_groups=mesh['row'=16,'cz'=8,'cx'=2] {'row'}, dimensions={3} | all-to-all | bytes 2097152 | tf_op jit(solution)/shard_map/all_to_all | solution.py:90
  124.3 2.1 %copy.52 = bf16[1,1,1,512,2,512]{5,4,3,2,1,0:T(2,128)(2,1)} copy(bf16[1,1,1,512,2,512]{3,5,4,2,1,0:T(8,128)(2,1)S(1)} %bitcast.133) | data formatting | bytes 2097152 | tf_op jit(solution)/shard_map/reshape | solution.py:91
  (64 shorter events, 8.5 us)
Async XLA Ops:
  0.0 13.1 %copy-start.2 = (bf16[1,1,1,512,2,512]{5,4,3,2,1,0:T(2,128)(2,1)S(1)}, bf16[1,1,1,512,2,512]{5,4,3,2,1,0:T(2,128)(2,1)}, u32[]{:S(2)}) copy-start(bf16[1,1,1,512,2,512]{5,4,3,2,1,0:T(2,128)(2,1)} %param.2) | copy-start | bytes 3145732
  1.0 4.5 %collective-permute-start = (bf16[2,2,32,512]{3,2,1,0:T(8,128)(2,1)S(1)}, bf16[2,2,32,512]{3,2,1,0:T(8,128)(2,1)S(1)}, u32[]{:S(2)}, u32[]{:S(2)}) collective-permute-start(bf16[2,2,32,512]{3,2,1,0:T(8,128)(2,1)S(1)} %slice.115), channel_id=1, source_target_pairs={{0,1},{1,0},{2,3},{3,2},{4,5},{5,4},{6,7},{7,6},{8,9},{9,8},{10,11... | collective-permute-start | bytes 393224 | tf_op jit(solution)/shard_map/ppermute | solution.py:35
  6.5 11.6 %collective-permute-start.1 = (bf16[2,2,2,32,512]{4,3,2,1,0:T(8,128)(2,1)S(1)}, bf16[2,2,2,32,512]{4,3,2,1,0:T(8,128)(2,1)S(1)}, u32[]{:S(2)}, u32[]{:S(2)}) collective-permute-start(bf16[2,2,2,32,512]{4,3,2,1,0:T(8,128)(2,1)S(1)} %pad_maximum_fusion.2), channel_id=1, source_target_pairs={{0,2},{2,4},{4,6},{6,8},{8,10},{10,12},{12,14},{14,0},{1,3},{3,5},... | collective-permute-start | bytes 786440 | tf_op jit(solution)/shard_map/ppermute | solution.py:35
  9.0 9.1 %collective-permute-start.2 = (bf16[2,2,2,32,512]{4,3,2,1,0:T(8,128)(2,1)S(1)}, bf16[2,2,2,32,512]{4,3,2,1,0:T(8,128)(2,1)S(1)}, u32[]{:S(2)}, u32[]{:S(2)}) collective-permute-start(bf16[2,2,2,32,512]{4,3,2,1,0:T(8,128)(2,1)S(1)} %pad_maximum_fusion.2), channel_id=1, source_target_pairs={{0,14},{2,0},{4,2},{6,4},{8,6},{10,8},{12,10},{14,12},{1,15},{3,1}... | collective-permute-start | bytes 786440 | tf_op jit(solution)/shard_map/ppermute | solution.py:35
  18.1 7.0 %collective-permute-start.3 = (bf16[2,2,2,32,512]{4,3,2,1,0:T(8,128)(2,1)S(1)}, bf16[2,2,2,32,512]{4,3,2,1,0:T(8,128)(2,1)S(1)}, u32[]{:S(2)}, u32[]{:S(2)}) collective-permute-start(bf16[2,2,2,32,512]{4,3,2,1,0:T(8,128)(2,1)S(1)} %collective-permute-done.1), channel_id=1, source_target_pairs={{0,2},{2,4},{4,6},{6,8},{8,10},{10,12},{12,14},{14,0},{1,3},{3,5},... | collective-permute-start | bytes 786440 | tf_op jit(solution)/shard_map/ppermute | solution.py:35
  18.1 7.0 %collective-permute-start.4 = (bf16[2,2,2,32,512]{4,3,2,1,0:T(8,128)(2,1)S(1)}, bf16[2,2,2,32,512]{4,3,2,1,0:T(8,128)(2,1)S(1)}, u32[]{:S(2)}, u32[]{:S(2)}) collective-permute-start(bf16[2,2,2,32,512]{4,3,2,1,0:T(8,128)(2,1)S(1)} %collective-permute-done.2), channel_id=1, source_target_pairs={{0,14},{2,0},{4,2},{6,4},{8,6},{10,8},{12,10},{14,12},{1,15},{3,1}... | collective-permute-start | bytes 786440 | tf_op jit(solution)/shard_map/ppermute | solution.py:35
  25.1 9.2 %collective-permute-start.5 = (bf16[2,2,2,32,512]{4,3,2,1,0:T(8,128)(2,1)S(1)}, bf16[2,2,2,32,512]{4,3,2,1,0:T(8,128)(2,1)S(1)}, u32[]{:S(2)}, u32[]{:S(2)}) collective-permute-start(bf16[2,2,2,32,512]{4,3,2,1,0:T(8,128)(2,1)S(1)} %collective-permute-done.3), channel_id=1, source_target_pairs={{0,2},{2,4},{4,6},{6,8},{8,10},{10,12},{12,14},{14,0},{1,3},{3,5},... | collective-permute-start | bytes 786440 | tf_op jit(solution)/shard_map/ppermute | solution.py:35
  25.1 6.0 %collective-permute-start.6 = (bf16[2,2,2,32,512]{4,3,2,1,0:T(8,128)(2,1)S(1)}, bf16[2,2,2,32,512]{4,3,2,1,0:T(8,128)(2,1)S(1)}, u32[]{:S(2)}, u32[]{:S(2)}) collective-permute-start(bf16[2,2,2,32,512]{4,3,2,1,0:T(8,128)(2,1)S(1)} %collective-permute-done.4), channel_id=1, source_target_pairs={{0,14},{2,0},{4,2},{6,4},{8,6},{10,8},{12,10},{14,12},{1,15},{3,1}... | collective-permute-start | bytes 786440 | tf_op jit(solution)/shard_map/ppermute | solution.py:35
  31.1 5.1 %collective-permute-start.8 = (bf16[2,2,2,16,512]{4,3,2,1,0:T(8,128)(2,1)S(1)}, bf16[2,2,2,16,512]{4,3,2,1,0:T(8,128)(2,1)S(1)}, u32[]{:S(2)}, u32[]{:S(2)}) collective-permute-start(bf16[2,2,2,16,512]{4,3,2,1,0:T(8,128)(2,1)S(1)} %slice.117), channel_id=1, source_target_pairs={{0,14},{2,0},{4,2},{6,4},{8,6},{10,8},{12,10},{14,12},{1,15},{3,1}... | collective-permute-start | bytes 393224 | tf_op jit(solution)/shard_map/ppermute | solution.py:35
  34.3 5.1 %collective-permute-start.7 = (bf16[2,2,2,16,512]{4,3,2,1,0:T(8,128)(2,1)S(1)}, bf16[2,2,2,16,512]{4,3,2,1,0:T(8,128)(2,1)S(1)}, u32[]{:S(2)}, u32[]{:S(2)}) collective-permute-start(bf16[2,2,2,16,512]{4,3,2,1,0:T(8,128)(2,1)S(1)} %slice.116), channel_id=1, source_target_pairs={{0,2},{2,4},{4,6},{6,8},{8,10},{10,12},{12,14},{14,0},{1,3},{3,5},... | collective-permute-start | bytes 393224 | tf_op jit(solution)/shard_map/ppermute | solution.py:35
  39.7 4.6 %collective-permute-start.9 = (bf16[2,2,32,512]{3,2,1,0:T(8,128)(2,1)S(1)}, bf16[2,2,32,512]{3,2,1,0:T(8,128)(2,1)S(1)}, u32[]{:S(2)}, u32[]{:S(2)}) collective-permute-start(bf16[2,2,32,512]{3,2,1,0:T(8,128)(2,1)S(1)} %get-tuple-element.8), channel_id=1, source_target_pairs={{0,1},{1,0},{2,3},{3,2},{4,5},{5,4},{6,7},{7,6},{8,9},{9,8},{10,11... | collective-permute-start | bytes 393224 | tf_op jit(solution)/shard_map/ppermute | solution.py:35
  45.0 17.9 %collective-permute-start.10 = (bf16[2,2,2,32,512]{4,3,1,0,2:T(8,128)(2,1)}, bf16[2,2,2,32,512]{4,3,1,0,2:T(8,128)(2,1)}, u32[]{:S(2)}, u32[]{:S(2)}) collective-permute-start(bf16[2,2,2,32,512]{4,3,1,0,2:T(8,128)(2,1)} %get-tuple-element.25), channel_id=1, source_target_pairs={{0,2},{2,4},{4,6},{6,8},{8,10},{10,12},{12,14},{14,0},{1,3},{3,5},... | collective-permute-start | bytes 786440 | tf_op jit(solution)/shard_map/ppermute | solution.py:35
  45.0 18.0 %collective-permute-start.11 = (bf16[2,2,2,32,512]{4,3,1,0,2:T(8,128)(2,1)}, bf16[2,2,2,32,512]{4,3,1,0,2:T(8,128)(2,1)}, u32[]{:S(2)}, u32[]{:S(2)}) collective-permute-start(bf16[2,2,2,32,512]{4,3,1,0,2:T(8,128)(2,1)} %get-tuple-element.25), channel_id=1, source_target_pairs={{0,14},{2,0},{4,2},{6,4},{8,6},{10,8},{12,10},{14,12},{1,15},{3,1}... | collective-permute-start | bytes 786440 | tf_op jit(solution)/shard_map/ppermute | solution.py:35
  48.8 34.7 %all-to-all-start = ((bf16[1,16,32,2,512]{4,2,3,0,1:T(8,128)(2,1)}), bf16[1,16,32,2,512]{4,2,3,0,1:T(8,128)(2,1)S(1)}, u32[]{:S(2)}, u32[]{:S(2)}) async-start(bf16[1,16,32,2,512]{4,2,3,0,1:T(8,128)(2,1)} %copy.38), calls=%async_computation | async-start | bytes 2097152 | tf_op jit(solution)/shard_map/all_to_all | solution.py:84
  62.9 9.3 %collective-permute-start.12 = (bf16[2,2,2,32,512]{4,3,1,0,2:T(8,128)(2,1)}, bf16[2,2,2,32,512]{4,3,1,0,2:T(8,128)(2,1)S(1)}, u32[]{:S(2)}, u32[]{:S(2)}) collective-permute-start(bf16[2,2,2,32,512]{4,3,1,0,2:T(8,128)(2,1)} %collective-permute-done.10), channel_id=1, source_target_pairs={{0,2},{2,4},{4,6},{6,8},{8,10},{10,12},{12,14},{14,0},{1,3},{3,5},... | collective-permute-start | bytes 786440 | tf_op jit(solution)/shard_map/ppermute | solution.py:35
  63.0 9.2 %collective-permute-start.13 = (bf16[2,2,2,32,512]{4,3,1,0,2:T(8,128)(2,1)}, bf16[2,2,2,32,512]{4,3,1,0,2:T(8,128)(2,1)S(1)}, u32[]{:S(2)}, u32[]{:S(2)}) collective-permute-start(bf16[2,2,2,32,512]{4,3,1,0,2:T(8,128)(2,1)} %collective-permute-done.11), channel_id=1, source_target_pairs={{0,14},{2,0},{4,2},{6,4},{8,6},{10,8},{12,10},{14,12},{1,15},{3,1}... | collective-permute-start | bytes 786440 | tf_op jit(solution)/shard_map/ppermute | solution.py:35
  72.2 10.6 %collective-permute-start.14 = (bf16[2,2,2,32,512]{4,3,1,0,2:T(8,128)(2,1)S(1)}, bf16[2,2,2,32,512]{4,3,1,0,2:T(8,128)(2,1)S(1)}, u32[]{:S(2)}, u32[]{:S(2)}) collective-permute-start(bf16[2,2,2,32,512]{4,3,1,0,2:T(8,128)(2,1)S(1)} %collective-permute-done.12), channel_id=1, source_target_pairs={{0,2},{2,4},{4,6},{6,8},{8,10},{10,12},{12,14},{14,0},{1,3},{3,5},... | collective-permute-start | bytes 786440 | tf_op jit(solution)/shard_map/ppermute | solution.py:35
  72.2 7.1 %collective-permute-start.15 = (bf16[2,2,2,32,512]{4,3,1,0,2:T(8,128)(2,1)S(1)}, bf16[2,2,2,32,512]{4,3,1,0,2:T(8,128)(2,1)S(1)}, u32[]{:S(2)}, u32[]{:S(2)}) collective-permute-start(bf16[2,2,2,32,512]{4,3,1,0,2:T(8,128)(2,1)S(1)} %collective-permute-done.13), channel_id=1, source_target_pairs={{0,14},{2,0},{4,2},{6,4},{8,6},{10,8},{12,10},{14,12},{1,15},{3,1}... | collective-permute-start | bytes 786440 | tf_op jit(solution)/shard_map/ppermute | solution.py:35
  79.3 8.8 %collective-permute-start.17 = (bf16[2,2,2,16,512]{4,3,1,0,2:T(8,128)(2,1)S(1)}, bf16[2,2,2,16,512]{4,3,1,0,2:T(8,128)(2,1)S(1)}, u32[]{:S(2)}, u32[]{:S(2)}) collective-permute-start(bf16[2,2,2,16,512]{4,3,1,0,2:T(8,128)(2,1)S(1)} %slice.123), channel_id=1, source_target_pairs={{0,14},{2,0},{4,2},{6,4},{8,6},{10,8},{12,10},{14,12},{1,15},{3,1}... | collective-permute-start | bytes 393224 | tf_op jit(solution)/shard_map/ppermute | solution.py:35
  83.5 5.2 %collective-permute-start.16 = (bf16[2,2,2,16,512]{4,3,1,0,2:T(8,128)(2,1)}, bf16[2,2,2,16,512]{4,3,1,0,2:T(8,128)(2,1)S(1)}, u32[]{:S(2)}, u32[]{:S(2)}) collective-permute-start(bf16[2,2,2,16,512]{4,3,1,0,2:T(8,128)(2,1)} %slice.122), channel_id=1, source_target_pairs={{0,2},{2,4},{4,6},{6,8},{8,10},{10,12},{12,14},{14,0},{1,3},{3,5},... | collective-permute-start | bytes 393224 | tf_op jit(solution)/shard_map/ppermute | solution.py:35
  88.9 0.8 copy-start
  92.6 3.3 %copy-start.1 = (bf16[1,1,8,2,32,512]{5,4,3,2,1,0:T(8,128)(2,1)S(1)}, bf16[1,1,8,2,32,512]{5,4,3,2,1,0:T(8,128)(2,1)}, u32[]{:S(2)}) copy-start(bf16[1,1,8,2,32,512]{5,4,3,2,1,0:T(8,128)(2,1)} %copy-done) | copy-start | bytes 1572868

commit v3 on v1

--- a/solution.py
+++ b/solution.py
@@ -41,29 +41,49 @@
     z = lax.axis_index("cz")
     x = lax.axis_index("cx")
     nb, comps, width, cols = t.shape
+    hw = width // 2
     other = shift(t, "cx", nx, 1)
     first = jnp.where(x == 0, t, other)
     second = jnp.where(x == 0, other, t)
     pair = jnp.stack([first, second], axis=2)
     buf = jnp.zeros((nb, comps, nz, nx, width, cols), t.dtype)
     buf = lax.dynamic_update_slice(buf, pair[:, :, None], (0, 0, z, 0, 0, 0))
+    payload = jnp.concatenate(
+        [pair[:, :, :, :hw].reshape(nb, comps, nx * hw, cols), t[:, :, hw:]], axis=2
+    )
+
+    def store(buf, piece, zs):
+        shared = piece[:, :, : nx * hw].reshape(nb, comps, 1, nx, hw, cols)
+        buf = lax.dynamic_update_slice(buf, shared, (0, 0, zs, 0, 0, 0))
+        own = piece[:, :, nx * hw :].reshape(nb, comps, 1, 1, hw, cols)
+        return lax.dynamic_update_slice(buf, own, (0, 0, zs, x, hw, 0))
+
+    def store_other(buf, piece, zs):
+        part = piece.reshape(nb, comps, 1, 1, hw, cols)
+        return lax.dynamic_update_slice(buf, part, (0, 0, zs, 1 - x, hw, 0))
+
     forward = nz // 2
-    backward = nz - 1 - forward
-    cur_f = pair
-    cur_b = pair
+    rows = payload.shape[2]
+    cur_f = payload
+    cur_b = payload
     for k in range(1, forward + 1):
-        if k == forward and nz % 2 == 0 and width % 2 == 0:
-            half = width // 2
-            a = shift(cur_f[:, :, :, :half], "cz", nz, 1)
-            b = shift(cur_b[:, :, :, half:], "cz", nz, -1)
-            piece = jnp.concatenate([a, b], axis=3)
-            buf = lax.dynamic_update_slice(buf, piece[:, :, None], (0, 0, (z - k) % nz, 0, 0, 0))
+        if k == forward and nz % 2 == 0:
+            a = shift(cur_f[:, :, : rows // 2], "cz", nz, 1)
+            b = shift(cur_b[:, :, rows // 2 :], "cz", nz, -1)
+            piece = jnp.concatenate([a, b], axis=2)
+            zs = (z - k) % nz
+            buf = store(buf, piece, zs)
+            got = shift(piece[:, :, nx * hw :], "cx", nx, 1)
+            buf = store_other(buf, got, zs)
             break
         cur_f = shift(cur_f, "cz", nz, 1)
-        buf = lax.dynamic_update_slice(buf, cur_f[:, :, None], (0, 0, (z - k) % nz, 0, 0, 0))
-        if k <= backward:
-            cur_b = shift(cur_b, "cz", nz, -1)
-            buf = lax.dynamic_update_slice(buf, cur_b[:, :, None], (0, 0, (z + k) % nz, 0, 0, 0))
+        cur_b = shift(cur_b, "cz", nz, -1)
+        buf = store(buf, cur_f, (z - k) % nz)
+        buf = store(buf, cur_b, (z + k) % nz)
+        sent = jnp.concatenate([cur_f[:, :, nx * hw :], cur_b[:, :, nx * hw :]], axis=2)
+        got = shift(sent, "cx", nx, 1)
+        buf = store_other(buf, got[:, :, :hw], (z - k) % nz)
+        buf = store_other(buf, got[:, :, hw:], (z + k) % nz)
     return buf.reshape(nb, comps, nz * nx * width, cols)
 
 
@@ -73,8 +93,9 @@
     row_count = lax.axis_size("row")
     share = order_size // row_count
     own_t = jnp.swapaxes(branch[0], -1, -2)
-    first_t = ring_gather(own_t[:2])
-    second_t = ring_gather(own_t[2:])
+    whole_t = ring_gather(own_t)
+    first_t = whole_t[:2]
+    second_t = whole_t[2:]
 
     block = stem[0, 0]
     half_first = right_piece(block, first_t[1]).astype(jnp.bfloat16)

time: 119 us -> 123 us (1.034)
  waiting for transfers between devices: 30.9 us -> 42.5 us
  starting transfers between devices: 41.2 us -> 34 us
  local copies, waits for them, and re-layouts: 15.5 us -> 13.4 us
  other arithmetic: 3.02 us -> 4.7 us
    ppermute x18 -> x13, waiting for transfers between devices: 19 us -> 30.3 us  [shift(): return lax.ppermute(x, axis, [(i, (i + d) % n) for i in range(n)])]
    ppermute x18 -> x13, starting transfers between devices: 29.4 us -> 20.9 us  [shift(): return lax.ppermute(x, axis, [(i, (i + d) % n) for i in range(n)])]
    slice x3, local copies, waits for them, and re-layouts: 2.18 us -> 0.35 us  [left_piece(): product[:, :rows_out, :]]
    all_to_all x1, starting transfers between devices: 11.8 us -> 13.1 us  [shards(): lax.all_to_all(outgoing, 'row', split_axis=1, concat_axis=1, tiled=True)]
  transfers between devices with their start and end apart: 19 -> 14, of which waited for: 9 -> 10; matrix products, arithmetic and copies ran while one was open for 6% -> 6% of each run, Pallas kernels for 0% -> 0%
where the time goes in v3:
time: 123 us; the launch traced here: 122 us
  waiting for transfers between devices  42.5 us (35%)
  starting transfers between devices  34 us (28%)
  blocking collectives  20.3 us (17%)
  local copies, waits for them, and re-layouts  13.4 us (11%)
  matrix products  7.09 us (6%)
  other arithmetic  4.7 us (4%)
    ppermute x13, waiting for transfers between devices, shift(): return lax.ppermute(x, axis, [(i, (i + d) % n) for i in range(n)])  30.3 us
    ppermute x13, starting transfers between devices, shift(): return lax.ppermute(x, axis, [(i, (i + d) % n) for i in range(n)])  20.9 us
    all_to_all x1, blocking collectives, shards(): lax.all_to_all(leaving, 'row', split_axis=3, concat_axis=3, tiled=True)  20.3 us
    all_to_all x1, starting transfers between devices, shards(): lax.all_to_all(outgoing, 'row', split_axis=1, concat_axis=1, tiled=True)  13.1 us
    all_to_all x1, waiting for transfers between devices, shards(): lax.all_to_all(outgoing, 'row', split_axis=1, concat_axis=1, tiled=True)  12.2 us
    dot_general x2, matrix products, right_piece(): product = jnp.dot(flat, weight, preferred_element_type=jnp.float32)  4.17 us
    dot_general x1, local copies, waits for them, and re-layouts, right_piece(): product = jnp.dot(flat, weight, preferred_element_type=jnp.float32)  2.57 us
  transfers between devices with their start and end apart: 14, of which 10 were waited for; matrix products, arithmetic and copies ran while one was open for 6% of the time, Pallas kernels for 0%

profile of v3, /device:TPU:1, one launch (start us, length us, event | category | flops | bytes accessed | tf_op | source)
XLA Modules:
  0.0 122.5 jit_solution(15218315627613297754)
XLA Ops:
  0.0 2.0 %collective-permute-start = (bf16[4,2,32,512]{3,2,1,0:T(8,128)(2,1)}, bf16[4,2,32,512]{3,2,1,0:T(8,128)(2,1)S(1)}, u32[]{:S(2)}, u32[]{:S(2)}) collective-permute-start(bf16[4,2,32,512]{3,2,1,0:T(8,128)(2,1)} %bitcast.184), channel_id=1, source_target_pairs={{0,1},{1,0},{2,3},{3,2},{4,5},{5,4},{6,7},{7,6},{8,9},{9,8},{10,11... | collective-permute-start | bytes 786440 | tf_op jit(solution)/shard_map/ppermute | solution.py:35
  2.0 0.9 slice.205
  3.0 4.1 %collective-permute-done = bf16[4,2,32,512]{3,2,1,0:T(8,128)(2,1)S(1)} collective-permute-done((bf16[4,2,32,512]{3,2,1,0:T(8,128)(2,1)}, bf16[4,2,32,512]{3,2,1,0:T(8,128)(2,1)S(1)}, u32[]{:S(2)}, u32[]{:S(2)}) %collective-permute-start) | collective-permute-done | bytes 262176 | tf_op jit(solution)/shard_map/ppermute | solution.py:35
  7.1 1.0 select_bitcast_fusion.1
  8.9 2.7 %collective-permute-start.1 = (bf16[4,2,48,512]{3,2,1,0:T(8,128)(2,1)}, bf16[4,2,48,512]{3,2,1,0:T(8,128)(2,1)S(1)}, u32[]{:S(2)}, u32[]{:S(2)}) collective-permute-start(bf16[4,2,48,512]{3,2,1,0:T(8,128)(2,1)} %pad_maximum_fusion.3), channel_id=1, source_target_pairs={{0,2},{2,4},{4,6},{6,8},{8,10},{10,12},{12,14},{14,0},{1,3},{3,5},... | collective-permute-start | bytes 1179656 | tf_op jit(solution)/shard_map/ppermute | solution.py:35
  11.7 3.9 %collective-permute-start.2 = (bf16[4,2,48,512]{3,2,1,0:T(8,128)(2,1)}, bf16[4,2,48,512]{3,2,1,0:T(8,128)(2,1)S(1)}, u32[]{:S(2)}, u32[]{:S(2)}) collective-permute-start(bf16[4,2,48,512]{3,2,1,0:T(8,128)(2,1)} %pad_maximum_fusion.3), channel_id=1, source_target_pairs={{0,14},{2,0},{4,2},{6,4},{8,6},{10,8},{12,10},{14,12},{1,15},{3,1}... | collective-permute-start | bytes 1179656 | tf_op jit(solution)/shard_map/ppermute | solution.py:35
  16.5 7.3 %collective-permute-done.1 = bf16[4,2,48,512]{3,2,1,0:T(8,128)(2,1)S(1)} collective-permute-done((bf16[4,2,48,512]{3,2,1,0:T(8,128)(2,1)}, bf16[4,2,48,512]{3,2,1,0:T(8,128)(2,1)S(1)}, u32[]{:S(2)}, u32[]{:S(2)}) %collective-permute-start.1) | collective-permute-done | bytes 393248 | tf_op jit(solution)/shard_map/ppermute | solution.py:35
  23.9 1.3 %collective-permute-start.3 = (bf16[4,2,32,512]{3,2,1,0:T(8,128)(2,1)S(1)}, bf16[4,2,32,512]{3,2,1,0:T(8,128)(2,1)S(1)}, u32[]{:S(2)}, u32[]{:S(2)}) collective-permute-start(bf16[4,2,32,512]{3,2,1,0:T(8,128)(2,1)S(1)} %pad_maximum_fusion.5), channel_id=1, source_target_pairs={{0,1},{1,0},{2,3},{3,2},{4,5},{5,4},{6,7},{7,6},{8,9},{9,8},{10,11... | collective-permute-start | bytes 786440 | tf_op jit(solution)/shard_map/ppermute | solution.py:35
  25.4 2.7 %collective-permute-start.5 = (bf16[4,2,48,512]{3,2,1,0:T(8,128)(2,1)S(1)}, bf16[4,2,48,512]{3,2,1,0:T(8,128)(2,1)S(1)}, u32[]{:S(2)}, u32[]{:S(2)}) collective-permute-start(bf16[4,2,48,512]{3,2,1,0:T(8,128)(2,1)S(1)} %collective-permute-done.2), channel_id=1, source_target_pairs={{0,14},{2,0},{4,2},{6,4},{8,6},{10,8},{12,10},{14,12},{1,15},{3,1}... | collective-permute-start | bytes 1179656 | tf_op jit(solution)/shard_map/ppermute | solution.py:35
  28.1 1.6 %collective-permute-done.3 = bf16[4,2,32,512]{3,2,1,0:T(8,128)(2,1)S(1)} collective-permute-done((bf16[4,2,32,512]{3,2,1,0:T(8,128)(2,1)S(1)}, bf16[4,2,32,512]{3,2,1,0:T(8,128)(2,1)S(1)}, u32[]{:S(2)}, u32[]{:S(2)}) %collective-permute-start.3) | collective-permute-done | bytes 262176 | tf_op jit(solution)/shard_map/ppermute | solution.py:35
  29.8 5.1 %collective-permute-done.4 = bf16[4,2,48,512]{3,2,1,0:T(8,128)(2,1)S(1)} collective-permute-done((bf16[4,2,48,512]{3,2,1,0:T(8,128)(2,1)S(1)}, bf16[4,2,48,512]{3,2,1,0:T(8,128)(2,1)S(1)}, u32[]{:S(2)}, u32[]{:S(2)}) %collective-permute-start.4) | collective-permute-done | bytes 393248 | tf_op jit(solution)/shard_map/ppermute | solution.py:35
  35.4 1.1 collective-permute-start.7
  36.5 1.7 %collective-permute-start.8 = (bf16[4,2,48,512]{3,2,1,0:T(8,128)(2,1)S(1)}, bf16[4,2,48,512]{3,2,1,0:T(8,128)(2,1)S(1)}, u32[]{:S(2)}, u32[]{:S(2)}) collective-permute-start(bf16[4,2,48,512]{3,2,1,0:T(8,128)(2,1)S(1)} %collective-permute-done.5), channel_id=1, source_target_pairs={{0,14},{2,0},{4,2},{6,4},{8,6},{10,8},{12,10},{14,12},{1,15},{3,1}... | collective-permute-start | bytes 1179656 | tf_op jit(solution)/shard_map/ppermute | solution.py:35
  38.2 2.1 %collective-permute-done.6 = bf16[4,2,32,512]{3,2,1,0:T(8,128)(2,1)S(1)} collective-permute-done((bf16[4,2,32,512]{3,2,1,0:T(8,128)(2,1)S(1)}, bf16[4,2,32,512]{3,2,1,0:T(8,128)(2,1)S(1)}, u32[]{:S(2)}, u32[]{:S(2)}) %collective-permute-start.6) | collective-permute-done | bytes 262176 | tf_op jit(solution)/shard_map/ppermute | solution.py:35
  40.3 3.6 %collective-permute-done.7 = bf16[4,2,48,512]{3,2,1,0:T(8,128)(2,1)S(1)} collective-permute-done((bf16[4,2,48,512]{3,2,1,0:T(8,128)(2,1)S(1)}, bf16[4,2,48,512]{3,2,1,0:T(8,128)(2,1)S(1)}, u32[]{:S(2)}, u32[]{:S(2)}) %collective-permute-start.7) | collective-permute-done | bytes 393248 | tf_op jit(solution)/shard_map/ppermute | solution.py:35
  43.9 1.3 %collective-permute-start.9 = (bf16[4,2,32,512]{3,2,1,0:T(8,128)(2,1)S(1)}, bf16[4,2,32,512]{3,2,1,0:T(8,128)(2,1)S(1)}, u32[]{:S(2)}, u32[]{:S(2)}) collective-permute-start(bf16[4,2,32,512]{3,2,1,0:T(8,128)(2,1)S(1)} %pad_maximum_fusion.7), channel_id=1, source_target_pairs={{0,1},{1,0},{2,3},{3,2},{4,5},{5,4},{6,7},{7,6},{8,9},{9,8},{10,11... | collective-permute-start | bytes 786440 | tf_op jit(solution)/shard_map/ppermute | solution.py:35
  45.3 2.2 %collective-permute-start.11 = (bf16[4,2,24,512]{3,2,1,0:T(8,128)(2,1)S(1)}, bf16[4,2,24,512]{3,2,1,0:T(8,128)(2,1)S(1)}, u32[]{:S(2)}, u32[]{:S(2)}) collective-permute-start(bf16[4,2,24,512]{3,2,1,0:T(8,128)(2,1)S(1)} %slice.225), channel_id=1, source_target_pairs={{0,14},{2,0},{4,2},{6,4},{8,6},{10,8},{12,10},{14,12},{1,15},{3,1}... | collective-permute-start | bytes 589832 | tf_op jit(solution)/shard_map/ppermute | solution.py:35
  47.7 2.3 %collective-permute-done.11 = bf16[4,2,24,512]{3,2,1,0:T(8,128)(2,1)S(1)} collective-permute-done((bf16[4,2,24,512]{3,2,1,0:T(8,128)(2,1)S(1)}, bf16[4,2,24,512]{3,2,1,0:T(8,128)(2,1)S(1)}, u32[]{:S(2)}, u32[]{:S(2)}) %collective-permute-start.11) | collective-permute-done | bytes 196640 | tf_op jit(solution)/shard_map/ppermute | solution.py:35
  50.1 1.5 %collective-permute-start.12 = (bf16[4,2,16,512]{3,2,1,0:T(8,128)(2,1)S(1)}, bf16[4,2,16,512]{3,2,1,0:T(8,128)(2,1)S(1)}, u32[]{:S(2)}, u32[]{:S(2)}) collective-permute-start(bf16[4,2,16,512]{3,2,1,0:T(8,128)(2,1)S(1)} %slice.226), channel_id=1, source_target_pairs={{0,1},{1,0},{2,3},{3,2},{4,5},{5,4},{6,7},{7,6},{8,9},{9,8},{10,11... | collective-permute-start | bytes 393224 | tf_op jit(solution)/shard_map/ppermute | solution.py:35
  51.6 1.7 %collective-permute-done.10 = bf16[4,2,24,512]{3,2,1,0:T(8,128)(2,1)S(1)} collective-permute-done((bf16[4,2,24,512]{3,2,1,0:T(8,128)(2,1)S(1)}, bf16[4,2,24,512]{3,2,1,0:T(8,128)(2,1)S(1)}, u32[]{:S(2)}, u32[]{:S(2)}) %collective-permute-start.10) | collective-permute-done | bytes 196640 | tf_op jit(solution)/shard_map/ppermute | solution.py:35
  53.4 2.4 %collective-permute-done.12 = bf16[4,2,16,512]{3,2,1,0:T(8,128)(2,1)S(1)} collective-permute-done((bf16[4,2,16,512]{3,2,1,0:T(8,128)(2,1)S(1)}, bf16[4,2,16,512]{3,2,1,0:T(8,128)(2,1)S(1)}, u32[]{:S(2)}, u32[]{:S(2)}) %collective-permute-start.12) | collective-permute-done | bytes 131104 | tf_op jit(solution)/shard_map/ppermute | solution.py:35
  55.9 1.3 %fusion.41 = (bf16[1,1,8,2,32,512]{5,4,3,2,1,0:T(8,128)(2,1)S(1)}, bf16[1,1,8,2,32,512]{5,4,3,2,1,0:T(8,128)(2,1)S(1)}, bf16[1,1,8,2,32,512]{5,4,3,2,1,0:T(8,128...) fusion(bf16[4,2,8,2,32,512]{5,4,3,2,1,0:T(8,128)(2,1)S(1)} %bit, ...), kind=kLoop, calls=%fused_computation.85 | loop fusion | bytes 8388608 | tf_op jit(solution)/shard_map/slice | solution.py:13
  57.3 1.3 %fusion.8 = bf16[1024,512]{1,0:T(8,128)(2,1)S(1)} fusion(bf16[512,1024]{1,0:T(8,128)(2,1)S(1)} %bitcast.183, bf16[512,512]{1,0:T(8,128)(2,1)S(1)} %bitcast.186, bf16[512,512]{1,0:T(8,128)(2,1)S(1)} %get-tuple-element.22, bf16[512,512]{1,0:T(8,128)(2,1)S(1)} %bitcast.167), kind=kOutput, calls=%fused_computation.11 | convolution fusion | flops 1082654720 | bytes 3670016 | tf_op jit(solution)/shard_map/dot_general | solution.py:15
  60.7 1.0 copy.86
  61.7 13.1 %all-to-all-start = ((bf16[1,16,32,2,512]{4,2,3,0,1:T(8,128)(2,1)}), bf16[1,16,32,2,512]{4,2,3,0,1:T(8,128)(2,1)}, u32[]{:S(2)}, u32[]{:S(2)}) async-start(bf16[1,16,32,2,512]{4,2,3,0,1:T(8,128)(2,1)} %copy.86), calls=%async_computation | async-start | bytes 2097152 | tf_op jit(solution)/shard_map/all_to_all | solution.py:104
  75.7 1.5 %maximum_bitcast_fusion = bf16[1024,1024]{0,1:T(8,128)(2,1)S(1)} fusion(bf16[512,512]{1,0:T(8,128)(2,1)} %bitcast.164, bf16[512,512]{1,0:T(8,128)(2,1)S(1)} %get-tuple-element.20, bf16[512,512]{1,0:T(8,128)(2,1)S(1)} %bitcast.159), kind=kLoop, calls=%fused_computation.8 | loop fusion | flops 8388608 | bytes 3670016 | tf_op jit(solution)/shard_map/dot_general | solution.py:15
  77.3 2.6 %copy.88 = bf16[1024,1024]{1,0:T(8,128)(2,1)} copy(bf16[1024,1024]{0,1:T(8,128)(2,1)S(1)} %maximum_bitcast_fusion) | data formatting | bytes 4194304 | tf_op jit(solution)/shard_map/dot_general | solution.py:15
  79.8 12.2 %all-to-all-done = bf16[1,16,32,2,512]{4,2,3,0,1:T(8,128)(2,1)} async-done(((bf16[1,16,32,2,512]{4,2,3,0,1:T(8,128)(2,1)}), bf16[1,16,32,2,512]{4,2,3,0,1:T(8,128)(2,1)}, u32[]{:S(2)}, u32[]{:S(2)}) %all-to-all-start) | async-done | bytes 1048608 | tf_op jit(solution)/shard_map/all_to_all | solution.py:104
  92.0 2.3 %copy.87 = bf16[1,16,32,2,512]{4,3,2,1,0:T(2,128)(2,1)S(1)} copy(bf16[1,16,32,2,512]{4,2,3,0,1:T(8,128)(2,1)} %all-to-all-done) | data formatting | bytes 2097152 | tf_op jit(solution)/shard_map/all_to_all | solution.py:104
  95.1 2.9 %fusion.11 = bf16[1,512,2,512]{3,1,2,0:T(8,128)(2,1)S(1)} fusion(bf16[512,1024,1]{1,0,2:T(8,128)(2,1)S(1)} %reshape.251, bf16[2,512,1024]{2,1,0:T(8,128)(2,1)} %bitcast.165), kind=kOutput, calls=%fused_computation.13 | convolution fusion | flops 1074266112 | bytes 4194304 | tf_op jit(solution)/shard_map/dot_general | solution.py:15
  100.0 20.3 %all_to_all.10 = bf16[1,512,2,16,32]{1,4,2,0,3:T(8,128)(2,1)S(1)} all-to-all(bf16[1,512,2,16,32]{1,4,2,0,3:T(8,128)(2,1)S(1)} %pad_maximum_fusion.1), channel_id=1, replica_groups=mesh['row'=16,'cz'=8,'cx'=2] {'row'}, dimensions={3} | all-to-all | bytes 2097152 | tf_op jit(solution)/shard_map/all_to_all | solution.py:110
  120.4 2.1 %copy.92 = bf16[1,1,1,512,2,512]{5,4,3,2,1,0:T(2,128)(2,1)} copy(bf16[1,1,1,512,2,512]{3,5,4,2,1,0:T(8,128)(2,1)S(1)} %bitcast.161) | data formatting | bytes 2097152 | tf_op jit(solution)/shard_map/reshape | solution.py:111
  (75 shorter events, 8.7 us)
Async XLA Ops:
  0.0 15.6 %copy-start.3 = (bf16[1,1,1,512,2,512]{5,4,3,2,1,0:T(2,128)(2,1)S(1)}, bf16[1,1,1,512,2,512]{5,4,3,2,1,0:T(2,128)(2,1)}, u32[]{:S(2)}) copy-start(bf16[1,1,1,512,2,512]{5,4,3,2,1,0:T(2,128)(2,1)} %param.2) | copy-start | bytes 3145732
  0.0 7.1 %collective-permute-start = (bf16[4,2,32,512]{3,2,1,0:T(8,128)(2,1)}, bf16[4,2,32,512]{3,2,1,0:T(8,128)(2,1)S(1)}, u32[]{:S(2)}, u32[]{:S(2)}) collective-permute-start(bf16[4,2,32,512]{3,2,1,0:T(8,128)(2,1)} %bitcast.184), channel_id=1, source_target_pairs={{0,1},{1,0},{2,3},{3,2},{4,5},{5,4},{6,7},{7,6},{8,9},{9,8},{10,11... | collective-permute-start | bytes 786440 | tf_op jit(solution)/shard_map/ppermute | solution.py:35
  8.9 14.9 %collective-permute-start.1 = (bf16[4,2,48,512]{3,2,1,0:T(8,128)(2,1)}, bf16[4,2,48,512]{3,2,1,0:T(8,128)(2,1)S(1)}, u32[]{:S(2)}, u32[]{:S(2)}) collective-permute-start(bf16[4,2,48,512]{3,2,1,0:T(8,128)(2,1)} %pad_maximum_fusion.3), channel_id=1, source_target_pairs={{0,2},{2,4},{4,6},{6,8},{8,10},{10,12},{12,14},{14,0},{1,3},{3,5},... | collective-permute-start | bytes 1179656 | tf_op jit(solution)/shard_map/ppermute | solution.py:35
  11.7 12.1 %collective-permute-start.2 = (bf16[4,2,48,512]{3,2,1,0:T(8,128)(2,1)}, bf16[4,2,48,512]{3,2,1,0:T(8,128)(2,1)S(1)}, u32[]{:S(2)}, u32[]{:S(2)}) collective-permute-start(bf16[4,2,48,512]{3,2,1,0:T(8,128)(2,1)} %pad_maximum_fusion.3), channel_id=1, source_target_pairs={{0,14},{2,0},{4,2},{6,4},{8,6},{10,8},{12,10},{14,12},{1,15},{3,1}... | collective-permute-start | bytes 1179656 | tf_op jit(solution)/shard_map/ppermute | solution.py:35
  23.9 5.8 %collective-permute-start.3 = (bf16[4,2,32,512]{3,2,1,0:T(8,128)(2,1)S(1)}, bf16[4,2,32,512]{3,2,1,0:T(8,128)(2,1)S(1)}, u32[]{:S(2)}, u32[]{:S(2)}) collective-permute-start(bf16[4,2,32,512]{3,2,1,0:T(8,128)(2,1)S(1)} %pad_maximum_fusion.5), channel_id=1, source_target_pairs={{0,1},{1,0},{2,3},{3,2},{4,5},{5,4},{6,7},{7,6},{8,9},{9,8},{10,11... | collective-permute-start | bytes 786440 | tf_op jit(solution)/shard_map/ppermute | solution.py:35
  25.3 9.6 %collective-permute-start.4 = (bf16[4,2,48,512]{3,2,1,0:T(8,128)(2,1)S(1)}, bf16[4,2,48,512]{3,2,1,0:T(8,128)(2,1)S(1)}, u32[]{:S(2)}, u32[]{:S(2)}) collective-permute-start(bf16[4,2,48,512]{3,2,1,0:T(8,128)(2,1)S(1)} %collective-permute-done.1), channel_id=1, source_target_pairs={{0,2},{2,4},{4,6},{6,8},{8,10},{10,12},{12,14},{14,0},{1,3},{3,5},... | collective-permute-start | bytes 1179656 | tf_op jit(solution)/shard_map/ppermute | solution.py:35
  25.4 9.5 %collective-permute-start.5 = (bf16[4,2,48,512]{3,2,1,0:T(8,128)(2,1)S(1)}, bf16[4,2,48,512]{3,2,1,0:T(8,128)(2,1)S(1)}, u32[]{:S(2)}, u32[]{:S(2)}) collective-permute-start(bf16[4,2,48,512]{3,2,1,0:T(8,128)(2,1)S(1)} %collective-permute-done.2), channel_id=1, source_target_pairs={{0,14},{2,0},{4,2},{6,4},{8,6},{10,8},{12,10},{14,12},{1,15},{3,1}... | collective-permute-start | bytes 1179656 | tf_op jit(solution)/shard_map/ppermute | solution.py:35
  35.0 5.3 %collective-permute-start.6 = (bf16[4,2,32,512]{3,2,1,0:T(8,128)(2,1)S(1)}, bf16[4,2,32,512]{3,2,1,0:T(8,128)(2,1)S(1)}, u32[]{:S(2)}, u32[]{:S(2)}) collective-permute-start(bf16[4,2,32,512]{3,2,1,0:T(8,128)(2,1)S(1)} %pad_maximum_fusion.6), channel_id=1, source_target_pairs={{0,1},{1,0},{2,3},{3,2},{4,5},{5,4},{6,7},{7,6},{8,9},{9,8},{10,11... | collective-permute-start | bytes 786440 | tf_op jit(solution)/shard_map/ppermute | solution.py:35
  35.4 8.4 %collective-permute-start.7 = (bf16[4,2,48,512]{3,2,1,0:T(8,128)(2,1)S(1)}, bf16[4,2,48,512]{3,2,1,0:T(8,128)(2,1)S(1)}, u32[]{:S(2)}, u32[]{:S(2)}) collective-permute-start(bf16[4,2,48,512]{3,2,1,0:T(8,128)(2,1)S(1)} %collective-permute-done.4), channel_id=1, source_target_pairs={{0,2},{2,4},{4,6},{6,8},{8,10},{10,12},{12,14},{14,0},{1,3},{3,5},... | collective-permute-start | bytes 1179656 | tf_op jit(solution)/shard_map/ppermute | solution.py:35
  36.5 7.4 %collective-permute-start.8 = (bf16[4,2,48,512]{3,2,1,0:T(8,128)(2,1)S(1)}, bf16[4,2,48,512]{3,2,1,0:T(8,128)(2,1)S(1)}, u32[]{:S(2)}, u32[]{:S(2)}) collective-permute-start(bf16[4,2,48,512]{3,2,1,0:T(8,128)(2,1)S(1)} %collective-permute-done.5), channel_id=1, source_target_pairs={{0,14},{2,0},{4,2},{6,4},{8,6},{10,8},{12,10},{14,12},{1,15},{3,1}... | collective-permute-start | bytes 1179656 | tf_op jit(solution)/shard_map/ppermute | solution.py:35
  43.9 9.4 %collective-permute-start.9 = (bf16[4,2,32,512]{3,2,1,0:T(8,128)(2,1)S(1)}, bf16[4,2,32,512]{3,2,1,0:T(8,128)(2,1)S(1)}, u32[]{:S(2)}, u32[]{:S(2)}) collective-permute-start(bf16[4,2,32,512]{3,2,1,0:T(8,128)(2,1)S(1)} %pad_maximum_fusion.7), channel_id=1, source_target_pairs={{0,1},{1,0},{2,3},{3,2},{4,5},{5,4},{6,7},{7,6},{8,9},{9,8},{10,11... | collective-permute-start | bytes 786440 | tf_op jit(solution)/shard_map/ppermute | solution.py:35
  45.3 4.8 %collective-permute-start.11 = (bf16[4,2,24,512]{3,2,1,0:T(8,128)(2,1)S(1)}, bf16[4,2,24,512]{3,2,1,0:T(8,128)(2,1)S(1)}, u32[]{:S(2)}, u32[]{:S(2)}) collective-permute-start(bf16[4,2,24,512]{3,2,1,0:T(8,128)(2,1)S(1)} %slice.225), channel_id=1, source_target_pairs={{0,14},{2,0},{4,2},{6,4},{8,6},{10,8},{12,10},{14,12},{1,15},{3,1}... | collective-permute-start | bytes 589832 | tf_op jit(solution)/shard_map/ppermute | solution.py:35
  47.5 5.8 %collective-permute-start.10 = (bf16[4,2,24,512]{3,2,1,0:T(8,128)(2,1)S(1)}, bf16[4,2,24,512]{3,2,1,0:T(8,128)(2,1)S(1)}, u32[]{:S(2)}, u32[]{:S(2)}) collective-permute-start(bf16[4,2,24,512]{3,2,1,0:T(8,128)(2,1)S(1)} %slice.224), channel_id=1, source_target_pairs={{0,2},{2,4},{4,6},{6,8},{8,10},{10,12},{12,14},{14,0},{1,3},{3,5},... | collective-permute-start | bytes 589832 | tf_op jit(solution)/shard_map/ppermute | solution.py:35
  50.1 5.8 %collective-permute-start.12 = (bf16[4,2,16,512]{3,2,1,0:T(8,128)(2,1)S(1)}, bf16[4,2,16,512]{3,2,1,0:T(8,128)(2,1)S(1)}, u32[]{:S(2)}, u32[]{:S(2)}) collective-permute-start(bf16[4,2,16,512]{3,2,1,0:T(8,128)(2,1)S(1)} %slice.226), channel_id=1, source_target_pairs={{0,1},{1,0},{2,3},{3,2},{4,5},{5,4},{6,7},{7,6},{8,9},{9,8},{10,11... | collective-permute-start | bytes 393224 | tf_op jit(solution)/shard_map/ppermute | solution.py:35
  57.2 17.6 %copy-start = (bf16[1,1,8,2,32,512]{5,4,3,2,1,0:T(8,128)(2,1)}, bf16[1,1,8,2,32,512]{5,4,3,2,1,0:T(8,128)(2,1)S(1)}, u32[]{:S(2)}) copy-start(bf16[1,1,8,2,32,512]{5,4,3,2,1,0:T(8,128)(2,1)S(1)} %get-tuple-element.6) | copy-start | bytes 1572868
  61.7 30.3 %all-to-all-start = ((bf16[1,16,32,2,512]{4,2,3,0,1:T(8,128)(2,1)}), bf16[1,16,32,2,512]{4,2,3,0,1:T(8,128)(2,1)}, u32[]{:S(2)}, u32[]{:S(2)}) async-start(bf16[1,16,32,2,512]{4,2,3,0,1:T(8,128)(2,1)} %copy.86), calls=%async_computation | async-start | bytes 2097152 | tf_op jit(solution)/shard_map/all_to_all | solution.py:104
  94.3 3.7 %copy-start.1 = (bf16[1,1,8,2,32,512]{5,4,3,2,1,0:T(8,128)(2,1)S(1)}, bf16[1,1,8,2,32,512]{5,4,3,2,1,0:T(8,128)(2,1)}, u32[]{:S(2)}) copy-start(bf16[1,1,8,2,32,512]{5,4,3,2,1,0:T(8,128)(2,1)} %copy-done) | copy-start | bytes 1572868
  98.0 1.0 copy-start.2

commit v4 on v1

--- a/solution.py
+++ b/solution.py
@@ -14,6 +14,28 @@
     weight = jnp.block([[real_t, imag_t], [-imag_t, real_t]])
     product = jnp.dot(flat, weight, preferred_element_type=jnp.float32)
     return product.reshape(items, order_size, 2, order_size)
+
+
+def right_planar(planar, piece_t):
+    real_t = piece_t[0]
+    imag_t = piece_t[1]
+    top = jnp.concatenate([real_t, imag_t], axis=1)
+    bottom = jnp.concatenate([-imag_t, real_t], axis=1)
+    product = jnp.dot(planar[0], top, preferred_element_type=jnp.float32)
+    product = product + jnp.dot(planar[1], bottom, preferred_element_type=jnp.float32)
+    return product.reshape(planar.shape[1], 2, piece_t.shape[2])
+
+
+def left_planar(block, piece_t):
+    real_w = piece_t[0]
+    imag_w = piece_t[1]
+    weight_real = jnp.concatenate([real_w, imag_w], axis=1)
+    weight_imag = jnp.concatenate([-imag_w, real_w], axis=1)
+    product = jnp.einsum("ix,ij->xj", weight_real, block[:, 0, :], preferred_element_type=jnp.float32)
+    product = product + jnp.einsum(
+        "ix,ij->xj", weight_imag, block[:, 1, :], preferred_element_type=jnp.float32
+    )
+    return product.reshape(2, piece_t.shape[2], block.shape[2])
 
 
 def left_piece(block, piece_t):
@@ -78,12 +100,11 @@
 
     block = stem[0, 0]
     half_first = right_piece(block, first_t[1]).astype(jnp.bfloat16)
-    step_first = left_piece(half_first, first_t[0]).astype(jnp.bfloat16)
-    outgoing = step_first.reshape(slab_count, row_count, share, 2, order_size)
+    step_first = left_planar(half_first[0], first_t[0]).astype(jnp.bfloat16)
+    outgoing = step_first.reshape(2, row_count, share, order_size)
     moved = lax.all_to_all(outgoing, "row", split_axis=1, concat_axis=1, tiled=True)
-    items = moved.shape[0]
-    flat = moved.reshape(items, order_size, 2, order_size)
-    half_second = right_piece(flat, second_t[1]).astype(jnp.bfloat16)
+    planar = moved.reshape(2, order_size, order_size)
+    half_second = right_planar(planar, second_t[1]).astype(jnp.bfloat16)[None]
     step_second = left_piece(half_second, second_t[0]).astype(jnp.bfloat16)
     leaving = step_second.reshape(slab_count, order_size, 2, row_count, share)
     arrived = lax.all_to_all(leaving, "row", split_axis=3, concat_axis=3, tiled=True)

time: 119 us -> 114 us (0.958)
  local copies, waits for them, and re-layouts: 15.5 us -> 12.4 us
  waiting for transfers between devices: 30.9 us -> 33.6 us
  other arithmetic: 3.02 us -> 1.38 us
  matrix products: 7.16 us -> 5.72 us
    dot_general x2 -> x1, matrix products: 4.27 us -> 1.31 us  [right_piece(): product = jnp.dot(flat, weight, preferred_element_type=jnp.float32)]
    dot_general x0 -> x4, matrix products: none -> 2.95 us  [the longest x1 0.76 us: left_planar(): jnp.einsum('ix,ij->xj', weight_imag, block[:, 1, :], preferred_element_ty...]
    slice x1 -> x3, local copies, waits for them, and re-layouts: 1 us -> 3.78 us  [the longest x1 1.5 us: left_piece(): imag_in = block[:, :, 1, :]]
    all_to_all x1, waiting for transfers between devices: 11.9 us -> 14.5 us  [shards(): lax.all_to_all(outgoing, 'row', split_axis=1, concat_axis=1, tiled=True)]
    dot_general x1 -> x0, local copies, waits for them, and re-layouts: 2.59 us -> none  [right_piece(): product = jnp.dot(flat, weight, preferred_element_type=jnp.float32)]
    slice x3 -> x1, local copies, waits for them, and re-layouts: 2.18 us -> 0.07 us  [left_piece(): product[:, :rows_out, :]]
    convert_element_type x0 -> x2, local copies, waits for them, and re-layouts: none -> 1.83 us  [the longest x1 1.04 us: shards(): step_first = left_planar(half_first[0], first_t[0]).astype(jnp.bfloat16)]
    another operation x4 -> x2, local copies, waits for them, and re-layouts: 2.3 us -> 0.48 us  [the longest x1 1.05 us: left_piece(): jnp.stack([product[:, :rows_out, :], product[:, rows_out:, :]], axis=2)]
  transfers between devices with their start and end apart: 19 -> 19, of which waited for: 9 -> 9; matrix products, arithmetic and copies ran while one was open for 6% -> 4% of each run, Pallas kernels for 0% -> 0%
where the time goes in v4:
time: 114 us
  starting transfers between devices  40.2 us (35%)
  waiting for transfers between devices  33.6 us (29%)
  blocking collectives  20.3 us (18%)
  local copies, waits for them, and re-layouts  12.4 us (11%)
  matrix products  5.72 us (5%)
  other arithmetic  1.38 us (1%)
    ppermute x18, starting transfers between devices, shift(): return lax.ppermute(x, axis, [(i, (i + d) % n) for i in range(n)])  29.4 us
    all_to_all x1, blocking collectives, shards(): lax.all_to_all(leaving, 'row', split_axis=3, concat_axis=3, tiled=True)  20.3 us
    ppermute x18, waiting for transfers between devices, shift(): return lax.ppermute(x, axis, [(i, (i + d) % n) for i in range(n)])  19.1 us
    all_to_all x1, waiting for transfers between devices, shards(): lax.all_to_all(outgoing, 'row', split_axis=1, concat_axis=1, tiled=True)  14.5 us
    all_to_all x1, starting transfers between devices, shards(): lax.all_to_all(outgoing, 'row', split_axis=1, concat_axis=1, tiled=True)  10.8 us
    unnamed x11, local copies, waits for them, and re-layouts  2.5 us
  transfers between devices with their start and end apart: 19, of which 9 were waited for; matrix products, arithmetic and copies ran while one was open for 4% of the time, Pallas kernels for 0%

profile of v4, /device:TPU:1, one launch (start us, length us, event | category | flops | bytes accessed | tf_op | source)
XLA Modules:
  0.0 114.1 jit_solution(12041863038145519145)
XLA Ops:
  0.0 1.0 slice.116
  1.0 2.1 %collective-permute-start = (bf16[2,2,32,512]{3,2,1,0:T(8,128)(2,1)S(1)}, bf16[2,2,32,512]{3,2,1,0:T(8,128)(2,1)S(1)}, u32[]{:S(2)}, u32[]{:S(2)}) collective-permute-start(bf16[2,2,32,512]{3,2,1,0:T(8,128)(2,1)S(1)} %slice.116), channel_id=1, source_target_pairs={{0,1},{1,0},{2,3},{3,2},{4,5},{5,4},{6,7},{7,6},{8,9},{9,8},{10,11... | collective-permute-start | bytes 393224 | tf_op jit(solution)/shard_map/ppermute | solution.py:57
  3.1 1.5 %copy.16 = bf16[64,8,2,512]{3,1,2,0:T(8,128)(2,1)S(1)} copy(bf16[64,8,2,512]{3,2,1,0:T(2,128)(2,1)} %bitcast.110) | data formatting | bytes 2097152
  4.6 0.8 collective-permute-done
  5.5 1.9 %collective-permute-start.9 = (bf16[2,2,32,512]{3,2,1,0:T(8,128)(2,1)S(1)}, bf16[2,2,32,512]{3,2,1,0:T(8,128)(2,1)S(1)}, u32[]{:S(2)}, u32[]{:S(2)}) collective-permute-start(bf16[2,2,32,512]{3,2,1,0:T(8,128)(2,1)S(1)} %get-tuple-element.23), channel_id=1, source_target_pairs={{0,1},{1,0},{2,3},{3,2},{4,5},{5,4},{6,7},{7,6},{8,9},{9,8},{10,11... | collective-permute-start | bytes 393224 | tf_op jit(solution)/shard_map/ppermute | solution.py:57
  7.4 1.9 %collective-permute-start.1 = (bf16[2,2,2,32,512]{4,3,1,0,2:T(8,128)(2,1)S(1)}, bf16[2,2,2,32,512]{4,3,1,0,2:T(8,128)(2,1)S(1)}, u32[]{:S(2)}, u32[]{:S(2)}) collective-permute-start(bf16[2,2,2,32,512]{4,3,1,0,2:T(8,128)(2,1)S(1)} %pad_maximum_fusion.1), channel_id=1, source_target_pairs={{0,2},{2,4},{4,6},{6,8},{8,10},{10,12},{12,14},{14,0},{1,3},{3,5},... | collective-permute-start | bytes 786440 | tf_op jit(solution)/shard_map/ppermute | solution.py:57
  9.4 4.0 %collective-permute-start.2 = (bf16[2,2,2,32,512]{4,3,1,0,2:T(8,128)(2,1)S(1)}, bf16[2,2,2,32,512]{4,3,1,0,2:T(8,128)(2,1)S(1)}, u32[]{:S(2)}, u32[]{:S(2)}) collective-permute-start(bf16[2,2,2,32,512]{4,3,1,0,2:T(8,128)(2,1)S(1)} %pad_maximum_fusion.1), channel_id=1, source_target_pairs={{0,14},{2,0},{4,2},{6,4},{8,6},{10,8},{12,10},{14,12},{1,15},{3,1}... | collective-permute-start | bytes 786440 | tf_op jit(solution)/shard_map/ppermute | solution.py:57
  13.8 2.7 %collective-permute-start.11 = (bf16[2,2,2,32,512]{4,3,1,0,2:T(8,128)(2,1)S(1)}, bf16[2,2,2,32,512]{4,3,1,0,2:T(8,128)(2,1)S(1)}, u32[]{:S(2)}, u32[]{:S(2)}) collective-permute-start(bf16[2,2,2,32,512]{4,3,1,0,2:T(8,128)(2,1)S(1)} %pad_maximum_fusion.2), channel_id=1, source_target_pairs={{0,14},{2,0},{4,2},{6,4},{8,6},{10,8},{12,10},{14,12},{1,15},{3,1}... | collective-permute-start | bytes 786440 | tf_op jit(solution)/shard_map/ppermute | solution.py:57
  16.8 1.4 %collective-permute-done.1 = bf16[2,2,2,32,512]{4,3,1,0,2:T(8,128)(2,1)S(1)} collective-permute-done((bf16[2,2,2,32,512]{4,3,1,0,2:T(8,128)(2,1)S(1)}, bf16[2,2,2,32,512]{4,3,1,0,2:T(8,128)(2,1)S(1)}, u32[]{:S(2)}, u32[]{:S(2)}) %collective-permute-start.1) | collective-permute-done | bytes 262176 | tf_op jit(solution)/shard_map/ppermute | solution.py:57
  18.2 2.7 %collective-permute-start.4 = (bf16[2,2,2,32,512]{4,3,1,0,2:T(8,128)(2,1)S(1)}, bf16[2,2,2,32,512]{4,3,1,0,2:T(8,128)(2,1)S(1)}, u32[]{:S(2)}, u32[]{:S(2)}) collective-permute-start(bf16[2,2,2,32,512]{4,3,1,0,2:T(8,128)(2,1)S(1)} %collective-permute-done.2), channel_id=1, source_target_pairs={{0,14},{2,0},{4,2},{6,4},{8,6},{10,8},{12,10},{14,12},{1,15},{3,1}... | collective-permute-start | bytes 786440 | tf_op jit(solution)/shard_map/ppermute | solution.py:57
  20.9 2.9 %collective-permute-done.10 = bf16[2,2,2,32,512]{4,3,1,0,2:T(8,128)(2,1)S(1)} collective-permute-done((bf16[2,2,2,32,512]{4,3,1,0,2:T(8,128)(2,1)S(1)}, bf16[2,2,2,32,512]{4,3,1,0,2:T(8,128)(2,1)S(1)}, u32[]{:S(2)}, u32[]{:S(2)}) %collective-permute-start.10) | collective-permute-done | bytes 262176 | tf_op jit(solution)/shard_map/ppermute | solution.py:57
  23.8 2.7 %collective-permute-start.13 = (bf16[2,2,2,32,512]{4,3,1,0,2:T(8,128)(2,1)S(1)}, bf16[2,2,2,32,512]{4,3,1,0,2:T(8,128)(2,1)S(1)}, u32[]{:S(2)}, u32[]{:S(2)}) collective-permute-start(bf16[2,2,2,32,512]{4,3,1,0,2:T(8,128)(2,1)S(1)} %collective-permute-done.11), channel_id=1, source_target_pairs={{0,14},{2,0},{4,2},{6,4},{8,6},{10,8},{12,10},{14,12},{1,15},{3,1}... | collective-permute-start | bytes 786440 | tf_op jit(solution)/shard_map/ppermute | solution.py:57
  26.6 2.8 %collective-permute-done.3 = bf16[2,2,2,32,512]{4,3,1,0,2:T(8,128)(2,1)S(1)} collective-permute-done((bf16[2,2,2,32,512]{4,3,1,0,2:T(8,128)(2,1)S(1)}, bf16[2,2,2,32,512]{4,3,1,0,2:T(8,128)(2,1)S(1)}, u32[]{:S(2)}, u32[]{:S(2)}) %collective-permute-start.3) | collective-permute-done | bytes 262176 | tf_op jit(solution)/shard_map/ppermute | solution.py:57
  29.4 2.7 %collective-permute-start.6 = (bf16[2,2,2,32,512]{4,3,1,0,2:T(8,128)(2,1)S(1)}, bf16[2,2,2,32,512]{4,3,1,0,2:T(8,128)(2,1)S(1)}, u32[]{:S(2)}, u32[]{:S(2)}) collective-permute-start(bf16[2,2,2,32,512]{4,3,1,0,2:T(8,128)(2,1)S(1)} %collective-permute-done.4), channel_id=1, source_target_pairs={{0,14},{2,0},{4,2},{6,4},{8,6},{10,8},{12,10},{14,12},{1,15},{3,1}... | collective-permute-start | bytes 786440 | tf_op jit(solution)/shard_map/ppermute | solution.py:57
  32.1 2.9 %collective-permute-done.12 = bf16[2,2,2,32,512]{4,3,1,0,2:T(8,128)(2,1)S(1)} collective-permute-done((bf16[2,2,2,32,512]{4,3,1,0,2:T(8,128)(2,1)S(1)}, bf16[2,2,2,32,512]{4,3,1,0,2:T(8,128)(2,1)S(1)}, u32[]{:S(2)}, u32[]{:S(2)}) %collective-permute-start.12) | collective-permute-done | bytes 262176 | tf_op jit(solution)/shard_map/ppermute | solution.py:57
  35.1 2.7 %collective-permute-start.15 = (bf16[2,2,2,32,512]{4,3,1,0,2:T(8,128)(2,1)S(1)}, bf16[2,2,2,32,512]{4,3,1,0,2:T(8,128)(2,1)S(1)}, u32[]{:S(2)}, u32[]{:S(2)}) collective-permute-start(bf16[2,2,2,32,512]{4,3,1,0,2:T(8,128)(2,1)S(1)} %collective-permute-done.13), channel_id=1, source_target_pairs={{0,14},{2,0},{4,2},{6,4},{8,6},{10,8},{12,10},{14,12},{1,15},{3,1}... | collective-permute-start | bytes 786440 | tf_op jit(solution)/shard_map/ppermute | solution.py:57
  37.8 2.8 %collective-permute-done.5 = bf16[2,2,2,32,512]{4,3,1,0,2:T(8,128)(2,1)S(1)} collective-permute-done((bf16[2,2,2,32,512]{4,3,1,0,2:T(8,128)(2,1)S(1)}, bf16[2,2,2,32,512]{4,3,1,0,2:T(8,128)(2,1)S(1)}, u32[]{:S(2)}, u32[]{:S(2)}) %collective-permute-start.5) | collective-permute-done | bytes 262176 | tf_op jit(solution)/shard_map/ppermute | solution.py:57
  40.8 2.9 %collective-permute-start.8 = (bf16[2,2,2,16,512]{4,3,1,0,2:T(8,128)(2,1)S(1)}, bf16[2,2,2,16,512]{4,3,1,0,2:T(8,128)(2,1)S(1)}, u32[]{:S(2)}, u32[]{:S(2)}) collective-permute-start(bf16[2,2,2,16,512]{4,3,1,0,2:T(8,128)(2,1)S(1)} %slice.118), channel_id=1, source_target_pairs={{0,14},{2,0},{4,2},{6,4},{8,6},{10,8},{12,10},{14,12},{1,15},{3,1}... | collective-permute-start | bytes 393224 | tf_op jit(solution)/shard_map/ppermute | solution.py:57
  43.7 2.5 %collective-permute-done.14 = bf16[2,2,2,32,512]{4,3,1,0,2:T(8,128)(2,1)S(1)} collective-permute-done((bf16[2,2,2,32,512]{4,3,1,0,2:T(8,128)(2,1)S(1)}, bf16[2,2,2,32,512]{4,3,1,0,2:T(8,128)(2,1)S(1)}, u32[]{:S(2)}, u32[]{:S(2)}) %collective-permute-start.14) | collective-permute-done | bytes 262176 | tf_op jit(solution)/shard_map/ppermute | solution.py:57
  46.4 2.7 %collective-permute-start.17 = (bf16[2,2,2,16,512]{4,3,1,0,2:T(8,128)(2,1)S(1)}, bf16[2,2,2,16,512]{4,3,1,0,2:T(8,128)(2,1)S(1)}, u32[]{:S(2)}, u32[]{:S(2)}) collective-permute-start(bf16[2,2,2,16,512]{4,3,1,0,2:T(8,128)(2,1)S(1)} %slice.128), channel_id=1, source_target_pairs={{0,14},{2,0},{4,2},{6,4},{8,6},{10,8},{12,10},{14,12},{1,15},{3,1}... | collective-permute-start | bytes 393224 | tf_op jit(solution)/shard_map/ppermute | solution.py:57
  49.2 3.0 %collective-permute-done.16 = bf16[2,2,2,16,512]{4,3,1,0,2:T(8,128)(2,1)S(1)} collective-permute-done((bf16[2,2,2,16,512]{4,3,1,0,2:T(8,128)(2,1)S(1)}, bf16[2,2,2,16,512]{4,3,1,0,2:T(8,128)(2,1)S(1)}, u32[]{:S(2)}, u32[]{:S(2)}) %collective-permute-start.16) | collective-permute-done | bytes 131104 | tf_op jit(solution)/shard_map/ppermute | solution.py:57
  52.6 1.3 %fusion.8 = bf16[1024,512]{1,0:T(8,128)(2,1)S(1)} fusion(bf16[512,1024]{1,0:T(8,128)(2,1)S(1)} %bitcast.111, bf16[512,512]{1,0:T(8,128)(2,1)S(1)} %bitcast.115, bf16[512,512]{1,0:T(8,128)(2,1)S(1)} %bitcast_negate_fusion.2, bf16[512,512]{1,0:T(8,128)(2,1)S(1)} %bitcast.109), kind=kOutput, calls=%fused_computation.11 | convolution fusion | flops 1082654720 | bytes 3670016 | tf_op jit(solution)/shard_map/dot_general | solution.py:15
  55.5 1.0 copy.7
  56.5 10.8 %all-to-all-start = ((bf16[2,16,32,512]{3,2,0,1:T(8,128)(2,1)}), bf16[2,16,32,512]{3,2,0,1:T(8,128)(2,1)}, u32[]{:S(2)}, u32[]{:S(2)}) async-start(bf16[2,16,32,512]{3,2,0,1:T(8,128)(2,1)} %copy.7), calls=%async_computation | async-start | bytes 2097152 | tf_op jit(solution)/shard_map/all_to_all | solution.py:105
  67.3 1.0 fusion.42
  69.1 0.9 bitcast_negate_fusion
  70.0 14.5 %all-to-all-done = bf16[2,16,32,512]{3,2,0,1:T(8,128)(2,1)} async-done(((bf16[2,16,32,512]{3,2,0,1:T(8,128)(2,1)}), bf16[2,16,32,512]{3,2,0,1:T(8,128)(2,1)}, u32[]{:S(2)}, u32[]{:S(2)}) %all-to-all-start) | async-done | bytes 1048608 | tf_op jit(solution)/shard_map/all_to_all | solution.py:105
  84.5 1.3 %fusion.46 = (bf16[1,16,32,512]{3,2,0,1:T(8,128)(2,1)S(1)}, bf16[1,16,32,512]{3,2,0,1:T(8,128)(2,1)S(1)}) fusion(bf16[2,16,32,512]{3,2,0,1:T(8,128)(2,1)} %all-to-all-done), kind=kLoop, calls=%fused_computation.78 | loop fusion | bytes 2097152 | tf_op jit(solution)/shard_map/slice | solution.py:25
  87.2 0.8 convert_element_type.48
  88.0 1.5 %fusion.45 = (bf16[1,512,1,512]{3,2,1,0:T(2,128)(2,1)S(1)}, bf16[1,512,1,512]{3,2,1,0:T(2,128)(2,1)S(1)}) fusion(bf16[1,512,2,512]{3,2,1,0:T(2,128)(2,1)S(1)} %convert_element_type.48), kind=kLoop, calls=%fused_computation.77 | loop fusion | bytes 2097152 | tf_op jit(solution)/shard_map/slice | solution.py:44
  91.5 20.3 %all_to_all.10 = bf16[1,512,2,16,32]{1,4,2,0,3:T(8,128)(2,1)S(1)} all-to-all(bf16[1,512,2,16,32]{1,4,2,0,3:T(8,128)(2,1)S(1)} %pad_maximum_fusion), channel_id=1, replica_groups=mesh['row'=16,'cz'=8,'cx'=2] {'row'}, dimensions={3} | all-to-all | bytes 2097152 | tf_op jit(solution)/shard_map/all_to_all | solution.py:110
  112.0 2.1 %copy.13 = bf16[1,1,1,512,2,512]{5,4,3,2,1,0:T(2,128)(2,1)} copy(bf16[1,1,1,512,2,512]{3,5,4,2,1,0:T(8,128)(2,1)S(1)} %bitcast.97) | data formatting | bytes 2097152 | tf_op jit(solution)/shard_map/reshape | solution.py:111
  (65 shorter events, 7.4 us)
Async XLA Ops:
  0.0 5.5 %copy-start.4 = (bf16[1,4,2,512,32]{3,4,2,1,0:T(8,128)(2,1)S(1)}, bf16[1,4,2,512,32]{3,4,2,1,0:T(8,128)(2,1)}, u32[]{:S(2)}) copy-start(bf16[1,4,2,512,32]{3,4,2,1,0:T(8,128)(2,1)} %param.3) | copy-start | bytes 786436
  1.0 4.5 %collective-permute-start = (bf16[2,2,32,512]{3,2,1,0:T(8,128)(2,1)S(1)}, bf16[2,2,32,512]{3,2,1,0:T(8,128)(2,1)S(1)}, u32[]{:S(2)}, u32[]{:S(2)}) collective-permute-start(bf16[2,2,32,512]{3,2,1,0:T(8,128)(2,1)S(1)} %slice.116), channel_id=1, source_target_pairs={{0,1},{1,0},{2,3},{3,2},{4,5},{5,4},{6,7},{7,6},{8,9},{9,8},{10,11... | collective-permute-start | bytes 393224 | tf_op jit(solution)/shard_map/ppermute | solution.py:57
  5.5 8.2 %collective-permute-start.9 = (bf16[2,2,32,512]{3,2,1,0:T(8,128)(2,1)S(1)}, bf16[2,2,32,512]{3,2,1,0:T(8,128)(2,1)S(1)}, u32[]{:S(2)}, u32[]{:S(2)}) collective-permute-start(bf16[2,2,32,512]{3,2,1,0:T(8,128)(2,1)S(1)} %get-tuple-element.23), channel_id=1, source_target_pairs={{0,1},{1,0},{2,3},{3,2},{4,5},{5,4},{6,7},{7,6},{8,9},{9,8},{10,11... | collective-permute-start | bytes 393224 | tf_op jit(solution)/shard_map/ppermute | solution.py:57
  7.4 10.8 %collective-permute-start.1 = (bf16[2,2,2,32,512]{4,3,1,0,2:T(8,128)(2,1)S(1)}, bf16[2,2,2,32,512]{4,3,1,0,2:T(8,128)(2,1)S(1)}, u32[]{:S(2)}, u32[]{:S(2)}) collective-permute-start(bf16[2,2,2,32,512]{4,3,1,0,2:T(8,128)(2,1)S(1)} %pad_maximum_fusion.1), channel_id=1, source_target_pairs={{0,2},{2,4},{4,6},{6,8},{8,10},{10,12},{12,14},{14,0},{1,3},{3,5},... | collective-permute-start | bytes 786440 | tf_op jit(solution)/shard_map/ppermute | solution.py:57
  9.4 8.8 %collective-permute-start.2 = (bf16[2,2,2,32,512]{4,3,1,0,2:T(8,128)(2,1)S(1)}, bf16[2,2,2,32,512]{4,3,1,0,2:T(8,128)(2,1)S(1)}, u32[]{:S(2)}, u32[]{:S(2)}) collective-permute-start(bf16[2,2,2,32,512]{4,3,1,0,2:T(8,128)(2,1)S(1)} %pad_maximum_fusion.1), channel_id=1, source_target_pairs={{0,14},{2,0},{4,2},{6,4},{8,6},{10,8},{12,10},{14,12},{1,15},{3,1}... | collective-permute-start | bytes 786440 | tf_op jit(solution)/shard_map/ppermute | solution.py:57
  13.7 10.0 %collective-permute-start.10 = (bf16[2,2,2,32,512]{4,3,1,0,2:T(8,128)(2,1)S(1)}, bf16[2,2,2,32,512]{4,3,1,0,2:T(8,128)(2,1)S(1)}, u32[]{:S(2)}, u32[]{:S(2)}) collective-permute-start(bf16[2,2,2,32,512]{4,3,1,0,2:T(8,128)(2,1)S(1)} %pad_maximum_fusion.2), channel_id=1, source_target_pairs={{0,2},{2,4},{4,6},{6,8},{8,10},{10,12},{12,14},{14,0},{1,3},{3,5},... | collective-permute-start | bytes 786440 | tf_op jit(solution)/shard_map/ppermute | solution.py:57
  13.8 10.0 %collective-permute-start.11 = (bf16[2,2,2,32,512]{4,3,1,0,2:T(8,128)(2,1)S(1)}, bf16[2,2,2,32,512]{4,3,1,0,2:T(8,128)(2,1)S(1)}, u32[]{:S(2)}, u32[]{:S(2)}) collective-permute-start(bf16[2,2,2,32,512]{4,3,1,0,2:T(8,128)(2,1)S(1)} %pad_maximum_fusion.2), channel_id=1, source_target_pairs={{0,14},{2,0},{4,2},{6,4},{8,6},{10,8},{12,10},{14,12},{1,15},{3,1}... | collective-permute-start | bytes 786440 | tf_op jit(solution)/shard_map/ppermute | solution.py:57
  18.2 11.2 %collective-permute-start.3 = (bf16[2,2,2,32,512]{4,3,1,0,2:T(8,128)(2,1)S(1)}, bf16[2,2,2,32,512]{4,3,1,0,2:T(8,128)(2,1)S(1)}, u32[]{:S(2)}, u32[]{:S(2)}) collective-permute-start(bf16[2,2,2,32,512]{4,3,1,0,2:T(8,128)(2,1)S(1)} %collective-permute-done.1), channel_id=1, source_target_pairs={{0,2},{2,4},{4,6},{6,8},{8,10},{10,12},{12,14},{14,0},{1,3},{3,5},... | collective-permute-start | bytes 786440 | tf_op jit(solution)/shard_map/ppermute | solution.py:57
  18.2 11.2 %collective-permute-start.4 = (bf16[2,2,2,32,512]{4,3,1,0,2:T(8,128)(2,1)S(1)}, bf16[2,2,2,32,512]{4,3,1,0,2:T(8,128)(2,1)S(1)}, u32[]{:S(2)}, u32[]{:S(2)}) collective-permute-start(bf16[2,2,2,32,512]{4,3,1,0,2:T(8,128)(2,1)S(1)} %collective-permute-done.2), channel_id=1, source_target_pairs={{0,14},{2,0},{4,2},{6,4},{8,6},{10,8},{12,10},{14,12},{1,15},{3,1}... | collective-permute-start | bytes 786440 | tf_op jit(solution)/shard_map/ppermute | solution.py:57
  23.8 11.2 %collective-permute-start.12 = (bf16[2,2,2,32,512]{4,3,1,0,2:T(8,128)(2,1)S(1)}, bf16[2,2,2,32,512]{4,3,1,0,2:T(8,128)(2,1)S(1)}, u32[]{:S(2)}, u32[]{:S(2)}) collective-permute-start(bf16[2,2,2,32,512]{4,3,1,0,2:T(8,128)(2,1)S(1)} %collective-permute-done.10), channel_id=1, source_target_pairs={{0,2},{2,4},{4,6},{6,8},{8,10},{10,12},{12,14},{14,0},{1,3},{3,5},... | collective-permute-start | bytes 786440 | tf_op jit(solution)/shard_map/ppermute | solution.py:57
  23.8 11.2 %collective-permute-start.13 = (bf16[2,2,2,32,512]{4,3,1,0,2:T(8,128)(2,1)S(1)}, bf16[2,2,2,32,512]{4,3,1,0,2:T(8,128)(2,1)S(1)}, u32[]{:S(2)}, u32[]{:S(2)}) collective-permute-start(bf16[2,2,2,32,512]{4,3,1,0,2:T(8,128)(2,1)S(1)} %collective-permute-done.11), channel_id=1, source_target_pairs={{0,14},{2,0},{4,2},{6,4},{8,6},{10,8},{12,10},{14,12},{1,15},{3,1}... | collective-permute-start | bytes 786440 | tf_op jit(solution)/shard_map/ppermute | solution.py:57
  29.4 11.2 %collective-permute-start.5 = (bf16[2,2,2,32,512]{4,3,1,0,2:T(8,128)(2,1)S(1)}, bf16[2,2,2,32,512]{4,3,1,0,2:T(8,128)(2,1)S(1)}, u32[]{:S(2)}, u32[]{:S(2)}) collective-permute-start(bf16[2,2,2,32,512]{4,3,1,0,2:T(8,128)(2,1)S(1)} %collective-permute-done.3), channel_id=1, source_target_pairs={{0,2},{2,4},{4,6},{6,8},{8,10},{10,12},{12,14},{14,0},{1,3},{3,5},... | collective-permute-start | bytes 786440 | tf_op jit(solution)/shard_map/ppermute | solution.py:57
  29.4 11.3 %collective-permute-start.6 = (bf16[2,2,2,32,512]{4,3,1,0,2:T(8,128)(2,1)S(1)}, bf16[2,2,2,32,512]{4,3,1,0,2:T(8,128)(2,1)S(1)}, u32[]{:S(2)}, u32[]{:S(2)}) collective-permute-start(bf16[2,2,2,32,512]{4,3,1,0,2:T(8,128)(2,1)S(1)} %collective-permute-done.4), channel_id=1, source_target_pairs={{0,14},{2,0},{4,2},{6,4},{8,6},{10,8},{12,10},{14,12},{1,15},{3,1}... | collective-permute-start | bytes 786440 | tf_op jit(solution)/shard_map/ppermute | solution.py:57
  35.0 11.2 %collective-permute-start.14 = (bf16[2,2,2,32,512]{4,3,1,0,2:T(8,128)(2,1)S(1)}, bf16[2,2,2,32,512]{4,3,1,0,2:T(8,128)(2,1)S(1)}, u32[]{:S(2)}, u32[]{:S(2)}) collective-permute-start(bf16[2,2,2,32,512]{4,3,1,0,2:T(8,128)(2,1)S(1)} %collective-permute-done.12), channel_id=1, source_target_pairs={{0,2},{2,4},{4,6},{6,8},{8,10},{10,12},{12,14},{14,0},{1,3},{3,5},... | collective-permute-start | bytes 786440 | tf_op jit(solution)/shard_map/ppermute | solution.py:57
  35.1 11.3 %collective-permute-start.15 = (bf16[2,2,2,32,512]{4,3,1,0,2:T(8,128)(2,1)S(1)}, bf16[2,2,2,32,512]{4,3,1,0,2:T(8,128)(2,1)S(1)}, u32[]{:S(2)}, u32[]{:S(2)}) collective-permute-start(bf16[2,2,2,32,512]{4,3,1,0,2:T(8,128)(2,1)S(1)} %collective-permute-done.13), channel_id=1, source_target_pairs={{0,14},{2,0},{4,2},{6,4},{8,6},{10,8},{12,10},{14,12},{1,15},{3,1}... | collective-permute-start | bytes 786440 | tf_op jit(solution)/shard_map/ppermute | solution.py:57
  40.7 8.5 %collective-permute-start.7 = (bf16[2,2,2,16,512]{4,3,1,0,2:T(8,128)(2,1)S(1)}, bf16[2,2,2,16,512]{4,3,1,0,2:T(8,128)(2,1)S(1)}, u32[]{:S(2)}, u32[]{:S(2)}) collective-permute-start(bf16[2,2,2,16,512]{4,3,1,0,2:T(8,128)(2,1)S(1)} %slice.117), channel_id=1, source_target_pairs={{0,2},{2,4},{4,6},{6,8},{8,10},{10,12},{12,14},{14,0},{1,3},{3,5},... | collective-permute-start | bytes 393224 | tf_op jit(solution)/shard_map/ppermute | solution.py:57
  40.8 8.4 %collective-permute-start.8 = (bf16[2,2,2,16,512]{4,3,1,0,2:T(8,128)(2,1)S(1)}, bf16[2,2,2,16,512]{4,3,1,0,2:T(8,128)(2,1)S(1)}, u32[]{:S(2)}, u32[]{:S(2)}) collective-permute-start(bf16[2,2,2,16,512]{4,3,1,0,2:T(8,128)(2,1)S(1)} %slice.118), channel_id=1, source_target_pairs={{0,14},{2,0},{4,2},{6,4},{8,6},{10,8},{12,10},{14,12},{1,15},{3,1}... | collective-permute-start | bytes 393224 | tf_op jit(solution)/shard_map/ppermute | solution.py:57
  46.3 5.9 %collective-permute-start.16 = (bf16[2,2,2,16,512]{4,3,1,0,2:T(8,128)(2,1)S(1)}, bf16[2,2,2,16,512]{4,3,1,0,2:T(8,128)(2,1)S(1)}, u32[]{:S(2)}, u32[]{:S(2)}) collective-permute-start(bf16[2,2,2,16,512]{4,3,1,0,2:T(8,128)(2,1)S(1)} %slice.127), channel_id=1, source_target_pairs={{0,2},{2,4},{4,6},{6,8},{8,10},{10,12},{12,14},{14,0},{1,3},{3,5},... | collective-permute-start | bytes 393224 | tf_op jit(solution)/shard_map/ppermute | solution.py:57
  46.4 5.8 %collective-permute-start.17 = (bf16[2,2,2,16,512]{4,3,1,0,2:T(8,128)(2,1)S(1)}, bf16[2,2,2,16,512]{4,3,1,0,2:T(8,128)(2,1)S(1)}, u32[]{:S(2)}, u32[]{:S(2)}) collective-permute-start(bf16[2,2,2,16,512]{4,3,1,0,2:T(8,128)(2,1)S(1)} %slice.128), channel_id=1, source_target_pairs={{0,14},{2,0},{4,2},{6,4},{8,6},{10,8},{12,10},{14,12},{1,15},{3,1}... | collective-permute-start | bytes 393224 | tf_op jit(solution)/shard_map/ppermute | solution.py:57
  56.5 28.0 %all-to-all-start = ((bf16[2,16,32,512]{3,2,0,1:T(8,128)(2,1)}), bf16[2,16,32,512]{3,2,0,1:T(8,128)(2,1)}, u32[]{:S(2)}, u32[]{:S(2)}) async-start(bf16[2,16,32,512]{3,2,0,1:T(8,128)(2,1)} %copy.7), calls=%async_computation | async-start | bytes 2097152 | tf_op jit(solution)/shard_map/all_to_all | solution.py:105
  68.3 0.8 copy-start.2
  88.0 1.5 %copy-start.1 = (bf16[1,1,8,2,32,512]{5,4,1,0,3,2:T(8,128)(2,1)S(1)}, bf16[1,1,8,2,32,512]{5,4,1,0,3,2:T(8,128)(2,1)}, u32[]{:S(2)}) copy-start(bf16[1,1,8,2,32,512]{5,4,1,0,3,2:T(8,128)(2,1)} %get-tuple-element.7) | copy-start | bytes 1572868
  88.0 1.5 %copy-start.3 = (bf16[1,1,8,2,32,512]{5,4,1,0,3,2:T(8,128)(2,1)S(1)}, bf16[1,1,8,2,32,512]{5,4,1,0,3,2:T(8,128)(2,1)}, u32[]{:S(2)}) copy-start(bf16[1,1,8,2,32,512]{5,4,1,0,3,2:T(8,128)(2,1)} %copy-done.2) | copy-start | bytes 1572868
  89.6 1.0 copy-start

commit v5 on v4

--- a/solution.py
+++ b/solution.py
@@ -23,7 +23,8 @@
     bottom = jnp.concatenate([-imag_t, real_t], axis=1)
     product = jnp.dot(planar[0], top, preferred_element_type=jnp.float32)
     product = product + jnp.dot(planar[1], bottom, preferred_element_type=jnp.float32)
-    return product.reshape(planar.shape[1], 2, piece_t.shape[2])
+    cols = piece_t.shape[2]
+    return product[:, :cols], product[:, cols:]
 
 
 def left_planar(block, piece_t):
@@ -36,6 +37,19 @@
         "ix,ij->xj", weight_imag, block[:, 1, :], preferred_element_type=jnp.float32
     )
     return product.reshape(2, piece_t.shape[2], block.shape[2])
+
+
+def left_halves(real_in, imag_in, piece_t):
+    rows_out = piece_t.shape[2]
+    real_w = piece_t[0]
+    imag_w = piece_t[1]
+    weight_real = jnp.concatenate([real_w, imag_w], axis=1)
+    weight_imag = jnp.concatenate([-imag_w, real_w], axis=1)
+    product = jnp.einsum("ix,ij->xj", weight_real, real_in, preferred_element_type=jnp.float32)
+    product = product + jnp.einsum(
+        "ix,ij->xj", weight_imag, imag_in, preferred_element_type=jnp.float32
+    )
+    return jnp.stack([product[:rows_out], product[rows_out:]], axis=1)
 
 
 def left_piece(block, piece_t):
@@ -104,8 +118,10 @@
     outgoing = step_first.reshape(2, row_count, share, order_size)
     moved = lax.all_to_all(outgoing, "row", split_axis=1, concat_axis=1, tiled=True)
     planar = moved.reshape(2, order_size, order_size)
-    half_second = right_planar(planar, second_t[1]).astype(jnp.bfloat16)[None]
-    step_second = left_piece(half_second, second_t[0]).astype(jnp.bfloat16)
+    real_half, imag_half = right_planar(planar, second_t[1])
+    step_second = left_halves(
+        real_half.astype(jnp.bfloat16), imag_half.astype(jnp.bfloat16), second_t[0]
+    ).astype(jnp.bfloat16)
     leaving = step_second.reshape(slab_count, order_size, 2, row_count, share)
     arrived = lax.all_to_all(leaving, "row", split_axis=3, concat_axis=3, tiled=True)
     return arrived.reshape(1, 1, slab_count, order_size, 2, order_size)

time: 114 us -> 112 us (0.982)
  local copies, waits for them, and re-layouts: 12.4 us -> 10.2 us
    slice x2 -> x1, local copies, waits for them, and re-layouts: 1.57 us -> 0.07 us  [left_halves(): return jnp.stack([product[:rows_out], product[rows_out:]], axis=1)]
    unnamed x11 -> x9, local copies, waits for them, and re-layouts: 2.5 us -> 2.65 us
  transfers between devices with their start and end apart: 19 -> 19, of which waited for: 9 -> 9; matrix products, arithmetic and copies ran while one was open for 4% -> 3% of each run, Pallas kernels for 0% -> 0%
where the time goes in v5:
time: 112 us
  starting transfers between devices  40.2 us (36%)
  waiting for transfers between devices  34.4 us (31%)
  blocking collectives  20.3 us (18%)
  local copies, waits for them, and re-layouts  10.2 us (9%)
  matrix products  5.79 us (5%)
    ppermute x18, starting transfers between devices, shift(): return lax.ppermute(x, axis, [(i, (i + d) % n) for i in range(n)])  29.4 us
    all_to_all x1, blocking collectives, shards(): lax.all_to_all(leaving, 'row', split_axis=3, concat_axis=3, tiled=True)  20.3 us
    ppermute x18, waiting for transfers between devices, shift(): return lax.ppermute(x, axis, [(i, (i + d) % n) for i in range(n)])  19.1 us
    all_to_all x1, waiting for transfers between devices, shards(): lax.all_to_all(outgoing, 'row', split_axis=1, concat_axis=1, tiled=True)  15.3 us
    all_to_all x1, starting transfers between devices, shards(): lax.all_to_all(outgoing, 'row', split_axis=1, concat_axis=1, tiled=True)  10.8 us
    unnamed x9, local copies, waits for them, and re-layouts  2.65 us
  transfers between devices with their start and end apart: 19, of which 9 were waited for; matrix products, arithmetic and copies ran while one was open for 3% of the time, Pallas kernels for 0%

profile of v5, /device:TPU:1, one launch (start us, length us, event | category | flops | bytes accessed | tf_op | source)
XLA Modules:
  0.0 112.0 jit_solution(5236661092822632385)
XLA Ops:
  0.0 1.0 slice.123
  1.0 2.1 %collective-permute-start.9 = (bf16[2,2,32,512]{3,2,1,0:T(8,128)(2,1)S(1)}, bf16[2,2,32,512]{3,2,1,0:T(8,128)(2,1)S(1)}, u32[]{:S(2)}, u32[]{:S(2)}) collective-permute-start(bf16[2,2,32,512]{3,2,1,0:T(8,128)(2,1)S(1)} %slice.123), channel_id=1, source_target_pairs={{0,1},{1,0},{2,3},{3,2},{4,5},{5,4},{6,7},{7,6},{8,9},{9,8},{10,11... | collective-permute-start | bytes 393224 | tf_op jit(solution)/shard_map/ppermute | solution.py:71
  3.1 1.5 %copy.10 = bf16[64,8,2,512]{3,1,2,0:T(8,128)(2,1)S(1)} copy(bf16[64,8,2,512]{3,2,1,0:T(2,128)(2,1)} %bitcast.100) | data formatting | bytes 2097152
  4.6 0.8 collective-permute-done.9
  5.5 1.9 %collective-permute-start = (bf16[2,2,32,512]{3,2,1,0:T(8,128)(2,1)S(1)}, bf16[2,2,32,512]{3,2,1,0:T(8,128)(2,1)S(1)}, u32[]{:S(2)}, u32[]{:S(2)}) collective-permute-start(bf16[2,2,32,512]{3,2,1,0:T(8,128)(2,1)S(1)} %get-tuple-element.21), channel_id=1, source_target_pairs={{0,1},{1,0},{2,3},{3,2},{4,5},{5,4},{6,7},{7,6},{8,9},{9,8},{10,11... | collective-permute-start | bytes 393224 | tf_op jit(solution)/shard_map/ppermute | solution.py:71
  7.4 1.9 %collective-permute-start.10 = (bf16[2,2,2,32,512]{4,3,1,0,2:T(8,128)(2,1)S(1)}, bf16[2,2,2,32,512]{4,3,1,0,2:T(8,128)(2,1)S(1)}, u32[]{:S(2)}, u32[]{:S(2)}) collective-permute-start(bf16[2,2,2,32,512]{4,3,1,0,2:T(8,128)(2,1)S(1)} %pad_maximum_fusion.2), channel_id=1, source_target_pairs={{0,2},{2,4},{4,6},{6,8},{8,10},{10,12},{12,14},{14,0},{1,3},{3,5},... | collective-permute-start | bytes 786440 | tf_op jit(solution)/shard_map/ppermute | solution.py:71
  9.4 4.0 %collective-permute-start.11 = (bf16[2,2,2,32,512]{4,3,1,0,2:T(8,128)(2,1)S(1)}, bf16[2,2,2,32,512]{4,3,1,0,2:T(8,128)(2,1)S(1)}, u32[]{:S(2)}, u32[]{:S(2)}) collective-permute-start(bf16[2,2,2,32,512]{4,3,1,0,2:T(8,128)(2,1)S(1)} %pad_maximum_fusion.2), channel_id=1, source_target_pairs={{0,14},{2,0},{4,2},{6,4},{8,6},{10,8},{12,10},{14,12},{1,15},{3,1}... | collective-permute-start | bytes 786440 | tf_op jit(solution)/shard_map/ppermute | solution.py:71
  13.8 2.7 %collective-permute-start.2 = (bf16[2,2,2,32,512]{4,3,1,0,2:T(8,128)(2,1)S(1)}, bf16[2,2,2,32,512]{4,3,1,0,2:T(8,128)(2,1)S(1)}, u32[]{:S(2)}, u32[]{:S(2)}) collective-permute-start(bf16[2,2,2,32,512]{4,3,1,0,2:T(8,128)(2,1)S(1)} %pad_maximum_fusion.1), channel_id=1, source_target_pairs={{0,14},{2,0},{4,2},{6,4},{8,6},{10,8},{12,10},{14,12},{1,15},{3,1}... | collective-permute-start | bytes 786440 | tf_op jit(solution)/shard_map/ppermute | solution.py:71
  16.8 1.4 %collective-permute-done.10 = bf16[2,2,2,32,512]{4,3,1,0,2:T(8,128)(2,1)S(1)} collective-permute-done((bf16[2,2,2,32,512]{4,3,1,0,2:T(8,128)(2,1)S(1)}, bf16[2,2,2,32,512]{4,3,1,0,2:T(8,128)(2,1)S(1)}, u32[]{:S(2)}, u32[]{:S(2)}) %collective-permute-start.10) | collective-permute-done | bytes 262176 | tf_op jit(solution)/shard_map/ppermute | solution.py:71
  18.2 2.7 %collective-permute-start.13 = (bf16[2,2,2,32,512]{4,3,1,0,2:T(8,128)(2,1)S(1)}, bf16[2,2,2,32,512]{4,3,1,0,2:T(8,128)(2,1)S(1)}, u32[]{:S(2)}, u32[]{:S(2)}) collective-permute-start(bf16[2,2,2,32,512]{4,3,1,0,2:T(8,128)(2,1)S(1)} %collective-permute-done.11), channel_id=1, source_target_pairs={{0,14},{2,0},{4,2},{6,4},{8,6},{10,8},{12,10},{14,12},{1,15},{3,1}... | collective-permute-start | bytes 786440 | tf_op jit(solution)/shard_map/ppermute | solution.py:71
  20.9 2.9 %collective-permute-done.1 = bf16[2,2,2,32,512]{4,3,1,0,2:T(8,128)(2,1)S(1)} collective-permute-done((bf16[2,2,2,32,512]{4,3,1,0,2:T(8,128)(2,1)S(1)}, bf16[2,2,2,32,512]{4,3,1,0,2:T(8,128)(2,1)S(1)}, u32[]{:S(2)}, u32[]{:S(2)}) %collective-permute-start.1) | collective-permute-done | bytes 262176 | tf_op jit(solution)/shard_map/ppermute | solution.py:71
  23.8 2.7 %collective-permute-start.4 = (bf16[2,2,2,32,512]{4,3,1,0,2:T(8,128)(2,1)S(1)}, bf16[2,2,2,32,512]{4,3,1,0,2:T(8,128)(2,1)S(1)}, u32[]{:S(2)}, u32[]{:S(2)}) collective-permute-start(bf16[2,2,2,32,512]{4,3,1,0,2:T(8,128)(2,1)S(1)} %collective-permute-done.2), channel_id=1, source_target_pairs={{0,14},{2,0},{4,2},{6,4},{8,6},{10,8},{12,10},{14,12},{1,15},{3,1}... | collective-permute-start | bytes 786440 | tf_op jit(solution)/shard_map/ppermute | solution.py:71
  26.6 2.8 %collective-permute-done.12 = bf16[2,2,2,32,512]{4,3,1,0,2:T(8,128)(2,1)S(1)} collective-permute-done((bf16[2,2,2,32,512]{4,3,1,0,2:T(8,128)(2,1)S(1)}, bf16[2,2,2,32,512]{4,3,1,0,2:T(8,128)(2,1)S(1)}, u32[]{:S(2)}, u32[]{:S(2)}) %collective-permute-start.12) | collective-permute-done | bytes 262176 | tf_op jit(solution)/shard_map/ppermute | solution.py:71
  29.4 2.7 %collective-permute-start.15 = (bf16[2,2,2,32,512]{4,3,1,0,2:T(8,128)(2,1)S(1)}, bf16[2,2,2,32,512]{4,3,1,0,2:T(8,128)(2,1)S(1)}, u32[]{:S(2)}, u32[]{:S(2)}) collective-permute-start(bf16[2,2,2,32,512]{4,3,1,0,2:T(8,128)(2,1)S(1)} %collective-permute-done.13), channel_id=1, source_target_pairs={{0,14},{2,0},{4,2},{6,4},{8,6},{10,8},{12,10},{14,12},{1,15},{3,1}... | collective-permute-start | bytes 786440 | tf_op jit(solution)/shard_map/ppermute | solution.py:71
  32.1 2.9 %collective-permute-done.3 = bf16[2,2,2,32,512]{4,3,1,0,2:T(8,128)(2,1)S(1)} collective-permute-done((bf16[2,2,2,32,512]{4,3,1,0,2:T(8,128)(2,1)S(1)}, bf16[2,2,2,32,512]{4,3,1,0,2:T(8,128)(2,1)S(1)}, u32[]{:S(2)}, u32[]{:S(2)}) %collective-permute-start.3) | collective-permute-done | bytes 262176 | tf_op jit(solution)/shard_map/ppermute | solution.py:71
  35.1 2.7 %collective-permute-start.6 = (bf16[2,2,2,32,512]{4,3,1,0,2:T(8,128)(2,1)S(1)}, bf16[2,2,2,32,512]{4,3,1,0,2:T(8,128)(2,1)S(1)}, u32[]{:S(2)}, u32[]{:S(2)}) collective-permute-start(bf16[2,2,2,32,512]{4,3,1,0,2:T(8,128)(2,1)S(1)} %collective-permute-done.4), channel_id=1, source_target_pairs={{0,14},{2,0},{4,2},{6,4},{8,6},{10,8},{12,10},{14,12},{1,15},{3,1}... | collective-permute-start | bytes 786440 | tf_op jit(solution)/shard_map/ppermute | solution.py:71
  37.8 2.8 %collective-permute-done.14 = bf16[2,2,2,32,512]{4,3,1,0,2:T(8,128)(2,1)S(1)} collective-permute-done((bf16[2,2,2,32,512]{4,3,1,0,2:T(8,128)(2,1)S(1)}, bf16[2,2,2,32,512]{4,3,1,0,2:T(8,128)(2,1)S(1)}, u32[]{:S(2)}, u32[]{:S(2)}) %collective-permute-start.14) | collective-permute-done | bytes 262176 | tf_op jit(solution)/shard_map/ppermute | solution.py:71
  40.8 2.9 %collective-permute-start.17 = (bf16[2,2,2,16,512]{4,3,1,0,2:T(8,128)(2,1)S(1)}, bf16[2,2,2,16,512]{4,3,1,0,2:T(8,128)(2,1)S(1)}, u32[]{:S(2)}, u32[]{:S(2)}) collective-permute-start(bf16[2,2,2,16,512]{4,3,1,0,2:T(8,128)(2,1)S(1)} %slice.125), channel_id=1, source_target_pairs={{0,14},{2,0},{4,2},{6,4},{8,6},{10,8},{12,10},{14,12},{1,15},{3,1}... | collective-permute-start | bytes 393224 | tf_op jit(solution)/shard_map/ppermute | solution.py:71
  43.7 2.5 %collective-permute-done.5 = bf16[2,2,2,32,512]{4,3,1,0,2:T(8,128)(2,1)S(1)} collective-permute-done((bf16[2,2,2,32,512]{4,3,1,0,2:T(8,128)(2,1)S(1)}, bf16[2,2,2,32,512]{4,3,1,0,2:T(8,128)(2,1)S(1)}, u32[]{:S(2)}, u32[]{:S(2)}) %collective-permute-start.5) | collective-permute-done | bytes 262176 | tf_op jit(solution)/shard_map/ppermute | solution.py:71
  46.4 2.7 %collective-permute-start.8 = (bf16[2,2,2,16,512]{4,3,1,0,2:T(8,128)(2,1)S(1)}, bf16[2,2,2,16,512]{4,3,1,0,2:T(8,128)(2,1)S(1)}, u32[]{:S(2)}, u32[]{:S(2)}) collective-permute-start(bf16[2,2,2,16,512]{4,3,1,0,2:T(8,128)(2,1)S(1)} %slice.120), channel_id=1, source_target_pairs={{0,14},{2,0},{4,2},{6,4},{8,6},{10,8},{12,10},{14,12},{1,15},{3,1}... | collective-permute-start | bytes 393224 | tf_op jit(solution)/shard_map/ppermute | solution.py:71
  49.2 3.0 %collective-permute-done.7 = bf16[2,2,2,16,512]{4,3,1,0,2:T(8,128)(2,1)S(1)} collective-permute-done((bf16[2,2,2,16,512]{4,3,1,0,2:T(8,128)(2,1)S(1)}, bf16[2,2,2,16,512]{4,3,1,0,2:T(8,128)(2,1)S(1)}, u32[]{:S(2)}, u32[]{:S(2)}) %collective-permute-start.7) | collective-permute-done | bytes 131104 | tf_op jit(solution)/shard_map/ppermute | solution.py:71
  52.6 1.3 %fusion.8 = bf16[1024,512]{1,0:T(8,128)(2,1)S(1)} fusion(bf16[512,1024]{1,0:T(8,128)(2,1)S(1)} %bitcast.101, bf16[512,512]{1,0:T(8,128)(2,1)S(1)} %bitcast.105, bf16[512,512]{1,0:T(8,128)(2,1)S(1)} %bitcast_negate_fusion.1, bf16[512,512]{1,0:T(8,128)(2,1)S(1)} %bitcast.99), kind=kOutput, calls=%fused_computation.11 | convolution fusion | flops 1082654720 | bytes 3670016 | tf_op jit(solution)/shard_map/dot_general | solution.py:15
  54.7 0.8 add_convert_fusion.2
  55.5 1.0 copy.5
  56.5 10.8 %all-to-all-start = ((bf16[2,16,32,512]{3,2,0,1:T(8,128)(2,1)}), bf16[2,16,32,512]{3,2,0,1:T(8,128)(2,1)}, u32[]{:S(2)}, u32[]{:S(2)}) async-start(bf16[2,16,32,512]{3,2,0,1:T(8,128)(2,1)} %copy.5), calls=%async_computation | async-start | bytes 2097152 | tf_op jit(solution)/shard_map/all_to_all | solution.py:119
  67.3 1.0 fusion.43
  69.2 15.3 %all-to-all-done = bf16[2,16,32,512]{3,2,0,1:T(8,128)(2,1)} async-done(((bf16[2,16,32,512]{3,2,0,1:T(8,128)(2,1)}), bf16[2,16,32,512]{3,2,0,1:T(8,128)(2,1)}, u32[]{:S(2)}, u32[]{:S(2)}) %all-to-all-start) | async-done | bytes 1048608 | tf_op jit(solution)/shard_map/all_to_all | solution.py:119
  84.5 1.3 %fusion.46 = (bf16[1,16,32,512]{3,2,0,1:T(8,128)(2,1)S(1)}, bf16[1,16,32,512]{3,2,0,1:T(8,128)(2,1)S(1)}) fusion(bf16[2,16,32,512]{3,2,0,1:T(8,128)(2,1)} %all-to-all-done), kind=kLoop, calls=%fused_computation.76 | loop fusion | bytes 2097152 | tf_op jit(solution)/shard_map/slice | solution.py:25
  87.7 0.8 fusion.11
  88.4 0.8 add_convert_fusion
  89.4 20.3 %all_to_all.10 = bf16[1,512,2,16,32]{1,4,2,0,3:T(8,128)(2,1)S(1)} all-to-all(bf16[1,512,2,16,32]{1,4,2,0,3:T(8,128)(2,1)S(1)} %pad_maximum_fusion), channel_id=1, replica_groups=mesh['row'=16,'cz'=8,'cx'=2] {'row'}, dimensions={3} | all-to-all | bytes 2097152 | tf_op jit(solution)/shard_map/all_to_all | solution.py:126
  109.9 2.1 %copy.9 = bf16[1,1,1,512,2,512]{5,4,3,2,1,0:T(2,128)(2,1)} copy(bf16[1,1,1,512,2,512]{3,5,4,2,1,0:T(8,128)(2,1)S(1)} %bitcast.87) | data formatting | bytes 2097152 | tf_op jit(solution)/shard_map/reshape | solution.py:127
  (61 shorter events, 5.4 us)
Async XLA Ops:
  0.0 5.5 %copy-start.3 = (bf16[1,4,2,512,32]{3,4,2,1,0:T(8,128)(2,1)S(1)}, bf16[1,4,2,512,32]{3,4,2,1,0:T(8,128)(2,1)}, u32[]{:S(2)}) copy-start(bf16[1,4,2,512,32]{3,4,2,1,0:T(8,128)(2,1)} %param.3) | copy-start | bytes 786436
  1.0 4.5 %collective-permute-start.9 = (bf16[2,2,32,512]{3,2,1,0:T(8,128)(2,1)S(1)}, bf16[2,2,32,512]{3,2,1,0:T(8,128)(2,1)S(1)}, u32[]{:S(2)}, u32[]{:S(2)}) collective-permute-start(bf16[2,2,32,512]{3,2,1,0:T(8,128)(2,1)S(1)} %slice.123), channel_id=1, source_target_pairs={{0,1},{1,0},{2,3},{3,2},{4,5},{5,4},{6,7},{7,6},{8,9},{9,8},{10,11... | collective-permute-start | bytes 393224 | tf_op jit(solution)/shard_map/ppermute | solution.py:71
  5.5 8.2 %collective-permute-start = (bf16[2,2,32,512]{3,2,1,0:T(8,128)(2,1)S(1)}, bf16[2,2,32,512]{3,2,1,0:T(8,128)(2,1)S(1)}, u32[]{:S(2)}, u32[]{:S(2)}) collective-permute-start(bf16[2,2,32,512]{3,2,1,0:T(8,128)(2,1)S(1)} %get-tuple-element.21), channel_id=1, source_target_pairs={{0,1},{1,0},{2,3},{3,2},{4,5},{5,4},{6,7},{7,6},{8,9},{9,8},{10,11... | collective-permute-start | bytes 393224 | tf_op jit(solution)/shard_map/ppermute | solution.py:71
  7.4 10.8 %collective-permute-start.10 = (bf16[2,2,2,32,512]{4,3,1,0,2:T(8,128)(2,1)S(1)}, bf16[2,2,2,32,512]{4,3,1,0,2:T(8,128)(2,1)S(1)}, u32[]{:S(2)}, u32[]{:S(2)}) collective-permute-start(bf16[2,2,2,32,512]{4,3,1,0,2:T(8,128)(2,1)S(1)} %pad_maximum_fusion.2), channel_id=1, source_target_pairs={{0,2},{2,4},{4,6},{6,8},{8,10},{10,12},{12,14},{14,0},{1,3},{3,5},... | collective-permute-start | bytes 786440 | tf_op jit(solution)/shard_map/ppermute | solution.py:71
  9.4 8.8 %collective-permute-start.11 = (bf16[2,2,2,32,512]{4,3,1,0,2:T(8,128)(2,1)S(1)}, bf16[2,2,2,32,512]{4,3,1,0,2:T(8,128)(2,1)S(1)}, u32[]{:S(2)}, u32[]{:S(2)}) collective-permute-start(bf16[2,2,2,32,512]{4,3,1,0,2:T(8,128)(2,1)S(1)} %pad_maximum_fusion.2), channel_id=1, source_target_pairs={{0,14},{2,0},{4,2},{6,4},{8,6},{10,8},{12,10},{14,12},{1,15},{3,1}... | collective-permute-start | bytes 786440 | tf_op jit(solution)/shard_map/ppermute | solution.py:71
  13.7 10.0 %collective-permute-start.1 = (bf16[2,2,2,32,512]{4,3,1,0,2:T(8,128)(2,1)S(1)}, bf16[2,2,2,32,512]{4,3,1,0,2:T(8,128)(2,1)S(1)}, u32[]{:S(2)}, u32[]{:S(2)}) collective-permute-start(bf16[2,2,2,32,512]{4,3,1,0,2:T(8,128)(2,1)S(1)} %pad_maximum_fusion.1), channel_id=1, source_target_pairs={{0,2},{2,4},{4,6},{6,8},{8,10},{10,12},{12,14},{14,0},{1,3},{3,5},... | collective-permute-start | bytes 786440 | tf_op jit(solution)/shard_map/ppermute | solution.py:71
  13.8 10.0 %collective-permute-start.2 = (bf16[2,2,2,32,512]{4,3,1,0,2:T(8,128)(2,1)S(1)}, bf16[2,2,2,32,512]{4,3,1,0,2:T(8,128)(2,1)S(1)}, u32[]{:S(2)}, u32[]{:S(2)}) collective-permute-start(bf16[2,2,2,32,512]{4,3,1,0,2:T(8,128)(2,1)S(1)} %pad_maximum_fusion.1), channel_id=1, source_target_pairs={{0,14},{2,0},{4,2},{6,4},{8,6},{10,8},{12,10},{14,12},{1,15},{3,1}... | collective-permute-start | bytes 786440 | tf_op jit(solution)/shard_map/ppermute | solution.py:71
  18.2 11.2 %collective-permute-start.12 = (bf16[2,2,2,32,512]{4,3,1,0,2:T(8,128)(2,1)S(1)}, bf16[2,2,2,32,512]{4,3,1,0,2:T(8,128)(2,1)S(1)}, u32[]{:S(2)}, u32[]{:S(2)}) collective-permute-start(bf16[2,2,2,32,512]{4,3,1,0,2:T(8,128)(2,1)S(1)} %collective-permute-done.10), channel_id=1, source_target_pairs={{0,2},{2,4},{4,6},{6,8},{8,10},{10,12},{12,14},{14,0},{1,3},{3,5},... | collective-permute-start | bytes 786440 | tf_op jit(solution)/shard_map/ppermute | solution.py:71
  18.2 11.2 %collective-permute-start.13 = (bf16[2,2,2,32,512]{4,3,1,0,2:T(8,128)(2,1)S(1)}, bf16[2,2,2,32,512]{4,3,1,0,2:T(8,128)(2,1)S(1)}, u32[]{:S(2)}, u32[]{:S(2)}) collective-permute-start(bf16[2,2,2,32,512]{4,3,1,0,2:T(8,128)(2,1)S(1)} %collective-permute-done.11), channel_id=1, source_target_pairs={{0,14},{2,0},{4,2},{6,4},{8,6},{10,8},{12,10},{14,12},{1,15},{3,1}... | collective-permute-start | bytes 786440 | tf_op jit(solution)/shard_map/ppermute | solution.py:71
  23.8 11.2 %collective-permute-start.3 = (bf16[2,2,2,32,512]{4,3,1,0,2:T(8,128)(2,1)S(1)}, bf16[2,2,2,32,512]{4,3,1,0,2:T(8,128)(2,1)S(1)}, u32[]{:S(2)}, u32[]{:S(2)}) collective-permute-start(bf16[2,2,2,32,512]{4,3,1,0,2:T(8,128)(2,1)S(1)} %collective-permute-done.1), channel_id=1, source_target_pairs={{0,2},{2,4},{4,6},{6,8},{8,10},{10,12},{12,14},{14,0},{1,3},{3,5},... | collective-permute-start | bytes 786440 | tf_op jit(solution)/shard_map/ppermute | solution.py:71
  23.8 11.2 %collective-permute-start.4 = (bf16[2,2,2,32,512]{4,3,1,0,2:T(8,128)(2,1)S(1)}, bf16[2,2,2,32,512]{4,3,1,0,2:T(8,128)(2,1)S(1)}, u32[]{:S(2)}, u32[]{:S(2)}) collective-permute-start(bf16[2,2,2,32,512]{4,3,1,0,2:T(8,128)(2,1)S(1)} %collective-permute-done.2), channel_id=1, source_target_pairs={{0,14},{2,0},{4,2},{6,4},{8,6},{10,8},{12,10},{14,12},{1,15},{3,1}... | collective-permute-start | bytes 786440 | tf_op jit(solution)/shard_map/ppermute | solution.py:71
  29.4 11.2 %collective-permute-start.14 = (bf16[2,2,2,32,512]{4,3,1,0,2:T(8,128)(2,1)S(1)}, bf16[2,2,2,32,512]{4,3,1,0,2:T(8,128)(2,1)S(1)}, u32[]{:S(2)}, u32[]{:S(2)}) collective-permute-start(bf16[2,2,2,32,512]{4,3,1,0,2:T(8,128)(2,1)S(1)} %collective-permute-done.12), channel_id=1, source_target_pairs={{0,2},{2,4},{4,6},{6,8},{8,10},{10,12},{12,14},{14,0},{1,3},{3,5},... | collective-permute-start | bytes 786440 | tf_op jit(solution)/shard_map/ppermute | solution.py:71
  29.4 11.3 %collective-permute-start.15 = (bf16[2,2,2,32,512]{4,3,1,0,2:T(8,128)(2,1)S(1)}, bf16[2,2,2,32,512]{4,3,1,0,2:T(8,128)(2,1)S(1)}, u32[]{:S(2)}, u32[]{:S(2)}) collective-permute-start(bf16[2,2,2,32,512]{4,3,1,0,2:T(8,128)(2,1)S(1)} %collective-permute-done.13), channel_id=1, source_target_pairs={{0,14},{2,0},{4,2},{6,4},{8,6},{10,8},{12,10},{14,12},{1,15},{3,1}... | collective-permute-start | bytes 786440 | tf_op jit(solution)/shard_map/ppermute | solution.py:71
  35.0 11.2 %collective-permute-start.5 = (bf16[2,2,2,32,512]{4,3,1,0,2:T(8,128)(2,1)S(1)}, bf16[2,2,2,32,512]{4,3,1,0,2:T(8,128)(2,1)S(1)}, u32[]{:S(2)}, u32[]{:S(2)}) collective-permute-start(bf16[2,2,2,32,512]{4,3,1,0,2:T(8,128)(2,1)S(1)} %collective-permute-done.3), channel_id=1, source_target_pairs={{0,2},{2,4},{4,6},{6,8},{8,10},{10,12},{12,14},{14,0},{1,3},{3,5},... | collective-permute-start | bytes 786440 | tf_op jit(solution)/shard_map/ppermute | solution.py:71
  35.1 11.3 %collective-permute-start.6 = (bf16[2,2,2,32,512]{4,3,1,0,2:T(8,128)(2,1)S(1)}, bf16[2,2,2,32,512]{4,3,1,0,2:T(8,128)(2,1)S(1)}, u32[]{:S(2)}, u32[]{:S(2)}) collective-permute-start(bf16[2,2,2,32,512]{4,3,1,0,2:T(8,128)(2,1)S(1)} %collective-permute-done.4), channel_id=1, source_target_pairs={{0,14},{2,0},{4,2},{6,4},{8,6},{10,8},{12,10},{14,12},{1,15},{3,1}... | collective-permute-start | bytes 786440 | tf_op jit(solution)/shard_map/ppermute | solution.py:71
  40.7 8.5 %collective-permute-start.16 = (bf16[2,2,2,16,512]{4,3,1,0,2:T(8,128)(2,1)S(1)}, bf16[2,2,2,16,512]{4,3,1,0,2:T(8,128)(2,1)S(1)}, u32[]{:S(2)}, u32[]{:S(2)}) collective-permute-start(bf16[2,2,2,16,512]{4,3,1,0,2:T(8,128)(2,1)S(1)} %slice.124), channel_id=1, source_target_pairs={{0,2},{2,4},{4,6},{6,8},{8,10},{10,12},{12,14},{14,0},{1,3},{3,5},... | collective-permute-start | bytes 393224 | tf_op jit(solution)/shard_map/ppermute | solution.py:71
  40.8 8.4 %collective-permute-start.17 = (bf16[2,2,2,16,512]{4,3,1,0,2:T(8,128)(2,1)S(1)}, bf16[2,2,2,16,512]{4,3,1,0,2:T(8,128)(2,1)S(1)}, u32[]{:S(2)}, u32[]{:S(2)}) collective-permute-start(bf16[2,2,2,16,512]{4,3,1,0,2:T(8,128)(2,1)S(1)} %slice.125), channel_id=1, source_target_pairs={{0,14},{2,0},{4,2},{6,4},{8,6},{10,8},{12,10},{14,12},{1,15},{3,1}... | collective-permute-start | bytes 393224 | tf_op jit(solution)/shard_map/ppermute | solution.py:71
  46.3 5.9 %collective-permute-start.7 = (bf16[2,2,2,16,512]{4,3,1,0,2:T(8,128)(2,1)S(1)}, bf16[2,2,2,16,512]{4,3,1,0,2:T(8,128)(2,1)S(1)}, u32[]{:S(2)}, u32[]{:S(2)}) collective-permute-start(bf16[2,2,2,16,512]{4,3,1,0,2:T(8,128)(2,1)S(1)} %slice.119), channel_id=1, source_target_pairs={{0,2},{2,4},{4,6},{6,8},{8,10},{10,12},{12,14},{14,0},{1,3},{3,5},... | collective-permute-start | bytes 393224 | tf_op jit(solution)/shard_map/ppermute | solution.py:71
  46.4 5.8 %collective-permute-start.8 = (bf16[2,2,2,16,512]{4,3,1,0,2:T(8,128)(2,1)S(1)}, bf16[2,2,2,16,512]{4,3,1,0,2:T(8,128)(2,1)S(1)}, u32[]{:S(2)}, u32[]{:S(2)}) collective-permute-start(bf16[2,2,2,16,512]{4,3,1,0,2:T(8,128)(2,1)S(1)} %slice.120), channel_id=1, source_target_pairs={{0,14},{2,0},{4,2},{6,4},{8,6},{10,8},{12,10},{14,12},{1,15},{3,1}... | collective-permute-start | bytes 393224 | tf_op jit(solution)/shard_map/ppermute | solution.py:71
  56.5 28.0 %all-to-all-start = ((bf16[2,16,32,512]{3,2,0,1:T(8,128)(2,1)}), bf16[2,16,32,512]{3,2,0,1:T(8,128)(2,1)}, u32[]{:S(2)}, u32[]{:S(2)}) async-start(bf16[2,16,32,512]{3,2,0,1:T(8,128)(2,1)} %copy.5), calls=%async_computation | async-start | bytes 2097152 | tf_op jit(solution)/shard_map/all_to_all | solution.py:119
  68.3 0.8 copy-start.1
  86.5 1.0 copy-start
  86.5 1.2 %copy-start.2 = (bf16[1,1,8,2,32,512]{5,4,1,0,3,2:T(8,128)(2,1)S(1)}, bf16[1,1,8,2,32,512]{5,4,1,0,3,2:T(8,128)(2,1)}, u32[]{:S(2)}) copy-start(bf16[1,1,8,2,32,512]{5,4,1,0,3,2:T(8,128)(2,1)} %copy-done.1) | copy-start | bytes 1572868

commit v6 on v5

--- a/solution.py
+++ b/solution.py
@@ -16,27 +16,29 @@
     return product.reshape(items, order_size, 2, order_size)
 
 
-def right_planar(planar, piece_t):
+def right_blocks(grouped, piece_t):
     real_t = piece_t[0]
     imag_t = piece_t[1]
     top = jnp.concatenate([real_t, imag_t], axis=1)
     bottom = jnp.concatenate([-imag_t, real_t], axis=1)
-    product = jnp.dot(planar[0], top, preferred_element_type=jnp.float32)
-    product = product + jnp.dot(planar[1], bottom, preferred_element_type=jnp.float32)
+    weight = jnp.stack([top, bottom], axis=0)
+    product = jnp.einsum("pcly,cyk->plk", grouped, weight, preferred_element_type=jnp.float32)
     cols = piece_t.shape[2]
+    product = product.reshape(-1, 2 * cols)
     return product[:, :cols], product[:, cols:]
 
 
-def left_planar(block, piece_t):
-    real_w = piece_t[0]
-    imag_w = piece_t[1]
-    weight_real = jnp.concatenate([real_w, imag_w], axis=1)
-    weight_imag = jnp.concatenate([-imag_w, real_w], axis=1)
+def left_blocks(block, piece_t, parts):
+    rows_in = piece_t.shape[1]
+    real_w = piece_t[0].reshape(rows_in, parts, 1, -1)
+    imag_w = piece_t[1].reshape(rows_in, parts, 1, -1)
+    weight_real = jnp.concatenate([real_w, imag_w], axis=2).reshape(rows_in, -1)
+    weight_imag = jnp.concatenate([-imag_w, real_w], axis=2).reshape(rows_in, -1)
     product = jnp.einsum("ix,ij->xj", weight_real, block[:, 0, :], preferred_element_type=jnp.float32)
     product = product + jnp.einsum(
         "ix,ij->xj", weight_imag, block[:, 1, :], preferred_element_type=jnp.float32
     )
-    return product.reshape(2, piece_t.shape[2], block.shape[2])
+    return product.reshape(parts, 2, -1, block.shape[2])
 
 
 def left_halves(real_in, imag_in, piece_t):
@@ -114,11 +116,9 @@
 
     block = stem[0, 0]
     half_first = right_piece(block, first_t[1]).astype(jnp.bfloat16)
-    step_first = left_planar(half_first[0], first_t[0]).astype(jnp.bfloat16)
-    outgoing = step_first.reshape(2, row_count, share, order_size)
-    moved = lax.all_to_all(outgoing, "row", split_axis=1, concat_axis=1, tiled=True)
-    planar = moved.reshape(2, order_size, order_size)
-    real_half, imag_half = right_planar(planar, second_t[1])
+    outgoing = left_blocks(half_first[0], first_t[0], row_count).astype(jnp.bfloat16)
+    moved = lax.all_to_all(outgoing, "row", split_axis=0, concat_axis=0, tiled=True)
+    real_half, imag_half = right_blocks(moved, second_t[1])
     step_second = left_halves(
         real_half.astype(jnp.bfloat16), imag_half.astype(jnp.bfloat16), second_t[0]
     ).astype(jnp.bfloat16)

time: 112 us -> 129 us (1.15)
  local copies, waits for them, and re-layouts: 10.2 us -> 17.8 us
  starting transfers between devices: 40.2 us -> 44.8 us
  other arithmetic: 0.58 us -> 3.68 us
  matrix products: 5.79 us -> 8.09 us
    another operation x2 -> x6, local copies, waits for them, and re-layouts: 0.48 us -> 6.16 us  [the longest x2 2.85 us: left_blocks(): real_w = piece_t[0].reshape(rows_in, parts, 1, -1)]
    all_to_all x1, starting transfers between devices: 10.8 us -> 14 us  [shards(): lax.all_to_all(outgoing, 'row', split_axis=0, concat_axis=0, tiled=True)]
    neg x0 -> x1, local copies, waits for them, and re-layouts: none -> 2.54 us  [left_blocks(): -imag_w]
    dot_general x4 -> x3, matrix products: 2.95 us -> 5.25 us  [the longest x1 2.79 us: right_blocks(): jnp.einsum('pcly,cyk->plk', grouped, weight, preferred_element_type=jnp.f...]
    slice x2 -> x1, local copies, waits for them, and re-layouts: 2.29 us -> 0.24 us  [right_blocks(): imag_t = piece_t[1]]
    neg x2, other arithmetic: 0.14 us -> 1.81 us  [the longest x1 1.74 us: left_blocks(): -imag_w]
    ppermute x18, starting transfers between devices: 29.4 us -> 30.8 us  [shift(): return lax.ppermute(x, axis, [(i, (i + d) % n) for i in range(n)])]
    unnamed x9 -> x13, local copies, waits for them, and re-layouts: 2.65 us -> 4.01 us
  transfers between devices with their start and end apart: 19 -> 19, of which waited for: 9 -> 10; matrix products, arithmetic and copies ran while one was open for 3% -> 4% of each run, Pallas kernels for 0% -> 0%
where the time goes in v6:
time: 129 us
  starting transfers between devices  44.8 us (35%)
  waiting for transfers between devices  33.4 us (26%)
  blocking collectives  20.3 us (16%)
  local copies, waits for them, and re-layouts  17.8 us (14%)
  matrix products  8.09 us (6%)
  other arithmetic  3.68 us (3%)
    ppermute x18, starting transfers between devices, shift(): return lax.ppermute(x, axis, [(i, (i + d) % n) for i in range(n)])  30.8 us
    all_to_all x1, blocking collectives, shards(): lax.all_to_all(leaving, 'row', split_axis=3, concat_axis=3, tiled=True)  20.3 us
    ppermute x18, waiting for transfers between devices, shift(): return lax.ppermute(x, axis, [(i, (i + d) % n) for i in range(n)])  17.9 us
    all_to_all x1, waiting for transfers between devices, shards(): lax.all_to_all(outgoing, 'row', split_axis=0, concat_axis=0, tiled=True)  15.5 us
    all_to_all x1, starting transfers between devices, shards(): lax.all_to_all(outgoing, 'row', split_axis=0, concat_axis=0, tiled=True)  14 us
    unnamed x13, local copies, waits for them, and re-layouts  4.01 us
    another operation x2, local copies, waits for them, and re-layouts, left_blocks(): real_w = piece_t[0].reshape(rows_in, parts, 1, -1)  2.85 us
    another operation x2, local copies, waits for them, and re-layouts, left_blocks(): imag_w = piece_t[1].reshape(rows_in, parts, 1, -1)  2.82 us
  transfers between devices with their start and end apart: 19, of which 10 were waited for; matrix products, arithmetic and copies ran while one was open for 4% of the time, Pallas kernels for 0%

profile of v6, /device:TPU:1, one launch (start us, length us, event | category | flops | bytes accessed | tf_op | source)
XLA Modules:
  0.0 128.5 jit_solution(2924331187497002378)
XLA Ops:
  1.0 2.1 %collective-permute-start.9 = (bf16[2,2,32,512]{3,2,1,0:T(8,128)(2,1)S(1)}, bf16[2,2,32,512]{3,2,1,0:T(8,128)(2,1)S(1)}, u32[]{:S(2)}, u32[]{:S(2)}) collective-permute-start(bf16[2,2,32,512]{3,2,1,0:T(8,128)(2,1)S(1)} %slice.113), channel_id=1, source_target_pairs={{0,1},{1,0},{2,3},{3,2},{4,5},{5,4},{6,7},{7,6},{8,9},{9,8},{10,11... | collective-permute-start | bytes 393224 | tf_op jit(solution)/shard_map/ppermute | solution.py:73
  3.1 2.4 %copy.64 = bf16[64,8,2,512]{3,1,2,0:T(8,128)(2,1)} copy(bf16[64,8,2,512]{3,2,1,0:T(2,128)(2,1)} %bitcast.122) | data formatting | bytes 2097152
  5.6 2.4 %collective-permute-start.10 = (bf16[2,2,2,32,512]{4,3,1,0,2:T(8,128)(2,1)S(1)}, bf16[2,2,2,32,512]{4,3,1,0,2:T(8,128)(2,1)S(1)}, u32[]{:S(2)}, u32[]{:S(2)}) collective-permute-start(bf16[2,2,2,32,512]{4,3,1,0,2:T(8,128)(2,1)S(1)} %get-tuple-element.23), channel_id=1, source_target_pairs={{0,2},{2,4},{4,6},{6,8},{8,10},{10,12},{12,14},{14,0},{1,3},{3,5},... | collective-permute-start | bytes 786440 | tf_op jit(solution)/shard_map/ppermute | solution.py:73
  8.1 4.0 %collective-permute-start.11 = (bf16[2,2,2,32,512]{4,3,1,0,2:T(8,128)(2,1)S(1)}, bf16[2,2,2,32,512]{4,3,1,0,2:T(8,128)(2,1)S(1)}, u32[]{:S(2)}, u32[]{:S(2)}) collective-permute-start(bf16[2,2,2,32,512]{4,3,1,0,2:T(8,128)(2,1)S(1)} %get-tuple-element.23), channel_id=1, source_target_pairs={{0,14},{2,0},{4,2},{6,4},{8,6},{10,8},{12,10},{14,12},{1,15},{3,1}... | collective-permute-start | bytes 786440 | tf_op jit(solution)/shard_map/ppermute | solution.py:73
  13.6 2.6 %collective-permute-done = bf16[2,2,32,512]{3,2,1,0:T(8,128)(2,1)S(1)} collective-permute-done((bf16[2,2,32,512]{3,2,1,0:T(8,128)(2,1)S(1)}, bf16[2,2,32,512]{3,2,1,0:T(8,128)(2,1)S(1)}, u32[]{:S(2)}, u32[]{:S(2)}) %collective-permute-start) | collective-permute-done | bytes 131104 | tf_op jit(solution)/shard_map/ppermute | solution.py:73
  16.4 2.7 %collective-permute-start.2 = (bf16[2,2,2,32,512]{4,3,1,0,2:T(8,128)(2,1)S(1)}, bf16[2,2,2,32,512]{4,3,1,0,2:T(8,128)(2,1)S(1)}, u32[]{:S(2)}, u32[]{:S(2)}) collective-permute-start(bf16[2,2,2,32,512]{4,3,1,0,2:T(8,128)(2,1)S(1)} %get-tuple-element.26), channel_id=1, source_target_pairs={{0,14},{2,0},{4,2},{6,4},{8,6},{10,8},{12,10},{14,12},{1,15},{3,1}... | collective-permute-start | bytes 786440 | tf_op jit(solution)/shard_map/ppermute | solution.py:73
  19.4 2.7 %collective-permute-start.13 = (bf16[2,2,2,32,512]{4,3,1,0,2:T(8,128)(2,1)S(1)}, bf16[2,2,2,32,512]{4,3,1,0,2:T(8,128)(2,1)S(1)}, u32[]{:S(2)}, u32[]{:S(2)}) collective-permute-start(bf16[2,2,2,32,512]{4,3,1,0,2:T(8,128)(2,1)S(1)} %collective-permute-done.11), channel_id=1, source_target_pairs={{0,14},{2,0},{4,2},{6,4},{8,6},{10,8},{12,10},{14,12},{1,15},{3,1}... | collective-permute-start | bytes 786440 | tf_op jit(solution)/shard_map/ppermute | solution.py:73
  22.8 2.7 %collective-permute-start.4 = (bf16[2,2,2,32,512]{4,3,1,0,2:T(8,128)(2,1)S(1)}, bf16[2,2,2,32,512]{4,3,1,0,2:T(8,128)(2,1)S(1)}, u32[]{:S(2)}, u32[]{:S(2)}) collective-permute-start(bf16[2,2,2,32,512]{4,3,1,0,2:T(8,128)(2,1)S(1)} %collective-permute-done.2), channel_id=1, source_target_pairs={{0,14},{2,0},{4,2},{6,4},{8,6},{10,8},{12,10},{14,12},{1,15},{3,1}... | collective-permute-start | bytes 786440 | tf_op jit(solution)/shard_map/ppermute | solution.py:73
  25.6 3.3 %collective-permute-done.12 = bf16[2,2,2,32,512]{4,3,1,0,2:T(8,128)(2,1)S(1)} collective-permute-done((bf16[2,2,2,32,512]{4,3,1,0,2:T(8,128)(2,1)S(1)}, bf16[2,2,2,32,512]{4,3,1,0,2:T(8,128)(2,1)S(1)}, u32[]{:S(2)}, u32[]{:S(2)}) %collective-permute-start.12) | collective-permute-done | bytes 262176 | tf_op jit(solution)/shard_map/ppermute | solution.py:73
  28.9 2.7 %collective-permute-start.15 = (bf16[2,2,2,32,512]{4,3,1,0,2:T(8,128)(2,1)S(1)}, bf16[2,2,2,32,512]{4,3,1,0,2:T(8,128)(2,1)S(1)}, u32[]{:S(2)}, u32[]{:S(2)}) collective-permute-start(bf16[2,2,2,32,512]{4,3,1,0,2:T(8,128)(2,1)S(1)} %collective-permute-done.13), channel_id=1, source_target_pairs={{0,14},{2,0},{4,2},{6,4},{8,6},{10,8},{12,10},{14,12},{1,15},{3,1}... | collective-permute-start | bytes 786440 | tf_op jit(solution)/shard_map/ppermute | solution.py:73
  31.6 2.9 %collective-permute-done.3 = bf16[2,2,2,32,512]{4,3,1,0,2:T(8,128)(2,1)S(1)} collective-permute-done((bf16[2,2,2,32,512]{4,3,1,0,2:T(8,128)(2,1)S(1)}, bf16[2,2,2,32,512]{4,3,1,0,2:T(8,128)(2,1)S(1)}, u32[]{:S(2)}, u32[]{:S(2)}) %collective-permute-start.3) | collective-permute-done | bytes 262176 | tf_op jit(solution)/shard_map/ppermute | solution.py:73
  34.5 2.7 %collective-permute-start.6 = (bf16[2,2,2,32,512]{4,3,1,0,2:T(8,128)(2,1)S(1)}, bf16[2,2,2,32,512]{4,3,1,0,2:T(8,128)(2,1)S(1)}, u32[]{:S(2)}, u32[]{:S(2)}) collective-permute-start(bf16[2,2,2,32,512]{4,3,1,0,2:T(8,128)(2,1)S(1)} %collective-permute-done.4), channel_id=1, source_target_pairs={{0,14},{2,0},{4,2},{6,4},{8,6},{10,8},{12,10},{14,12},{1,15},{3,1}... | collective-permute-start | bytes 786440 | tf_op jit(solution)/shard_map/ppermute | solution.py:73
  37.3 1.8 %collective-permute-done.15 = bf16[2,2,2,32,512]{4,3,1,0,2:T(8,128)(2,1)S(1)} collective-permute-done((bf16[2,2,2,32,512]{4,3,1,0,2:T(8,128)(2,1)S(1)}, bf16[2,2,2,32,512]{4,3,1,0,2:T(8,128)(2,1)S(1)}, u32[]{:S(2)}, u32[]{:S(2)}) %collective-permute-start.15) | collective-permute-done | bytes 262176 | tf_op jit(solution)/shard_map/ppermute | solution.py:73
  39.1 3.5 %collective-permute-start.17 = (bf16[2,2,2,16,512]{4,3,1,0,2:T(8,128)(2,1)S(1)}, bf16[2,2,2,16,512]{4,3,1,0,2:T(8,128)(2,1)S(1)}, u32[]{:S(2)}, u32[]{:S(2)}) collective-permute-start(bf16[2,2,2,16,512]{4,3,1,0,2:T(8,128)(2,1)S(1)} %slice.115), channel_id=1, source_target_pairs={{0,14},{2,0},{4,2},{6,4},{8,6},{10,8},{12,10},{14,12},{1,15},{3,1}... | collective-permute-start | bytes 393224 | tf_op jit(solution)/shard_map/ppermute | solution.py:73
  43.0 1.8 %collective-permute-done.6 = bf16[2,2,2,32,512]{4,3,1,0,2:T(8,128)(2,1)S(1)} collective-permute-done((bf16[2,2,2,32,512]{4,3,1,0,2:T(8,128)(2,1)S(1)}, bf16[2,2,2,32,512]{4,3,1,0,2:T(8,128)(2,1)S(1)}, u32[]{:S(2)}, u32[]{:S(2)}) %collective-permute-start.6) | collective-permute-done | bytes 262176 | tf_op jit(solution)/shard_map/ppermute | solution.py:73
  44.7 3.5 %collective-permute-start.8 = (bf16[2,2,2,16,512]{4,3,1,0,2:T(8,128)(2,1)S(1)}, bf16[2,2,2,16,512]{4,3,1,0,2:T(8,128)(2,1)S(1)}, u32[]{:S(2)}, u32[]{:S(2)}) collective-permute-start(bf16[2,2,2,16,512]{4,3,1,0,2:T(8,128)(2,1)S(1)} %slice.110), channel_id=1, source_target_pairs={{0,14},{2,0},{4,2},{6,4},{8,6},{10,8},{12,10},{14,12},{1,15},{3,1}... | collective-permute-start | bytes 393224 | tf_op jit(solution)/shard_map/ppermute | solution.py:73
  49.6 1.5 %collective-permute-done.8 = bf16[2,2,2,16,512]{4,3,1,0,2:T(8,128)(2,1)S(1)} collective-permute-done((bf16[2,2,2,16,512]{4,3,1,0,2:T(8,128)(2,1)S(1)}, bf16[2,2,2,16,512]{4,3,1,0,2:T(8,128)(2,1)S(1)}, u32[]{:S(2)}, u32[]{:S(2)}) %collective-permute-start.8) | collective-permute-done | bytes 131104 | tf_op jit(solution)/shard_map/ppermute | solution.py:73
  51.1 2.2 %collective-permute-done.7 = bf16[2,2,2,16,512]{4,3,1,0,2:T(8,128)(2,1)S(1)} collective-permute-done((bf16[2,2,2,16,512]{4,3,1,0,2:T(8,128)(2,1)S(1)}, bf16[2,2,2,16,512]{4,3,1,0,2:T(8,128)(2,1)S(1)}, u32[]{:S(2)}, u32[]{:S(2)}) %collective-permute-start.7) | collective-permute-done | bytes 131104 | tf_op jit(solution)/shard_map/ppermute | solution.py:73
  53.4 1.3 fusion.31
  56.3 1.7 %neg.21 = bf16[512,16,1,32]{3,1,0,2:T(8,128)(2,1)} negate(bf16[512,16,1,32]{3,1,0,2:T(8,128)(2,1)S(1)} %reshape_squeeze.10) | non-fusion elementwise | flops 262144 | bytes 1048576 | tf_op jit(solution)/shard_map/neg | solution.py:36
  58.0 1.6 %copy.56 = bf16[512,16,1,32]{0,3,2,1:T(8,128)(2,1)S(1)} copy(bf16[512,16,1,32]{3,1,0,2:T(8,128)(2,1)S(1)} %reshape_squeeze.10) | data formatting | bytes 1048576 | tf_op jit(solution)/shard_map/reshape;squeeze | solution.py:34
  59.6 1.2 reshape_squeeze.9
  60.8 1.6 %copy.55 = bf16[512,16,1,32]{0,3,2,1:T(8,128)(2,1)S(1)} copy(bf16[512,16,1,32]{3,1,0,2:T(8,128)(2,1)S(1)} %reshape_squeeze.9) | data formatting | bytes 1048576 | tf_op jit(solution)/shard_map/reshape;squeeze | solution.py:33
  62.5 2.5 %copy.57 = bf16[512,16,1,32]{0,3,2,1:T(8,128)(2,1)S(1)} copy(bf16[512,16,1,32]{3,1,0,2:T(8,128)(2,1)} %neg.21) | data formatting | bytes 1048576 | tf_op jit(solution)/shard_map/neg | solution.py:36
  66.5 1.3 %fusion.11 = bf16[1024,512]{1,0:T(8,128)(2,1)S(1)} fusion(bf16[512,1024]{1,0:T(8,128)(2,1)S(1)} %bitcast.123, bf16[512,512]{1,0:T(8,128)(2,1)S(1)} %bitcast.127, bf16[512,512]{1,0:T(8,128)(2,1)S(1)} %bitcast_negate_fusion.1, bf16[512,512]{1,0:T(8,128)(2,1)S(1)} %bitcast.118), kind=kOutput, calls=%fused_computation.15 | convolution fusion | flops 1082654720 | bytes 3670016 | tf_op jit(solution)/shard_map/dot_general | solution.py:15
  68.5 1.7 %add_convert_fusion.1 = bf16[1024,512]{1,0:T(8,128)(2,1)} fusion(f32[1024,512]{1,0:T(8,128)S(1)} %fusion.23, bf16[512,1024]{0,1:T(8,128)(2,1)S(1)} %bitcast.111, bf16[512,2,512]{0,2,1:T(8,128)(2,1)S(1)} %bitcast.121), kind=kOutput, calls=%fused_computation.14 | convolution fusion | flops 537919488 | bytes 4718592 | tf_op jit(solution)/shard_map/ix,ij->xj/dot_general | solution.py:38
  70.2 14.0 %all-to-all-start = ((bf16[16,2,32,512]{3,2,1,0:T(8,128)(2,1)}), bf16[16,2,32,512]{3,2,1,0:T(8,128)(2,1)}, u32[]{:S(2)}, u32[]{:S(2)}) async-start(bf16[16,2,32,512]{3,2,1,0:T(8,128)(2,1)} %bitcast.34), calls=%async_computation | async-start | bytes 2097152 | tf_op jit(solution)/shard_map/all_to_all | solution.py:120
  84.6 1.3 %maximum_bitcast_fusion.4 = (bf16[1,512,1024]{2,1,0:T(8,128)(2,1)S(1)}, bf16[1,512,1024]{2,1,0:T(8,128)(2,1)}) fusion(bf16[512,512]{1,0:T(8,128)(2,1)S(1)} %bitcast.109, bf16[512,512]{1,0:T(8,128)(2,1)S(1)} %bitcast.115, bf16[512,512]{1,0:T(8,128)(2,1)S(1)} %bitcast_negate_fusion), kind=kLoop, calls=%fused_computation.22 | loop fusion | flops 4194304 | bytes 3670016 | tf_op jit(solution)/shard_map/stack | solution.py:24
  86.0 15.5 %all-to-all-done = bf16[16,2,32,512]{3,2,1,0:T(8,128)(2,1)} async-done(((bf16[16,2,32,512]{3,2,1,0:T(8,128)(2,1)}), bf16[16,2,32,512]{3,2,1,0:T(8,128)(2,1)}, u32[]{:S(2)}, u32[]{:S(2)}) %all-to-all-start) | async-done | bytes 1048608 | tf_op jit(solution)/shard_map/all_to_all | solution.py:120
  101.4 2.8 %bitcast_convert_fusion = bf16[16,32,1024]{2,1,0:T(8,128)(2,1)S(1)} fusion(bf16[16,2,32,512]{3,2,1,0:T(8,128)(2,1)} %all-to-all-done, bf16[1,512,1024]{2,1,0:T(8,128)(2,1)} %get-tuple-element.16, bf16[1,512,1024]{2,1,0:T(8,128)(2,1)S(1)} %get-tuple-element.15), kind=kOutput, calls=%fused_computation.12 | convolution fusion | flops 1075314688 | bytes 4194304 | tf_op jit(solution)/shard_map/pcly,cyk->plk/dot_general | solution.py:25
  106.0 20.3 %all_to_all.10 = bf16[1,512,2,16,32]{1,4,2,0,3:T(8,128)(2,1)S(1)} all-to-all(bf16[1,512,2,16,32]{1,4,2,0,3:T(8,128)(2,1)S(1)} %pad_maximum_fusion.2), channel_id=1, replica_groups=mesh['row'=16,'cz'=8,'cx'=2] {'row'}, dimensions={3} | all-to-all | bytes 2097152 | tf_op jit(solution)/shard_map/all_to_all | solution.py:126
  126.4 2.1 %copy.62 = bf16[1,1,1,512,2,512]{5,4,3,2,1,0:T(2,128)(2,1)} copy(bf16[1,1,1,512,2,512]{3,5,4,2,1,0:T(8,128)(2,1)S(1)} %bitcast.112) | data formatting | bytes 2097152 | tf_op jit(solution)/shard_map/reshape | solution.py:127
  (69 shorter events, 11.5 us)
Async XLA Ops:
  0.0 5.6 %copy-start.4 = (bf16[1,4,2,512,32]{3,4,2,1,0:T(8,128)(2,1)S(1)}, bf16[1,4,2,512,32]{3,4,2,1,0:T(8,128)(2,1)}, u32[]{:S(2)}) copy-start(bf16[1,4,2,512,32]{3,4,2,1,0:T(8,128)(2,1)} %param.3) | copy-start | bytes 786436
  1.0 4.6 %collective-permute-start.9 = (bf16[2,2,32,512]{3,2,1,0:T(8,128)(2,1)S(1)}, bf16[2,2,32,512]{3,2,1,0:T(8,128)(2,1)S(1)}, u32[]{:S(2)}, u32[]{:S(2)}) collective-permute-start(bf16[2,2,32,512]{3,2,1,0:T(8,128)(2,1)S(1)} %slice.113), channel_id=1, source_target_pairs={{0,1},{1,0},{2,3},{3,2},{4,5},{5,4},{6,7},{7,6},{8,9},{9,8},{10,11... | collective-permute-start | bytes 393224 | tf_op jit(solution)/shard_map/ppermute | solution.py:73
  5.6 13.7 %collective-permute-start.10 = (bf16[2,2,2,32,512]{4,3,1,0,2:T(8,128)(2,1)S(1)}, bf16[2,2,2,32,512]{4,3,1,0,2:T(8,128)(2,1)S(1)}, u32[]{:S(2)}, u32[]{:S(2)}) collective-permute-start(bf16[2,2,2,32,512]{4,3,1,0,2:T(8,128)(2,1)S(1)} %get-tuple-element.23), channel_id=1, source_target_pairs={{0,2},{2,4},{4,6},{6,8},{8,10},{10,12},{12,14},{14,0},{1,3},{3,5},... | collective-permute-start | bytes 786440 | tf_op jit(solution)/shard_map/ppermute | solution.py:73
  8.1 11.4 %collective-permute-start.11 = (bf16[2,2,2,32,512]{4,3,1,0,2:T(8,128)(2,1)S(1)}, bf16[2,2,2,32,512]{4,3,1,0,2:T(8,128)(2,1)S(1)}, u32[]{:S(2)}, u32[]{:S(2)}) collective-permute-start(bf16[2,2,2,32,512]{4,3,1,0,2:T(8,128)(2,1)S(1)} %get-tuple-element.23), channel_id=1, source_target_pairs={{0,14},{2,0},{4,2},{6,4},{8,6},{10,8},{12,10},{14,12},{1,15},{3,1}... | collective-permute-start | bytes 786440 | tf_op jit(solution)/shard_map/ppermute | solution.py:73
  12.1 4.1 %collective-permute-start = (bf16[2,2,32,512]{3,2,1,0:T(8,128)(2,1)S(1)}, bf16[2,2,32,512]{3,2,1,0:T(8,128)(2,1)S(1)}, u32[]{:S(2)}, u32[]{:S(2)}) collective-permute-start(bf16[2,2,32,512]{3,2,1,0:T(8,128)(2,1)S(1)} %get-tuple-element.25), channel_id=1, source_target_pairs={{0,1},{1,0},{2,3},{3,2},{4,5},{5,4},{6,7},{7,6},{8,9},{9,8},{10,11... | collective-permute-start | bytes 393224 | tf_op jit(solution)/shard_map/ppermute | solution.py:73
  16.3 6.5 %collective-permute-start.1 = (bf16[2,2,2,32,512]{4,3,1,0,2:T(8,128)(2,1)S(1)}, bf16[2,2,2,32,512]{4,3,1,0,2:T(8,128)(2,1)S(1)}, u32[]{:S(2)}, u32[]{:S(2)}) collective-permute-start(bf16[2,2,2,32,512]{4,3,1,0,2:T(8,128)(2,1)S(1)} %get-tuple-element.26), channel_id=1, source_target_pairs={{0,2},{2,4},{4,6},{6,8},{8,10},{10,12},{12,14},{14,0},{1,3},{3,5},... | collective-permute-start | bytes 786440 | tf_op jit(solution)/shard_map/ppermute | solution.py:73
  16.4 6.5 %collective-permute-start.2 = (bf16[2,2,2,32,512]{4,3,1,0,2:T(8,128)(2,1)S(1)}, bf16[2,2,2,32,512]{4,3,1,0,2:T(8,128)(2,1)S(1)}, u32[]{:S(2)}, u32[]{:S(2)}) collective-permute-start(bf16[2,2,2,32,512]{4,3,1,0,2:T(8,128)(2,1)S(1)} %get-tuple-element.26), channel_id=1, source_target_pairs={{0,14},{2,0},{4,2},{6,4},{8,6},{10,8},{12,10},{14,12},{1,15},{3,1}... | collective-permute-start | bytes 786440 | tf_op jit(solution)/shard_map/ppermute | solution.py:73
  19.3 9.5 %collective-permute-start.12 = (bf16[2,2,2,32,512]{4,3,1,0,2:T(8,128)(2,1)S(1)}, bf16[2,2,2,32,512]{4,3,1,0,2:T(8,128)(2,1)S(1)}, u32[]{:S(2)}, u32[]{:S(2)}) collective-permute-start(bf16[2,2,2,32,512]{4,3,1,0,2:T(8,128)(2,1)S(1)} %collective-permute-done.10), channel_id=1, source_target_pairs={{0,2},{2,4},{4,6},{6,8},{8,10},{10,12},{12,14},{14,0},{1,3},{3,5},... | collective-permute-start | bytes 786440 | tf_op jit(solution)/shard_map/ppermute | solution.py:73
  19.4 9.4 %collective-permute-start.13 = (bf16[2,2,2,32,512]{4,3,1,0,2:T(8,128)(2,1)S(1)}, bf16[2,2,2,32,512]{4,3,1,0,2:T(8,128)(2,1)S(1)}, u32[]{:S(2)}, u32[]{:S(2)}) collective-permute-start(bf16[2,2,2,32,512]{4,3,1,0,2:T(8,128)(2,1)S(1)} %collective-permute-done.11), channel_id=1, source_target_pairs={{0,14},{2,0},{4,2},{6,4},{8,6},{10,8},{12,10},{14,12},{1,15},{3,1}... | collective-permute-start | bytes 786440 | tf_op jit(solution)/shard_map/ppermute | solution.py:73
  22.8 11.7 %collective-permute-start.3 = (bf16[2,2,2,32,512]{4,3,1,0,2:T(8,128)(2,1)S(1)}, bf16[2,2,2,32,512]{4,3,1,0,2:T(8,128)(2,1)S(1)}, u32[]{:S(2)}, u32[]{:S(2)}) collective-permute-start(bf16[2,2,2,32,512]{4,3,1,0,2:T(8,128)(2,1)S(1)} %collective-permute-done.1), channel_id=1, source_target_pairs={{0,2},{2,4},{4,6},{6,8},{8,10},{10,12},{12,14},{14,0},{1,3},{3,5},... | collective-permute-start | bytes 786440 | tf_op jit(solution)/shard_map/ppermute | solution.py:73
  22.8 11.7 %collective-permute-start.4 = (bf16[2,2,2,32,512]{4,3,1,0,2:T(8,128)(2,1)S(1)}, bf16[2,2,2,32,512]{4,3,1,0,2:T(8,128)(2,1)S(1)}, u32[]{:S(2)}, u32[]{:S(2)}) collective-permute-start(bf16[2,2,2,32,512]{4,3,1,0,2:T(8,128)(2,1)S(1)} %collective-permute-done.2), channel_id=1, source_target_pairs={{0,14},{2,0},{4,2},{6,4},{8,6},{10,8},{12,10},{14,12},{1,15},{3,1}... | collective-permute-start | bytes 786440 | tf_op jit(solution)/shard_map/ppermute | solution.py:73
  28.9 13.7 %collective-permute-start.14 = (bf16[2,2,2,32,512]{4,3,1,0,2:T(8,128)(2,1)S(1)}, bf16[2,2,2,32,512]{4,3,1,0,2:T(8,128)(2,1)S(1)}, u32[]{:S(2)}, u32[]{:S(2)}) collective-permute-start(bf16[2,2,2,32,512]{4,3,1,0,2:T(8,128)(2,1)S(1)} %collective-permute-done.12), channel_id=1, source_target_pairs={{0,2},{2,4},{4,6},{6,8},{8,10},{10,12},{12,14},{14,0},{1,3},{3,5},... | collective-permute-start | bytes 786440 | tf_op jit(solution)/shard_map/ppermute | solution.py:73
  28.9 10.2 %collective-permute-start.15 = (bf16[2,2,2,32,512]{4,3,1,0,2:T(8,128)(2,1)S(1)}, bf16[2,2,2,32,512]{4,3,1,0,2:T(8,128)(2,1)S(1)}, u32[]{:S(2)}, u32[]{:S(2)}) collective-permute-start(bf16[2,2,2,32,512]{4,3,1,0,2:T(8,128)(2,1)S(1)} %collective-permute-done.13), channel_id=1, source_target_pairs={{0,14},{2,0},{4,2},{6,4},{8,6},{10,8},{12,10},{14,12},{1,15},{3,1}... | collective-permute-start | bytes 786440 | tf_op jit(solution)/shard_map/ppermute | solution.py:73
  34.5 13.7 %collective-permute-start.5 = (bf16[2,2,2,32,512]{4,3,1,0,2:T(8,128)(2,1)S(1)}, bf16[2,2,2,32,512]{4,3,1,0,2:T(8,128)(2,1)S(1)}, u32[]{:S(2)}, u32[]{:S(2)}) collective-permute-start(bf16[2,2,2,32,512]{4,3,1,0,2:T(8,128)(2,1)S(1)} %collective-permute-done.3), channel_id=1, source_target_pairs={{0,2},{2,4},{4,6},{6,8},{8,10},{10,12},{12,14},{14,0},{1,3},{3,5},... | collective-permute-start | bytes 786440 | tf_op jit(solution)/shard_map/ppermute | solution.py:73
  34.5 10.2 %collective-permute-start.6 = (bf16[2,2,2,32,512]{4,3,1,0,2:T(8,128)(2,1)S(1)}, bf16[2,2,2,32,512]{4,3,1,0,2:T(8,128)(2,1)S(1)}, u32[]{:S(2)}, u32[]{:S(2)}) collective-permute-start(bf16[2,2,2,32,512]{4,3,1,0,2:T(8,128)(2,1)S(1)} %collective-permute-done.4), channel_id=1, source_target_pairs={{0,14},{2,0},{4,2},{6,4},{8,6},{10,8},{12,10},{14,12},{1,15},{3,1}... | collective-permute-start | bytes 786440 | tf_op jit(solution)/shard_map/ppermute | solution.py:73
  39.1 9.3 %collective-permute-start.17 = (bf16[2,2,2,16,512]{4,3,1,0,2:T(8,128)(2,1)S(1)}, bf16[2,2,2,16,512]{4,3,1,0,2:T(8,128)(2,1)S(1)}, u32[]{:S(2)}, u32[]{:S(2)}) collective-permute-start(bf16[2,2,2,16,512]{4,3,1,0,2:T(8,128)(2,1)S(1)} %slice.115), channel_id=1, source_target_pairs={{0,14},{2,0},{4,2},{6,4},{8,6},{10,8},{12,10},{14,12},{1,15},{3,1}... | collective-permute-start | bytes 393224 | tf_op jit(solution)/shard_map/ppermute | solution.py:73
  42.6 7.0 %collective-permute-start.16 = (bf16[2,2,2,16,512]{4,3,1,0,2:T(8,128)(2,1)S(1)}, bf16[2,2,2,16,512]{4,3,1,0,2:T(8,128)(2,1)S(1)}, u32[]{:S(2)}, u32[]{:S(2)}) collective-permute-start(bf16[2,2,2,16,512]{4,3,1,0,2:T(8,128)(2,1)S(1)} %slice.114), channel_id=1, source_target_pairs={{0,2},{2,4},{4,6},{6,8},{8,10},{10,12},{12,14},{14,0},{1,3},{3,5},... | collective-permute-start | bytes 393224 | tf_op jit(solution)/shard_map/ppermute | solution.py:73
  44.7 6.4 %collective-permute-start.8 = (bf16[2,2,2,16,512]{4,3,1,0,2:T(8,128)(2,1)S(1)}, bf16[2,2,2,16,512]{4,3,1,0,2:T(8,128)(2,1)S(1)}, u32[]{:S(2)}, u32[]{:S(2)}) collective-permute-start(bf16[2,2,2,16,512]{4,3,1,0,2:T(8,128)(2,1)S(1)} %slice.110), channel_id=1, source_target_pairs={{0,14},{2,0},{4,2},{6,4},{8,6},{10,8},{12,10},{14,12},{1,15},{3,1}... | collective-permute-start | bytes 393224 | tf_op jit(solution)/shard_map/ppermute | solution.py:73
  48.2 5.1 %collective-permute-start.7 = (bf16[2,2,2,16,512]{4,3,1,0,2:T(8,128)(2,1)S(1)}, bf16[2,2,2,16,512]{4,3,1,0,2:T(8,128)(2,1)S(1)}, u32[]{:S(2)}, u32[]{:S(2)}) collective-permute-start(bf16[2,2,2,16,512]{4,3,1,0,2:T(8,128)(2,1)S(1)} %slice.109), channel_id=1, source_target_pairs={{0,2},{2,4},{4,6},{6,8},{8,10},{10,12},{12,14},{14,0},{1,3},{3,5},... | collective-permute-start | bytes 393224 | tf_op jit(solution)/shard_map/ppermute | solution.py:73
  53.4 1.7 %copy-start = (bf16[2,2,8,2,32,512]{5,4,3,2,1,0:T(8,128)(2,1)}, bf16[2,2,8,2,32,512]{5,4,3,2,1,0:T(8,128)(2,1)S(1)}, u32[]{:S(2)}) copy-start(bf16[2,2,8,2,32,512]{5,4,3,2,1,0:T(8,128)(2,1)S(1)} %get-tuple-element.29) | copy-start | bytes 6291460
  62.5 2.6 %copy-start.2 = (bf16[1,1,8,2,32,512]{5,4,3,2,1,0:T(8,128)(2,1)S(1)}, bf16[1,1,8,2,32,512]{5,4,3,2,1,0:T(8,128)(2,1)}, u32[]{:S(2)}) copy-start(bf16[1,1,8,2,32,512]{5,4,3,2,1,0:T(8,128)(2,1)} %get-tuple-element.9) | copy-start | bytes 1572868
  65.1 1.2 copy-start.3
  65.1 1.3 %copy-start.5 = (bf16[1,1,8,2,32,512]{5,4,3,2,1,0:T(8,128)(2,1)S(1)}, bf16[1,1,8,2,32,512]{5,4,3,2,1,0:T(8,128)(2,1)}, u32[]{:S(2)}) copy-start(bf16[1,1,8,2,32,512]{5,4,3,2,1,0:T(8,128)(2,1)} %get-tuple-element.10) | copy-start | bytes 1572868
  70.2 14.0 %copy-start.1 = (bf16[2,2,8,2,32,512]{5,4,3,2,1,0:T(8,128)(2,1)S(1)}, bf16[2,2,8,2,32,512]{5,4,3,2,1,0:T(8,128)(2,1)}, u32[]{:S(2)}) copy-start(bf16[2,2,8,2,32,512]{5,4,3,2,1,0:T(8,128)(2,1)} %copy-done) | copy-start | bytes 6291460
  70.2 31.2 %all-to-all-start = ((bf16[16,2,32,512]{3,2,1,0:T(8,128)(2,1)}), bf16[16,2,32,512]{3,2,1,0:T(8,128)(2,1)}, u32[]{:S(2)}, u32[]{:S(2)}) async-start(bf16[16,2,32,512]{3,2,1,0:T(8,128)(2,1)} %bitcast.34), calls=%async_computation | async-start | bytes 2097152 | tf_op jit(solution)/shard_map/all_to_all | solution.py:120

commit v7 on v5

--- a/solution.py
+++ b/solution.py
@@ -71,13 +71,12 @@
     return lax.ppermute(x, axis, [(i, (i + d) % n) for i in range(n)])
 
 
-def ring_gather(t):
+def ring_gather(t, other):
     nz = lax.axis_size("cz")
     nx = lax.axis_size("cx")
     z = lax.axis_index("cz")
     x = lax.axis_index("cx")
     nb, comps, width, cols = t.shape
-    other = shift(t, "cx", nx, 1)
     first = jnp.where(x == 0, t, other)
     second = jnp.where(x == 0, other, t)
     pair = jnp.stack([first, second], axis=2)
@@ -109,8 +108,9 @@
     row_count = lax.axis_size("row")
     share = order_size // row_count
     own_t = jnp.swapaxes(branch[0], -1, -2)
-    first_t = ring_gather(own_t[:2])
-    second_t = ring_gather(own_t[2:])
+    partner_t = shift(own_t, "cx", lax.axis_size("cx"), 1)
+    first_t = ring_gather(own_t[:2], partner_t[:2])
+    second_t = ring_gather(own_t[2:], partner_t[2:])
 
     block = stem[0, 0]
     half_first = right_piece(block, first_t[1]).astype(jnp.bfloat16)

time: 112 us -> 115 us (1.027)
  other arithmetic: 0.58 us -> 2.92 us
  starting transfers between devices: 40.2 us -> 38.8 us
    another operation x4 -> x3, other arithmetic: 0.11 us -> 2.45 us  [ring_gather(): pair = jnp.stack([first, second], axis=2)]
    dynamic_update_slice x6, local copies, waits for them, and re-layouts: 0.12 us -> 2.03 us  [ring_gather(): lax.dynamic_update_slice(buf, cur_f[:, :, None], (0, 0, (z - k) % nz, 0,...]
    unnamed x9, local copies, waits for them, and re-layouts: 2.65 us -> 1.42 us
    ppermute x18 -> x17, starting transfers between devices: 29.4 us -> 28.2 us  [shift(): return lax.ppermute(x, axis, [(i, (i + d) % n) for i in range(n)])]
    ppermute x18 -> x17, waiting for transfers between devices: 19.1 us -> 20.2 us  [shift(): return lax.ppermute(x, axis, [(i, (i + d) % n) for i in range(n)])]
  transfers between devices with their start and end apart: 19 -> 18, of which waited for: 9 -> 9; matrix products, arithmetic and copies ran while one was open for 3% -> 5% of each run, Pallas kernels for 0% -> 0%
where the time goes in v7:
time: 115 us
  starting transfers between devices  38.8 us (34%)
  waiting for transfers between devices  35.5 us (31%)
  blocking collectives  20.3 us (18%)
  local copies, waits for them, and re-layouts  10.9 us (9%)
  matrix products  5.79 us (5%)
  other arithmetic  2.92 us (3%)
    ppermute x17, starting transfers between devices, shift(): return lax.ppermute(x, axis, [(i, (i + d) % n) for i in range(n)])  28.2 us
    all_to_all x1, blocking collectives, shards(): lax.all_to_all(leaving, 'row', split_axis=3, concat_axis=3, tiled=True)  20.3 us
    ppermute x17, waiting for transfers between devices, shift(): return lax.ppermute(x, axis, [(i, (i + d) % n) for i in range(n)])  20.2 us
    all_to_all x1, waiting for transfers between devices, shards(): lax.all_to_all(outgoing, 'row', split_axis=1, concat_axis=1, tiled=True)  15.3 us
    all_to_all x1, starting transfers between devices, shards(): lax.all_to_all(outgoing, 'row', split_axis=1, concat_axis=1, tiled=True)  10.6 us
    another operation x3, other arithmetic, ring_gather(): pair = jnp.stack([first, second], axis=2)  2.45 us
  transfers between devices with their start and end apart: 18, of which 9 were waited for; matrix products, arithmetic and copies ran while one was open for 5% of the time, Pallas kernels for 0%

profile of v7, /device:TPU:1, one launch (start us, length us, event | category | flops | bytes accessed | tf_op | source)
XLA Modules:
  0.0 114.7 jit_solution(8678192047657300659)
XLA Ops:
  0.0 2.0 %collective-permute-start = (bf16[4,2,32,512]{3,2,1,0:T(8,128)(2,1)}, bf16[4,2,32,512]{3,2,1,0:T(8,128)(2,1)S(1)}, u32[]{:S(2)}, u32[]{:S(2)}) collective-permute-start(bf16[4,2,32,512]{3,2,1,0:T(8,128)(2,1)} %bitcast.105), channel_id=1, source_target_pairs={{0,1},{1,0},{2,3},{3,2},{4,5},{5,4},{6,7},{7,6},{8,9},{9,8},{10,11... | collective-permute-start | bytes 786440 | tf_op jit(solution)/shard_map/ppermute | solution.py:71
  2.0 5.1 %collective-permute-done = bf16[4,2,32,512]{3,2,1,0:T(8,128)(2,1)S(1)} collective-permute-done((bf16[4,2,32,512]{3,2,1,0:T(8,128)(2,1)}, bf16[4,2,32,512]{3,2,1,0:T(8,128)(2,1)S(1)}, u32[]{:S(2)}, u32[]{:S(2)}) %collective-permute-start) | collective-permute-done | bytes 262176 | tf_op jit(solution)/shard_map/ppermute | solution.py:71
  7.1 1.0 select_bitcast_fusion.1
  8.8 2.7 %collective-permute-start.9 = (bf16[2,2,2,32,512]{4,3,1,0,2:T(8,128)(2,1)}, bf16[2,2,2,32,512]{4,3,1,0,2:T(8,128)(2,1)}, u32[]{:S(2)}, u32[]{:S(2)}) collective-permute-start(bf16[2,2,2,32,512]{4,3,1,0,2:T(8,128)(2,1)} %pad_maximum_fusion.2), channel_id=1, source_target_pairs={{0,2},{2,4},{4,6},{6,8},{8,10},{10,12},{12,14},{14,0},{1,3},{3,5},... | collective-permute-start | bytes 786440 | tf_op jit(solution)/shard_map/ppermute | solution.py:71
  11.6 3.9 %collective-permute-start.10 = (bf16[2,2,2,32,512]{4,3,1,0,2:T(8,128)(2,1)}, bf16[2,2,2,32,512]{4,3,1,0,2:T(8,128)(2,1)}, u32[]{:S(2)}, u32[]{:S(2)}) collective-permute-start(bf16[2,2,2,32,512]{4,3,1,0,2:T(8,128)(2,1)} %pad_maximum_fusion.2), channel_id=1, source_target_pairs={{0,14},{2,0},{4,2},{6,4},{8,6},{10,8},{12,10},{14,12},{1,15},{3,1}... | collective-permute-start | bytes 786440 | tf_op jit(solution)/shard_map/ppermute | solution.py:71
  16.5 2.7 %collective-permute-start.2 = (bf16[2,2,2,32,512]{4,3,1,0,2:T(8,128)(2,1)}, bf16[2,2,2,32,512]{4,3,1,0,2:T(8,128)(2,1)S(1)}, u32[]{:S(2)}, u32[]{:S(2)}) collective-permute-start(bf16[2,2,2,32,512]{4,3,1,0,2:T(8,128)(2,1)} %pad_maximum_fusion.1), channel_id=1, source_target_pairs={{0,14},{2,0},{4,2},{6,4},{8,6},{10,8},{12,10},{14,12},{1,15},{3,1}... | collective-permute-start | bytes 786440 | tf_op jit(solution)/shard_map/ppermute | solution.py:71
  19.9 1.1 collective-permute-done.9
  21.0 2.7 %collective-permute-start.12 = (bf16[2,2,2,32,512]{4,3,1,0,2:T(8,128)(2,1)}, bf16[2,2,2,32,512]{4,3,1,0,2:T(8,128)(2,1)S(1)}, u32[]{:S(2)}, u32[]{:S(2)}) collective-permute-start(bf16[2,2,2,32,512]{4,3,1,0,2:T(8,128)(2,1)} %collective-permute-done.10), channel_id=1, source_target_pairs={{0,14},{2,0},{4,2},{6,4},{8,6},{10,8},{12,10},{14,12},{1,15},{3,1}... | collective-permute-start | bytes 786440 | tf_op jit(solution)/shard_map/ppermute | solution.py:71
  23.7 2.9 %collective-permute-done.1 = bf16[2,2,2,32,512]{4,3,1,0,2:T(8,128)(2,1)} collective-permute-done((bf16[2,2,2,32,512]{4,3,1,0,2:T(8,128)(2,1)}, bf16[2,2,2,32,512]{4,3,1,0,2:T(8,128)(2,1)}, u32[]{:S(2)}, u32[]{:S(2)}) %collective-permute-start.1) | collective-permute-done | bytes 262176 | tf_op jit(solution)/shard_map/ppermute | solution.py:71
  26.6 1.0 bitcast_dynamic-update-slice_fusion.5
  27.6 1.0 bitcast_dynamic-update-slice_fusion.12
  28.6 2.7 %collective-permute-start.4 = (bf16[2,2,2,32,512]{4,3,1,0,2:T(8,128)(2,1)S(1)}, bf16[2,2,2,32,512]{4,3,1,0,2:T(8,128)(2,1)S(1)}, u32[]{:S(2)}, u32[]{:S(2)}) collective-permute-start(bf16[2,2,2,32,512]{4,3,1,0,2:T(8,128)(2,1)S(1)} %collective-permute-done.2), channel_id=1, source_target_pairs={{0,14},{2,0},{4,2},{6,4},{8,6},{10,8},{12,10},{14,12},{1,15},{3,1}... | collective-permute-start | bytes 786440 | tf_op jit(solution)/shard_map/ppermute | solution.py:71
  31.3 1.0 bitcast_dynamic-update-slice_fusion.4
  32.4 2.7 %collective-permute-start.14 = (bf16[2,2,2,32,512]{4,3,1,0,2:T(8,128)(2,1)S(1)}, bf16[2,2,2,32,512]{4,3,1,0,2:T(8,128)(2,1)S(1)}, u32[]{:S(2)}, u32[]{:S(2)}) collective-permute-start(bf16[2,2,2,32,512]{4,3,1,0,2:T(8,128)(2,1)S(1)} %collective-permute-done.12), channel_id=1, source_target_pairs={{0,14},{2,0},{4,2},{6,4},{8,6},{10,8},{12,10},{14,12},{1,15},{3,1}... | collective-permute-start | bytes 786440 | tf_op jit(solution)/shard_map/ppermute | solution.py:71
  35.1 2.6 %collective-permute-done.3 = bf16[2,2,2,32,512]{4,3,1,0,2:T(8,128)(2,1)S(1)} collective-permute-done((bf16[2,2,2,32,512]{4,3,1,0,2:T(8,128)(2,1)}, bf16[2,2,2,32,512]{4,3,1,0,2:T(8,128)(2,1)S(1)}, u32[]{:S(2)}, u32[]{:S(2)}) %collective-permute-start.3) | collective-permute-done | bytes 262176 | tf_op jit(solution)/shard_map/ppermute | solution.py:71
  37.8 2.7 %collective-permute-start.6 = (bf16[2,2,2,32,512]{4,3,1,0,2:T(8,128)(2,1)S(1)}, bf16[2,2,2,32,512]{4,3,1,0,2:T(8,128)(2,1)S(1)}, u32[]{:S(2)}, u32[]{:S(2)}) collective-permute-start(bf16[2,2,2,32,512]{4,3,1,0,2:T(8,128)(2,1)S(1)} %collective-permute-done.4), channel_id=1, source_target_pairs={{0,14},{2,0},{4,2},{6,4},{8,6},{10,8},{12,10},{14,12},{1,15},{3,1}... | collective-permute-start | bytes 786440 | tf_op jit(solution)/shard_map/ppermute | solution.py:71
  40.6 2.7 %collective-permute-done.13 = bf16[2,2,2,32,512]{4,3,1,0,2:T(8,128)(2,1)S(1)} collective-permute-done((bf16[2,2,2,32,512]{4,3,1,0,2:T(8,128)(2,1)S(1)}, bf16[2,2,2,32,512]{4,3,1,0,2:T(8,128)(2,1)S(1)}, u32[]{:S(2)}, u32[]{:S(2)}) %collective-permute-start.13) | collective-permute-done | bytes 262176 | tf_op jit(solution)/shard_map/ppermute | solution.py:71
  43.5 2.9 %collective-permute-start.16 = (bf16[2,2,2,16,512]{4,3,1,0,2:T(8,128)(2,1)S(1)}, bf16[2,2,2,16,512]{4,3,1,0,2:T(8,128)(2,1)S(1)}, u32[]{:S(2)}, u32[]{:S(2)}) collective-permute-start(bf16[2,2,2,16,512]{4,3,1,0,2:T(8,128)(2,1)S(1)} %slice.135), channel_id=1, source_target_pairs={{0,14},{2,0},{4,2},{6,4},{8,6},{10,8},{12,10},{14,12},{1,15},{3,1}... | collective-permute-start | bytes 393224 | tf_op jit(solution)/shard_map/ppermute | solution.py:71
  46.4 2.6 %collective-permute-done.5 = bf16[2,2,2,32,512]{4,3,1,0,2:T(8,128)(2,1)S(1)} collective-permute-done((bf16[2,2,2,32,512]{4,3,1,0,2:T(8,128)(2,1)S(1)}, bf16[2,2,2,32,512]{4,3,1,0,2:T(8,128)(2,1)S(1)}, u32[]{:S(2)}, u32[]{:S(2)}) %collective-permute-start.5) | collective-permute-done | bytes 262176 | tf_op jit(solution)/shard_map/ppermute | solution.py:71
  49.1 2.7 %collective-permute-start.8 = (bf16[2,2,2,16,512]{4,3,1,0,2:T(8,128)(2,1)S(1)}, bf16[2,2,2,16,512]{4,3,1,0,2:T(8,128)(2,1)S(1)}, u32[]{:S(2)}, u32[]{:S(2)}) collective-permute-start(bf16[2,2,2,16,512]{4,3,1,0,2:T(8,128)(2,1)S(1)} %slice.129), channel_id=1, source_target_pairs={{0,14},{2,0},{4,2},{6,4},{8,6},{10,8},{12,10},{14,12},{1,15},{3,1}... | collective-permute-start | bytes 393224 | tf_op jit(solution)/shard_map/ppermute | solution.py:71
  52.0 2.6 %collective-permute-done.7 = bf16[2,2,2,16,512]{4,3,1,0,2:T(8,128)(2,1)S(1)} collective-permute-done((bf16[2,2,2,16,512]{4,3,1,0,2:T(8,128)(2,1)S(1)}, bf16[2,2,2,16,512]{4,3,1,0,2:T(8,128)(2,1)S(1)}, u32[]{:S(2)}, u32[]{:S(2)}) %collective-permute-start.7) | collective-permute-done | bytes 131104 | tf_op jit(solution)/shard_map/ppermute | solution.py:71
  55.5 1.3 %fusion.8 = bf16[1024,512]{1,0:T(8,128)(2,1)S(1)} fusion(bf16[512,1024]{1,0:T(8,128)(2,1)S(1)} %bitcast.101, bf16[512,512]{1,0:T(8,128)(2,1)S(1)} %bitcast.102, bf16[512,512]{1,0:T(8,128)(2,1)S(1)} %bitcast_negate_fusion.1, bf16[512,512]{1,0:T(8,128)(2,1)S(1)} %bitcast.99), kind=kOutput, calls=%fused_computation.11 | convolution fusion | flops 1082654720 | bytes 3670016 | tf_op jit(solution)/shard_map/dot_general | solution.py:15
  57.6 0.8 add_convert_fusion.2
  58.3 1.0 copy.5
  59.4 10.6 %all-to-all-start = ((bf16[2,16,32,512]{3,2,0,1:T(8,128)(2,1)}), bf16[2,16,32,512]{3,2,0,1:T(8,128)(2,1)}, u32[]{:S(2)}, u32[]{:S(2)}) async-start(bf16[2,16,32,512]{3,2,0,1:T(8,128)(2,1)} %copy.5), calls=%async_computation | async-start | bytes 2097152 | tf_op jit(solution)/shard_map/all_to_all | solution.py:119
  70.0 1.0 fusion.43
  71.9 15.3 %all-to-all-done = bf16[2,16,32,512]{3,2,0,1:T(8,128)(2,1)} async-done(((bf16[2,16,32,512]{3,2,0,1:T(8,128)(2,1)}), bf16[2,16,32,512]{3,2,0,1:T(8,128)(2,1)}, u32[]{:S(2)}, u32[]{:S(2)}) %all-to-all-start) | async-done | bytes 1048608 | tf_op jit(solution)/shard_map/all_to_all | solution.py:119
  87.2 1.3 %fusion.46 = (bf16[1,16,32,512]{3,2,0,1:T(8,128)(2,1)S(1)}, bf16[1,16,32,512]{3,2,0,1:T(8,128)(2,1)S(1)}) fusion(bf16[2,16,32,512]{3,2,0,1:T(8,128)(2,1)} %all-to-all-done), kind=kLoop, calls=%fused_computation.76 | loop fusion | bytes 2097152 | tf_op jit(solution)/shard_map/slice | solution.py:25
  90.4 0.8 fusion.11
  91.2 0.8 add_convert_fusion
  92.2 20.3 %all_to_all.10 = bf16[1,512,2,16,32]{1,4,2,0,3:T(8,128)(2,1)S(1)} all-to-all(bf16[1,512,2,16,32]{1,4,2,0,3:T(8,128)(2,1)S(1)} %pad_maximum_fusion), channel_id=1, replica_groups=mesh['row'=16,'cz'=8,'cx'=2] {'row'}, dimensions={3} | all-to-all | bytes 2097152 | tf_op jit(solution)/shard_map/all_to_all | solution.py:126
  112.6 2.1 %copy.9 = bf16[1,1,1,512,2,512]{5,4,3,2,1,0:T(2,128)(2,1)} copy(bf16[1,1,1,512,2,512]{3,5,4,2,1,0:T(8,128)(2,1)S(1)} %bitcast.87) | data formatting | bytes 2097152 | tf_op jit(solution)/shard_map/reshape | solution.py:127
  (57 shorter events, 7.4 us)
Async XLA Ops:
  0.0 16.3 %copy-start.3 = (bf16[1,1,1,512,2,512]{5,4,3,2,1,0:T(2,128)(2,1)S(1)}, bf16[1,1,1,512,2,512]{5,4,3,2,1,0:T(2,128)(2,1)}, u32[]{:S(2)}) copy-start(bf16[1,1,1,512,2,512]{5,4,3,2,1,0:T(2,128)(2,1)} %param.2) | copy-start | bytes 3145732
  0.0 7.1 %collective-permute-start = (bf16[4,2,32,512]{3,2,1,0:T(8,128)(2,1)}, bf16[4,2,32,512]{3,2,1,0:T(8,128)(2,1)S(1)}, u32[]{:S(2)}, u32[]{:S(2)}) collective-permute-start(bf16[4,2,32,512]{3,2,1,0:T(8,128)(2,1)} %bitcast.105), channel_id=1, source_target_pairs={{0,1},{1,0},{2,3},{3,2},{4,5},{5,4},{6,7},{7,6},{8,9},{9,8},{10,11... | collective-permute-start | bytes 786440 | tf_op jit(solution)/shard_map/ppermute | solution.py:71
  8.8 12.1 %collective-permute-start.9 = (bf16[2,2,2,32,512]{4,3,1,0,2:T(8,128)(2,1)}, bf16[2,2,2,32,512]{4,3,1,0,2:T(8,128)(2,1)}, u32[]{:S(2)}, u32[]{:S(2)}) collective-permute-start(bf16[2,2,2,32,512]{4,3,1,0,2:T(8,128)(2,1)} %pad_maximum_fusion.2), channel_id=1, source_target_pairs={{0,2},{2,4},{4,6},{6,8},{8,10},{10,12},{12,14},{14,0},{1,3},{3,5},... | collective-permute-start | bytes 786440 | tf_op jit(solution)/shard_map/ppermute | solution.py:71
  11.6 9.4 %collective-permute-start.10 = (bf16[2,2,2,32,512]{4,3,1,0,2:T(8,128)(2,1)}, bf16[2,2,2,32,512]{4,3,1,0,2:T(8,128)(2,1)}, u32[]{:S(2)}, u32[]{:S(2)}) collective-permute-start(bf16[2,2,2,32,512]{4,3,1,0,2:T(8,128)(2,1)} %pad_maximum_fusion.2), channel_id=1, source_target_pairs={{0,14},{2,0},{4,2},{6,4},{8,6},{10,8},{12,10},{14,12},{1,15},{3,1}... | collective-permute-start | bytes 786440 | tf_op jit(solution)/shard_map/ppermute | solution.py:71
  16.3 10.4 %collective-permute-start.1 = (bf16[2,2,2,32,512]{4,3,1,0,2:T(8,128)(2,1)}, bf16[2,2,2,32,512]{4,3,1,0,2:T(8,128)(2,1)}, u32[]{:S(2)}, u32[]{:S(2)}) collective-permute-start(bf16[2,2,2,32,512]{4,3,1,0,2:T(8,128)(2,1)} %pad_maximum_fusion.1), channel_id=1, source_target_pairs={{0,2},{2,4},{4,6},{6,8},{8,10},{10,12},{12,14},{14,0},{1,3},{3,5},... | collective-permute-start | bytes 786440 | tf_op jit(solution)/shard_map/ppermute | solution.py:71
  16.5 12.0 %collective-permute-start.2 = (bf16[2,2,2,32,512]{4,3,1,0,2:T(8,128)(2,1)}, bf16[2,2,2,32,512]{4,3,1,0,2:T(8,128)(2,1)S(1)}, u32[]{:S(2)}, u32[]{:S(2)}) collective-permute-start(bf16[2,2,2,32,512]{4,3,1,0,2:T(8,128)(2,1)} %pad_maximum_fusion.1), channel_id=1, source_target_pairs={{0,14},{2,0},{4,2},{6,4},{8,6},{10,8},{12,10},{14,12},{1,15},{3,1}... | collective-permute-start | bytes 786440 | tf_op jit(solution)/shard_map/ppermute | solution.py:71
  21.0 11.3 %collective-permute-start.11 = (bf16[2,2,2,32,512]{4,3,1,0,2:T(8,128)(2,1)}, bf16[2,2,2,32,512]{4,3,1,0,2:T(8,128)(2,1)S(1)}, u32[]{:S(2)}, u32[]{:S(2)}) collective-permute-start(bf16[2,2,2,32,512]{4,3,1,0,2:T(8,128)(2,1)} %collective-permute-done.9), channel_id=1, source_target_pairs={{0,2},{2,4},{4,6},{6,8},{8,10},{10,12},{12,14},{14,0},{1,3},{3,5},... | collective-permute-start | bytes 786440 | tf_op jit(solution)/shard_map/ppermute | solution.py:71
  21.0 11.4 %collective-permute-start.12 = (bf16[2,2,2,32,512]{4,3,1,0,2:T(8,128)(2,1)}, bf16[2,2,2,32,512]{4,3,1,0,2:T(8,128)(2,1)S(1)}, u32[]{:S(2)}, u32[]{:S(2)}) collective-permute-start(bf16[2,2,2,32,512]{4,3,1,0,2:T(8,128)(2,1)} %collective-permute-done.10), channel_id=1, source_target_pairs={{0,14},{2,0},{4,2},{6,4},{8,6},{10,8},{12,10},{14,12},{1,15},{3,1}... | collective-permute-start | bytes 786440 | tf_op jit(solution)/shard_map/ppermute | solution.py:71
  26.6 11.1 %collective-permute-start.3 = (bf16[2,2,2,32,512]{4,3,1,0,2:T(8,128)(2,1)}, bf16[2,2,2,32,512]{4,3,1,0,2:T(8,128)(2,1)S(1)}, u32[]{:S(2)}, u32[]{:S(2)}) collective-permute-start(bf16[2,2,2,32,512]{4,3,1,0,2:T(8,128)(2,1)} %collective-permute-done.1), channel_id=1, source_target_pairs={{0,2},{2,4},{4,6},{6,8},{8,10},{10,12},{12,14},{14,0},{1,3},{3,5},... | collective-permute-start | bytes 786440 | tf_op jit(solution)/shard_map/ppermute | solution.py:71
  28.6 9.2 %collective-permute-start.4 = (bf16[2,2,2,32,512]{4,3,1,0,2:T(8,128)(2,1)S(1)}, bf16[2,2,2,32,512]{4,3,1,0,2:T(8,128)(2,1)S(1)}, u32[]{:S(2)}, u32[]{:S(2)}) collective-permute-start(bf16[2,2,2,32,512]{4,3,1,0,2:T(8,128)(2,1)S(1)} %collective-permute-done.2), channel_id=1, source_target_pairs={{0,14},{2,0},{4,2},{6,4},{8,6},{10,8},{12,10},{14,12},{1,15},{3,1}... | collective-permute-start | bytes 786440 | tf_op jit(solution)/shard_map/ppermute | solution.py:71
  32.3 11.0 %collective-permute-start.13 = (bf16[2,2,2,32,512]{4,3,1,0,2:T(8,128)(2,1)S(1)}, bf16[2,2,2,32,512]{4,3,1,0,2:T(8,128)(2,1)S(1)}, u32[]{:S(2)}, u32[]{:S(2)}) collective-permute-start(bf16[2,2,2,32,512]{4,3,1,0,2:T(8,128)(2,1)S(1)} %collective-permute-done.11), channel_id=1, source_target_pairs={{0,2},{2,4},{4,6},{6,8},{8,10},{10,12},{12,14},{14,0},{1,3},{3,5},... | collective-permute-start | bytes 786440 | tf_op jit(solution)/shard_map/ppermute | solution.py:71
  32.4 11.0 %collective-permute-start.14 = (bf16[2,2,2,32,512]{4,3,1,0,2:T(8,128)(2,1)S(1)}, bf16[2,2,2,32,512]{4,3,1,0,2:T(8,128)(2,1)S(1)}, u32[]{:S(2)}, u32[]{:S(2)}) collective-permute-start(bf16[2,2,2,32,512]{4,3,1,0,2:T(8,128)(2,1)S(1)} %collective-permute-done.12), channel_id=1, source_target_pairs={{0,14},{2,0},{4,2},{6,4},{8,6},{10,8},{12,10},{14,12},{1,15},{3,1}... | collective-permute-start | bytes 786440 | tf_op jit(solution)/shard_map/ppermute | solution.py:71
  37.7 11.2 %collective-permute-start.5 = (bf16[2,2,2,32,512]{4,3,1,0,2:T(8,128)(2,1)S(1)}, bf16[2,2,2,32,512]{4,3,1,0,2:T(8,128)(2,1)S(1)}, u32[]{:S(2)}, u32[]{:S(2)}) collective-permute-start(bf16[2,2,2,32,512]{4,3,1,0,2:T(8,128)(2,1)S(1)} %collective-permute-done.3), channel_id=1, source_target_pairs={{0,2},{2,4},{4,6},{6,8},{8,10},{10,12},{12,14},{14,0},{1,3},{3,5},... | collective-permute-start | bytes 786440 | tf_op jit(solution)/shard_map/ppermute | solution.py:71
  37.8 11.3 %collective-permute-start.6 = (bf16[2,2,2,32,512]{4,3,1,0,2:T(8,128)(2,1)S(1)}, bf16[2,2,2,32,512]{4,3,1,0,2:T(8,128)(2,1)S(1)}, u32[]{:S(2)}, u32[]{:S(2)}) collective-permute-start(bf16[2,2,2,32,512]{4,3,1,0,2:T(8,128)(2,1)S(1)} %collective-permute-done.4), channel_id=1, source_target_pairs={{0,14},{2,0},{4,2},{6,4},{8,6},{10,8},{12,10},{14,12},{1,15},{3,1}... | collective-permute-start | bytes 786440 | tf_op jit(solution)/shard_map/ppermute | solution.py:71
  43.4 8.6 %collective-permute-start.15 = (bf16[2,2,2,16,512]{4,3,1,0,2:T(8,128)(2,1)S(1)}, bf16[2,2,2,16,512]{4,3,1,0,2:T(8,128)(2,1)S(1)}, u32[]{:S(2)}, u32[]{:S(2)}) collective-permute-start(bf16[2,2,2,16,512]{4,3,1,0,2:T(8,128)(2,1)S(1)} %slice.134), channel_id=1, source_target_pairs={{0,2},{2,4},{4,6},{6,8},{8,10},{10,12},{12,14},{14,0},{1,3},{3,5},... | collective-permute-start | bytes 393224 | tf_op jit(solution)/shard_map/ppermute | solution.py:71
  43.5 8.5 %collective-permute-start.16 = (bf16[2,2,2,16,512]{4,3,1,0,2:T(8,128)(2,1)S(1)}, bf16[2,2,2,16,512]{4,3,1,0,2:T(8,128)(2,1)S(1)}, u32[]{:S(2)}, u32[]{:S(2)}) collective-permute-start(bf16[2,2,2,16,512]{4,3,1,0,2:T(8,128)(2,1)S(1)} %slice.135), channel_id=1, source_target_pairs={{0,14},{2,0},{4,2},{6,4},{8,6},{10,8},{12,10},{14,12},{1,15},{3,1}... | collective-permute-start | bytes 393224 | tf_op jit(solution)/shard_map/ppermute | solution.py:71
  49.0 5.6 %collective-permute-start.7 = (bf16[2,2,2,16,512]{4,3,1,0,2:T(8,128)(2,1)S(1)}, bf16[2,2,2,16,512]{4,3,1,0,2:T(8,128)(2,1)S(1)}, u32[]{:S(2)}, u32[]{:S(2)}) collective-permute-start(bf16[2,2,2,16,512]{4,3,1,0,2:T(8,128)(2,1)S(1)} %slice.128), channel_id=1, source_target_pairs={{0,2},{2,4},{4,6},{6,8},{8,10},{10,12},{12,14},{14,0},{1,3},{3,5},... | collective-permute-start | bytes 393224 | tf_op jit(solution)/shard_map/ppermute | solution.py:71
  49.1 6.0 %collective-permute-start.8 = (bf16[2,2,2,16,512]{4,3,1,0,2:T(8,128)(2,1)S(1)}, bf16[2,2,2,16,512]{4,3,1,0,2:T(8,128)(2,1)S(1)}, u32[]{:S(2)}, u32[]{:S(2)}) collective-permute-start(bf16[2,2,2,16,512]{4,3,1,0,2:T(8,128)(2,1)S(1)} %slice.129), channel_id=1, source_target_pairs={{0,14},{2,0},{4,2},{6,4},{8,6},{10,8},{12,10},{14,12},{1,15},{3,1}... | collective-permute-start | bytes 393224 | tf_op jit(solution)/shard_map/ppermute | solution.py:71
  59.4 27.8 %all-to-all-start = ((bf16[2,16,32,512]{3,2,0,1:T(8,128)(2,1)}), bf16[2,16,32,512]{3,2,0,1:T(8,128)(2,1)}, u32[]{:S(2)}, u32[]{:S(2)}) async-start(bf16[2,16,32,512]{3,2,0,1:T(8,128)(2,1)} %copy.5), calls=%async_computation | async-start | bytes 2097152 | tf_op jit(solution)/shard_map/all_to_all | solution.py:119
  71.0 0.8 copy-start.1
  89.2 1.0 copy-start
  89.2 1.2 %copy-start.2 = (bf16[1,1,8,2,32,512]{5,4,1,0,3,2:T(8,128)(2,1)S(1)}, bf16[1,1,8,2,32,512]{5,4,1,0,3,2:T(8,128)(2,1)}, u32[]{:S(2)}) copy-start(bf16[1,1,8,2,32,512]{5,4,1,0,3,2:T(8,128)(2,1)} %copy-done.1) | copy-start | bytes 1572868

commit v8 on v5

--- a/solution.py
+++ b/solution.py
@@ -71,7 +71,7 @@
     return lax.ppermute(x, axis, [(i, (i + d) % n) for i in range(n)])
 
 
-def ring_gather(t):
+def ring_gather(t, hold=None):
     nz = lax.axis_size("cz")
     nx = lax.axis_size("cx")
     z = lax.axis_index("cz")
@@ -90,6 +90,8 @@
     for k in range(1, forward + 1):
         if k == forward and nz % 2 == 0 and width % 2 == 0:
             half = width // 2
+            if hold is not None:
+                (cur_f, cur_b), hold = lax.optimization_barrier(((cur_f, cur_b), hold))
             a = shift(cur_f[:, :, :, :half], "cz", nz, 1)
             b = shift(cur_b[:, :, :, half:], "cz", nz, -1)
             piece = jnp.concatenate([a, b], axis=3)
@@ -100,7 +102,7 @@
         if k <= backward:
             cur_b = shift(cur_b, "cz", nz, -1)
             buf = lax.dynamic_update_slice(buf, cur_b[:, :, None], (0, 0, (z + k) % nz, 0, 0, 0))
-    return buf.reshape(nb, comps, nz * nx * width, cols)
+    return buf.reshape(nb, comps, nz * nx * width, cols), hold
 
 
 def shards(stem, branch):
@@ -109,12 +111,12 @@
     row_count = lax.axis_size("row")
     share = order_size // row_count
     own_t = jnp.swapaxes(branch[0], -1, -2)
-    first_t = ring_gather(own_t[:2])
-    second_t = ring_gather(own_t[2:])
+    first_t, _ = ring_gather(own_t[:2])
 
     block = stem[0, 0]
     half_first = right_piece(block, first_t[1]).astype(jnp.bfloat16)
     step_first = left_planar(half_first[0], first_t[0]).astype(jnp.bfloat16)
+    second_t, step_first = ring_gather(own_t[2:], hold=step_first)
     outgoing = step_first.reshape(2, row_count, share, order_size)
     moved = lax.all_to_all(outgoing, "row", split_axis=1, concat_axis=1, tiled=True)
     planar = moved.reshape(2, order_size, order_size)

time: 112 us -> 112 us (level)
  starting transfers between devices: 40.2 us -> 38.9 us
    unnamed x9 -> x13, local copies, waits for them, and re-layouts: 2.65 us -> 3.24 us
  transfers between devices with their start and end apart: 19 -> 19, of which waited for: 9 -> 8; matrix products, arithmetic and copies ran while one was open for 3% -> 7% of each run, Pallas kernels for 0% -> 0%
where the time goes in v8:
time: 112 us; the launch traced here: 111 us
  starting transfers between devices  38.9 us (35%)
  waiting for transfers between devices  34.3 us (31%)
  blocking collectives  20.3 us (18%)
  local copies, waits for them, and re-layouts  10.8 us (10%)
  matrix products  5.79 us (5%)
    ppermute x18, starting transfers between devices, shift(): return lax.ppermute(x, axis, [(i, (i + d) % n) for i in range(n)])  29 us
    all_to_all x1, blocking collectives, shards(): lax.all_to_all(leaving, 'row', split_axis=3, concat_axis=3, tiled=True)  20.3 us
    ppermute x18, waiting for transfers between devices, shift(): return lax.ppermute(x, axis, [(i, (i + d) % n) for i in range(n)])  19.1 us
    all_to_all x1, waiting for transfers between devices, shards(): lax.all_to_all(outgoing, 'row', split_axis=1, concat_axis=1, tiled=True)  15.2 us
    all_to_all x1, starting transfers between devices, shards(): lax.all_to_all(outgoing, 'row', split_axis=1, concat_axis=1, tiled=True)  9.89 us
    unnamed x13, local copies, waits for them, and re-layouts  3.24 us
  transfers between devices with their start and end apart: 19, of which 8 were waited for; matrix products, arithmetic and copies ran while one was open for 7% of the time, Pallas kernels for 0%

profile of v8, /device:TPU:1, one launch (start us, length us, event | category | flops | bytes accessed | tf_op | source)
XLA Modules:
  0.0 111.2 jit_solution(6456617001077379766)
XLA Ops:
  0.0 1.0 slice.119
  1.0 2.1 %collective-permute-start.7 = (bf16[2,2,32,512]{3,2,1,0:T(8,128)(2,1)S(1)}, bf16[2,2,32,512]{3,2,1,0:T(8,128)(2,1)S(1)}, u32[]{:S(2)}, u32[]{:S(2)}) collective-permute-start(bf16[2,2,32,512]{3,2,1,0:T(8,128)(2,1)S(1)} %slice.119), channel_id=1, source_target_pairs={{0,1},{1,0},{2,3},{3,2},{4,5},{5,4},{6,7},{7,6},{8,9},{9,8},{10,11... | collective-permute-start | bytes 393224 | tf_op jit(solution)/shard_map/ppermute | solution.py:71
  3.1 1.5 %copy.14 = bf16[64,8,2,512]{3,1,2,0:T(8,128)(2,1)S(1)} copy(bf16[64,8,2,512]{3,2,1,0:T(2,128)(2,1)} %bitcast.101) | data formatting | bytes 2097152
  4.6 0.8 collective-permute-done.7
  5.5 1.9 %collective-permute-start = (bf16[2,2,32,512]{3,2,1,0:T(8,128)(2,1)S(1)}, bf16[2,2,32,512]{3,2,1,0:T(8,128)(2,1)S(1)}, u32[]{:S(2)}, u32[]{:S(2)}) collective-permute-start(bf16[2,2,32,512]{3,2,1,0:T(8,128)(2,1)S(1)} %get-tuple-element.27), channel_id=1, source_target_pairs={{0,1},{1,0},{2,3},{3,2},{4,5},{5,4},{6,7},{7,6},{8,9},{9,8},{10,11... | collective-permute-start | bytes 393224 | tf_op jit(solution)/shard_map/ppermute | solution.py:71
  7.4 1.9 %collective-permute-start.8 = (bf16[2,2,2,32,512]{4,3,1,0,2:T(8,128)(2,1)S(1)}, bf16[2,2,2,32,512]{4,3,1,0,2:T(8,128)(2,1)S(1)}, u32[]{:S(2)}, u32[]{:S(2)}) collective-permute-start(bf16[2,2,2,32,512]{4,3,1,0,2:T(8,128)(2,1)S(1)} %pad_maximum_fusion.2), channel_id=1, source_target_pairs={{0,2},{2,4},{4,6},{6,8},{8,10},{10,12},{12,14},{14,0},{1,3},{3,5},... | collective-permute-start | bytes 786440 | tf_op jit(solution)/shard_map/ppermute | solution.py:71
  9.4 4.0 %collective-permute-start.9 = (bf16[2,2,2,32,512]{4,3,1,0,2:T(8,128)(2,1)S(1)}, bf16[2,2,2,32,512]{4,3,1,0,2:T(8,128)(2,1)S(1)}, u32[]{:S(2)}, u32[]{:S(2)}) collective-permute-start(bf16[2,2,2,32,512]{4,3,1,0,2:T(8,128)(2,1)S(1)} %pad_maximum_fusion.2), channel_id=1, source_target_pairs={{0,14},{2,0},{4,2},{6,4},{8,6},{10,8},{12,10},{14,12},{1,15},{3,1}... | collective-permute-start | bytes 786440 | tf_op jit(solution)/shard_map/ppermute | solution.py:71
  13.8 2.7 %collective-permute-start.2 = (bf16[2,2,2,32,512]{4,3,1,0,2:T(8,128)(2,1)S(1)}, bf16[2,2,2,32,512]{4,3,1,0,2:T(8,128)(2,1)S(1)}, u32[]{:S(2)}, u32[]{:S(2)}) collective-permute-start(bf16[2,2,2,32,512]{4,3,1,0,2:T(8,128)(2,1)S(1)} %pad_maximum_fusion.1), channel_id=1, source_target_pairs={{0,14},{2,0},{4,2},{6,4},{8,6},{10,8},{12,10},{14,12},{1,15},{3,1}... | collective-permute-start | bytes 786440 | tf_op jit(solution)/shard_map/ppermute | solution.py:71
  16.8 1.4 %collective-permute-done.8 = bf16[2,2,2,32,512]{4,3,1,0,2:T(8,128)(2,1)S(1)} collective-permute-done((bf16[2,2,2,32,512]{4,3,1,0,2:T(8,128)(2,1)S(1)}, bf16[2,2,2,32,512]{4,3,1,0,2:T(8,128)(2,1)S(1)}, u32[]{:S(2)}, u32[]{:S(2)}) %collective-permute-start.8) | collective-permute-done | bytes 262176 | tf_op jit(solution)/shard_map/ppermute | solution.py:71
  18.2 2.7 %collective-permute-start.11 = (bf16[2,2,2,32,512]{4,3,1,0,2:T(8,128)(2,1)S(1)}, bf16[2,2,2,32,512]{4,3,1,0,2:T(8,128)(2,1)S(1)}, u32[]{:S(2)}, u32[]{:S(2)}) collective-permute-start(bf16[2,2,2,32,512]{4,3,1,0,2:T(8,128)(2,1)S(1)} %collective-permute-done.9), channel_id=1, source_target_pairs={{0,14},{2,0},{4,2},{6,4},{8,6},{10,8},{12,10},{14,12},{1,15},{3,1}... | collective-permute-start | bytes 786440 | tf_op jit(solution)/shard_map/ppermute | solution.py:71
  20.9 2.9 %collective-permute-done.1 = bf16[2,2,2,32,512]{4,3,1,0,2:T(8,128)(2,1)S(1)} collective-permute-done((bf16[2,2,2,32,512]{4,3,1,0,2:T(8,128)(2,1)S(1)}, bf16[2,2,2,32,512]{4,3,1,0,2:T(8,128)(2,1)S(1)}, u32[]{:S(2)}, u32[]{:S(2)}) %collective-permute-start.1) | collective-permute-done | bytes 262176 | tf_op jit(solution)/shard_map/ppermute | solution.py:71
  23.8 2.7 %collective-permute-start.4 = (bf16[2,2,2,32,512]{4,3,1,0,2:T(8,128)(2,1)S(1)}, bf16[2,2,2,32,512]{4,3,1,0,2:T(8,128)(2,1)S(1)}, u32[]{:S(2)}, u32[]{:S(2)}) collective-permute-start(bf16[2,2,2,32,512]{4,3,1,0,2:T(8,128)(2,1)S(1)} %collective-permute-done.2), channel_id=1, source_target_pairs={{0,14},{2,0},{4,2},{6,4},{8,6},{10,8},{12,10},{14,12},{1,15},{3,1}... | collective-permute-start | bytes 786440 | tf_op jit(solution)/shard_map/ppermute | solution.py:71
  26.5 2.9 %collective-permute-done.10 = bf16[2,2,2,32,512]{4,3,1,0,2:T(8,128)(2,1)S(1)} collective-permute-done((bf16[2,2,2,32,512]{4,3,1,0,2:T(8,128)(2,1)S(1)}, bf16[2,2,2,32,512]{4,3,1,0,2:T(8,128)(2,1)S(1)}, u32[]{:S(2)}, u32[]{:S(2)}) %collective-permute-start.10) | collective-permute-done | bytes 262176 | tf_op jit(solution)/shard_map/ppermute | solution.py:71
  29.4 2.7 %collective-permute-start.13 = (bf16[2,2,2,32,512]{4,3,1,0,2:T(8,128)(2,1)S(1)}, bf16[2,2,2,32,512]{4,3,1,0,2:T(8,128)(2,1)S(1)}, u32[]{:S(2)}, u32[]{:S(2)}) collective-permute-start(bf16[2,2,2,32,512]{4,3,1,0,2:T(8,128)(2,1)S(1)} %collective-permute-done.11), channel_id=1, source_target_pairs={{0,14},{2,0},{4,2},{6,4},{8,6},{10,8},{12,10},{14,12},{1,15},{3,1}... | collective-permute-start | bytes 786440 | tf_op jit(solution)/shard_map/ppermute | solution.py:71
  32.1 2.9 %collective-permute-done.3 = bf16[2,2,2,32,512]{4,3,1,0,2:T(8,128)(2,1)S(1)} collective-permute-done((bf16[2,2,2,32,512]{4,3,1,0,2:T(8,128)(2,1)S(1)}, bf16[2,2,2,32,512]{4,3,1,0,2:T(8,128)(2,1)S(1)}, u32[]{:S(2)}, u32[]{:S(2)}) %collective-permute-start.3) | collective-permute-done | bytes 262176 | tf_op jit(solution)/shard_map/ppermute | solution.py:71
  35.0 2.7 %collective-permute-start.6 = (bf16[2,2,2,32,512]{4,3,1,0,2:T(8,128)(2,1)S(1)}, bf16[2,2,2,32,512]{4,3,1,0,2:T(8,128)(2,1)S(1)}, u32[]{:S(2)}, u32[]{:S(2)}) collective-permute-start(bf16[2,2,2,32,512]{4,3,1,0,2:T(8,128)(2,1)S(1)} %collective-permute-done.4), channel_id=1, source_target_pairs={{0,14},{2,0},{4,2},{6,4},{8,6},{10,8},{12,10},{14,12},{1,15},{3,1}... | collective-permute-start | bytes 786440 | tf_op jit(solution)/shard_map/ppermute | solution.py:71
  37.8 2.9 %collective-permute-done.12 = bf16[2,2,2,32,512]{4,3,1,0,2:T(8,128)(2,1)S(1)} collective-permute-done((bf16[2,2,2,32,512]{4,3,1,0,2:T(8,128)(2,1)S(1)}, bf16[2,2,2,32,512]{4,3,1,0,2:T(8,128)(2,1)S(1)}, u32[]{:S(2)}, u32[]{:S(2)}) %collective-permute-start.12) | collective-permute-done | bytes 262176 | tf_op jit(solution)/shard_map/ppermute | solution.py:71
  40.8 2.9 %collective-permute-start.15 = (bf16[2,2,2,16,512]{4,3,1,0,2:T(8,128)(2,1)S(1)}, bf16[2,2,2,16,512]{4,3,1,0,2:T(8,128)(2,1)S(1)}, u32[]{:S(2)}, u32[]{:S(2)}) collective-permute-start(bf16[2,2,2,16,512]{4,3,1,0,2:T(8,128)(2,1)S(1)} %slice.121), channel_id=1, source_target_pairs={{0,14},{2,0},{4,2},{6,4},{8,6},{10,8},{12,10},{14,12},{1,15},{3,1}... | collective-permute-start | bytes 393224 | tf_op jit(solution)/shard_map/ppermute | solution.py:71
  43.7 5.3 %collective-permute-done.14 = bf16[2,2,2,16,512]{4,3,1,0,2:T(8,128)(2,1)S(1)} collective-permute-done((bf16[2,2,2,16,512]{4,3,1,0,2:T(8,128)(2,1)S(1)}, bf16[2,2,2,16,512]{4,3,1,0,2:T(8,128)(2,1)S(1)}, u32[]{:S(2)}, u32[]{:S(2)}) %collective-permute-start.14) | collective-permute-done | bytes 131104 | tf_op jit(solution)/shard_map/ppermute | solution.py:71
  49.5 1.3 %fusion.8 = bf16[1024,512]{1,0:T(8,128)(2,1)S(1)} fusion(bf16[512,1024]{1,0:T(8,128)(2,1)S(1)} %bitcast.102, bf16[512,512]{1,0:T(8,128)(2,1)S(1)} %bitcast.106, bf16[512,512]{1,0:T(8,128)(2,1)S(1)} %get-tuple-element.28, bf16[512,512]{1,0:T(8,128)(2,1)S(1)} %bitcast.100), kind=kOutput, calls=%fused_computation.11 | convolution fusion | flops 1082654720 | bytes 3670016 | tf_op jit(solution)/shard_map/dot_general | solution.py:15
  50.8 0.8 fusion.11
  51.6 0.8 add_convert_fusion.2
  53.1 2.6 %collective-permute-start.17 = (bf16[2,2,2,16,512]{4,3,1,0,2:T(8,128)(2,1)S(1)}, bf16[2,2,2,16,512]{4,3,1,0,2:T(8,128)(2,1)S(1)}, u32[]{:S(2)}, u32[]{:S(2)}) collective-permute-start(bf16[2,2,2,16,512]{4,3,1,0,2:T(8,128)(2,1)S(1)} %slice.107), channel_id=1, source_target_pairs={{0,14},{2,0},{4,2},{6,4},{8,6},{10,8},{12,10},{14,12},{1,15},{3,1}... | collective-permute-start | bytes 393224 | tf_op jit(solution)/shard_map/ppermute | solution.py:71
  55.6 1.0 copy.9
  56.7 9.9 %all-to-all-start = ((bf16[2,16,32,512]{3,2,0,1:T(8,128)(2,1)}), bf16[2,16,32,512]{3,2,0,1:T(8,128)(2,1)}, u32[]{:S(2)}, u32[]{:S(2)}) async-start(bf16[2,16,32,512]{3,2,0,1:T(8,128)(2,1)} %copy.9), calls=%async_computation | async-start | bytes 2097152 | tf_op jit(solution)/shard_map/all_to_all | solution.py:121
  66.7 1.0 fusion.43
  68.6 15.2 %all-to-all-done = bf16[2,16,32,512]{3,2,0,1:T(8,128)(2,1)} async-done(((bf16[2,16,32,512]{3,2,0,1:T(8,128)(2,1)}), bf16[2,16,32,512]{3,2,0,1:T(8,128)(2,1)}, u32[]{:S(2)}, u32[]{:S(2)}) %all-to-all-start) | async-done | bytes 1048608 | tf_op jit(solution)/shard_map/all_to_all | solution.py:121
  83.7 1.3 %fusion.46 = (bf16[1,16,32,512]{3,2,0,1:T(8,128)(2,1)S(1)}, bf16[1,16,32,512]{3,2,0,1:T(8,128)(2,1)S(1)}) fusion(bf16[2,16,32,512]{3,2,0,1:T(8,128)(2,1)} %all-to-all-done), kind=kLoop, calls=%fused_computation.76 | loop fusion | bytes 2097152 | tf_op jit(solution)/shard_map/slice | solution.py:25
  86.9 0.8 fusion.18
  87.7 0.8 add_convert_fusion
  88.7 20.3 %all_to_all.10 = bf16[1,512,2,16,32]{1,4,2,0,3:T(8,128)(2,1)S(1)} all-to-all(bf16[1,512,2,16,32]{1,4,2,0,3:T(8,128)(2,1)S(1)} %pad_maximum_fusion), channel_id=1, replica_groups=mesh['row'=16,'cz'=8,'cx'=2] {'row'}, dimensions={3} | all-to-all | bytes 2097152 | tf_op jit(solution)/shard_map/all_to_all | solution.py:128
  109.1 2.1 %copy.13 = bf16[1,1,1,512,2,512]{5,4,3,2,1,0:T(2,128)(2,1)} copy(bf16[1,1,1,512,2,512]{3,5,4,2,1,0:T(8,128)(2,1)S(1)} %bitcast.88) | data formatting | bytes 2097152 | tf_op jit(solution)/shard_map/reshape | solution.py:129
  (65 shorter events, 5.3 us)
Async XLA Ops:
  0.0 5.5 %copy-start.3 = (bf16[1,4,2,512,32]{3,4,2,1,0:T(8,128)(2,1)S(1)}, bf16[1,4,2,512,32]{3,4,2,1,0:T(8,128)(2,1)}, u32[]{:S(2)}) copy-start(bf16[1,4,2,512,32]{3,4,2,1,0:T(8,128)(2,1)} %param.3) | copy-start | bytes 786436
  1.0 4.5 %collective-permute-start.7 = (bf16[2,2,32,512]{3,2,1,0:T(8,128)(2,1)S(1)}, bf16[2,2,32,512]{3,2,1,0:T(8,128)(2,1)S(1)}, u32[]{:S(2)}, u32[]{:S(2)}) collective-permute-start(bf16[2,2,32,512]{3,2,1,0:T(8,128)(2,1)S(1)} %slice.119), channel_id=1, source_target_pairs={{0,1},{1,0},{2,3},{3,2},{4,5},{5,4},{6,7},{7,6},{8,9},{9,8},{10,11... | collective-permute-start | bytes 393224 | tf_op jit(solution)/shard_map/ppermute | solution.py:71
  5.5 8.2 %collective-permute-start = (bf16[2,2,32,512]{3,2,1,0:T(8,128)(2,1)S(1)}, bf16[2,2,32,512]{3,2,1,0:T(8,128)(2,1)S(1)}, u32[]{:S(2)}, u32[]{:S(2)}) collective-permute-start(bf16[2,2,32,512]{3,2,1,0:T(8,128)(2,1)S(1)} %get-tuple-element.27), channel_id=1, source_target_pairs={{0,1},{1,0},{2,3},{3,2},{4,5},{5,4},{6,7},{7,6},{8,9},{9,8},{10,11... | collective-permute-start | bytes 393224 | tf_op jit(solution)/shard_map/ppermute | solution.py:71
  7.4 10.8 %collective-permute-start.8 = (bf16[2,2,2,32,512]{4,3,1,0,2:T(8,128)(2,1)S(1)}, bf16[2,2,2,32,512]{4,3,1,0,2:T(8,128)(2,1)S(1)}, u32[]{:S(2)}, u32[]{:S(2)}) collective-permute-start(bf16[2,2,2,32,512]{4,3,1,0,2:T(8,128)(2,1)S(1)} %pad_maximum_fusion.2), channel_id=1, source_target_pairs={{0,2},{2,4},{4,6},{6,8},{8,10},{10,12},{12,14},{14,0},{1,3},{3,5},... | collective-permute-start | bytes 786440 | tf_op jit(solution)/shard_map/ppermute | solution.py:71
  9.4 8.8 %collective-permute-start.9 = (bf16[2,2,2,32,512]{4,3,1,0,2:T(8,128)(2,1)S(1)}, bf16[2,2,2,32,512]{4,3,1,0,2:T(8,128)(2,1)S(1)}, u32[]{:S(2)}, u32[]{:S(2)}) collective-permute-start(bf16[2,2,2,32,512]{4,3,1,0,2:T(8,128)(2,1)S(1)} %pad_maximum_fusion.2), channel_id=1, source_target_pairs={{0,14},{2,0},{4,2},{6,4},{8,6},{10,8},{12,10},{14,12},{1,15},{3,1}... | collective-permute-start | bytes 786440 | tf_op jit(solution)/shard_map/ppermute | solution.py:71
  13.7 10.0 %collective-permute-start.1 = (bf16[2,2,2,32,512]{4,3,1,0,2:T(8,128)(2,1)S(1)}, bf16[2,2,2,32,512]{4,3,1,0,2:T(8,128)(2,1)S(1)}, u32[]{:S(2)}, u32[]{:S(2)}) collective-permute-start(bf16[2,2,2,32,512]{4,3,1,0,2:T(8,128)(2,1)S(1)} %pad_maximum_fusion.1), channel_id=1, source_target_pairs={{0,2},{2,4},{4,6},{6,8},{8,10},{10,12},{12,14},{14,0},{1,3},{3,5},... | collective-permute-start | bytes 786440 | tf_op jit(solution)/shard_map/ppermute | solution.py:71
  13.8 10.0 %collective-permute-start.2 = (bf16[2,2,2,32,512]{4,3,1,0,2:T(8,128)(2,1)S(1)}, bf16[2,2,2,32,512]{4,3,1,0,2:T(8,128)(2,1)S(1)}, u32[]{:S(2)}, u32[]{:S(2)}) collective-permute-start(bf16[2,2,2,32,512]{4,3,1,0,2:T(8,128)(2,1)S(1)} %pad_maximum_fusion.1), channel_id=1, source_target_pairs={{0,14},{2,0},{4,2},{6,4},{8,6},{10,8},{12,10},{14,12},{1,15},{3,1}... | collective-permute-start | bytes 786440 | tf_op jit(solution)/shard_map/ppermute | solution.py:71
  18.2 11.2 %collective-permute-start.10 = (bf16[2,2,2,32,512]{4,3,1,0,2:T(8,128)(2,1)S(1)}, bf16[2,2,2,32,512]{4,3,1,0,2:T(8,128)(2,1)S(1)}, u32[]{:S(2)}, u32[]{:S(2)}) collective-permute-start(bf16[2,2,2,32,512]{4,3,1,0,2:T(8,128)(2,1)S(1)} %collective-permute-done.8), channel_id=1, source_target_pairs={{0,2},{2,4},{4,6},{6,8},{8,10},{10,12},{12,14},{14,0},{1,3},{3,5},... | collective-permute-start | bytes 786440 | tf_op jit(solution)/shard_map/ppermute | solution.py:71
  18.2 11.2 %collective-permute-start.11 = (bf16[2,2,2,32,512]{4,3,1,0,2:T(8,128)(2,1)S(1)}, bf16[2,2,2,32,512]{4,3,1,0,2:T(8,128)(2,1)S(1)}, u32[]{:S(2)}, u32[]{:S(2)}) collective-permute-start(bf16[2,2,2,32,512]{4,3,1,0,2:T(8,128)(2,1)S(1)} %collective-permute-done.9), channel_id=1, source_target_pairs={{0,14},{2,0},{4,2},{6,4},{8,6},{10,8},{12,10},{14,12},{1,15},{3,1}... | collective-permute-start | bytes 786440 | tf_op jit(solution)/shard_map/ppermute | solution.py:71
  23.8 11.2 %collective-permute-start.3 = (bf16[2,2,2,32,512]{4,3,1,0,2:T(8,128)(2,1)S(1)}, bf16[2,2,2,32,512]{4,3,1,0,2:T(8,128)(2,1)S(1)}, u32[]{:S(2)}, u32[]{:S(2)}) collective-permute-start(bf16[2,2,2,32,512]{4,3,1,0,2:T(8,128)(2,1)S(1)} %collective-permute-done.1), channel_id=1, source_target_pairs={{0,2},{2,4},{4,6},{6,8},{8,10},{10,12},{12,14},{14,0},{1,3},{3,5},... | collective-permute-start | bytes 786440 | tf_op jit(solution)/shard_map/ppermute | solution.py:71
  23.8 11.2 %collective-permute-start.4 = (bf16[2,2,2,32,512]{4,3,1,0,2:T(8,128)(2,1)S(1)}, bf16[2,2,2,32,512]{4,3,1,0,2:T(8,128)(2,1)S(1)}, u32[]{:S(2)}, u32[]{:S(2)}) collective-permute-start(bf16[2,2,2,32,512]{4,3,1,0,2:T(8,128)(2,1)S(1)} %collective-permute-done.2), channel_id=1, source_target_pairs={{0,14},{2,0},{4,2},{6,4},{8,6},{10,8},{12,10},{14,12},{1,15},{3,1}... | collective-permute-start | bytes 786440 | tf_op jit(solution)/shard_map/ppermute | solution.py:71
  29.4 11.2 %collective-permute-start.12 = (bf16[2,2,2,32,512]{4,3,1,0,2:T(8,128)(2,1)S(1)}, bf16[2,2,2,32,512]{4,3,1,0,2:T(8,128)(2,1)S(1)}, u32[]{:S(2)}, u32[]{:S(2)}) collective-permute-start(bf16[2,2,2,32,512]{4,3,1,0,2:T(8,128)(2,1)S(1)} %collective-permute-done.10), channel_id=1, source_target_pairs={{0,2},{2,4},{4,6},{6,8},{8,10},{10,12},{12,14},{14,0},{1,3},{3,5},... | collective-permute-start | bytes 786440 | tf_op jit(solution)/shard_map/ppermute | solution.py:71
  29.4 11.3 %collective-permute-start.13 = (bf16[2,2,2,32,512]{4,3,1,0,2:T(8,128)(2,1)S(1)}, bf16[2,2,2,32,512]{4,3,1,0,2:T(8,128)(2,1)S(1)}, u32[]{:S(2)}, u32[]{:S(2)}) collective-permute-start(bf16[2,2,2,32,512]{4,3,1,0,2:T(8,128)(2,1)S(1)} %collective-permute-done.11), channel_id=1, source_target_pairs={{0,14},{2,0},{4,2},{6,4},{8,6},{10,8},{12,10},{14,12},{1,15},{3,1}... | collective-permute-start | bytes 786440 | tf_op jit(solution)/shard_map/ppermute | solution.py:71
  35.0 17.3 %collective-permute-start.5 = (bf16[2,2,2,32,512]{4,3,1,0,2:T(8,128)(2,1)S(1)}, bf16[2,2,2,32,512]{4,3,1,0,2:T(8,128)(2,1)S(1)}, u32[]{:S(2)}, u32[]{:S(2)}) collective-permute-start(bf16[2,2,2,32,512]{4,3,1,0,2:T(8,128)(2,1)S(1)} %collective-permute-done.3), channel_id=1, source_target_pairs={{0,2},{2,4},{4,6},{6,8},{8,10},{10,12},{12,14},{14,0},{1,3},{3,5},... | collective-permute-start | bytes 786440 | tf_op jit(solution)/shard_map/ppermute | solution.py:71
  35.0 17.3 %collective-permute-start.6 = (bf16[2,2,2,32,512]{4,3,1,0,2:T(8,128)(2,1)S(1)}, bf16[2,2,2,32,512]{4,3,1,0,2:T(8,128)(2,1)S(1)}, u32[]{:S(2)}, u32[]{:S(2)}) collective-permute-start(bf16[2,2,2,32,512]{4,3,1,0,2:T(8,128)(2,1)S(1)} %collective-permute-done.4), channel_id=1, source_target_pairs={{0,14},{2,0},{4,2},{6,4},{8,6},{10,8},{12,10},{14,12},{1,15},{3,1}... | collective-permute-start | bytes 786440 | tf_op jit(solution)/shard_map/ppermute | solution.py:71
  40.7 8.4 %collective-permute-start.14 = (bf16[2,2,2,16,512]{4,3,1,0,2:T(8,128)(2,1)S(1)}, bf16[2,2,2,16,512]{4,3,1,0,2:T(8,128)(2,1)S(1)}, u32[]{:S(2)}, u32[]{:S(2)}) collective-permute-start(bf16[2,2,2,16,512]{4,3,1,0,2:T(8,128)(2,1)S(1)} %slice.120), channel_id=1, source_target_pairs={{0,2},{2,4},{4,6},{6,8},{8,10},{10,12},{12,14},{14,0},{1,3},{3,5},... | collective-permute-start | bytes 393224 | tf_op jit(solution)/shard_map/ppermute | solution.py:71
  40.8 8.3 %collective-permute-start.15 = (bf16[2,2,2,16,512]{4,3,1,0,2:T(8,128)(2,1)S(1)}, bf16[2,2,2,16,512]{4,3,1,0,2:T(8,128)(2,1)S(1)}, u32[]{:S(2)}, u32[]{:S(2)}) collective-permute-start(bf16[2,2,2,16,512]{4,3,1,0,2:T(8,128)(2,1)S(1)} %slice.121), channel_id=1, source_target_pairs={{0,14},{2,0},{4,2},{6,4},{8,6},{10,8},{12,10},{14,12},{1,15},{3,1}... | collective-permute-start | bytes 393224 | tf_op jit(solution)/shard_map/ppermute | solution.py:71
  52.4 0.7 copy-start.4
  52.4 14.2 %collective-permute-start.16 = (bf16[2,2,2,16,512]{4,3,1,0,2:T(8,128)(2,1)S(1)}, bf16[2,2,2,16,512]{4,3,1,0,2:T(8,128)(2,1)S(1)}, u32[]{:S(2)}, u32[]{:S(2)}) collective-permute-start(bf16[2,2,2,16,512]{4,3,1,0,2:T(8,128)(2,1)S(1)} %slice.106), channel_id=1, source_target_pairs={{0,2},{2,4},{4,6},{6,8},{8,10},{10,12},{12,14},{14,0},{1,3},{3,5},... | collective-permute-start | bytes 393224 | tf_op jit(solution)/shard_map/ppermute | solution.py:71
  53.1 13.6 %collective-permute-start.17 = (bf16[2,2,2,16,512]{4,3,1,0,2:T(8,128)(2,1)S(1)}, bf16[2,2,2,16,512]{4,3,1,0,2:T(8,128)(2,1)S(1)}, u32[]{:S(2)}, u32[]{:S(2)}) collective-permute-start(bf16[2,2,2,16,512]{4,3,1,0,2:T(8,128)(2,1)S(1)} %slice.107), channel_id=1, source_target_pairs={{0,14},{2,0},{4,2},{6,4},{8,6},{10,8},{12,10},{14,12},{1,15},{3,1}... | collective-permute-start | bytes 393224 | tf_op jit(solution)/shard_map/ppermute | solution.py:71
  55.6 11.0 %copy-start.5 = (bf16[2,2,2,32,512]{4,3,1,0,2:T(8,128)(2,1)S(1)}, bf16[2,2,2,32,512]{4,3,1,0,2:T(8,128)(2,1)}, u32[]{:S(2)}) copy-start(bf16[2,2,2,32,512]{4,3,1,0,2:T(8,128)(2,1)} %copy-done.4) | copy-start | bytes 786436
  56.7 27.1 %all-to-all-start = ((bf16[2,16,32,512]{3,2,0,1:T(8,128)(2,1)}), bf16[2,16,32,512]{3,2,0,1:T(8,128)(2,1)}, u32[]{:S(2)}, u32[]{:S(2)}) async-start(bf16[2,16,32,512]{3,2,0,1:T(8,128)(2,1)} %copy.9), calls=%async_computation | async-start | bytes 2097152 | tf_op jit(solution)/shard_map/all_to_all | solution.py:121
  67.7 0.8 copy-start.1
  85.7 1.0 copy-start
  85.7 1.2 %copy-start.2 = (bf16[1,1,8,2,32,512]{5,4,1,0,3,2:T(8,128)(2,1)S(1)}, bf16[1,1,8,2,32,512]{5,4,1,0,3,2:T(8,128)(2,1)}, u32[]{:S(2)}) copy-start(bf16[1,1,8,2,32,512]{5,4,1,0,3,2:T(8,128)(2,1)} %copy-done.1) | copy-start | bytes 1572868

commit v9 on v8

--- a/solution.py
+++ b/solution.py
@@ -91,7 +91,10 @@
         if k == forward and nz % 2 == 0 and width % 2 == 0:
             half = width // 2
             if hold is not None:
-                (cur_f, cur_b), hold = lax.optimization_barrier(((cur_f, cur_b), hold))
+                cur_f, hold = lax.optimization_barrier((cur_f, hold))
+                piece = shift(cur_f, "cz", nz, 1)
+                buf = lax.dynamic_update_slice(buf, piece[:, :, None], (0, 0, (z - k) % nz, 0, 0, 0))
+                break
             a = shift(cur_f[:, :, :, :half], "cz", nz, 1)
             b = shift(cur_b[:, :, :, half:], "cz", nz, -1)
             piece = jnp.concatenate([a, b], axis=3)

time: 112 us -> 110 us (0.982)
  the two profiles are of different devices: /device:TPU:1 before, /device:TPU:64 now
where the time goes in v9:
time: 110 us; the launch traced here: 109 us
  waiting for transfers between devices  39.4 us (36%)
  starting transfers between devices  30.6 us (28%)
  blocking collectives  20.6 us (19%)
  local copies, waits for them, and re-layouts  12.1 us (11%)
  matrix products  5.79 us (5%)
    ppermute x17, waiting for transfers between devices, shift(): return lax.ppermute(x, axis, [(i, (i + d) % n) for i in range(n)])  25.2 us
    ppermute x17, starting transfers between devices, shift(): return lax.ppermute(x, axis, [(i, (i + d) % n) for i in range(n)])  23.8 us
    all_to_all x1, blocking collectives, shards(): lax.all_to_all(leaving, 'row', split_axis=3, concat_axis=3, tiled=True)  20.6 us
    all_to_all x1, waiting for transfers between devices, shards(): lax.all_to_all(outgoing, 'row', split_axis=1, concat_axis=1, tiled=True)  14.2 us
    all_to_all x1, starting transfers between devices, shards(): lax.all_to_all(outgoing, 'row', split_axis=1, concat_axis=1, tiled=True)  6.79 us
    unnamed x9, local copies, waits for them, and re-layouts  2.65 us
  transfers between devices with their start and end apart: 18, of which 15 were waited for; matrix products, arithmetic and copies ran while one was open for 9% of the time, Pallas kernels for 0%

profile of v9, /device:TPU:64, one launch (start us, length us, event | category | flops | bytes accessed | tf_op | source)
XLA Modules:
  0.0 109.4 jit_solution(7074526050071957871)
XLA Ops:
  0.0 1.0 slice.111
  1.0 1.6 %collective-permute-start.7 = (bf16[2,2,32,512]{3,2,1,0:T(8,128)(2,1)S(1)}, bf16[2,2,32,512]{3,2,1,0:T(8,128)(2,1)S(1)}, u32[]{:S(2)}, u32[]{:S(2)}) collective-permute-start(bf16[2,2,32,512]{3,2,1,0:T(8,128)(2,1)S(1)} %slice.111), channel_id=1, source_target_pairs={{0,1},{1,0},{2,3},{3,2},{4,5},{5,4},{6,7},{7,6},{8,9},{9,8},{10,11... | collective-permute-start | bytes 393224 | tf_op jit(solution)/shard_map/ppermute | solution.py:71
  2.6 1.5 %copy.14 = bf16[64,8,2,512]{3,1,2,0:T(8,128)(2,1)S(1)} copy(bf16[64,8,2,512]{3,2,1,0:T(2,128)(2,1)} %bitcast.99) | data formatting | bytes 2097152
  4.1 2.2 %collective-permute-done.7 = bf16[2,2,32,512]{3,2,1,0:T(8,128)(2,1)S(1)} collective-permute-done((bf16[2,2,32,512]{3,2,1,0:T(8,128)(2,1)S(1)}, bf16[2,2,32,512]{3,2,1,0:T(8,128)(2,1)S(1)}, u32[]{:S(2)}, u32[]{:S(2)}) %collective-permute-start.7) | collective-permute-done | bytes 131104 | tf_op jit(solution)/shard_map/ppermute | solution.py:71
  6.4 1.6 %collective-permute-start = (bf16[2,2,32,512]{3,2,1,0:T(8,128)(2,1)S(1)}, bf16[2,2,32,512]{3,2,1,0:T(8,128)(2,1)S(1)}, u32[]{:S(2)}, u32[]{:S(2)}) collective-permute-start(bf16[2,2,32,512]{3,2,1,0:T(8,128)(2,1)S(1)} %get-tuple-element.25), channel_id=1, source_target_pairs={{0,1},{1,0},{2,3},{3,2},{4,5},{5,4},{6,7},{7,6},{8,9},{9,8},{10,11... | collective-permute-start | bytes 393224 | tf_op jit(solution)/shard_map/ppermute | solution.py:71
  8.0 2.0 %collective-permute-start.8 = (bf16[2,2,2,32,512]{4,3,1,0,2:T(8,128)(2,1)S(1)}, bf16[2,2,2,32,512]{4,3,1,0,2:T(8,128)(2,1)S(1)}, u32[]{:S(2)}, u32[]{:S(2)}) collective-permute-start(bf16[2,2,2,32,512]{4,3,1,0,2:T(8,128)(2,1)S(1)} %pad_maximum_fusion.2), channel_id=1, source_target_pairs={{0,2},{2,4},{4,6},{6,8},{8,10},{10,12},{12,14},{14,0},{1,3},{3,5},... | collective-permute-start | bytes 786440 | tf_op jit(solution)/shard_map/ppermute | solution.py:71
  10.3 1.1 collective-permute-done
  11.5 2.1 %collective-permute-start.1 = (bf16[2,2,2,32,512]{4,3,1,0,2:T(8,128)(2,1)S(1)}, bf16[2,2,2,32,512]{4,3,1,0,2:T(8,128)(2,1)S(1)}, u32[]{:S(2)}, u32[]{:S(2)}) collective-permute-start(bf16[2,2,2,32,512]{4,3,1,0,2:T(8,128)(2,1)S(1)} %pad_maximum_fusion.1), channel_id=1, source_target_pairs={{0,2},{2,4},{4,6},{6,8},{8,10},{10,12},{12,14},{14,0},{1,3},{3,5},... | collective-permute-start | bytes 786440 | tf_op jit(solution)/shard_map/ppermute | solution.py:71
  13.9 3.4 %collective-permute-done.8 = bf16[2,2,2,32,512]{4,3,1,0,2:T(8,128)(2,1)S(1)} collective-permute-done((bf16[2,2,2,32,512]{4,3,1,0,2:T(8,128)(2,1)S(1)}, bf16[2,2,2,32,512]{4,3,1,0,2:T(8,128)(2,1)S(1)}, u32[]{:S(2)}, u32[]{:S(2)}) %collective-permute-start.8) | collective-permute-done | bytes 262176 | tf_op jit(solution)/shard_map/ppermute | solution.py:71
  17.2 2.6 %collective-permute-start.10 = (bf16[2,2,2,32,512]{4,3,1,0,2:T(8,128)(2,1)S(1)}, bf16[2,2,2,32,512]{4,3,1,0,2:T(8,128)(2,1)S(1)}, u32[]{:S(2)}, u32[]{:S(2)}) collective-permute-start(bf16[2,2,2,32,512]{4,3,1,0,2:T(8,128)(2,1)S(1)} %collective-permute-done.8), channel_id=1, source_target_pairs={{0,2},{2,4},{4,6},{6,8},{8,10},{10,12},{12,14},{14,0},{1,3},{3,5},... | collective-permute-start | bytes 786440 | tf_op jit(solution)/shard_map/ppermute | solution.py:71
  20.3 2.5 %collective-permute-done.1 = bf16[2,2,2,32,512]{4,3,1,0,2:T(8,128)(2,1)S(1)} collective-permute-done((bf16[2,2,2,32,512]{4,3,1,0,2:T(8,128)(2,1)S(1)}, bf16[2,2,2,32,512]{4,3,1,0,2:T(8,128)(2,1)S(1)}, u32[]{:S(2)}, u32[]{:S(2)}) %collective-permute-start.1) | collective-permute-done | bytes 262176 | tf_op jit(solution)/shard_map/ppermute | solution.py:71
  22.8 2.6 %collective-permute-start.3 = (bf16[2,2,2,32,512]{4,3,1,0,2:T(8,128)(2,1)S(1)}, bf16[2,2,2,32,512]{4,3,1,0,2:T(8,128)(2,1)S(1)}, u32[]{:S(2)}, u32[]{:S(2)}) collective-permute-start(bf16[2,2,2,32,512]{4,3,1,0,2:T(8,128)(2,1)S(1)} %collective-permute-done.1), channel_id=1, source_target_pairs={{0,2},{2,4},{4,6},{6,8},{8,10},{10,12},{12,14},{14,0},{1,3},{3,5},... | collective-permute-start | bytes 786440 | tf_op jit(solution)/shard_map/ppermute | solution.py:71
  25.9 2.6 %collective-permute-done.10 = bf16[2,2,2,32,512]{4,3,1,0,2:T(8,128)(2,1)S(1)} collective-permute-done((bf16[2,2,2,32,512]{4,3,1,0,2:T(8,128)(2,1)S(1)}, bf16[2,2,2,32,512]{4,3,1,0,2:T(8,128)(2,1)S(1)}, u32[]{:S(2)}, u32[]{:S(2)}) %collective-permute-start.10) | collective-permute-done | bytes 262176 | tf_op jit(solution)/shard_map/ppermute | solution.py:71
  28.4 2.6 %collective-permute-start.12 = (bf16[2,2,2,32,512]{4,3,1,0,2:T(8,128)(2,1)S(1)}, bf16[2,2,2,32,512]{4,3,1,0,2:T(8,128)(2,1)S(1)}, u32[]{:S(2)}, u32[]{:S(2)}) collective-permute-start(bf16[2,2,2,32,512]{4,3,1,0,2:T(8,128)(2,1)S(1)} %collective-permute-done.10), channel_id=1, source_target_pairs={{0,2},{2,4},{4,6},{6,8},{8,10},{10,12},{12,14},{14,0},{1,3},{3,5},... | collective-permute-start | bytes 786440 | tf_op jit(solution)/shard_map/ppermute | solution.py:71
  31.5 2.5 %collective-permute-done.3 = bf16[2,2,2,32,512]{4,3,1,0,2:T(8,128)(2,1)S(1)} collective-permute-done((bf16[2,2,2,32,512]{4,3,1,0,2:T(8,128)(2,1)S(1)}, bf16[2,2,2,32,512]{4,3,1,0,2:T(8,128)(2,1)S(1)}, u32[]{:S(2)}, u32[]{:S(2)}) %collective-permute-start.3) | collective-permute-done | bytes 262176 | tf_op jit(solution)/shard_map/ppermute | solution.py:71
  34.1 2.6 %collective-permute-start.5 = (bf16[2,2,2,32,512]{4,3,1,0,2:T(8,128)(2,1)S(1)}, bf16[2,2,2,32,512]{4,3,1,0,2:T(8,128)(2,1)}, u32[]{:S(2)}, u32[]{:S(2)}) collective-permute-start(bf16[2,2,2,32,512]{4,3,1,0,2:T(8,128)(2,1)S(1)} %collective-permute-done.3), channel_id=1, source_target_pairs={{0,2},{2,4},{4,6},{6,8},{8,10},{10,12},{12,14},{14,0},{1,3},{3,5},... | collective-permute-start | bytes 786440 | tf_op jit(solution)/shard_map/ppermute | solution.py:71
  37.1 2.6 %collective-permute-done.12 = bf16[2,2,2,32,512]{4,3,1,0,2:T(8,128)(2,1)S(1)} collective-permute-done((bf16[2,2,2,32,512]{4,3,1,0,2:T(8,128)(2,1)S(1)}, bf16[2,2,2,32,512]{4,3,1,0,2:T(8,128)(2,1)S(1)}, u32[]{:S(2)}, u32[]{:S(2)}) %collective-permute-start.12) | collective-permute-done | bytes 262176 | tf_op jit(solution)/shard_map/ppermute | solution.py:71
  39.7 2.6 %collective-permute-start.14 = (bf16[2,2,2,16,512]{4,3,1,0,2:T(8,128)(2,1)S(1)}, bf16[2,2,2,16,512]{4,3,1,0,2:T(8,128)(2,1)S(1)}, u32[]{:S(2)}, u32[]{:S(2)}) collective-permute-start(bf16[2,2,2,16,512]{4,3,1,0,2:T(8,128)(2,1)S(1)} %slice.112), channel_id=1, source_target_pairs={{0,2},{2,4},{4,6},{6,8},{8,10},{10,12},{12,14},{14,0},{1,3},{3,5},... | collective-permute-start | bytes 393224 | tf_op jit(solution)/shard_map/ppermute | solution.py:71
  43.1 2.8 %collective-permute-done.14 = bf16[2,2,2,16,512]{4,3,1,0,2:T(8,128)(2,1)S(1)} collective-permute-done((bf16[2,2,2,16,512]{4,3,1,0,2:T(8,128)(2,1)S(1)}, bf16[2,2,2,16,512]{4,3,1,0,2:T(8,128)(2,1)S(1)}, u32[]{:S(2)}, u32[]{:S(2)}) %collective-permute-start.14) | collective-permute-done | bytes 131104 | tf_op jit(solution)/shard_map/ppermute | solution.py:71
  45.8 3.4 %collective-permute-done.15 = bf16[2,2,2,16,512]{4,3,1,0,2:T(8,128)(2,1)S(1)} collective-permute-done((bf16[2,2,2,16,512]{4,3,1,0,2:T(8,128)(2,1)S(1)}, bf16[2,2,2,16,512]{4,3,1,0,2:T(8,128)(2,1)S(1)}, u32[]{:S(2)}, u32[]{:S(2)}) %collective-permute-start.15) | collective-permute-done | bytes 131104 | tf_op jit(solution)/shard_map/ppermute | solution.py:71
  49.7 1.3 %fusion.8 = bf16[1024,512]{1,0:T(8,128)(2,1)S(1)} fusion(bf16[512,1024]{1,0:T(8,128)(2,1)S(1)} %bitcast.100, bf16[512,512]{1,0:T(8,128)(2,1)S(1)} %bitcast.104, bf16[512,512]{1,0:T(8,128)(2,1)S(1)} %get-tuple-element.26, bf16[512,512]{1,0:T(8,128)(2,1)S(1)} %bitcast.98), kind=kOutput, calls=%fused_computation.11 | convolution fusion | flops 1082654720 | bytes 3670016 | tf_op jit(solution)/shard_map/dot_general | solution.py:15
  52.5 3.3 %collective-permute-start.16 = (bf16[2,2,2,32,512]{4,3,1,0,2:T(8,128)(2,1)}, bf16[2,2,2,32,512]{4,3,1,0,2:T(8,128)(2,1)S(1)}, u32[]{:S(2)}, u32[]{:S(2)}) collective-permute-start(bf16[2,2,2,32,512]{4,3,1,0,2:T(8,128)(2,1)} %collective-permute-done.5), channel_id=1, source_target_pairs={{0,2},{2,4},{4,6},{6,8},{8,10},{10,12},{12,14},{14,0},{1,3},{3,5},... | collective-permute-start | bytes 786440 | tf_op jit(solution)/shard_map/ppermute | solution.py:71
  55.8 1.0 copy.9
  56.9 6.8 %all-to-all-start = ((bf16[2,16,32,512]{3,2,0,1:T(8,128)(2,1)}), bf16[2,16,32,512]{3,2,0,1:T(8,128)(2,1)}, u32[]{:S(2)}, u32[]{:S(2)}) async-start(bf16[2,16,32,512]{3,2,0,1:T(8,128)(2,1)} %copy.9), calls=%async_computation | async-start | bytes 2097152 | tf_op jit(solution)/shard_map/all_to_all | solution.py:124
  63.7 1.0 bitcast_dynamic-update-slice_fusion.9
  64.7 1.0 bitcast_dynamic-update-slice_fusion.8
  65.7 1.0 fusion.42
  67.6 14.2 %all-to-all-done = bf16[2,16,32,512]{3,2,0,1:T(8,128)(2,1)} async-done(((bf16[2,16,32,512]{3,2,0,1:T(8,128)(2,1)}), bf16[2,16,32,512]{3,2,0,1:T(8,128)(2,1)}, u32[]{:S(2)}, u32[]{:S(2)}) %all-to-all-start) | async-done | bytes 1048608 | tf_op jit(solution)/shard_map/all_to_all | solution.py:124
  81.7 1.3 %fusion.45 = (bf16[1,16,32,512]{3,2,0,1:T(8,128)(2,1)S(1)}, bf16[1,16,32,512]{3,2,0,1:T(8,128)(2,1)S(1)}) fusion(bf16[2,16,32,512]{3,2,0,1:T(8,128)(2,1)} %all-to-all-done), kind=kLoop, calls=%fused_computation.75 | loop fusion | bytes 2097152 | tf_op jit(solution)/shard_map/slice | solution.py:25
  85.7 0.8 add_convert_fusion
  86.7 20.6 %all_to_all.10 = bf16[1,512,2,16,32]{1,4,2,0,3:T(8,128)(2,1)S(1)} all-to-all(bf16[1,512,2,16,32]{1,4,2,0,3:T(8,128)(2,1)S(1)} %pad_maximum_fusion), channel_id=1, replica_groups=mesh['row'=16,'cz'=8,'cx'=2] {'row'}, dimensions={3} | all-to-all | bytes 2097152 | tf_op jit(solution)/shard_map/all_to_all | solution.py:131
  107.3 2.1 %copy.13 = bf16[1,1,1,512,2,512]{5,4,3,2,1,0:T(2,128)(2,1)} copy(bf16[1,1,1,512,2,512]{3,5,4,2,1,0:T(8,128)(2,1)S(1)} %bitcast.86) | data formatting | bytes 2097152 | tf_op jit(solution)/shard_map/reshape | solution.py:132
  (57 shorter events, 9.2 us)
Async XLA Ops:
  0.0 6.3 %copy-start.3 = (bf16[1,4,2,512,32]{3,4,2,1,0:T(8,128)(2,1)S(1)}, bf16[1,4,2,512,32]{3,4,2,1,0:T(8,128)(2,1)}, u32[]{:S(2)}) copy-start(bf16[1,4,2,512,32]{3,4,2,1,0:T(8,128)(2,1)} %param.3) | copy-start | bytes 786436
  1.0 5.3 %collective-permute-start.7 = (bf16[2,2,32,512]{3,2,1,0:T(8,128)(2,1)S(1)}, bf16[2,2,32,512]{3,2,1,0:T(8,128)(2,1)S(1)}, u32[]{:S(2)}, u32[]{:S(2)}) collective-permute-start(bf16[2,2,32,512]{3,2,1,0:T(8,128)(2,1)S(1)} %slice.111), channel_id=1, source_target_pairs={{0,1},{1,0},{2,3},{3,2},{4,5},{5,4},{6,7},{7,6},{8,9},{9,8},{10,11... | collective-permute-start | bytes 393224 | tf_op jit(solution)/shard_map/ppermute | solution.py:71
  6.4 5.1 %collective-permute-start = (bf16[2,2,32,512]{3,2,1,0:T(8,128)(2,1)S(1)}, bf16[2,2,32,512]{3,2,1,0:T(8,128)(2,1)S(1)}, u32[]{:S(2)}, u32[]{:S(2)}) collective-permute-start(bf16[2,2,32,512]{3,2,1,0:T(8,128)(2,1)S(1)} %get-tuple-element.25), channel_id=1, source_target_pairs={{0,1},{1,0},{2,3},{3,2},{4,5},{5,4},{6,7},{7,6},{8,9},{9,8},{10,11... | collective-permute-start | bytes 393224 | tf_op jit(solution)/shard_map/ppermute | solution.py:71
  8.0 9.3 %collective-permute-start.8 = (bf16[2,2,2,32,512]{4,3,1,0,2:T(8,128)(2,1)S(1)}, bf16[2,2,2,32,512]{4,3,1,0,2:T(8,128)(2,1)S(1)}, u32[]{:S(2)}, u32[]{:S(2)}) collective-permute-start(bf16[2,2,2,32,512]{4,3,1,0,2:T(8,128)(2,1)S(1)} %pad_maximum_fusion.2), channel_id=1, source_target_pairs={{0,2},{2,4},{4,6},{6,8},{8,10},{10,12},{12,14},{14,0},{1,3},{3,5},... | collective-permute-start | bytes 786440 | tf_op jit(solution)/shard_map/ppermute | solution.py:71
  10.0 10.3 %collective-permute-start.9 = (bf16[2,2,2,32,512]{4,3,1,0,2:T(8,128)(2,1)S(1)}, bf16[2,2,2,32,512]{4,3,1,0,2:T(8,128)(2,1)S(1)}, u32[]{:S(2)}, u32[]{:S(2)}) collective-permute-start(bf16[2,2,2,32,512]{4,3,1,0,2:T(8,128)(2,1)S(1)} %pad_maximum_fusion.2), channel_id=1, source_target_pairs={{0,14},{2,0},{4,2},{6,4},{8,6},{10,8},{12,10},{14,12},{1,15},{3,1}... | collective-permute-start | bytes 786440 | tf_op jit(solution)/shard_map/ppermute | solution.py:71
  11.5 11.4 %collective-permute-start.1 = (bf16[2,2,2,32,512]{4,3,1,0,2:T(8,128)(2,1)S(1)}, bf16[2,2,2,32,512]{4,3,1,0,2:T(8,128)(2,1)S(1)}, u32[]{:S(2)}, u32[]{:S(2)}) collective-permute-start(bf16[2,2,2,32,512]{4,3,1,0,2:T(8,128)(2,1)S(1)} %pad_maximum_fusion.1), channel_id=1, source_target_pairs={{0,2},{2,4},{4,6},{6,8},{8,10},{10,12},{12,14},{14,0},{1,3},{3,5},... | collective-permute-start | bytes 786440 | tf_op jit(solution)/shard_map/ppermute | solution.py:71
  13.5 12.3 %collective-permute-start.2 = (bf16[2,2,2,32,512]{4,3,1,0,2:T(8,128)(2,1)S(1)}, bf16[2,2,2,32,512]{4,3,1,0,2:T(8,128)(2,1)S(1)}, u32[]{:S(2)}, u32[]{:S(2)}) collective-permute-start(bf16[2,2,2,32,512]{4,3,1,0,2:T(8,128)(2,1)S(1)} %pad_maximum_fusion.1), channel_id=1, source_target_pairs={{0,14},{2,0},{4,2},{6,4},{8,6},{10,8},{12,10},{14,12},{1,15},{3,1}... | collective-permute-start | bytes 786440 | tf_op jit(solution)/shard_map/ppermute | solution.py:71
  17.2 11.2 %collective-permute-start.10 = (bf16[2,2,2,32,512]{4,3,1,0,2:T(8,128)(2,1)S(1)}, bf16[2,2,2,32,512]{4,3,1,0,2:T(8,128)(2,1)S(1)}, u32[]{:S(2)}, u32[]{:S(2)}) collective-permute-start(bf16[2,2,2,32,512]{4,3,1,0,2:T(8,128)(2,1)S(1)} %collective-permute-done.8), channel_id=1, source_target_pairs={{0,2},{2,4},{4,6},{6,8},{8,10},{10,12},{12,14},{14,0},{1,3},{3,5},... | collective-permute-start | bytes 786440 | tf_op jit(solution)/shard_map/ppermute | solution.py:71
  20.2 11.2 %collective-permute-start.11 = (bf16[2,2,2,32,512]{4,3,1,0,2:T(8,128)(2,1)S(1)}, bf16[2,2,2,32,512]{4,3,1,0,2:T(8,128)(2,1)S(1)}, u32[]{:S(2)}, u32[]{:S(2)}) collective-permute-start(bf16[2,2,2,32,512]{4,3,1,0,2:T(8,128)(2,1)S(1)} %collective-permute-done.9), channel_id=1, source_target_pairs={{0,14},{2,0},{4,2},{6,4},{8,6},{10,8},{12,10},{14,12},{1,15},{3,1}... | collective-permute-start | bytes 786440 | tf_op jit(solution)/shard_map/ppermute | solution.py:71
  22.8 11.2 %collective-permute-start.3 = (bf16[2,2,2,32,512]{4,3,1,0,2:T(8,128)(2,1)S(1)}, bf16[2,2,2,32,512]{4,3,1,0,2:T(8,128)(2,1)S(1)}, u32[]{:S(2)}, u32[]{:S(2)}) collective-permute-start(bf16[2,2,2,32,512]{4,3,1,0,2:T(8,128)(2,1)S(1)} %collective-permute-done.1), channel_id=1, source_target_pairs={{0,2},{2,4},{4,6},{6,8},{8,10},{10,12},{12,14},{14,0},{1,3},{3,5},... | collective-permute-start | bytes 786440 | tf_op jit(solution)/shard_map/ppermute | solution.py:71
  25.9 11.2 %collective-permute-start.4 = (bf16[2,2,2,32,512]{4,3,1,0,2:T(8,128)(2,1)S(1)}, bf16[2,2,2,32,512]{4,3,1,0,2:T(8,128)(2,1)S(1)}, u32[]{:S(2)}, u32[]{:S(2)}) collective-permute-start(bf16[2,2,2,32,512]{4,3,1,0,2:T(8,128)(2,1)S(1)} %collective-permute-done.2), channel_id=1, source_target_pairs={{0,14},{2,0},{4,2},{6,4},{8,6},{10,8},{12,10},{14,12},{1,15},{3,1}... | collective-permute-start | bytes 786440 | tf_op jit(solution)/shard_map/ppermute | solution.py:71
  28.4 11.2 %collective-permute-start.12 = (bf16[2,2,2,32,512]{4,3,1,0,2:T(8,128)(2,1)S(1)}, bf16[2,2,2,32,512]{4,3,1,0,2:T(8,128)(2,1)S(1)}, u32[]{:S(2)}, u32[]{:S(2)}) collective-permute-start(bf16[2,2,2,32,512]{4,3,1,0,2:T(8,128)(2,1)S(1)} %collective-permute-done.10), channel_id=1, source_target_pairs={{0,2},{2,4},{4,6},{6,8},{8,10},{10,12},{12,14},{14,0},{1,3},{3,5},... | collective-permute-start | bytes 786440 | tf_op jit(solution)/shard_map/ppermute | solution.py:71
  31.5 11.2 %collective-permute-start.13 = (bf16[2,2,2,32,512]{4,3,1,0,2:T(8,128)(2,1)S(1)}, bf16[2,2,2,32,512]{4,3,1,0,2:T(8,128)(2,1)S(1)}, u32[]{:S(2)}, u32[]{:S(2)}) collective-permute-start(bf16[2,2,2,32,512]{4,3,1,0,2:T(8,128)(2,1)S(1)} %collective-permute-done.11), channel_id=1, source_target_pairs={{0,14},{2,0},{4,2},{6,4},{8,6},{10,8},{12,10},{14,12},{1,15},{3,1}... | collective-permute-start | bytes 786440 | tf_op jit(solution)/shard_map/ppermute | solution.py:71
  34.1 18.5 %collective-permute-start.5 = (bf16[2,2,2,32,512]{4,3,1,0,2:T(8,128)(2,1)S(1)}, bf16[2,2,2,32,512]{4,3,1,0,2:T(8,128)(2,1)}, u32[]{:S(2)}, u32[]{:S(2)}) collective-permute-start(bf16[2,2,2,32,512]{4,3,1,0,2:T(8,128)(2,1)S(1)} %collective-permute-done.3), channel_id=1, source_target_pairs={{0,2},{2,4},{4,6},{6,8},{8,10},{10,12},{12,14},{14,0},{1,3},{3,5},... | collective-permute-start | bytes 786440 | tf_op jit(solution)/shard_map/ppermute | solution.py:71
  37.1 27.6 %collective-permute-start.6 = (bf16[2,2,2,32,512]{4,3,1,0,2:T(8,128)(2,1)S(1)}, bf16[2,2,2,32,512]{4,3,1,0,2:T(8,128)(2,1)}, u32[]{:S(2)}, u32[]{:S(2)}) collective-permute-start(bf16[2,2,2,32,512]{4,3,1,0,2:T(8,128)(2,1)S(1)} %collective-permute-done.4), channel_id=1, source_target_pairs={{0,14},{2,0},{4,2},{6,4},{8,6},{10,8},{12,10},{14,12},{1,15},{3,1}... | collective-permute-start | bytes 786440 | tf_op jit(solution)/shard_map/ppermute | solution.py:71
  39.7 6.1 %collective-permute-start.14 = (bf16[2,2,2,16,512]{4,3,1,0,2:T(8,128)(2,1)S(1)}, bf16[2,2,2,16,512]{4,3,1,0,2:T(8,128)(2,1)S(1)}, u32[]{:S(2)}, u32[]{:S(2)}) collective-permute-start(bf16[2,2,2,16,512]{4,3,1,0,2:T(8,128)(2,1)S(1)} %slice.112), channel_id=1, source_target_pairs={{0,2},{2,4},{4,6},{6,8},{8,10},{10,12},{12,14},{14,0},{1,3},{3,5},... | collective-permute-start | bytes 393224 | tf_op jit(solution)/shard_map/ppermute | solution.py:71
  42.7 6.5 %collective-permute-start.15 = (bf16[2,2,2,16,512]{4,3,1,0,2:T(8,128)(2,1)S(1)}, bf16[2,2,2,16,512]{4,3,1,0,2:T(8,128)(2,1)S(1)}, u32[]{:S(2)}, u32[]{:S(2)}) collective-permute-start(bf16[2,2,2,16,512]{4,3,1,0,2:T(8,128)(2,1)S(1)} %slice.113), channel_id=1, source_target_pairs={{0,14},{2,0},{4,2},{6,4},{8,6},{10,8},{12,10},{14,12},{1,15},{3,1}... | collective-permute-start | bytes 393224 | tf_op jit(solution)/shard_map/ppermute | solution.py:71
  52.5 13.1 %collective-permute-start.16 = (bf16[2,2,2,32,512]{4,3,1,0,2:T(8,128)(2,1)}, bf16[2,2,2,32,512]{4,3,1,0,2:T(8,128)(2,1)S(1)}, u32[]{:S(2)}, u32[]{:S(2)}) collective-permute-start(bf16[2,2,2,32,512]{4,3,1,0,2:T(8,128)(2,1)} %collective-permute-done.5), channel_id=1, source_target_pairs={{0,2},{2,4},{4,6},{6,8},{8,10},{10,12},{12,14},{14,0},{1,3},{3,5},... | collective-permute-start | bytes 786440 | tf_op jit(solution)/shard_map/ppermute | solution.py:71
  56.9 24.8 %all-to-all-start = ((bf16[2,16,32,512]{3,2,0,1:T(8,128)(2,1)}), bf16[2,16,32,512]{3,2,0,1:T(8,128)(2,1)}, u32[]{:S(2)}, u32[]{:S(2)}) async-start(bf16[2,16,32,512]{3,2,0,1:T(8,128)(2,1)} %copy.9), calls=%async_computation | async-start | bytes 2097152 | tf_op jit(solution)/shard_map/all_to_all | solution.py:124
  66.7 0.8 copy-start.1
  83.7 1.0 copy-start
  83.7 1.2 %copy-start.2 = (bf16[1,1,8,2,32,512]{5,4,1,0,3,2:T(8,128)(2,1)S(1)}, bf16[1,1,8,2,32,512]{5,4,1,0,3,2:T(8,128)(2,1)}, u32[]{:S(2)}) copy-start(bf16[1,1,8,2,32,512]{5,4,1,0,3,2:T(8,128)(2,1)} %copy-done.1) | copy-start | bytes 1572868

commit v10 on v9

--- a/solution.py
+++ b/solution.py
@@ -91,7 +91,6 @@
         if k == forward and nz % 2 == 0 and width % 2 == 0:
             half = width // 2
             if hold is not None:
-                cur_f, hold = lax.optimization_barrier((cur_f, hold))
                 piece = shift(cur_f, "cz", nz, 1)
                 buf = lax.dynamic_update_slice(buf, piece[:, :, None], (0, 0, (z - k) % nz, 0, 0, 0))
                 break
@@ -100,6 +99,8 @@
             piece = jnp.concatenate([a, b], axis=3)
             buf = lax.dynamic_update_slice(buf, piece[:, :, None], (0, 0, (z - k) % nz, 0, 0, 0))
             break
+        if hold is not None and k == forward - 1:
+            (cur_f, cur_b), hold = lax.optimization_barrier(((cur_f, cur_b), hold))
         cur_f = shift(cur_f, "cz", nz, 1)
         buf = lax.dynamic_update_slice(buf, cur_f[:, :, None], (0, 0, (z - k) % nz, 0, 0, 0))
         if k <= backward:

time: 110 us -> 110 us (level)
  the two profiles are of different devices: /device:TPU:64 before, /device:TPU:1 now
where the time goes in v10:
time: 110 us
  starting transfers between devices  37.7 us (34%)
  waiting for transfers between devices  33.6 us (31%)
  blocking collectives  20.3 us (18%)
  local copies, waits for them, and re-layouts  11.2 us (10%)
  matrix products  5.79 us (5%)
    ppermute x17, waiting for transfers between devices, shift(): return lax.ppermute(x, axis, [(i, (i + d) % n) for i in range(n)])  27.5 us
    ppermute x17, starting transfers between devices, shift(): return lax.ppermute(x, axis, [(i, (i + d) % n) for i in range(n)])  26.9 us
    all_to_all x1, blocking collectives, shards(): lax.all_to_all(leaving, 'row', split_axis=3, concat_axis=3, tiled=True)  20.3 us
    all_to_all x1, starting transfers between devices, shards(): lax.all_to_all(outgoing, 'row', split_axis=1, concat_axis=1, tiled=True)  10.7 us
    all_to_all x1, waiting for transfers between devices, shards(): lax.all_to_all(outgoing, 'row', split_axis=1, concat_axis=1, tiled=True)  6.18 us
    unnamed x9, local copies, waits for them, and re-layouts  2.65 us
  transfers between devices with their start and end apart: 18, of which 8 were waited for; matrix products, arithmetic and copies ran while one was open for 8% of the time, Pallas kernels for 0%

profile of v10, /device:TPU:1, one launch (start us, length us, event | category | flops | bytes accessed | tf_op | source)
XLA Modules:
  0.0 109.6 jit_solution(15511980253760035128)
XLA Ops:
  0.0 1.0 slice.111
  1.0 2.1 %collective-permute-start.5 = (bf16[2,2,32,512]{3,2,1,0:T(8,128)(2,1)S(1)}, bf16[2,2,32,512]{3,2,1,0:T(8,128)(2,1)S(1)}, u32[]{:S(2)}, u32[]{:S(2)}) collective-permute-start(bf16[2,2,32,512]{3,2,1,0:T(8,128)(2,1)S(1)} %slice.111), channel_id=1, source_target_pairs={{0,1},{1,0},{2,3},{3,2},{4,5},{5,4},{6,7},{7,6},{8,9},{9,8},{10,11... | collective-permute-start | bytes 393224 | tf_op jit(solution)/shard_map/ppermute | solution.py:71
  3.1 1.5 %copy.14 = bf16[64,8,2,512]{3,1,2,0:T(8,128)(2,1)S(1)} copy(bf16[64,8,2,512]{3,2,1,0:T(2,128)(2,1)} %bitcast.99) | data formatting | bytes 2097152
  4.6 0.8 collective-permute-done.5
  5.5 1.9 %collective-permute-start = (bf16[2,2,32,512]{3,2,1,0:T(8,128)(2,1)S(1)}, bf16[2,2,32,512]{3,2,1,0:T(8,128)(2,1)S(1)}, u32[]{:S(2)}, u32[]{:S(2)}) collective-permute-start(bf16[2,2,32,512]{3,2,1,0:T(8,128)(2,1)S(1)} %get-tuple-element.27), channel_id=1, source_target_pairs={{0,1},{1,0},{2,3},{3,2},{4,5},{5,4},{6,7},{7,6},{8,9},{9,8},{10,11... | collective-permute-start | bytes 393224 | tf_op jit(solution)/shard_map/ppermute | solution.py:71
  7.4 1.9 %collective-permute-start.6 = (bf16[2,2,2,32,512]{4,3,1,0,2:T(8,128)(2,1)S(1)}, bf16[2,2,2,32,512]{4,3,1,0,2:T(8,128)(2,1)S(1)}, u32[]{:S(2)}, u32[]{:S(2)}) collective-permute-start(bf16[2,2,2,32,512]{4,3,1,0,2:T(8,128)(2,1)S(1)} %pad_maximum_fusion.2), channel_id=1, source_target_pairs={{0,2},{2,4},{4,6},{6,8},{8,10},{10,12},{12,14},{14,0},{1,3},{3,5},... | collective-permute-start | bytes 786440 | tf_op jit(solution)/shard_map/ppermute | solution.py:71
  9.4 4.0 %collective-permute-start.7 = (bf16[2,2,2,32,512]{4,3,1,0,2:T(8,128)(2,1)S(1)}, bf16[2,2,2,32,512]{4,3,1,0,2:T(8,128)(2,1)S(1)}, u32[]{:S(2)}, u32[]{:S(2)}) collective-permute-start(bf16[2,2,2,32,512]{4,3,1,0,2:T(8,128)(2,1)S(1)} %pad_maximum_fusion.2), channel_id=1, source_target_pairs={{0,14},{2,0},{4,2},{6,4},{8,6},{10,8},{12,10},{14,12},{1,15},{3,1}... | collective-permute-start | bytes 786440 | tf_op jit(solution)/shard_map/ppermute | solution.py:71
  13.8 2.7 %collective-permute-start.2 = (bf16[2,2,2,32,512]{4,3,1,0,2:T(8,128)(2,1)S(1)}, bf16[2,2,2,32,512]{4,3,1,0,2:T(8,128)(2,1)S(1)}, u32[]{:S(2)}, u32[]{:S(2)}) collective-permute-start(bf16[2,2,2,32,512]{4,3,1,0,2:T(8,128)(2,1)S(1)} %pad_maximum_fusion.1), channel_id=1, source_target_pairs={{0,14},{2,0},{4,2},{6,4},{8,6},{10,8},{12,10},{14,12},{1,15},{3,1}... | collective-permute-start | bytes 786440 | tf_op jit(solution)/shard_map/ppermute | solution.py:71
  16.8 1.4 %collective-permute-done.6 = bf16[2,2,2,32,512]{4,3,1,0,2:T(8,128)(2,1)S(1)} collective-permute-done((bf16[2,2,2,32,512]{4,3,1,0,2:T(8,128)(2,1)S(1)}, bf16[2,2,2,32,512]{4,3,1,0,2:T(8,128)(2,1)S(1)}, u32[]{:S(2)}, u32[]{:S(2)}) %collective-permute-start.6) | collective-permute-done | bytes 262176 | tf_op jit(solution)/shard_map/ppermute | solution.py:71
  18.2 2.7 %collective-permute-start.9 = (bf16[2,2,2,32,512]{4,3,1,0,2:T(8,128)(2,1)S(1)}, bf16[2,2,2,32,512]{4,3,1,0,2:T(8,128)(2,1)S(1)}, u32[]{:S(2)}, u32[]{:S(2)}) collective-permute-start(bf16[2,2,2,32,512]{4,3,1,0,2:T(8,128)(2,1)S(1)} %collective-permute-done.7), channel_id=1, source_target_pairs={{0,14},{2,0},{4,2},{6,4},{8,6},{10,8},{12,10},{14,12},{1,15},{3,1}... | collective-permute-start | bytes 786440 | tf_op jit(solution)/shard_map/ppermute | solution.py:71
  20.9 2.9 %collective-permute-done.1 = bf16[2,2,2,32,512]{4,3,1,0,2:T(8,128)(2,1)S(1)} collective-permute-done((bf16[2,2,2,32,512]{4,3,1,0,2:T(8,128)(2,1)S(1)}, bf16[2,2,2,32,512]{4,3,1,0,2:T(8,128)(2,1)S(1)}, u32[]{:S(2)}, u32[]{:S(2)}) %collective-permute-start.1) | collective-permute-done | bytes 262176 | tf_op jit(solution)/shard_map/ppermute | solution.py:71
  23.8 2.7 %collective-permute-start.4 = (bf16[2,2,2,32,512]{4,3,1,0,2:T(8,128)(2,1)S(1)}, bf16[2,2,2,32,512]{4,3,1,0,2:T(8,128)(2,1)S(1)}, u32[]{:S(2)}, u32[]{:S(2)}) collective-permute-start(bf16[2,2,2,32,512]{4,3,1,0,2:T(8,128)(2,1)S(1)} %collective-permute-done.2), channel_id=1, source_target_pairs={{0,14},{2,0},{4,2},{6,4},{8,6},{10,8},{12,10},{14,12},{1,15},{3,1}... | collective-permute-start | bytes 786440 | tf_op jit(solution)/shard_map/ppermute | solution.py:71
  26.5 2.9 %collective-permute-done.8 = bf16[2,2,2,32,512]{4,3,1,0,2:T(8,128)(2,1)S(1)} collective-permute-done((bf16[2,2,2,32,512]{4,3,1,0,2:T(8,128)(2,1)S(1)}, bf16[2,2,2,32,512]{4,3,1,0,2:T(8,128)(2,1)S(1)}, u32[]{:S(2)}, u32[]{:S(2)}) %collective-permute-start.8) | collective-permute-done | bytes 262176 | tf_op jit(solution)/shard_map/ppermute | solution.py:71
  29.4 2.7 %collective-permute-start.11 = (bf16[2,2,2,32,512]{4,3,1,0,2:T(8,128)(2,1)S(1)}, bf16[2,2,2,32,512]{4,3,1,0,2:T(8,128)(2,1)S(1)}, u32[]{:S(2)}, u32[]{:S(2)}) collective-permute-start(bf16[2,2,2,32,512]{4,3,1,0,2:T(8,128)(2,1)S(1)} %collective-permute-done.9), channel_id=1, source_target_pairs={{0,14},{2,0},{4,2},{6,4},{8,6},{10,8},{12,10},{14,12},{1,15},{3,1}... | collective-permute-start | bytes 786440 | tf_op jit(solution)/shard_map/ppermute | solution.py:71
  32.1 8.5 %collective-permute-done.10 = bf16[2,2,2,32,512]{4,3,1,0,2:T(8,128)(2,1)S(1)} collective-permute-done((bf16[2,2,2,32,512]{4,3,1,0,2:T(8,128)(2,1)S(1)}, bf16[2,2,2,32,512]{4,3,1,0,2:T(8,128)(2,1)S(1)}, u32[]{:S(2)}, u32[]{:S(2)}) %collective-permute-start.10) | collective-permute-done | bytes 262176 | tf_op jit(solution)/shard_map/ppermute | solution.py:71
  40.8 2.9 %collective-permute-start.13 = (bf16[2,2,2,16,512]{4,3,1,0,2:T(8,128)(2,1)S(1)}, bf16[2,2,2,16,512]{4,3,1,0,2:T(8,128)(2,1)S(1)}, u32[]{:S(2)}, u32[]{:S(2)}) collective-permute-start(bf16[2,2,2,16,512]{4,3,1,0,2:T(8,128)(2,1)S(1)} %slice.113), channel_id=1, source_target_pairs={{0,14},{2,0},{4,2},{6,4},{8,6},{10,8},{12,10},{14,12},{1,15},{3,1}... | collective-permute-start | bytes 393224 | tf_op jit(solution)/shard_map/ppermute | solution.py:71
  43.7 2.0 %collective-permute-done.12 = bf16[2,2,2,16,512]{4,3,1,0,2:T(8,128)(2,1)S(1)} collective-permute-done((bf16[2,2,2,16,512]{4,3,1,0,2:T(8,128)(2,1)S(1)}, bf16[2,2,2,16,512]{4,3,1,0,2:T(8,128)(2,1)S(1)}, u32[]{:S(2)}, u32[]{:S(2)}) %collective-permute-start.12) | collective-permute-done | bytes 131104 | tf_op jit(solution)/shard_map/ppermute | solution.py:71
  46.2 1.3 %fusion.8 = bf16[1024,512]{1,0:T(8,128)(2,1)S(1)} fusion(bf16[512,1024]{1,0:T(8,128)(2,1)S(1)} %bitcast.100, bf16[512,512]{1,0:T(8,128)(2,1)S(1)} %bitcast.104, bf16[512,512]{1,0:T(8,128)(2,1)S(1)} %get-tuple-element.28, bf16[512,512]{1,0:T(8,128)(2,1)S(1)} %bitcast.98), kind=kOutput, calls=%fused_computation.11 | convolution fusion | flops 1082654720 | bytes 3670016 | tf_op jit(solution)/shard_map/dot_general | solution.py:15
  47.5 0.8 fusion.11
  48.3 0.8 add_convert_fusion.2
  49.1 1.0 bitcast_dynamic-update-slice_fusion.11
  50.1 3.0 %collective-permute-start.15 = (bf16[2,2,2,32,512]{4,3,1,0,2:T(8,128)(2,1)S(1)}, bf16[2,2,2,32,512]{4,3,1,0,2:T(8,128)(2,1)S(1)}, u32[]{:S(2)}, u32[]{:S(2)}) collective-permute-start(bf16[2,2,2,32,512]{4,3,1,0,2:T(8,128)(2,1)S(1)} %collective-permute-done.4), channel_id=1, source_target_pairs={{0,14},{2,0},{4,2},{6,4},{8,6},{10,8},{12,10},{14,12},{1,15},{3,1}... | collective-permute-start | bytes 786440 | tf_op jit(solution)/shard_map/ppermute | solution.py:71
  53.2 1.0 copy.9
  54.2 10.7 %all-to-all-start = ((bf16[2,16,32,512]{3,2,0,1:T(8,128)(2,1)}), bf16[2,16,32,512]{3,2,0,1:T(8,128)(2,1)}, u32[]{:S(2)}, u32[]{:S(2)}) async-start(bf16[2,16,32,512]{3,2,0,1:T(8,128)(2,1)} %copy.9), calls=%async_computation | async-start | bytes 2097152 | tf_op jit(solution)/shard_map/all_to_all | solution.py:125
  65.1 8.9 %collective-permute-done.16 = bf16[2,2,2,32,512]{4,3,1,0,2:T(8,128)(2,1)S(1)} collective-permute-done((bf16[2,2,2,32,512]{4,3,1,0,2:T(8,128)(2,1)S(1)}, bf16[2,2,2,32,512]{4,3,1,0,2:T(8,128)(2,1)S(1)}, u32[]{:S(2)}, u32[]{:S(2)}) %collective-permute-start.16) | collective-permute-done | bytes 262176 | tf_op jit(solution)/shard_map/ppermute | solution.py:71
  74.1 1.0 fusion.42
  76.0 6.2 %all-to-all-done = bf16[2,16,32,512]{3,2,0,1:T(8,128)(2,1)} async-done(((bf16[2,16,32,512]{3,2,0,1:T(8,128)(2,1)}), bf16[2,16,32,512]{3,2,0,1:T(8,128)(2,1)}, u32[]{:S(2)}, u32[]{:S(2)}) %all-to-all-start) | async-done | bytes 1048608 | tf_op jit(solution)/shard_map/all_to_all | solution.py:125
  82.2 1.3 %fusion.45 = (bf16[1,16,32,512]{3,2,0,1:T(8,128)(2,1)S(1)}, bf16[1,16,32,512]{3,2,0,1:T(8,128)(2,1)S(1)}) fusion(bf16[2,16,32,512]{3,2,0,1:T(8,128)(2,1)} %all-to-all-done), kind=kLoop, calls=%fused_computation.75 | loop fusion | bytes 2097152 | tf_op jit(solution)/shard_map/slice | solution.py:25
  85.3 0.8 fusion.18
  86.1 0.8 add_convert_fusion
  87.1 20.3 %all_to_all.10 = bf16[1,512,2,16,32]{1,4,2,0,3:T(8,128)(2,1)S(1)} all-to-all(bf16[1,512,2,16,32]{1,4,2,0,3:T(8,128)(2,1)S(1)} %pad_maximum_fusion), channel_id=1, replica_groups=mesh['row'=16,'cz'=8,'cx'=2] {'row'}, dimensions={3} | all-to-all | bytes 2097152 | tf_op jit(solution)/shard_map/all_to_all | solution.py:132
  107.5 2.1 %copy.13 = bf16[1,1,1,512,2,512]{5,4,3,2,1,0:T(2,128)(2,1)} copy(bf16[1,1,1,512,2,512]{3,5,4,2,1,0:T(8,128)(2,1)S(1)} %bitcast.86) | data formatting | bytes 2097152 | tf_op jit(solution)/shard_map/reshape | solution.py:133
  (57 shorter events, 4.7 us)
Async XLA Ops:
  0.0 5.5 %copy-start.3 = (bf16[1,4,2,512,32]{3,4,2,1,0:T(8,128)(2,1)S(1)}, bf16[1,4,2,512,32]{3,4,2,1,0:T(8,128)(2,1)}, u32[]{:S(2)}) copy-start(bf16[1,4,2,512,32]{3,4,2,1,0:T(8,128)(2,1)} %param.3) | copy-start | bytes 786436
  1.0 4.5 %collective-permute-start.5 = (bf16[2,2,32,512]{3,2,1,0:T(8,128)(2,1)S(1)}, bf16[2,2,32,512]{3,2,1,0:T(8,128)(2,1)S(1)}, u32[]{:S(2)}, u32[]{:S(2)}) collective-permute-start(bf16[2,2,32,512]{3,2,1,0:T(8,128)(2,1)S(1)} %slice.111), channel_id=1, source_target_pairs={{0,1},{1,0},{2,3},{3,2},{4,5},{5,4},{6,7},{7,6},{8,9},{9,8},{10,11... | collective-permute-start | bytes 393224 | tf_op jit(solution)/shard_map/ppermute | solution.py:71
  5.5 8.2 %collective-permute-start = (bf16[2,2,32,512]{3,2,1,0:T(8,128)(2,1)S(1)}, bf16[2,2,32,512]{3,2,1,0:T(8,128)(2,1)S(1)}, u32[]{:S(2)}, u32[]{:S(2)}) collective-permute-start(bf16[2,2,32,512]{3,2,1,0:T(8,128)(2,1)S(1)} %get-tuple-element.27), channel_id=1, source_target_pairs={{0,1},{1,0},{2,3},{3,2},{4,5},{5,4},{6,7},{7,6},{8,9},{9,8},{10,11... | collective-permute-start | bytes 393224 | tf_op jit(solution)/shard_map/ppermute | solution.py:71
  7.4 10.8 %collective-permute-start.6 = (bf16[2,2,2,32,512]{4,3,1,0,2:T(8,128)(2,1)S(1)}, bf16[2,2,2,32,512]{4,3,1,0,2:T(8,128)(2,1)S(1)}, u32[]{:S(2)}, u32[]{:S(2)}) collective-permute-start(bf16[2,2,2,32,512]{4,3,1,0,2:T(8,128)(2,1)S(1)} %pad_maximum_fusion.2), channel_id=1, source_target_pairs={{0,2},{2,4},{4,6},{6,8},{8,10},{10,12},{12,14},{14,0},{1,3},{3,5},... | collective-permute-start | bytes 786440 | tf_op jit(solution)/shard_map/ppermute | solution.py:71
  9.4 8.8 %collective-permute-start.7 = (bf16[2,2,2,32,512]{4,3,1,0,2:T(8,128)(2,1)S(1)}, bf16[2,2,2,32,512]{4,3,1,0,2:T(8,128)(2,1)S(1)}, u32[]{:S(2)}, u32[]{:S(2)}) collective-permute-start(bf16[2,2,2,32,512]{4,3,1,0,2:T(8,128)(2,1)S(1)} %pad_maximum_fusion.2), channel_id=1, source_target_pairs={{0,14},{2,0},{4,2},{6,4},{8,6},{10,8},{12,10},{14,12},{1,15},{3,1}... | collective-permute-start | bytes 786440 | tf_op jit(solution)/shard_map/ppermute | solution.py:71
  13.7 10.0 %collective-permute-start.1 = (bf16[2,2,2,32,512]{4,3,1,0,2:T(8,128)(2,1)S(1)}, bf16[2,2,2,32,512]{4,3,1,0,2:T(8,128)(2,1)S(1)}, u32[]{:S(2)}, u32[]{:S(2)}) collective-permute-start(bf16[2,2,2,32,512]{4,3,1,0,2:T(8,128)(2,1)S(1)} %pad_maximum_fusion.1), channel_id=1, source_target_pairs={{0,2},{2,4},{4,6},{6,8},{8,10},{10,12},{12,14},{14,0},{1,3},{3,5},... | collective-permute-start | bytes 786440 | tf_op jit(solution)/shard_map/ppermute | solution.py:71
  13.8 10.0 %collective-permute-start.2 = (bf16[2,2,2,32,512]{4,3,1,0,2:T(8,128)(2,1)S(1)}, bf16[2,2,2,32,512]{4,3,1,0,2:T(8,128)(2,1)S(1)}, u32[]{:S(2)}, u32[]{:S(2)}) collective-permute-start(bf16[2,2,2,32,512]{4,3,1,0,2:T(8,128)(2,1)S(1)} %pad_maximum_fusion.1), channel_id=1, source_target_pairs={{0,14},{2,0},{4,2},{6,4},{8,6},{10,8},{12,10},{14,12},{1,15},{3,1}... | collective-permute-start | bytes 786440 | tf_op jit(solution)/shard_map/ppermute | solution.py:71
  18.2 11.2 %collective-permute-start.8 = (bf16[2,2,2,32,512]{4,3,1,0,2:T(8,128)(2,1)S(1)}, bf16[2,2,2,32,512]{4,3,1,0,2:T(8,128)(2,1)S(1)}, u32[]{:S(2)}, u32[]{:S(2)}) collective-permute-start(bf16[2,2,2,32,512]{4,3,1,0,2:T(8,128)(2,1)S(1)} %collective-permute-done.6), channel_id=1, source_target_pairs={{0,2},{2,4},{4,6},{6,8},{8,10},{10,12},{12,14},{14,0},{1,3},{3,5},... | collective-permute-start | bytes 786440 | tf_op jit(solution)/shard_map/ppermute | solution.py:71
  18.2 11.2 %collective-permute-start.9 = (bf16[2,2,2,32,512]{4,3,1,0,2:T(8,128)(2,1)S(1)}, bf16[2,2,2,32,512]{4,3,1,0,2:T(8,128)(2,1)S(1)}, u32[]{:S(2)}, u32[]{:S(2)}) collective-permute-start(bf16[2,2,2,32,512]{4,3,1,0,2:T(8,128)(2,1)S(1)} %collective-permute-done.7), channel_id=1, source_target_pairs={{0,14},{2,0},{4,2},{6,4},{8,6},{10,8},{12,10},{14,12},{1,15},{3,1}... | collective-permute-start | bytes 786440 | tf_op jit(solution)/shard_map/ppermute | solution.py:71
  23.8 25.2 %collective-permute-start.3 = (bf16[2,2,2,32,512]{4,3,1,0,2:T(8,128)(2,1)S(1)}, bf16[2,2,2,32,512]{4,3,1,0,2:T(8,128)(2,1)}, u32[]{:S(2)}, u32[]{:S(2)}) collective-permute-start(bf16[2,2,2,32,512]{4,3,1,0,2:T(8,128)(2,1)S(1)} %collective-permute-done.1), channel_id=1, source_target_pairs={{0,2},{2,4},{4,6},{6,8},{8,10},{10,12},{12,14},{14,0},{1,3},{3,5},... | collective-permute-start | bytes 786440 | tf_op jit(solution)/shard_map/ppermute | solution.py:71
  23.8 25.3 %collective-permute-start.4 = (bf16[2,2,2,32,512]{4,3,1,0,2:T(8,128)(2,1)S(1)}, bf16[2,2,2,32,512]{4,3,1,0,2:T(8,128)(2,1)S(1)}, u32[]{:S(2)}, u32[]{:S(2)}) collective-permute-start(bf16[2,2,2,32,512]{4,3,1,0,2:T(8,128)(2,1)S(1)} %collective-permute-done.2), channel_id=1, source_target_pairs={{0,14},{2,0},{4,2},{6,4},{8,6},{10,8},{12,10},{14,12},{1,15},{3,1}... | collective-permute-start | bytes 786440 | tf_op jit(solution)/shard_map/ppermute | solution.py:71
  29.4 11.2 %collective-permute-start.10 = (bf16[2,2,2,32,512]{4,3,1,0,2:T(8,128)(2,1)S(1)}, bf16[2,2,2,32,512]{4,3,1,0,2:T(8,128)(2,1)S(1)}, u32[]{:S(2)}, u32[]{:S(2)}) collective-permute-start(bf16[2,2,2,32,512]{4,3,1,0,2:T(8,128)(2,1)S(1)} %collective-permute-done.8), channel_id=1, source_target_pairs={{0,2},{2,4},{4,6},{6,8},{8,10},{10,12},{12,14},{14,0},{1,3},{3,5},... | collective-permute-start | bytes 786440 | tf_op jit(solution)/shard_map/ppermute | solution.py:71
  29.4 11.3 %collective-permute-start.11 = (bf16[2,2,2,32,512]{4,3,1,0,2:T(8,128)(2,1)S(1)}, bf16[2,2,2,32,512]{4,3,1,0,2:T(8,128)(2,1)S(1)}, u32[]{:S(2)}, u32[]{:S(2)}) collective-permute-start(bf16[2,2,2,32,512]{4,3,1,0,2:T(8,128)(2,1)S(1)} %collective-permute-done.9), channel_id=1, source_target_pairs={{0,14},{2,0},{4,2},{6,4},{8,6},{10,8},{12,10},{14,12},{1,15},{3,1}... | collective-permute-start | bytes 786440 | tf_op jit(solution)/shard_map/ppermute | solution.py:71
  40.7 5.1 %collective-permute-start.12 = (bf16[2,2,2,16,512]{4,3,1,0,2:T(8,128)(2,1)S(1)}, bf16[2,2,2,16,512]{4,3,1,0,2:T(8,128)(2,1)S(1)}, u32[]{:S(2)}, u32[]{:S(2)}) collective-permute-start(bf16[2,2,2,16,512]{4,3,1,0,2:T(8,128)(2,1)S(1)} %slice.112), channel_id=1, source_target_pairs={{0,2},{2,4},{4,6},{6,8},{8,10},{10,12},{12,14},{14,0},{1,3},{3,5},... | collective-permute-start | bytes 393224 | tf_op jit(solution)/shard_map/ppermute | solution.py:71
  40.8 5.0 %collective-permute-start.13 = (bf16[2,2,2,16,512]{4,3,1,0,2:T(8,128)(2,1)S(1)}, bf16[2,2,2,16,512]{4,3,1,0,2:T(8,128)(2,1)S(1)}, u32[]{:S(2)}, u32[]{:S(2)}) collective-permute-start(bf16[2,2,2,16,512]{4,3,1,0,2:T(8,128)(2,1)S(1)} %slice.113), channel_id=1, source_target_pairs={{0,14},{2,0},{4,2},{6,4},{8,6},{10,8},{12,10},{14,12},{1,15},{3,1}... | collective-permute-start | bytes 393224 | tf_op jit(solution)/shard_map/ppermute | solution.py:71
  49.1 15.9 %collective-permute-start.14 = (bf16[2,2,2,32,512]{4,3,1,0,2:T(8,128)(2,1)}, bf16[2,2,2,32,512]{4,3,1,0,2:T(8,128)(2,1)S(1)}, u32[]{:S(2)}, u32[]{:S(2)}) collective-permute-start(bf16[2,2,2,32,512]{4,3,1,0,2:T(8,128)(2,1)} %collective-permute-done.3), channel_id=1, source_target_pairs={{0,2},{2,4},{4,6},{6,8},{8,10},{10,12},{12,14},{14,0},{1,3},{3,5},... | collective-permute-start | bytes 786440 | tf_op jit(solution)/shard_map/ppermute | solution.py:71
  50.1 15.0 %collective-permute-start.15 = (bf16[2,2,2,32,512]{4,3,1,0,2:T(8,128)(2,1)S(1)}, bf16[2,2,2,32,512]{4,3,1,0,2:T(8,128)(2,1)S(1)}, u32[]{:S(2)}, u32[]{:S(2)}) collective-permute-start(bf16[2,2,2,32,512]{4,3,1,0,2:T(8,128)(2,1)S(1)} %collective-permute-done.4), channel_id=1, source_target_pairs={{0,14},{2,0},{4,2},{6,4},{8,6},{10,8},{12,10},{14,12},{1,15},{3,1}... | collective-permute-start | bytes 786440 | tf_op jit(solution)/shard_map/ppermute | solution.py:71
  54.2 27.9 %all-to-all-start = ((bf16[2,16,32,512]{3,2,0,1:T(8,128)(2,1)}), bf16[2,16,32,512]{3,2,0,1:T(8,128)(2,1)}, u32[]{:S(2)}, u32[]{:S(2)}) async-start(bf16[2,16,32,512]{3,2,0,1:T(8,128)(2,1)} %copy.9), calls=%async_computation | async-start | bytes 2097152 | tf_op jit(solution)/shard_map/all_to_all | solution.py:125
  65.0 9.1 %collective-permute-start.16 = (bf16[2,2,2,32,512]{4,3,1,0,2:T(8,128)(2,1)S(1)}, bf16[2,2,2,32,512]{4,3,1,0,2:T(8,128)(2,1)S(1)}, u32[]{:S(2)}, u32[]{:S(2)}) collective-permute-start(bf16[2,2,2,32,512]{4,3,1,0,2:T(8,128)(2,1)S(1)} %collective-permute-done.14), channel_id=1, source_target_pairs={{0,2},{2,4},{4,6},{6,8},{8,10},{10,12},{12,14},{14,0},{1,3},{3,5},... | collective-permute-start | bytes 786440 | tf_op jit(solution)/shard_map/ppermute | solution.py:71
  75.1 0.8 copy-start.1
  84.1 1.0 copy-start
  84.2 1.2 %copy-start.2 = (bf16[1,1,8,2,32,512]{5,4,1,0,3,2:T(8,128)(2,1)S(1)}, bf16[1,1,8,2,32,512]{5,4,1,0,3,2:T(8,128)(2,1)}, u32[]{:S(2)}) copy-start(bf16[1,1,8,2,32,512]{5,4,1,0,3,2:T(8,128)(2,1)} %copy-done.1) | copy-start | bytes 1572868

commit v11 on v9

--- a/solution.py
+++ b/solution.py
@@ -91,7 +91,6 @@
         if k == forward and nz % 2 == 0 and width % 2 == 0:
             half = width // 2
             if hold is not None:
-                cur_f, hold = lax.optimization_barrier((cur_f, hold))
                 piece = shift(cur_f, "cz", nz, 1)
                 buf = lax.dynamic_update_slice(buf, piece[:, :, None], (0, 0, (z - k) % nz, 0, 0, 0))
                 break
@@ -100,11 +99,13 @@
             piece = jnp.concatenate([a, b], axis=3)
             buf = lax.dynamic_update_slice(buf, piece[:, :, None], (0, 0, (z - k) % nz, 0, 0, 0))
             break
-        cur_f = shift(cur_f, "cz", nz, 1)
-        buf = lax.dynamic_update_slice(buf, cur_f[:, :, None], (0, 0, (z - k) % nz, 0, 0, 0))
         if k <= backward:
             cur_b = shift(cur_b, "cz", nz, -1)
             buf = lax.dynamic_update_slice(buf, cur_b[:, :, None], (0, 0, (z + k) % nz, 0, 0, 0))
+        if hold is not None and k == forward - 1:
+            cur_f, hold = lax.optimization_barrier((cur_f, hold))
+        cur_f = shift(cur_f, "cz", nz, 1)
+        buf = lax.dynamic_update_slice(buf, cur_f[:, :, None], (0, 0, (z - k) % nz, 0, 0, 0))
     return buf.reshape(nb, comps, nz * nx * width, cols), hold
 
 

time: 110 us -> 109 us (level)
  the two profiles are of different devices: /device:TPU:64 before, /device:TPU:1 now
where the time goes in v11:
time: 109 us
  starting transfers between devices  38 us (35%)
  waiting for transfers between devices  31.5 us (29%)
  blocking collectives  20.3 us (19%)
  local copies, waits for them, and re-layouts  12.1 us (11%)
  matrix products  5.79 us (5%)
    ppermute x17, starting transfers between devices, shift(): return lax.ppermute(x, axis, [(i, (i + d) % n) for i in range(n)])  28.5 us
    ppermute x17, waiting for transfers between devices, shift(): return lax.ppermute(x, axis, [(i, (i + d) % n) for i in range(n)])  26.2 us
    all_to_all x1, blocking collectives, shards(): lax.all_to_all(leaving, 'row', split_axis=3, concat_axis=3, tiled=True)  20.3 us
    all_to_all x1, starting transfers between devices, shards(): lax.all_to_all(outgoing, 'row', split_axis=1, concat_axis=1, tiled=True)  9.51 us
    all_to_all x1, waiting for transfers between devices, shards(): lax.all_to_all(outgoing, 'row', split_axis=1, concat_axis=1, tiled=True)  5.28 us
    unnamed x9, local copies, waits for them, and re-layouts  2.65 us
  transfers between devices with their start and end apart: 18, of which 9 were waited for; matrix products, arithmetic and copies ran while one was open for 9% of the time, Pallas kernels for 0%

profile of v11, /device:TPU:1, one launch (start us, length us, event | category | flops | bytes accessed | tf_op | source)
XLA Modules:
  0.0 108.7 jit_solution(7574739020667071398)
XLA Ops:
  0.0 1.0 slice.111
  1.0 2.1 %collective-permute-start.6 = (bf16[2,2,32,512]{3,2,1,0:T(8,128)(2,1)S(1)}, bf16[2,2,32,512]{3,2,1,0:T(8,128)(2,1)S(1)}, u32[]{:S(2)}, u32[]{:S(2)}) collective-permute-start(bf16[2,2,32,512]{3,2,1,0:T(8,128)(2,1)S(1)} %slice.111), channel_id=1, source_target_pairs={{0,1},{1,0},{2,3},{3,2},{4,5},{5,4},{6,7},{7,6},{8,9},{9,8},{10,11... | collective-permute-start | bytes 393224 | tf_op jit(solution)/shard_map/ppermute | solution.py:71
  3.1 1.5 %copy.14 = bf16[64,8,2,512]{3,1,2,0:T(8,128)(2,1)S(1)} copy(bf16[64,8,2,512]{3,2,1,0:T(2,128)(2,1)} %bitcast.99) | data formatting | bytes 2097152
  4.6 0.8 collective-permute-done.6
  5.5 1.9 %collective-permute-start = (bf16[2,2,32,512]{3,2,1,0:T(8,128)(2,1)S(1)}, bf16[2,2,32,512]{3,2,1,0:T(8,128)(2,1)S(1)}, u32[]{:S(2)}, u32[]{:S(2)}) collective-permute-start(bf16[2,2,32,512]{3,2,1,0:T(8,128)(2,1)S(1)} %get-tuple-element.25), channel_id=1, source_target_pairs={{0,1},{1,0},{2,3},{3,2},{4,5},{5,4},{6,7},{7,6},{8,9},{9,8},{10,11... | collective-permute-start | bytes 393224 | tf_op jit(solution)/shard_map/ppermute | solution.py:71
  7.4 5.9 %collective-permute-start.7 = (bf16[2,2,2,32,512]{4,3,1,0,2:T(8,128)(2,1)S(1)}, bf16[2,2,2,32,512]{4,3,1,0,2:T(8,128)(2,1)S(1)}, u32[]{:S(2)}, u32[]{:S(2)}) collective-permute-start(bf16[2,2,2,32,512]{4,3,1,0,2:T(8,128)(2,1)S(1)} %pad_maximum_fusion.2), channel_id=1, source_target_pairs={{0,14},{2,0},{4,2},{6,4},{8,6},{10,8},{12,10},{14,12},{1,15},{3,1}... | collective-permute-start | bytes 786440 | tf_op jit(solution)/shard_map/ppermute | solution.py:71
  13.7 2.7 %collective-permute-start.1 = (bf16[2,2,2,32,512]{4,3,1,0,2:T(8,128)(2,1)S(1)}, bf16[2,2,2,32,512]{4,3,1,0,2:T(8,128)(2,1)S(1)}, u32[]{:S(2)}, u32[]{:S(2)}) collective-permute-start(bf16[2,2,2,32,512]{4,3,1,0,2:T(8,128)(2,1)S(1)} %pad_maximum_fusion.1), channel_id=1, source_target_pairs={{0,14},{2,0},{4,2},{6,4},{8,6},{10,8},{12,10},{14,12},{1,15},{3,1}... | collective-permute-start | bytes 786440 | tf_op jit(solution)/shard_map/ppermute | solution.py:71
  17.1 3.4 %collective-permute-start.9 = (bf16[2,2,2,32,512]{4,3,1,0,2:T(8,128)(2,1)S(1)}, bf16[2,2,2,32,512]{4,3,1,0,2:T(8,128)(2,1)S(1)}, u32[]{:S(2)}, u32[]{:S(2)}) collective-permute-start(bf16[2,2,2,32,512]{4,3,1,0,2:T(8,128)(2,1)S(1)} %collective-permute-done.7), channel_id=1, source_target_pairs={{0,14},{2,0},{4,2},{6,4},{8,6},{10,8},{12,10},{14,12},{1,15},{3,1}... | collective-permute-start | bytes 786440 | tf_op jit(solution)/shard_map/ppermute | solution.py:71
  20.6 5.3 %collective-permute-done.2 = bf16[2,2,2,32,512]{4,3,1,0,2:T(8,128)(2,1)S(1)} collective-permute-done((bf16[2,2,2,32,512]{4,3,1,0,2:T(8,128)(2,1)S(1)}, bf16[2,2,2,32,512]{4,3,1,0,2:T(8,128)(2,1)S(1)}, u32[]{:S(2)}, u32[]{:S(2)}) %collective-permute-start.2) | collective-permute-done | bytes 262176 | tf_op jit(solution)/shard_map/ppermute | solution.py:71
  25.9 2.7 %collective-permute-start.3 = (bf16[2,2,2,32,512]{4,3,1,0,2:T(8,128)(2,1)S(1)}, bf16[2,2,2,32,512]{4,3,1,0,2:T(8,128)(2,1)}, u32[]{:S(2)}, u32[]{:S(2)}) collective-permute-start(bf16[2,2,2,32,512]{4,3,1,0,2:T(8,128)(2,1)S(1)} %collective-permute-done.1), channel_id=1, source_target_pairs={{0,14},{2,0},{4,2},{6,4},{8,6},{10,8},{12,10},{14,12},{1,15},{3,1}... | collective-permute-start | bytes 786440 | tf_op jit(solution)/shard_map/ppermute | solution.py:71
  28.6 3.1 %collective-permute-start.11 = (bf16[2,2,2,32,512]{4,3,1,0,2:T(8,128)(2,1)S(1)}, bf16[2,2,2,32,512]{4,3,1,0,2:T(8,128)(2,1)S(1)}, u32[]{:S(2)}, u32[]{:S(2)}) collective-permute-start(bf16[2,2,2,32,512]{4,3,1,0,2:T(8,128)(2,1)S(1)} %collective-permute-done.9), channel_id=1, source_target_pairs={{0,14},{2,0},{4,2},{6,4},{8,6},{10,8},{12,10},{14,12},{1,15},{3,1}... | collective-permute-start | bytes 786440 | tf_op jit(solution)/shard_map/ppermute | solution.py:71
  31.9 1.6 %collective-permute-done.3 = bf16[2,2,2,32,512]{4,3,1,0,2:T(8,128)(2,1)} collective-permute-done((bf16[2,2,2,32,512]{4,3,1,0,2:T(8,128)(2,1)S(1)}, bf16[2,2,2,32,512]{4,3,1,0,2:T(8,128)(2,1)}, u32[]{:S(2)}, u32[]{:S(2)}) %collective-permute-start.3) | collective-permute-done | bytes 262176 | tf_op jit(solution)/shard_map/ppermute | solution.py:71
  33.5 3.2 %collective-permute-start.5 = (bf16[2,2,2,32,512]{4,3,1,0,2:T(8,128)(2,1)}, bf16[2,2,2,32,512]{4,3,1,0,2:T(8,128)(2,1)}, u32[]{:S(2)}, u32[]{:S(2)}) collective-permute-start(bf16[2,2,2,32,512]{4,3,1,0,2:T(8,128)(2,1)} %collective-permute-done.3), channel_id=1, source_target_pairs={{0,14},{2,0},{4,2},{6,4},{8,6},{10,8},{12,10},{14,12},{1,15},{3,1}... | collective-permute-start | bytes 786440 | tf_op jit(solution)/shard_map/ppermute | solution.py:71
  36.7 6.1 %collective-permute-done.12 = bf16[2,2,2,32,512]{4,3,1,0,2:T(8,128)(2,1)S(1)} collective-permute-done((bf16[2,2,2,32,512]{4,3,1,0,2:T(8,128)(2,1)S(1)}, bf16[2,2,2,32,512]{4,3,1,0,2:T(8,128)(2,1)S(1)}, u32[]{:S(2)}, u32[]{:S(2)}) %collective-permute-start.12) | collective-permute-done | bytes 262176 | tf_op jit(solution)/shard_map/ppermute | solution.py:71
  42.9 2.9 %collective-permute-start.14 = (bf16[2,2,2,16,512]{4,3,1,0,2:T(8,128)(2,1)S(1)}, bf16[2,2,2,16,512]{4,3,1,0,2:T(8,128)(2,1)S(1)}, u32[]{:S(2)}, u32[]{:S(2)}) collective-permute-start(bf16[2,2,2,16,512]{4,3,1,0,2:T(8,128)(2,1)S(1)} %slice.113), channel_id=1, source_target_pairs={{0,14},{2,0},{4,2},{6,4},{8,6},{10,8},{12,10},{14,12},{1,15},{3,1}... | collective-permute-start | bytes 393224 | tf_op jit(solution)/shard_map/ppermute | solution.py:71
  45.9 2.0 %collective-permute-done.13 = bf16[2,2,2,16,512]{4,3,1,0,2:T(8,128)(2,1)S(1)} collective-permute-done((bf16[2,2,2,16,512]{4,3,1,0,2:T(8,128)(2,1)S(1)}, bf16[2,2,2,16,512]{4,3,1,0,2:T(8,128)(2,1)S(1)}, u32[]{:S(2)}, u32[]{:S(2)}) %collective-permute-start.13) | collective-permute-done | bytes 131104 | tf_op jit(solution)/shard_map/ppermute | solution.py:71
  47.9 1.2 %collective-permute-done.14 = bf16[2,2,2,16,512]{4,3,1,0,2:T(8,128)(2,1)S(1)} collective-permute-done((bf16[2,2,2,16,512]{4,3,1,0,2:T(8,128)(2,1)S(1)}, bf16[2,2,2,16,512]{4,3,1,0,2:T(8,128)(2,1)S(1)}, u32[]{:S(2)}, u32[]{:S(2)}) %collective-permute-start.14) | collective-permute-done | bytes 131104 | tf_op jit(solution)/shard_map/ppermute | solution.py:71
  49.5 1.3 %fusion.8 = bf16[1024,512]{1,0:T(8,128)(2,1)S(1)} fusion(bf16[512,1024]{1,0:T(8,128)(2,1)S(1)} %bitcast.100, bf16[512,512]{1,0:T(8,128)(2,1)S(1)} %bitcast.104, bf16[512,512]{1,0:T(8,128)(2,1)S(1)} %get-tuple-element.26, bf16[512,512]{1,0:T(8,128)(2,1)S(1)} %bitcast.98), kind=kOutput, calls=%fused_computation.11 | convolution fusion | flops 1082654720 | bytes 3670016 | tf_op jit(solution)/shard_map/dot_general | solution.py:15
  50.8 0.8 fusion.11
  51.6 0.8 add_convert_fusion.2
  52.5 1.0 bitcast_dynamic-update-slice_fusion.11
  53.5 1.0 copy.9
  54.5 9.5 %all-to-all-start = ((bf16[2,16,32,512]{3,2,0,1:T(8,128)(2,1)}), bf16[2,16,32,512]{3,2,0,1:T(8,128)(2,1)}, u32[]{:S(2)}, u32[]{:S(2)}) async-start(bf16[2,16,32,512]{3,2,0,1:T(8,128)(2,1)} %copy.9), calls=%async_computation | async-start | bytes 2097152 | tf_op jit(solution)/shard_map/all_to_all | solution.py:125
  64.3 1.0 bitcast_dynamic-update-slice_fusion.9
  65.3 8.8 %collective-permute-done.16 = bf16[2,2,2,32,512]{4,3,1,0,2:T(8,128)(2,1)S(1)} collective-permute-done((bf16[2,2,2,32,512]{4,3,1,0,2:T(8,128)(2,1)S(1)}, bf16[2,2,2,32,512]{4,3,1,0,2:T(8,128)(2,1)S(1)}, u32[]{:S(2)}, u32[]{:S(2)}) %collective-permute-start.16) | collective-permute-done | bytes 262176 | tf_op jit(solution)/shard_map/ppermute | solution.py:71
  74.1 1.0 fusion.42
  75.9 5.3 %all-to-all-done = bf16[2,16,32,512]{3,2,0,1:T(8,128)(2,1)} async-done(((bf16[2,16,32,512]{3,2,0,1:T(8,128)(2,1)}), bf16[2,16,32,512]{3,2,0,1:T(8,128)(2,1)}, u32[]{:S(2)}, u32[]{:S(2)}) %all-to-all-start) | async-done | bytes 1048608 | tf_op jit(solution)/shard_map/all_to_all | solution.py:125
  81.2 1.3 %fusion.45 = (bf16[1,16,32,512]{3,2,0,1:T(8,128)(2,1)S(1)}, bf16[1,16,32,512]{3,2,0,1:T(8,128)(2,1)S(1)}) fusion(bf16[2,16,32,512]{3,2,0,1:T(8,128)(2,1)} %all-to-all-done), kind=kLoop, calls=%fused_computation.75 | loop fusion | bytes 2097152 | tf_op jit(solution)/shard_map/slice | solution.py:25
  84.4 0.8 fusion.18
  85.2 0.8 add_convert_fusion
  86.2 20.3 %all_to_all.10 = bf16[1,512,2,16,32]{1,4,2,0,3:T(8,128)(2,1)S(1)} all-to-all(bf16[1,512,2,16,32]{1,4,2,0,3:T(8,128)(2,1)S(1)} %pad_maximum_fusion), channel_id=1, replica_groups=mesh['row'=16,'cz'=8,'cx'=2] {'row'}, dimensions={3} | all-to-all | bytes 2097152 | tf_op jit(solution)/shard_map/all_to_all | solution.py:132
  106.6 2.1 %copy.13 = bf16[1,1,1,512,2,512]{5,4,3,2,1,0:T(2,128)(2,1)} copy(bf16[1,1,1,512,2,512]{3,5,4,2,1,0:T(8,128)(2,1)S(1)} %bitcast.86) | data formatting | bytes 2097152 | tf_op jit(solution)/shard_map/reshape | solution.py:133
  (57 shorter events, 5.2 us)
Async XLA Ops:
  0.0 5.5 %copy-start.3 = (bf16[1,4,2,512,32]{3,4,2,1,0:T(8,128)(2,1)S(1)}, bf16[1,4,2,512,32]{3,4,2,1,0:T(8,128)(2,1)}, u32[]{:S(2)}) copy-start(bf16[1,4,2,512,32]{3,4,2,1,0:T(8,128)(2,1)} %param.3) | copy-start | bytes 786436
  1.0 4.5 %collective-permute-start.6 = (bf16[2,2,32,512]{3,2,1,0:T(8,128)(2,1)S(1)}, bf16[2,2,32,512]{3,2,1,0:T(8,128)(2,1)S(1)}, u32[]{:S(2)}, u32[]{:S(2)}) collective-permute-start(bf16[2,2,32,512]{3,2,1,0:T(8,128)(2,1)S(1)} %slice.111), channel_id=1, source_target_pairs={{0,1},{1,0},{2,3},{3,2},{4,5},{5,4},{6,7},{7,6},{8,9},{9,8},{10,11... | collective-permute-start | bytes 393224 | tf_op jit(solution)/shard_map/ppermute | solution.py:71
  5.5 8.1 %collective-permute-start = (bf16[2,2,32,512]{3,2,1,0:T(8,128)(2,1)S(1)}, bf16[2,2,32,512]{3,2,1,0:T(8,128)(2,1)S(1)}, u32[]{:S(2)}, u32[]{:S(2)}) collective-permute-start(bf16[2,2,32,512]{3,2,1,0:T(8,128)(2,1)S(1)} %get-tuple-element.25), channel_id=1, source_target_pairs={{0,1},{1,0},{2,3},{3,2},{4,5},{5,4},{6,7},{7,6},{8,9},{9,8},{10,11... | collective-permute-start | bytes 393224 | tf_op jit(solution)/shard_map/ppermute | solution.py:71
  7.4 9.7 %collective-permute-start.7 = (bf16[2,2,2,32,512]{4,3,1,0,2:T(8,128)(2,1)S(1)}, bf16[2,2,2,32,512]{4,3,1,0,2:T(8,128)(2,1)S(1)}, u32[]{:S(2)}, u32[]{:S(2)}) collective-permute-start(bf16[2,2,2,32,512]{4,3,1,0,2:T(8,128)(2,1)S(1)} %pad_maximum_fusion.2), channel_id=1, source_target_pairs={{0,14},{2,0},{4,2},{6,4},{8,6},{10,8},{12,10},{14,12},{1,15},{3,1}... | collective-permute-start | bytes 786440 | tf_op jit(solution)/shard_map/ppermute | solution.py:71
  13.3 7.3 %collective-permute-start.8 = (bf16[2,2,2,32,512]{4,3,1,0,2:T(8,128)(2,1)S(1)}, bf16[2,2,2,32,512]{4,3,1,0,2:T(8,128)(2,1)S(1)}, u32[]{:S(2)}, u32[]{:S(2)}) collective-permute-start(bf16[2,2,2,32,512]{4,3,1,0,2:T(8,128)(2,1)S(1)} %pad_maximum_fusion.2), channel_id=1, source_target_pairs={{0,2},{2,4},{4,6},{6,8},{8,10},{10,12},{12,14},{14,0},{1,3},{3,5},... | collective-permute-start | bytes 786440 | tf_op jit(solution)/shard_map/ppermute | solution.py:71
  13.7 12.2 %collective-permute-start.2 = (bf16[2,2,2,32,512]{4,3,1,0,2:T(8,128)(2,1)S(1)}, bf16[2,2,2,32,512]{4,3,1,0,2:T(8,128)(2,1)S(1)}, u32[]{:S(2)}, u32[]{:S(2)}) collective-permute-start(bf16[2,2,2,32,512]{4,3,1,0,2:T(8,128)(2,1)S(1)} %pad_maximum_fusion.1), channel_id=1, source_target_pairs={{0,2},{2,4},{4,6},{6,8},{8,10},{10,12},{12,14},{14,0},{1,3},{3,5},... | collective-permute-start | bytes 786440 | tf_op jit(solution)/shard_map/ppermute | solution.py:71
  13.7 12.2 %collective-permute-start.1 = (bf16[2,2,2,32,512]{4,3,1,0,2:T(8,128)(2,1)S(1)}, bf16[2,2,2,32,512]{4,3,1,0,2:T(8,128)(2,1)S(1)}, u32[]{:S(2)}, u32[]{:S(2)}) collective-permute-start(bf16[2,2,2,32,512]{4,3,1,0,2:T(8,128)(2,1)S(1)} %pad_maximum_fusion.1), channel_id=1, source_target_pairs={{0,14},{2,0},{4,2},{6,4},{8,6},{10,8},{12,10},{14,12},{1,15},{3,1}... | collective-permute-start | bytes 786440 | tf_op jit(solution)/shard_map/ppermute | solution.py:71
  17.1 11.5 %collective-permute-start.9 = (bf16[2,2,2,32,512]{4,3,1,0,2:T(8,128)(2,1)S(1)}, bf16[2,2,2,32,512]{4,3,1,0,2:T(8,128)(2,1)S(1)}, u32[]{:S(2)}, u32[]{:S(2)}) collective-permute-start(bf16[2,2,2,32,512]{4,3,1,0,2:T(8,128)(2,1)S(1)} %collective-permute-done.7), channel_id=1, source_target_pairs={{0,14},{2,0},{4,2},{6,4},{8,6},{10,8},{12,10},{14,12},{1,15},{3,1}... | collective-permute-start | bytes 786440 | tf_op jit(solution)/shard_map/ppermute | solution.py:71
  20.6 11.2 %collective-permute-start.10 = (bf16[2,2,2,32,512]{4,3,1,0,2:T(8,128)(2,1)S(1)}, bf16[2,2,2,32,512]{4,3,1,0,2:T(8,128)(2,1)S(1)}, u32[]{:S(2)}, u32[]{:S(2)}) collective-permute-start(bf16[2,2,2,32,512]{4,3,1,0,2:T(8,128)(2,1)S(1)} %collective-permute-done.8), channel_id=1, source_target_pairs={{0,2},{2,4},{4,6},{6,8},{8,10},{10,12},{12,14},{14,0},{1,3},{3,5},... | collective-permute-start | bytes 786440 | tf_op jit(solution)/shard_map/ppermute | solution.py:71
  25.9 26.5 %collective-permute-start.4 = (bf16[2,2,2,32,512]{4,3,1,0,2:T(8,128)(2,1)S(1)}, bf16[2,2,2,32,512]{4,3,1,0,2:T(8,128)(2,1)S(1)}, u32[]{:S(2)}, u32[]{:S(2)}) collective-permute-start(bf16[2,2,2,32,512]{4,3,1,0,2:T(8,128)(2,1)S(1)} %collective-permute-done.2), channel_id=1, source_target_pairs={{0,2},{2,4},{4,6},{6,8},{8,10},{10,12},{12,14},{14,0},{1,3},{3,5},... | collective-permute-start | bytes 786440 | tf_op jit(solution)/shard_map/ppermute | solution.py:71
  25.9 7.6 %collective-permute-start.3 = (bf16[2,2,2,32,512]{4,3,1,0,2:T(8,128)(2,1)S(1)}, bf16[2,2,2,32,512]{4,3,1,0,2:T(8,128)(2,1)}, u32[]{:S(2)}, u32[]{:S(2)}) collective-permute-start(bf16[2,2,2,32,512]{4,3,1,0,2:T(8,128)(2,1)S(1)} %collective-permute-done.1), channel_id=1, source_target_pairs={{0,14},{2,0},{4,2},{6,4},{8,6},{10,8},{12,10},{14,12},{1,15},{3,1}... | collective-permute-start | bytes 786440 | tf_op jit(solution)/shard_map/ppermute | solution.py:71
  28.6 14.2 %collective-permute-start.11 = (bf16[2,2,2,32,512]{4,3,1,0,2:T(8,128)(2,1)S(1)}, bf16[2,2,2,32,512]{4,3,1,0,2:T(8,128)(2,1)S(1)}, u32[]{:S(2)}, u32[]{:S(2)}) collective-permute-start(bf16[2,2,2,32,512]{4,3,1,0,2:T(8,128)(2,1)S(1)} %collective-permute-done.9), channel_id=1, source_target_pairs={{0,14},{2,0},{4,2},{6,4},{8,6},{10,8},{12,10},{14,12},{1,15},{3,1}... | collective-permute-start | bytes 786440 | tf_op jit(solution)/shard_map/ppermute | solution.py:71
  31.8 11.0 %collective-permute-start.12 = (bf16[2,2,2,32,512]{4,3,1,0,2:T(8,128)(2,1)S(1)}, bf16[2,2,2,32,512]{4,3,1,0,2:T(8,128)(2,1)S(1)}, u32[]{:S(2)}, u32[]{:S(2)}) collective-permute-start(bf16[2,2,2,32,512]{4,3,1,0,2:T(8,128)(2,1)S(1)} %collective-permute-done.10), channel_id=1, source_target_pairs={{0,2},{2,4},{4,6},{6,8},{8,10},{10,12},{12,14},{14,0},{1,3},{3,5},... | collective-permute-start | bytes 786440 | tf_op jit(solution)/shard_map/ppermute | solution.py:71
  33.5 30.8 %collective-permute-start.5 = (bf16[2,2,2,32,512]{4,3,1,0,2:T(8,128)(2,1)}, bf16[2,2,2,32,512]{4,3,1,0,2:T(8,128)(2,1)}, u32[]{:S(2)}, u32[]{:S(2)}) collective-permute-start(bf16[2,2,2,32,512]{4,3,1,0,2:T(8,128)(2,1)} %collective-permute-done.3), channel_id=1, source_target_pairs={{0,14},{2,0},{4,2},{6,4},{8,6},{10,8},{12,10},{14,12},{1,15},{3,1}... | collective-permute-start | bytes 786440 | tf_op jit(solution)/shard_map/ppermute | solution.py:71
  42.8 5.1 %collective-permute-start.13 = (bf16[2,2,2,16,512]{4,3,1,0,2:T(8,128)(2,1)S(1)}, bf16[2,2,2,16,512]{4,3,1,0,2:T(8,128)(2,1)S(1)}, u32[]{:S(2)}, u32[]{:S(2)}) collective-permute-start(bf16[2,2,2,16,512]{4,3,1,0,2:T(8,128)(2,1)S(1)} %slice.112), channel_id=1, source_target_pairs={{0,2},{2,4},{4,6},{6,8},{8,10},{10,12},{12,14},{14,0},{1,3},{3,5},... | collective-permute-start | bytes 393224 | tf_op jit(solution)/shard_map/ppermute | solution.py:71
  42.9 6.2 %collective-permute-start.14 = (bf16[2,2,2,16,512]{4,3,1,0,2:T(8,128)(2,1)S(1)}, bf16[2,2,2,16,512]{4,3,1,0,2:T(8,128)(2,1)S(1)}, u32[]{:S(2)}, u32[]{:S(2)}) collective-permute-start(bf16[2,2,2,16,512]{4,3,1,0,2:T(8,128)(2,1)S(1)} %slice.113), channel_id=1, source_target_pairs={{0,14},{2,0},{4,2},{6,4},{8,6},{10,8},{12,10},{14,12},{1,15},{3,1}... | collective-permute-start | bytes 393224 | tf_op jit(solution)/shard_map/ppermute | solution.py:71
  52.4 11.7 %collective-permute-start.15 = (bf16[2,2,2,32,512]{4,3,1,0,2:T(8,128)(2,1)S(1)}, bf16[2,2,2,32,512]{4,3,1,0,2:T(8,128)(2,1)S(1)}, u32[]{:S(2)}, u32[]{:S(2)}) collective-permute-start(bf16[2,2,2,32,512]{4,3,1,0,2:T(8,128)(2,1)S(1)} %collective-permute-done.4), channel_id=1, source_target_pairs={{0,2},{2,4},{4,6},{6,8},{8,10},{10,12},{12,14},{14,0},{1,3},{3,5},... | collective-permute-start | bytes 786440 | tf_op jit(solution)/shard_map/ppermute | solution.py:71
  54.5 26.7 %all-to-all-start = ((bf16[2,16,32,512]{3,2,0,1:T(8,128)(2,1)}), bf16[2,16,32,512]{3,2,0,1:T(8,128)(2,1)}, u32[]{:S(2)}, u32[]{:S(2)}) async-start(bf16[2,16,32,512]{3,2,0,1:T(8,128)(2,1)} %copy.9), calls=%async_computation | async-start | bytes 2097152 | tf_op jit(solution)/shard_map/all_to_all | solution.py:125
  64.0 10.0 %collective-permute-start.16 = (bf16[2,2,2,32,512]{4,3,1,0,2:T(8,128)(2,1)S(1)}, bf16[2,2,2,32,512]{4,3,1,0,2:T(8,128)(2,1)S(1)}, u32[]{:S(2)}, u32[]{:S(2)}) collective-permute-start(bf16[2,2,2,32,512]{4,3,1,0,2:T(8,128)(2,1)S(1)} %collective-permute-done.15), channel_id=1, source_target_pairs={{0,2},{2,4},{4,6},{6,8},{8,10},{10,12},{12,14},{14,0},{1,3},{3,5},... | collective-permute-start | bytes 786440 | tf_op jit(solution)/shard_map/ppermute | solution.py:71
  75.1 0.8 copy-start.1
  83.2 1.0 copy-start
  83.2 1.2 %copy-start.2 = (bf16[1,1,8,2,32,512]{5,4,1,0,3,2:T(8,128)(2,1)S(1)}, bf16[1,1,8,2,32,512]{5,4,1,0,3,2:T(8,128)(2,1)}, u32[]{:S(2)}) copy-start(bf16[1,1,8,2,32,512]{5,4,1,0,3,2:T(8,128)(2,1)} %copy-done.1) | copy-start | bytes 1572868

commit v12 on v11

--- a/solution.py
+++ b/solution.py
@@ -37,6 +37,18 @@
         "ix,ij->xj", weight_imag, block[:, 1, :], preferred_element_type=jnp.float32
     )
     return product.reshape(2, piece_t.shape[2], block.shape[2])
+
+
+def right_grouped(grouped, piece_t):
+    real_t = piece_t[0]
+    imag_t = piece_t[1]
+    top = jnp.concatenate([real_t, imag_t], axis=1)
+    bottom = jnp.concatenate([-imag_t, real_t], axis=1)
+    weight = jnp.stack([top, bottom], axis=0)
+    product = jnp.einsum("pcly,cyk->plk", grouped, weight, preferred_element_type=jnp.float32)
+    cols = piece_t.shape[2]
+    product = product.reshape(-1, 2 * cols)
+    return product[:, :cols], product[:, cols:]
 
 
 def left_halves(real_in, imag_in, piece_t):
@@ -115,16 +127,32 @@
     row_count = lax.axis_size("row")
     share = order_size // row_count
     own_t = jnp.swapaxes(branch[0], -1, -2)
-    first_t, _ = ring_gather(own_t[:2])
+    width = own_t.shape[2]
+    left_cols = own_t[0].reshape(2, width, row_count, share).transpose(1, 2, 0, 3)
+    right_cols = own_t[1].transpose(1, 0, 2)
+    early = jnp.stack([left_cols.reshape(width, -1), right_cols.reshape(width, -1)])
+    first_w, _ = ring_gather(early[:, None])
+    left_w = first_w[0, 0]
+    top = first_w[1, 0]
+    bottom = jnp.concatenate([-top[:, order_size:], top[:, :order_size]], axis=1)
 
     block = stem[0, 0]
-    half_first = right_piece(block, first_t[1]).astype(jnp.bfloat16)
-    step_first = left_planar(half_first[0], first_t[0]).astype(jnp.bfloat16)
+    flat = block.reshape(order_size, 2 * order_size)
+    weight = jnp.concatenate([top, bottom], axis=0)
+    half_first = jnp.dot(flat, weight, preferred_element_type=jnp.float32)
+    half_first = half_first.astype(jnp.bfloat16).reshape(order_size, 2, order_size)
+    real_slot = (jnp.arange(left_w.shape[1]) % (2 * share)) < share
+    left_imag = jnp.where(
+        real_slot, -jnp.roll(left_w, -share, axis=1), jnp.roll(left_w, share, axis=1)
+    )
+    product = jnp.einsum("ix,ij->xj", left_w, half_first[:, 0, :], preferred_element_type=jnp.float32)
+    product = product + jnp.einsum(
+        "ix,ij->xj", left_imag, half_first[:, 1, :], preferred_element_type=jnp.float32
+    )
+    step_first = product.astype(jnp.bfloat16).reshape(row_count, 2, share, order_size)
     second_t, step_first = ring_gather(own_t[2:], hold=step_first)
-    outgoing = step_first.reshape(2, row_count, share, order_size)
-    moved = lax.all_to_all(outgoing, "row", split_axis=1, concat_axis=1, tiled=True)
-    planar = moved.reshape(2, order_size, order_size)
-    real_half, imag_half = right_planar(planar, second_t[1])
+    moved = lax.all_to_all(step_first, "row", split_axis=0, concat_axis=0, tiled=True)
+    real_half, imag_half = right_grouped(moved, second_t[1])
     step_second = left_halves(
         real_half.astype(jnp.bfloat16), imag_half.astype(jnp.bfloat16), second_t[0]
     ).astype(jnp.bfloat16)

time: 109 us -> 117 us (1.073)
  waiting for transfers between devices: 31.5 us -> 39.6 us
  local copies, waits for them, and re-layouts: 12.1 us -> 7.48 us
  matrix products: 5.79 us -> 8.8 us
  other arithmetic: 0.56 us -> 1.78 us
    all_to_all x1, waiting for transfers between devices: 5.28 us -> 15.4 us  [shards(): lax.all_to_all(step_first, 'row', split_axis=0, concat_axis=0, tiled=True)]
    dot_general x5 -> x4, matrix products: 4.25 us -> 7.26 us  [the longest x1 2.79 us: right_grouped(): jnp.einsum('pcly,cyk->plk', grouped, weight, preferred_element_type=jnp.f...]
    unnamed x9 -> x5, local copies, waits for them, and re-layouts: 2.65 us -> 0.25 us
    ppermute x17, waiting for transfers between devices: 26.2 us -> 24.2 us  [shift(): return lax.ppermute(x, axis, [(i, (i + d) % n) for i in range(n)])]
    dynamic_update_slice x6, local copies, waits for them, and re-layouts: 2.02 us -> 0.13 us  [ring_gather(): lax.dynamic_update_slice(buf, cur_b[:, :, None], (0, 0, (z + k) % nz, 0,...]
    ppermute x17, starting transfers between devices: 28.5 us -> 27 us  [shift(): return lax.ppermute(x, axis, [(i, (i + d) % n) for i in range(n)])]
    all_to_all x1, starting transfers between devices: 9.51 us -> 10.9 us  [shards(): lax.all_to_all(step_first, 'row', split_axis=0, concat_axis=0, tiled=True)]
    another operation x0 -> x1, other arithmetic: none -> 1.29 us  [right_grouped(): weight = jnp.stack([top, bottom], axis=0)]
  transfers between devices with their start and end apart: 18 -> 18, of which waited for: 9 -> 8; matrix products, arithmetic and copies ran while one was open for 9% -> 8% of each run, Pallas kernels for 0% -> 0%
where the time goes in v12:
time: 117 us; the launch traced here: 116 us
  waiting for transfers between devices  39.6 us (34%)
  starting transfers between devices  37.9 us (32%)
  blocking collectives  20.3 us (17%)
  matrix products  8.8 us (8%)
  local copies, waits for them, and re-layouts  7.48 us (6%)
  other arithmetic  1.78 us (2%)
    ppermute x17, starting transfers between devices, shift(): return lax.ppermute(x, axis, [(i, (i + d) % n) for i in range(n)])  27 us
    ppermute x17, waiting for transfers between devices, shift(): return lax.ppermute(x, axis, [(i, (i + d) % n) for i in range(n)])  24.2 us
    all_to_all x1, blocking collectives, shards(): lax.all_to_all(leaving, 'row', split_axis=3, concat_axis=3, tiled=True)  20.3 us
    all_to_all x1, waiting for transfers between devices, shards(): lax.all_to_all(step_first, 'row', split_axis=0, concat_axis=0, tiled=True)  15.4 us
    all_to_all x1, starting transfers between devices, shards(): lax.all_to_all(step_first, 'row', split_axis=0, concat_axis=0, tiled=True)  10.9 us
    dot_general x1, matrix products, right_grouped(): jnp.einsum('pcly,cyk->plk', grouped, weight, preferred_element_type=jnp.f...  2.79 us
    dot_general x1, matrix products, shards(): jnp.einsum('ix,ij->xj', left_imag, half_first[:, 1, :], preferred_element...  2.4 us
  transfers between devices with their start and end apart: 18, of which 8 were waited for; matrix products, arithmetic and copies ran while one was open for 8% of the time, Pallas kernels for 0%

profile of v12, /device:TPU:1, one launch (start us, length us, event | category | flops | bytes accessed | tf_op | source)
XLA Modules:
  0.0 116.5 jit_solution(6087794944822938122)
XLA Ops:
  0.0 1.0 fusion.46
  1.2 0.3 copy.56
  1.4 0.3 stack_reshape.6
  1.9 2.1 %collective-permute-start.6 = (bf16[2,1,32,1024]{3,2,0,1:T(8,128)(2,1)S(1)}, bf16[2,1,32,1024]{3,2,0,1:T(8,128)(2,1)S(1)}, u32[]{:S(2)}, u32[]{:S(2)}) collective-permute-start(bf16[2,1,32,1024]{3,2,0,1:T(8,128)(2,1)S(1)} %maximum_bitcast_fusion.7), channel_id=1, source_target_pairs={{0,1},{1,0},{2,3},{3,2},{4,5},{5,4},{6,7},{7,6},{8,9},{9,8},{10,11... | collective-permute-start | bytes 393224 | tf_op jit(solution)/shard_map/ppermute | solution.py:83
  4.0 0.9 slice.114
  5.4 0.9 collective-permute-done.6
  6.4 6.5 %collective-permute-start.7 = (bf16[2,1,2,32,1024]{4,3,0,2,1:T(8,128)(2,1)S(1)}, bf16[2,1,2,32,1024]{4,3,0,2,1:T(8,128)(2,1)S(1)}, u32[]{:S(2)}, u32[]{:S(2)}) collective-permute-start(bf16[2,1,2,32,1024]{4,3,0,2,1:T(8,128)(2,1)S(1)} %pad_maximum_fusion.2), channel_id=1, source_target_pairs={{0,14},{2,0},{4,2},{6,4},{8,6},{10,8},{12,10},{14,12},{1,15},{3,1}... | collective-permute-start | bytes 786440 | tf_op jit(solution)/shard_map/ppermute | solution.py:83
  13.1 3.0 %collective-permute-start.1 = (bf16[2,2,2,32,512]{4,3,1,0,2:T(8,128)(2,1)S(1)}, bf16[2,2,2,32,512]{4,3,1,0,2:T(8,128)(2,1)S(1)}, u32[]{:S(2)}, u32[]{:S(2)}) collective-permute-start(bf16[2,2,2,32,512]{4,3,1,0,2:T(8,128)(2,1)S(1)} %get-tuple-element.31), channel_id=1, source_target_pairs={{0,14},{2,0},{4,2},{6,4},{8,6},{10,8},{12,10},{14,12},{1,15},{3,1}... | collective-permute-start | bytes 786440 | tf_op jit(solution)/shard_map/ppermute | solution.py:83
  16.7 3.1 %collective-permute-start.9 = (bf16[2,1,2,32,1024]{4,3,0,2,1:T(8,128)(2,1)S(1)}, bf16[2,1,2,32,1024]{4,3,0,2,1:T(8,128)(2,1)S(1)}, u32[]{:S(2)}, u32[]{:S(2)}) collective-permute-start(bf16[2,1,2,32,1024]{4,3,0,2,1:T(8,128)(2,1)S(1)} %collective-permute-done.7), channel_id=1, source_target_pairs={{0,14},{2,0},{4,2},{6,4},{8,6},{10,8},{12,10},{14,12},{1,15},{3,1}... | collective-permute-start | bytes 786440 | tf_op jit(solution)/shard_map/ppermute | solution.py:83
  19.8 5.3 %collective-permute-done.2 = bf16[2,2,2,32,512]{4,3,1,0,2:T(8,128)(2,1)S(1)} collective-permute-done((bf16[2,2,2,32,512]{4,3,1,0,2:T(8,128)(2,1)S(1)}, bf16[2,2,2,32,512]{4,3,1,0,2:T(8,128)(2,1)S(1)}, u32[]{:S(2)}, u32[]{:S(2)}) %collective-permute-start.2) | collective-permute-done | bytes 262176 | tf_op jit(solution)/shard_map/ppermute | solution.py:83
  25.2 2.7 %collective-permute-start.3 = (bf16[2,2,2,32,512]{4,3,1,0,2:T(8,128)(2,1)S(1)}, bf16[2,2,2,32,512]{4,3,1,0,2:T(8,128)(2,1)S(1)}, u32[]{:S(2)}, u32[]{:S(2)}) collective-permute-start(bf16[2,2,2,32,512]{4,3,1,0,2:T(8,128)(2,1)S(1)} %collective-permute-done.1), channel_id=1, source_target_pairs={{0,14},{2,0},{4,2},{6,4},{8,6},{10,8},{12,10},{14,12},{1,15},{3,1}... | collective-permute-start | bytes 786440 | tf_op jit(solution)/shard_map/ppermute | solution.py:83
  28.0 3.3 %collective-permute-start.11 = (bf16[2,1,2,32,1024]{4,3,0,2,1:T(8,128)(2,1)S(1)}, bf16[2,1,2,32,1024]{4,3,0,2,1:T(8,128)(2,1)S(1)}, u32[]{:S(2)}, u32[]{:S(2)}) collective-permute-start(bf16[2,1,2,32,1024]{4,3,0,2,1:T(8,128)(2,1)S(1)} %collective-permute-done.9), channel_id=1, source_target_pairs={{0,14},{2,0},{4,2},{6,4},{8,6},{10,8},{12,10},{14,12},{1,15},{3,1}... | collective-permute-start | bytes 786440 | tf_op jit(solution)/shard_map/ppermute | solution.py:83
  31.3 1.8 %collective-permute-done.3 = bf16[2,2,2,32,512]{4,3,1,0,2:T(8,128)(2,1)S(1)} collective-permute-done((bf16[2,2,2,32,512]{4,3,1,0,2:T(8,128)(2,1)S(1)}, bf16[2,2,2,32,512]{4,3,1,0,2:T(8,128)(2,1)S(1)}, u32[]{:S(2)}, u32[]{:S(2)}) %collective-permute-start.3) | collective-permute-done | bytes 262176 | tf_op jit(solution)/shard_map/ppermute | solution.py:83
  33.0 3.1 %collective-permute-start.5 = (bf16[2,2,2,32,512]{4,3,1,0,2:T(8,128)(2,1)S(1)}, bf16[2,2,2,32,512]{4,3,1,0,2:T(8,128)(2,1)S(1)}, u32[]{:S(2)}, u32[]{:S(2)}) collective-permute-start(bf16[2,2,2,32,512]{4,3,1,0,2:T(8,128)(2,1)S(1)} %collective-permute-done.3), channel_id=1, source_target_pairs={{0,14},{2,0},{4,2},{6,4},{8,6},{10,8},{12,10},{14,12},{1,15},{3,1}... | collective-permute-start | bytes 786440 | tf_op jit(solution)/shard_map/ppermute | solution.py:83
  36.2 5.8 %collective-permute-done.12 = bf16[2,1,2,32,1024]{4,3,0,2,1:T(8,128)(2,1)S(1)} collective-permute-done((bf16[2,1,2,32,1024]{4,3,0,2,1:T(8,128)(2,1)S(1)}, bf16[2,1,2,32,1024]{4,3,0,2,1:T(8,128)(2,1)S(1)}, u32[]{:S(2)}, u32[]{:S(2)}) %collective-permute-start.12) | collective-permute-done | bytes 262176 | tf_op jit(solution)/shard_map/ppermute | solution.py:83
  42.2 2.9 %collective-permute-start.14 = (bf16[2,1,2,16,1024]{4,3,0,2,1:T(8,128)(2,1)S(1)}, bf16[2,1,2,16,1024]{4,3,0,2,1:T(8,128)(2,1)S(1)}, u32[]{:S(2)}, u32[]{:S(2)}) collective-permute-start(bf16[2,1,2,16,1024]{4,3,0,2,1:T(8,128)(2,1)S(1)} %slice.118), channel_id=1, source_target_pairs={{0,14},{2,0},{4,2},{6,4},{8,6},{10,8},{12,10},{14,12},{1,15},{3,1}... | collective-permute-start | bytes 393224 | tf_op jit(solution)/shard_map/ppermute | solution.py:83
  45.1 2.0 %collective-permute-done.13 = bf16[2,1,2,16,1024]{4,3,0,2,1:T(8,128)(2,1)S(1)} collective-permute-done((bf16[2,1,2,16,1024]{4,3,0,2,1:T(8,128)(2,1)S(1)}, bf16[2,1,2,16,1024]{4,3,0,2,1:T(8,128)(2,1)S(1)}, u32[]{:S(2)}, u32[]{:S(2)}) %collective-permute-start.13) | collective-permute-done | bytes 131104 | tf_op jit(solution)/shard_map/ppermute | solution.py:83
  47.1 1.2 %collective-permute-done.14 = bf16[2,1,2,16,1024]{4,3,0,2,1:T(8,128)(2,1)S(1)} collective-permute-done((bf16[2,1,2,16,1024]{4,3,0,2,1:T(8,128)(2,1)S(1)}, bf16[2,1,2,16,1024]{4,3,0,2,1:T(8,128)(2,1)S(1)}, u32[]{:S(2)}, u32[]{:S(2)}) %collective-permute-start.14) | collective-permute-done | bytes 131104 | tf_op jit(solution)/shard_map/ppermute | solution.py:83
  48.4 0.3 fusion.42
  48.7 0.8 fusion.45
  49.7 1.3 %fusion.9 = bf16[1024,512]{1,0:T(8,128)(2,1)S(1)} fusion(bf16[512,1024]{1,0:T(8,128)(2,1)S(1)} %bitcast.126, bf16[512,512]{1,0:T(8,128)(2,1)S(1)} %get-tuple-element.22, bf16[512,512]{1,0:T(8,128)(2,1)S(1)} %get-tuple-element.21, bf16[512,1024]{1,0:T(8,128)(2,1)S(1)} %bitcast.117), kind=kOutput, calls=%fused_computation.13 | convolution fusion | flops 1080557568 | bytes 4194304 | tf_op jit(solution)/shard_map/dot_general | solution.py:142
  51.0 0.8 fusion.29
  51.7 2.4 %add_convert_fusion.1 = bf16[1024,512]{1,0:T(8,128)(2,1)} fusion(f32[1024,512]{1,0:T(8,128)S(1)} %fusion.29, bf16[512,32]{1,0:T(8,128)(2,1)S(1)} %get-tuple-element.18, bf16[512,992]{1,0:T(8,128)(2,1)S(1)} %get-tuple-element.20, bf16[512,992]{1,0:T(8,128)(2,1)S(1)} %get-tuple-element.19, bf16[512,32]{1,0:T(8,128)(2,1)S(1)} %get-tuple-element.17, ...), kind=kOutput, calls=%fused_computation.12 | convolution fusion | flops 543162368 | bytes 6030336 | tf_op jit(solution)/shard_map/ix,ij->xj/dot_general | solution.py:149
  54.2 7.1 %collective-permute-done.15 = bf16[2,2,2,32,512]{4,3,1,0,2:T(8,128)(2,1)S(1)} collective-permute-done((bf16[2,2,2,32,512]{4,3,1,0,2:T(8,128)(2,1)S(1)}, bf16[2,2,2,32,512]{4,3,1,0,2:T(8,128)(2,1)S(1)}, u32[]{:S(2)}, u32[]{:S(2)}) %collective-permute-start.15) | collective-permute-done | bytes 262176 | tf_op jit(solution)/shard_map/ppermute | solution.py:83
  61.4 10.9 %all-to-all-start = ((bf16[16,2,32,512]{3,2,1,0:T(8,128)(2,1)}), bf16[16,2,32,512]{3,2,1,0:T(8,128)(2,1)}, u32[]{:S(2)}, u32[]{:S(2)}) async-start(bf16[16,2,32,512]{3,2,1,0:T(8,128)(2,1)} %bitcast.32), calls=%async_computation | async-start | bytes 2097152 | tf_op jit(solution)/shard_map/all_to_all | solution.py:154
  72.6 1.3 %maximum_bitcast_fusion.4 = (bf16[1,512,1024]{2,1,0:T(8,128)(2,1)S(1)}, bf16[1,512,1024]{2,1,0:T(8,128)(2,1)}) fusion(bf16[512,512]{1,0:T(8,128)(2,1)S(1)} %bitcast.114, bf16[512,512]{1,0:T(8,128)(2,1)S(1)} %bitcast.120, bf16[512,512]{1,0:T(8,128)(2,1)S(1)} %bitcast_negate_fusion), kind=kLoop, calls=%fused_computation.25 | loop fusion | flops 4194304 | bytes 3670016 | tf_op jit(solution)/shard_map/stack | solution.py:47
  74.0 15.4 %all-to-all-done = bf16[16,2,32,512]{3,2,1,0:T(8,128)(2,1)} async-done(((bf16[16,2,32,512]{3,2,1,0:T(8,128)(2,1)}), bf16[16,2,32,512]{3,2,1,0:T(8,128)(2,1)}, u32[]{:S(2)}, u32[]{:S(2)}) %all-to-all-start) | async-done | bytes 1048608 | tf_op jit(solution)/shard_map/all_to_all | solution.py:154
  89.4 2.8 %bitcast_convert_fusion = bf16[16,32,1024]{2,1,0:T(8,128)(2,1)S(1)} fusion(bf16[16,2,32,512]{3,2,1,0:T(8,128)(2,1)} %all-to-all-done, bf16[1,512,1024]{2,1,0:T(8,128)(2,1)} %get-tuple-element.24, bf16[1,512,1024]{2,1,0:T(8,128)(2,1)S(1)} %get-tuple-element.23), kind=kOutput, calls=%fused_computation.10 | convolution fusion | flops 1075314688 | bytes 4194304 | tf_op jit(solution)/shard_map/pcly,cyk->plk/dot_general | solution.py:48
  92.2 0.8 fusion.19
  93.0 0.8 add_convert_fusion
  94.0 20.3 %all_to_all.10 = bf16[1,512,2,16,32]{1,4,2,0,3:T(8,128)(2,1)S(1)} all-to-all(bf16[1,512,2,16,32]{1,4,2,0,3:T(8,128)(2,1)S(1)} %pad_maximum_fusion), channel_id=1, replica_groups=mesh['row'=16,'cz'=8,'cx'=2] {'row'}, dimensions={3} | all-to-all | bytes 2097152 | tf_op jit(solution)/shard_map/all_to_all | solution.py:160
  114.4 2.1 %copy.44 = bf16[1,1,1,512,2,512]{5,4,3,2,1,0:T(2,128)(2,1)} copy(bf16[1,1,1,512,2,512]{3,5,4,2,1,0:T(8,128)(2,1)S(1)} %bitcast.115) | data formatting | bytes 2097152 | tf_op jit(solution)/shard_map/reshape | solution.py:161
  (61 shorter events, 2.7 us)
Async XLA Ops:
  0.0 5.1 %copy-start = (bf16[1,1,1,512,2,512]{5,4,3,2,1,0:T(2,128)(2,1)S(1)}, bf16[1,1,1,512,2,512]{5,4,3,2,1,0:T(2,128)(2,1)}, u32[]{:S(2)}) copy-start(bf16[1,1,1,512,2,512]{5,4,3,2,1,0:T(2,128)(2,1)} %param.2) | copy-start | bytes 3145732
  1.7 11.2 %copy-start.1 = (bf16[1,4,2,512,32]{3,4,2,1,0:T(8,128)(2,1)S(1)}, bf16[1,4,2,512,32]{3,4,2,1,0:T(8,128)(2,1)}, u32[]{:S(2)}) copy-start(bf16[1,4,2,512,32]{3,4,2,1,0:T(8,128)(2,1)} %param.3) | copy-start | bytes 786436
  1.9 4.5 %collective-permute-start.6 = (bf16[2,1,32,1024]{3,2,0,1:T(8,128)(2,1)S(1)}, bf16[2,1,32,1024]{3,2,0,1:T(8,128)(2,1)S(1)}, u32[]{:S(2)}, u32[]{:S(2)}) collective-permute-start(bf16[2,1,32,1024]{3,2,0,1:T(8,128)(2,1)S(1)} %maximum_bitcast_fusion.7), channel_id=1, source_target_pairs={{0,1},{1,0},{2,3},{3,2},{4,5},{5,4},{6,7},{7,6},{8,9},{9,8},{10,11... | collective-permute-start | bytes 393224 | tf_op jit(solution)/shard_map/ppermute | solution.py:83
  4.9 8.0 %collective-permute-start = (bf16[2,2,32,512]{3,2,1,0:T(8,128)(2,1)S(1)}, bf16[2,2,32,512]{3,2,1,0:T(8,128)(2,1)S(1)}, u32[]{:S(2)}, u32[]{:S(2)}) collective-permute-start(bf16[2,2,32,512]{3,2,1,0:T(8,128)(2,1)S(1)} %slice.114), channel_id=1, source_target_pairs={{0,1},{1,0},{2,3},{3,2},{4,5},{5,4},{6,7},{7,6},{8,9},{9,8},{10,11... | collective-permute-start | bytes 393224 | tf_op jit(solution)/shard_map/ppermute | solution.py:83
  6.4 10.3 %collective-permute-start.7 = (bf16[2,1,2,32,1024]{4,3,0,2,1:T(8,128)(2,1)S(1)}, bf16[2,1,2,32,1024]{4,3,0,2,1:T(8,128)(2,1)S(1)}, u32[]{:S(2)}, u32[]{:S(2)}) collective-permute-start(bf16[2,1,2,32,1024]{4,3,0,2,1:T(8,128)(2,1)S(1)} %pad_maximum_fusion.2), channel_id=1, source_target_pairs={{0,14},{2,0},{4,2},{6,4},{8,6},{10,8},{12,10},{14,12},{1,15},{3,1}... | collective-permute-start | bytes 786440 | tf_op jit(solution)/shard_map/ppermute | solution.py:83
  12.9 7.0 %collective-permute-start.8 = (bf16[2,1,2,32,1024]{4,3,0,2,1:T(8,128)(2,1)S(1)}, bf16[2,1,2,32,1024]{4,3,0,2,1:T(8,128)(2,1)S(1)}, u32[]{:S(2)}, u32[]{:S(2)}) collective-permute-start(bf16[2,1,2,32,1024]{4,3,0,2,1:T(8,128)(2,1)S(1)} %pad_maximum_fusion.2), channel_id=1, source_target_pairs={{0,2},{2,4},{4,6},{6,8},{8,10},{10,12},{12,14},{14,0},{1,3},{3,5},... | collective-permute-start | bytes 786440 | tf_op jit(solution)/shard_map/ppermute | solution.py:83
  13.0 12.2 %collective-permute-start.2 = (bf16[2,2,2,32,512]{4,3,1,0,2:T(8,128)(2,1)S(1)}, bf16[2,2,2,32,512]{4,3,1,0,2:T(8,128)(2,1)S(1)}, u32[]{:S(2)}, u32[]{:S(2)}) collective-permute-start(bf16[2,2,2,32,512]{4,3,1,0,2:T(8,128)(2,1)S(1)} %get-tuple-element.31), channel_id=1, source_target_pairs={{0,2},{2,4},{4,6},{6,8},{8,10},{10,12},{12,14},{14,0},{1,3},{3,5},... | collective-permute-start | bytes 786440 | tf_op jit(solution)/shard_map/ppermute | solution.py:83
  13.1 12.1 %collective-permute-start.1 = (bf16[2,2,2,32,512]{4,3,1,0,2:T(8,128)(2,1)S(1)}, bf16[2,2,2,32,512]{4,3,1,0,2:T(8,128)(2,1)S(1)}, u32[]{:S(2)}, u32[]{:S(2)}) collective-permute-start(bf16[2,2,2,32,512]{4,3,1,0,2:T(8,128)(2,1)S(1)} %get-tuple-element.31), channel_id=1, source_target_pairs={{0,14},{2,0},{4,2},{6,4},{8,6},{10,8},{12,10},{14,12},{1,15},{3,1}... | collective-permute-start | bytes 786440 | tf_op jit(solution)/shard_map/ppermute | solution.py:83
  16.7 11.3 %collective-permute-start.9 = (bf16[2,1,2,32,1024]{4,3,0,2,1:T(8,128)(2,1)S(1)}, bf16[2,1,2,32,1024]{4,3,0,2,1:T(8,128)(2,1)S(1)}, u32[]{:S(2)}, u32[]{:S(2)}) collective-permute-start(bf16[2,1,2,32,1024]{4,3,0,2,1:T(8,128)(2,1)S(1)} %collective-permute-done.7), channel_id=1, source_target_pairs={{0,14},{2,0},{4,2},{6,4},{8,6},{10,8},{12,10},{14,12},{1,15},{3,1}... | collective-permute-start | bytes 786440 | tf_op jit(solution)/shard_map/ppermute | solution.py:83
  19.8 11.4 %collective-permute-start.10 = (bf16[2,1,2,32,1024]{4,3,0,2,1:T(8,128)(2,1)S(1)}, bf16[2,1,2,32,1024]{4,3,0,2,1:T(8,128)(2,1)S(1)}, u32[]{:S(2)}, u32[]{:S(2)}) collective-permute-start(bf16[2,1,2,32,1024]{4,3,0,2,1:T(8,128)(2,1)S(1)} %collective-permute-done.8), channel_id=1, source_target_pairs={{0,2},{2,4},{4,6},{6,8},{8,10},{10,12},{12,14},{14,0},{1,3},{3,5},... | collective-permute-start | bytes 786440 | tf_op jit(solution)/shard_map/ppermute | solution.py:83
  25.2 29.0 %collective-permute-start.4 = (bf16[2,2,2,32,512]{4,3,1,0,2:T(8,128)(2,1)S(1)}, bf16[2,2,2,32,512]{4,3,1,0,2:T(8,128)(2,1)S(1)}, u32[]{:S(2)}, u32[]{:S(2)}) collective-permute-start(bf16[2,2,2,32,512]{4,3,1,0,2:T(8,128)(2,1)S(1)} %collective-permute-done.2), channel_id=1, source_target_pairs={{0,2},{2,4},{4,6},{6,8},{8,10},{10,12},{12,14},{14,0},{1,3},{3,5},... | collective-permute-start | bytes 786440 | tf_op jit(solution)/shard_map/ppermute | solution.py:83
  25.2 7.9 %collective-permute-start.3 = (bf16[2,2,2,32,512]{4,3,1,0,2:T(8,128)(2,1)S(1)}, bf16[2,2,2,32,512]{4,3,1,0,2:T(8,128)(2,1)S(1)}, u32[]{:S(2)}, u32[]{:S(2)}) collective-permute-start(bf16[2,2,2,32,512]{4,3,1,0,2:T(8,128)(2,1)S(1)} %collective-permute-done.1), channel_id=1, source_target_pairs={{0,14},{2,0},{4,2},{6,4},{8,6},{10,8},{12,10},{14,12},{1,15},{3,1}... | collective-permute-start | bytes 786440 | tf_op jit(solution)/shard_map/ppermute | solution.py:83
  28.0 14.1 %collective-permute-start.11 = (bf16[2,1,2,32,1024]{4,3,0,2,1:T(8,128)(2,1)S(1)}, bf16[2,1,2,32,1024]{4,3,0,2,1:T(8,128)(2,1)S(1)}, u32[]{:S(2)}, u32[]{:S(2)}) collective-permute-start(bf16[2,1,2,32,1024]{4,3,0,2,1:T(8,128)(2,1)S(1)} %collective-permute-done.9), channel_id=1, source_target_pairs={{0,14},{2,0},{4,2},{6,4},{8,6},{10,8},{12,10},{14,12},{1,15},{3,1}... | collective-permute-start | bytes 786440 | tf_op jit(solution)/shard_map/ppermute | solution.py:83
  31.3 10.8 %collective-permute-start.12 = (bf16[2,1,2,32,1024]{4,3,0,2,1:T(8,128)(2,1)S(1)}, bf16[2,1,2,32,1024]{4,3,0,2,1:T(8,128)(2,1)S(1)}, u32[]{:S(2)}, u32[]{:S(2)}) collective-permute-start(bf16[2,1,2,32,1024]{4,3,0,2,1:T(8,128)(2,1)S(1)} %collective-permute-done.10), channel_id=1, source_target_pairs={{0,2},{2,4},{4,6},{6,8},{8,10},{10,12},{12,14},{14,0},{1,3},{3,5},... | collective-permute-start | bytes 786440 | tf_op jit(solution)/shard_map/ppermute | solution.py:83
  33.0 28.3 %collective-permute-start.5 = (bf16[2,2,2,32,512]{4,3,1,0,2:T(8,128)(2,1)S(1)}, bf16[2,2,2,32,512]{4,3,1,0,2:T(8,128)(2,1)S(1)}, u32[]{:S(2)}, u32[]{:S(2)}) collective-permute-start(bf16[2,2,2,32,512]{4,3,1,0,2:T(8,128)(2,1)S(1)} %collective-permute-done.3), channel_id=1, source_target_pairs={{0,14},{2,0},{4,2},{6,4},{8,6},{10,8},{12,10},{14,12},{1,15},{3,1}... | collective-permute-start | bytes 786440 | tf_op jit(solution)/shard_map/ppermute | solution.py:83
  42.0 5.1 %collective-permute-start.13 = (bf16[2,1,2,16,1024]{4,3,0,2,1:T(8,128)(2,1)S(1)}, bf16[2,1,2,16,1024]{4,3,0,2,1:T(8,128)(2,1)S(1)}, u32[]{:S(2)}, u32[]{:S(2)}) collective-permute-start(bf16[2,1,2,16,1024]{4,3,0,2,1:T(8,128)(2,1)S(1)} %slice.117), channel_id=1, source_target_pairs={{0,2},{2,4},{4,6},{6,8},{8,10},{10,12},{12,14},{14,0},{1,3},{3,5},... | collective-permute-start | bytes 393224 | tf_op jit(solution)/shard_map/ppermute | solution.py:83
  42.2 6.2 %collective-permute-start.14 = (bf16[2,1,2,16,1024]{4,3,0,2,1:T(8,128)(2,1)S(1)}, bf16[2,1,2,16,1024]{4,3,0,2,1:T(8,128)(2,1)S(1)}, u32[]{:S(2)}, u32[]{:S(2)}) collective-permute-start(bf16[2,1,2,16,1024]{4,3,0,2,1:T(8,128)(2,1)S(1)} %slice.118), channel_id=1, source_target_pairs={{0,14},{2,0},{4,2},{6,4},{8,6},{10,8},{12,10},{14,12},{1,15},{3,1}... | collective-permute-start | bytes 393224 | tf_op jit(solution)/shard_map/ppermute | solution.py:83
  54.1 7.2 %collective-permute-start.15 = (bf16[2,2,2,32,512]{4,3,1,0,2:T(8,128)(2,1)S(1)}, bf16[2,2,2,32,512]{4,3,1,0,2:T(8,128)(2,1)S(1)}, u32[]{:S(2)}, u32[]{:S(2)}) collective-permute-start(bf16[2,2,2,32,512]{4,3,1,0,2:T(8,128)(2,1)S(1)} %collective-permute-done.4), channel_id=1, source_target_pairs={{0,2},{2,4},{4,6},{6,8},{8,10},{10,12},{12,14},{14,0},{1,3},{3,5},... | collective-permute-start | bytes 786440 | tf_op jit(solution)/shard_map/ppermute | solution.py:83
  61.3 10.9 %collective-permute-start.16 = (bf16[2,2,2,32,512]{4,3,1,0,2:T(8,128)(2,1)S(1)}, bf16[2,2,2,32,512]{4,3,1,0,2:T(8,128)(2,1)S(1)}, u32[]{:S(2)}, u32[]{:S(2)}) collective-permute-start(bf16[2,2,2,32,512]{4,3,1,0,2:T(8,128)(2,1)S(1)} %collective-permute-done.15), channel_id=1, source_target_pairs={{0,2},{2,4},{4,6},{6,8},{8,10},{10,12},{12,14},{14,0},{1,3},{3,5},... | collective-permute-start | bytes 786440 | tf_op jit(solution)/shard_map/ppermute | solution.py:83
  61.4 28.1 %all-to-all-start = ((bf16[16,2,32,512]{3,2,1,0:T(8,128)(2,1)}), bf16[16,2,32,512]{3,2,1,0:T(8,128)(2,1)}, u32[]{:S(2)}, u32[]{:S(2)}) async-start(bf16[16,2,32,512]{3,2,1,0:T(8,128)(2,1)} %bitcast.32), calls=%async_computation | async-start | bytes 2097152 | tf_op jit(solution)/shard_map/all_to_all | solution.py:154

commit v13 on v12

--- a/solution.py
+++ b/solution.py
@@ -103,6 +103,7 @@
         if k == forward and nz % 2 == 0 and width % 2 == 0:
             half = width // 2
             if hold is not None:
+                cur_f, hold = lax.optimization_barrier((cur_f, hold))
                 piece = shift(cur_f, "cz", nz, 1)
                 buf = lax.dynamic_update_slice(buf, piece[:, :, None], (0, 0, (z - k) % nz, 0, 0, 0))
                 break
@@ -114,8 +115,6 @@
         if k <= backward:
             cur_b = shift(cur_b, "cz", nz, -1)
             buf = lax.dynamic_update_slice(buf, cur_b[:, :, None], (0, 0, (z + k) % nz, 0, 0, 0))
-        if hold is not None and k == forward - 1:
-            cur_f, hold = lax.optimization_barrier((cur_f, hold))
         cur_f = shift(cur_f, "cz", nz, 1)
         buf = lax.dynamic_update_slice(buf, cur_f[:, :, None], (0, 0, (z - k) % nz, 0, 0, 0))
     return buf.reshape(nb, comps, nz * nx * width, cols), hold

time: 117 us -> 112 us (0.957)
  waiting for transfers between devices: 39.6 us -> 35.2 us
    ppermute x17, waiting for transfers between devices: 24.2 us -> 19.7 us  [shift(): return lax.ppermute(x, axis, [(i, (i + d) % n) for i in range(n)])]
  transfers between devices with their start and end apart: 18 -> 18, of which waited for: 8 -> 6; matrix products, arithmetic and copies ran while one was open for 8% -> 9% of each run, Pallas kernels for 0% -> 0%
where the time goes in v13:
time: 112 us
  starting transfers between devices  37.6 us (34%)
  waiting for transfers between devices  35.2 us (31%)
  blocking collectives  20.3 us (18%)
  matrix products  8.8 us (8%)
  local copies, waits for them, and re-layouts  7.49 us (7%)
  other arithmetic  1.78 us (2%)
    ppermute x17, starting transfers between devices, shift(): return lax.ppermute(x, axis, [(i, (i + d) % n) for i in range(n)])  26.4 us
    all_to_all x1, blocking collectives, shards(): lax.all_to_all(leaving, 'row', split_axis=3, concat_axis=3, tiled=True)  20.3 us
    ppermute x17, waiting for transfers between devices, shift(): return lax.ppermute(x, axis, [(i, (i + d) % n) for i in range(n)])  19.7 us
    all_to_all x1, waiting for transfers between devices, shards(): lax.all_to_all(step_first, 'row', split_axis=0, concat_axis=0, tiled=True)  15.5 us
    all_to_all x1, starting transfers between devices, shards(): lax.all_to_all(step_first, 'row', split_axis=0, concat_axis=0, tiled=True)  11.2 us
    dot_general x1, matrix products, right_grouped(): jnp.einsum('pcly,cyk->plk', grouped, weight, preferred_element_type=jnp.f...  2.79 us
    dot_general x1, matrix products, shards(): jnp.einsum('ix,ij->xj', left_imag, half_first[:, 1, :], preferred_element...  2.41 us
  transfers between devices with their start and end apart: 18, of which 6 were waited for; matrix products, arithmetic and copies ran while one was open for 9% of the time, Pallas kernels for 0%

profile of v13, /device:TPU:1, one launch (start us, length us, event | category | flops | bytes accessed | tf_op | source)
XLA Modules:
  0.0 111.8 jit_solution(1670199641404253424)
XLA Ops:
  0.0 1.0 fusion.46
  1.2 0.3 copy.56
  1.4 0.3 stack_reshape.6
  1.9 2.1 %collective-permute-start.7 = (bf16[2,1,32,1024]{3,2,0,1:T(8,128)(2,1)S(1)}, bf16[2,1,32,1024]{3,2,0,1:T(8,128)(2,1)S(1)}, u32[]{:S(2)}, u32[]{:S(2)}) collective-permute-start(bf16[2,1,32,1024]{3,2,0,1:T(8,128)(2,1)S(1)} %maximum_bitcast_fusion.7), channel_id=1, source_target_pairs={{0,1},{1,0},{2,3},{3,2},{4,5},{5,4},{6,7},{7,6},{8,9},{9,8},{10,11... | collective-permute-start | bytes 393224 | tf_op jit(solution)/shard_map/ppermute | solution.py:83
  4.0 0.9 slice.114
  5.4 0.9 collective-permute-done.7
  6.4 6.5 %collective-permute-start.8 = (bf16[2,1,2,32,1024]{4,3,0,2,1:T(8,128)(2,1)S(1)}, bf16[2,1,2,32,1024]{4,3,0,2,1:T(8,128)(2,1)S(1)}, u32[]{:S(2)}, u32[]{:S(2)}) collective-permute-start(bf16[2,1,2,32,1024]{4,3,0,2,1:T(8,128)(2,1)S(1)} %pad_maximum_fusion.2), channel_id=1, source_target_pairs={{0,14},{2,0},{4,2},{6,4},{8,6},{10,8},{12,10},{14,12},{1,15},{3,1}... | collective-permute-start | bytes 786440 | tf_op jit(solution)/shard_map/ppermute | solution.py:83
  13.1 3.0 %collective-permute-start.1 = (bf16[2,2,2,32,512]{4,3,1,0,2:T(8,128)(2,1)S(1)}, bf16[2,2,2,32,512]{4,3,1,0,2:T(8,128)(2,1)S(1)}, u32[]{:S(2)}, u32[]{:S(2)}) collective-permute-start(bf16[2,2,2,32,512]{4,3,1,0,2:T(8,128)(2,1)S(1)} %get-tuple-element.31), channel_id=1, source_target_pairs={{0,14},{2,0},{4,2},{6,4},{8,6},{10,8},{12,10},{14,12},{1,15},{3,1}... | collective-permute-start | bytes 786440 | tf_op jit(solution)/shard_map/ppermute | solution.py:83
  16.1 0.3 broadcast_in_dim.69
  16.4 0.2 broadcast_in_dim.61
  16.7 3.1 %collective-permute-start.10 = (bf16[2,1,2,32,1024]{4,3,0,2,1:T(8,128)(2,1)S(1)}, bf16[2,1,2,32,1024]{4,3,0,2,1:T(8,128)(2,1)S(1)}, u32[]{:S(2)}, u32[]{:S(2)}) collective-permute-start(bf16[2,1,2,32,1024]{4,3,0,2,1:T(8,128)(2,1)S(1)} %collective-permute-done.8), channel_id=1, source_target_pairs={{0,14},{2,0},{4,2},{6,4},{8,6},{10,8},{12,10},{14,12},{1,15},{3,1}... | collective-permute-start | bytes 786440 | tf_op jit(solution)/shard_map/ppermute | solution.py:83
  19.8 5.3 %collective-permute-done.2 = bf16[2,2,2,32,512]{4,3,1,0,2:T(8,128)(2,1)S(1)} collective-permute-done((bf16[2,2,2,32,512]{4,3,1,0,2:T(8,128)(2,1)S(1)}, bf16[2,2,2,32,512]{4,3,1,0,2:T(8,128)(2,1)S(1)}, u32[]{:S(2)}, u32[]{:S(2)}) %collective-permute-start.2) | collective-permute-done | bytes 262176 | tf_op jit(solution)/shard_map/ppermute | solution.py:83
  25.2 2.7 %collective-permute-start.3 = (bf16[2,2,2,32,512]{4,3,1,0,2:T(8,128)(2,1)S(1)}, bf16[2,2,2,32,512]{4,3,1,0,2:T(8,128)(2,1)S(1)}, u32[]{:S(2)}, u32[]{:S(2)}) collective-permute-start(bf16[2,2,2,32,512]{4,3,1,0,2:T(8,128)(2,1)S(1)} %collective-permute-done.1), channel_id=1, source_target_pairs={{0,14},{2,0},{4,2},{6,4},{8,6},{10,8},{12,10},{14,12},{1,15},{3,1}... | collective-permute-start | bytes 786440 | tf_op jit(solution)/shard_map/ppermute | solution.py:83
  28.0 3.3 %collective-permute-start.12 = (bf16[2,1,2,32,1024]{4,3,0,2,1:T(8,128)(2,1)S(1)}, bf16[2,1,2,32,1024]{4,3,0,2,1:T(8,128)(2,1)S(1)}, u32[]{:S(2)}, u32[]{:S(2)}) collective-permute-start(bf16[2,1,2,32,1024]{4,3,0,2,1:T(8,128)(2,1)S(1)} %collective-permute-done.10), channel_id=1, source_target_pairs={{0,14},{2,0},{4,2},{6,4},{8,6},{10,8},{12,10},{14,12},{1,15},{3,1}... | collective-permute-start | bytes 786440 | tf_op jit(solution)/shard_map/ppermute | solution.py:83
  31.3 5.1 %collective-permute-done.4 = bf16[2,2,2,32,512]{4,3,1,0,2:T(8,128)(2,1)S(1)} collective-permute-done((bf16[2,2,2,32,512]{4,3,1,0,2:T(8,128)(2,1)S(1)}, bf16[2,2,2,32,512]{4,3,1,0,2:T(8,128)(2,1)S(1)}, u32[]{:S(2)}, u32[]{:S(2)}) %collective-permute-start.4) | collective-permute-done | bytes 262176 | tf_op jit(solution)/shard_map/ppermute | solution.py:83
  36.4 2.7 %collective-permute-start.5 = (bf16[2,2,2,32,512]{4,3,1,0,2:T(8,128)(2,1)S(1)}, bf16[2,2,2,32,512]{4,3,1,0,2:T(8,128)(2,1)S(1)}, u32[]{:S(2)}, u32[]{:S(2)}) collective-permute-start(bf16[2,2,2,32,512]{4,3,1,0,2:T(8,128)(2,1)S(1)} %collective-permute-done.3), channel_id=1, source_target_pairs={{0,14},{2,0},{4,2},{6,4},{8,6},{10,8},{12,10},{14,12},{1,15},{3,1}... | collective-permute-start | bytes 786440 | tf_op jit(solution)/shard_map/ppermute | solution.py:83
  39.2 2.8 %collective-permute-done.13 = bf16[2,1,2,32,1024]{4,3,0,2,1:T(8,128)(2,1)S(1)} collective-permute-done((bf16[2,1,2,32,1024]{4,3,0,2,1:T(8,128)(2,1)S(1)}, bf16[2,1,2,32,1024]{4,3,0,2,1:T(8,128)(2,1)S(1)}, u32[]{:S(2)}, u32[]{:S(2)}) %collective-permute-start.13) | collective-permute-done | bytes 262176 | tf_op jit(solution)/shard_map/ppermute | solution.py:83
  42.2 2.7 %collective-permute-start.15 = (bf16[2,1,2,16,1024]{4,3,0,2,1:T(8,128)(2,1)S(1)}, bf16[2,1,2,16,1024]{4,3,0,2,1:T(8,128)(2,1)S(1)}, u32[]{:S(2)}, u32[]{:S(2)}) collective-permute-start(bf16[2,1,2,16,1024]{4,3,0,2,1:T(8,128)(2,1)S(1)} %slice.118), channel_id=1, source_target_pairs={{0,14},{2,0},{4,2},{6,4},{8,6},{10,8},{12,10},{14,12},{1,15},{3,1}... | collective-permute-start | bytes 393224 | tf_op jit(solution)/shard_map/ppermute | solution.py:83
  44.9 5.5 %collective-permute-done.14 = bf16[2,1,2,16,1024]{4,3,0,2,1:T(8,128)(2,1)S(1)} collective-permute-done((bf16[2,1,2,16,1024]{4,3,0,2,1:T(8,128)(2,1)S(1)}, bf16[2,1,2,16,1024]{4,3,0,2,1:T(8,128)(2,1)S(1)}, u32[]{:S(2)}, u32[]{:S(2)}) %collective-permute-start.14) | collective-permute-done | bytes 131104 | tf_op jit(solution)/shard_map/ppermute | solution.py:83
  50.5 0.3 fusion.42
  50.7 0.8 fusion.45
  51.7 1.3 %fusion.9 = bf16[1024,512]{1,0:T(8,128)(2,1)S(1)} fusion(bf16[512,1024]{1,0:T(8,128)(2,1)S(1)} %bitcast.126, bf16[512,512]{1,0:T(8,128)(2,1)S(1)} %get-tuple-element.22, bf16[512,512]{1,0:T(8,128)(2,1)S(1)} %get-tuple-element.21, bf16[512,1024]{1,0:T(8,128)(2,1)S(1)} %bitcast.117), kind=kOutput, calls=%fused_computation.13 | convolution fusion | flops 1080557568 | bytes 4194304 | tf_op jit(solution)/shard_map/dot_general | solution.py:141
  53.0 0.8 fusion.29
  53.8 2.4 %add_convert_fusion.1 = bf16[1024,512]{1,0:T(8,128)(2,1)} fusion(f32[1024,512]{1,0:T(8,128)S(1)} %fusion.29, bf16[512,32]{1,0:T(8,128)(2,1)S(1)} %get-tuple-element.18, bf16[512,992]{1,0:T(8,128)(2,1)S(1)} %get-tuple-element.20, bf16[512,992]{1,0:T(8,128)(2,1)S(1)} %get-tuple-element.19, bf16[512,32]{1,0:T(8,128)(2,1)S(1)} %get-tuple-element.17, ...), kind=kOutput, calls=%fused_computation.12 | convolution fusion | flops 543162368 | bytes 6030336 | tf_op jit(solution)/shard_map/ix,ij->xj/dot_general | solution.py:148
  56.3 11.2 %all-to-all-start = ((bf16[16,2,32,512]{3,2,1,0:T(8,128)(2,1)}), bf16[16,2,32,512]{3,2,1,0:T(8,128)(2,1)}, u32[]{:S(2)}, u32[]{:S(2)}) async-start(bf16[16,2,32,512]{3,2,1,0:T(8,128)(2,1)} %bitcast.33), calls=%async_computation | async-start | bytes 2097152 | tf_op jit(solution)/shard_map/all_to_all | solution.py:153
  67.9 1.3 %maximum_bitcast_fusion.4 = (bf16[1,512,1024]{2,1,0:T(8,128)(2,1)S(1)}, bf16[1,512,1024]{2,1,0:T(8,128)(2,1)}) fusion(bf16[512,512]{1,0:T(8,128)(2,1)S(1)} %bitcast.114, bf16[512,512]{1,0:T(8,128)(2,1)S(1)} %bitcast.120, bf16[512,512]{1,0:T(8,128)(2,1)S(1)} %bitcast_negate_fusion), kind=kLoop, calls=%fused_computation.25 | loop fusion | flops 4194304 | bytes 3670016 | tf_op jit(solution)/shard_map/stack | solution.py:47
  69.2 15.5 %all-to-all-done = bf16[16,2,32,512]{3,2,1,0:T(8,128)(2,1)} async-done(((bf16[16,2,32,512]{3,2,1,0:T(8,128)(2,1)}), bf16[16,2,32,512]{3,2,1,0:T(8,128)(2,1)}, u32[]{:S(2)}, u32[]{:S(2)}) %all-to-all-start) | async-done | bytes 1048608 | tf_op jit(solution)/shard_map/all_to_all | solution.py:153
  84.7 2.8 %bitcast_convert_fusion = bf16[16,32,1024]{2,1,0:T(8,128)(2,1)S(1)} fusion(bf16[16,2,32,512]{3,2,1,0:T(8,128)(2,1)} %all-to-all-done, bf16[1,512,1024]{2,1,0:T(8,128)(2,1)} %get-tuple-element.24, bf16[1,512,1024]{2,1,0:T(8,128)(2,1)S(1)} %get-tuple-element.23), kind=kOutput, calls=%fused_computation.10 | convolution fusion | flops 1075314688 | bytes 4194304 | tf_op jit(solution)/shard_map/pcly,cyk->plk/dot_general | solution.py:48
  87.5 0.8 fusion.19
  88.3 0.8 add_convert_fusion
  89.2 20.3 %all_to_all.10 = bf16[1,512,2,16,32]{1,4,2,0,3:T(8,128)(2,1)S(1)} all-to-all(bf16[1,512,2,16,32]{1,4,2,0,3:T(8,128)(2,1)S(1)} %pad_maximum_fusion), channel_id=1, replica_groups=mesh['row'=16,'cz'=8,'cx'=2] {'row'}, dimensions={3} | all-to-all | bytes 2097152 | tf_op jit(solution)/shard_map/all_to_all | solution.py:159
  109.7 2.1 %copy.44 = bf16[1,1,1,512,2,512]{5,4,3,2,1,0:T(2,128)(2,1)} copy(bf16[1,1,1,512,2,512]{3,5,4,2,1,0:T(8,128)(2,1)S(1)} %bitcast.115) | data formatting | bytes 2097152 | tf_op jit(solution)/shard_map/reshape | solution.py:160
  (61 shorter events, 2.2 us)
Async XLA Ops:
  0.0 5.1 %copy-start = (bf16[1,1,1,512,2,512]{5,4,3,2,1,0:T(2,128)(2,1)S(1)}, bf16[1,1,1,512,2,512]{5,4,3,2,1,0:T(2,128)(2,1)}, u32[]{:S(2)}) copy-start(bf16[1,1,1,512,2,512]{5,4,3,2,1,0:T(2,128)(2,1)} %param.2) | copy-start | bytes 3145732
  1.7 11.2 %copy-start.1 = (bf16[1,4,2,512,32]{3,4,2,1,0:T(8,128)(2,1)S(1)}, bf16[1,4,2,512,32]{3,4,2,1,0:T(8,128)(2,1)}, u32[]{:S(2)}) copy-start(bf16[1,4,2,512,32]{3,4,2,1,0:T(8,128)(2,1)} %param.3) | copy-start | bytes 786436
  1.9 4.5 %collective-permute-start.7 = (bf16[2,1,32,1024]{3,2,0,1:T(8,128)(2,1)S(1)}, bf16[2,1,32,1024]{3,2,0,1:T(8,128)(2,1)S(1)}, u32[]{:S(2)}, u32[]{:S(2)}) collective-permute-start(bf16[2,1,32,1024]{3,2,0,1:T(8,128)(2,1)S(1)} %maximum_bitcast_fusion.7), channel_id=1, source_target_pairs={{0,1},{1,0},{2,3},{3,2},{4,5},{5,4},{6,7},{7,6},{8,9},{9,8},{10,11... | collective-permute-start | bytes 393224 | tf_op jit(solution)/shard_map/ppermute | solution.py:83
  4.9 8.0 %collective-permute-start = (bf16[2,2,32,512]{3,2,1,0:T(8,128)(2,1)S(1)}, bf16[2,2,32,512]{3,2,1,0:T(8,128)(2,1)S(1)}, u32[]{:S(2)}, u32[]{:S(2)}) collective-permute-start(bf16[2,2,32,512]{3,2,1,0:T(8,128)(2,1)S(1)} %slice.114), channel_id=1, source_target_pairs={{0,1},{1,0},{2,3},{3,2},{4,5},{5,4},{6,7},{7,6},{8,9},{9,8},{10,11... | collective-permute-start | bytes 393224 | tf_op jit(solution)/shard_map/ppermute | solution.py:83
  6.4 10.3 %collective-permute-start.8 = (bf16[2,1,2,32,1024]{4,3,0,2,1:T(8,128)(2,1)S(1)}, bf16[2,1,2,32,1024]{4,3,0,2,1:T(8,128)(2,1)S(1)}, u32[]{:S(2)}, u32[]{:S(2)}) collective-permute-start(bf16[2,1,2,32,1024]{4,3,0,2,1:T(8,128)(2,1)S(1)} %pad_maximum_fusion.2), channel_id=1, source_target_pairs={{0,14},{2,0},{4,2},{6,4},{8,6},{10,8},{12,10},{14,12},{1,15},{3,1}... | collective-permute-start | bytes 786440 | tf_op jit(solution)/shard_map/ppermute | solution.py:83
  12.9 7.0 %collective-permute-start.9 = (bf16[2,1,2,32,1024]{4,3,0,2,1:T(8,128)(2,1)S(1)}, bf16[2,1,2,32,1024]{4,3,0,2,1:T(8,128)(2,1)S(1)}, u32[]{:S(2)}, u32[]{:S(2)}) collective-permute-start(bf16[2,1,2,32,1024]{4,3,0,2,1:T(8,128)(2,1)S(1)} %pad_maximum_fusion.2), channel_id=1, source_target_pairs={{0,2},{2,4},{4,6},{6,8},{8,10},{10,12},{12,14},{14,0},{1,3},{3,5},... | collective-permute-start | bytes 786440 | tf_op jit(solution)/shard_map/ppermute | solution.py:83
  13.0 12.2 %collective-permute-start.2 = (bf16[2,2,2,32,512]{4,3,1,0,2:T(8,128)(2,1)S(1)}, bf16[2,2,2,32,512]{4,3,1,0,2:T(8,128)(2,1)S(1)}, u32[]{:S(2)}, u32[]{:S(2)}) collective-permute-start(bf16[2,2,2,32,512]{4,3,1,0,2:T(8,128)(2,1)S(1)} %get-tuple-element.31), channel_id=1, source_target_pairs={{0,2},{2,4},{4,6},{6,8},{8,10},{10,12},{12,14},{14,0},{1,3},{3,5},... | collective-permute-start | bytes 786440 | tf_op jit(solution)/shard_map/ppermute | solution.py:83
  13.1 12.1 %collective-permute-start.1 = (bf16[2,2,2,32,512]{4,3,1,0,2:T(8,128)(2,1)S(1)}, bf16[2,2,2,32,512]{4,3,1,0,2:T(8,128)(2,1)S(1)}, u32[]{:S(2)}, u32[]{:S(2)}) collective-permute-start(bf16[2,2,2,32,512]{4,3,1,0,2:T(8,128)(2,1)S(1)} %get-tuple-element.31), channel_id=1, source_target_pairs={{0,14},{2,0},{4,2},{6,4},{8,6},{10,8},{12,10},{14,12},{1,15},{3,1}... | collective-permute-start | bytes 786440 | tf_op jit(solution)/shard_map/ppermute | solution.py:83
  16.7 11.3 %collective-permute-start.10 = (bf16[2,1,2,32,1024]{4,3,0,2,1:T(8,128)(2,1)S(1)}, bf16[2,1,2,32,1024]{4,3,0,2,1:T(8,128)(2,1)S(1)}, u32[]{:S(2)}, u32[]{:S(2)}) collective-permute-start(bf16[2,1,2,32,1024]{4,3,0,2,1:T(8,128)(2,1)S(1)} %collective-permute-done.8), channel_id=1, source_target_pairs={{0,14},{2,0},{4,2},{6,4},{8,6},{10,8},{12,10},{14,12},{1,15},{3,1}... | collective-permute-start | bytes 786440 | tf_op jit(solution)/shard_map/ppermute | solution.py:83
  19.8 11.4 %collective-permute-start.11 = (bf16[2,1,2,32,1024]{4,3,0,2,1:T(8,128)(2,1)S(1)}, bf16[2,1,2,32,1024]{4,3,0,2,1:T(8,128)(2,1)S(1)}, u32[]{:S(2)}, u32[]{:S(2)}) collective-permute-start(bf16[2,1,2,32,1024]{4,3,0,2,1:T(8,128)(2,1)S(1)} %collective-permute-done.9), channel_id=1, source_target_pairs={{0,2},{2,4},{4,6},{6,8},{8,10},{10,12},{12,14},{14,0},{1,3},{3,5},... | collective-permute-start | bytes 786440 | tf_op jit(solution)/shard_map/ppermute | solution.py:83
  25.2 11.2 %collective-permute-start.4 = (bf16[2,2,2,32,512]{4,3,1,0,2:T(8,128)(2,1)S(1)}, bf16[2,2,2,32,512]{4,3,1,0,2:T(8,128)(2,1)S(1)}, u32[]{:S(2)}, u32[]{:S(2)}) collective-permute-start(bf16[2,2,2,32,512]{4,3,1,0,2:T(8,128)(2,1)S(1)} %collective-permute-done.2), channel_id=1, source_target_pairs={{0,2},{2,4},{4,6},{6,8},{8,10},{10,12},{12,14},{14,0},{1,3},{3,5},... | collective-permute-start | bytes 786440 | tf_op jit(solution)/shard_map/ppermute | solution.py:83
  25.2 11.2 %collective-permute-start.3 = (bf16[2,2,2,32,512]{4,3,1,0,2:T(8,128)(2,1)S(1)}, bf16[2,2,2,32,512]{4,3,1,0,2:T(8,128)(2,1)S(1)}, u32[]{:S(2)}, u32[]{:S(2)}) collective-permute-start(bf16[2,2,2,32,512]{4,3,1,0,2:T(8,128)(2,1)S(1)} %collective-permute-done.1), channel_id=1, source_target_pairs={{0,14},{2,0},{4,2},{6,4},{8,6},{10,8},{12,10},{14,12},{1,15},{3,1}... | collective-permute-start | bytes 786440 | tf_op jit(solution)/shard_map/ppermute | solution.py:83
  28.0 14.1 %collective-permute-start.12 = (bf16[2,1,2,32,1024]{4,3,0,2,1:T(8,128)(2,1)S(1)}, bf16[2,1,2,32,1024]{4,3,0,2,1:T(8,128)(2,1)S(1)}, u32[]{:S(2)}, u32[]{:S(2)}) collective-permute-start(bf16[2,1,2,32,1024]{4,3,0,2,1:T(8,128)(2,1)S(1)} %collective-permute-done.10), channel_id=1, source_target_pairs={{0,14},{2,0},{4,2},{6,4},{8,6},{10,8},{12,10},{14,12},{1,15},{3,1}... | collective-permute-start | bytes 786440 | tf_op jit(solution)/shard_map/ppermute | solution.py:83
  31.3 10.8 %collective-permute-start.13 = (bf16[2,1,2,32,1024]{4,3,0,2,1:T(8,128)(2,1)S(1)}, bf16[2,1,2,32,1024]{4,3,0,2,1:T(8,128)(2,1)S(1)}, u32[]{:S(2)}, u32[]{:S(2)}) collective-permute-start(bf16[2,1,2,32,1024]{4,3,0,2,1:T(8,128)(2,1)S(1)} %collective-permute-done.11), channel_id=1, source_target_pairs={{0,2},{2,4},{4,6},{6,8},{8,10},{10,12},{12,14},{14,0},{1,3},{3,5},... | collective-permute-start | bytes 786440 | tf_op jit(solution)/shard_map/ppermute | solution.py:83
  36.4 19.8 %collective-permute-start.6 = (bf16[2,2,2,32,512]{4,3,1,0,2:T(8,128)(2,1)S(1)}, bf16[2,2,2,32,512]{4,3,1,0,2:T(8,128)(2,1)S(1)}, u32[]{:S(2)}, u32[]{:S(2)}) collective-permute-start(bf16[2,2,2,32,512]{4,3,1,0,2:T(8,128)(2,1)S(1)} %collective-permute-done.4), channel_id=1, source_target_pairs={{0,2},{2,4},{4,6},{6,8},{8,10},{10,12},{12,14},{14,0},{1,3},{3,5},... | collective-permute-start | bytes 786440 | tf_op jit(solution)/shard_map/ppermute | solution.py:83
  36.4 19.8 %collective-permute-start.5 = (bf16[2,2,2,32,512]{4,3,1,0,2:T(8,128)(2,1)S(1)}, bf16[2,2,2,32,512]{4,3,1,0,2:T(8,128)(2,1)S(1)}, u32[]{:S(2)}, u32[]{:S(2)}) collective-permute-start(bf16[2,2,2,32,512]{4,3,1,0,2:T(8,128)(2,1)S(1)} %collective-permute-done.3), channel_id=1, source_target_pairs={{0,14},{2,0},{4,2},{6,4},{8,6},{10,8},{12,10},{14,12},{1,15},{3,1}... | collective-permute-start | bytes 786440 | tf_op jit(solution)/shard_map/ppermute | solution.py:83
  42.0 8.4 %collective-permute-start.14 = (bf16[2,1,2,16,1024]{4,3,0,2,1:T(8,128)(2,1)S(1)}, bf16[2,1,2,16,1024]{4,3,0,2,1:T(8,128)(2,1)S(1)}, u32[]{:S(2)}, u32[]{:S(2)}) collective-permute-start(bf16[2,1,2,16,1024]{4,3,0,2,1:T(8,128)(2,1)S(1)} %slice.117), channel_id=1, source_target_pairs={{0,2},{2,4},{4,6},{6,8},{8,10},{10,12},{12,14},{14,0},{1,3},{3,5},... | collective-permute-start | bytes 393224 | tf_op jit(solution)/shard_map/ppermute | solution.py:83
  42.2 8.3 %collective-permute-start.15 = (bf16[2,1,2,16,1024]{4,3,0,2,1:T(8,128)(2,1)S(1)}, bf16[2,1,2,16,1024]{4,3,0,2,1:T(8,128)(2,1)S(1)}, u32[]{:S(2)}, u32[]{:S(2)}) collective-permute-start(bf16[2,1,2,16,1024]{4,3,0,2,1:T(8,128)(2,1)S(1)} %slice.118), channel_id=1, source_target_pairs={{0,14},{2,0},{4,2},{6,4},{8,6},{10,8},{12,10},{14,12},{1,15},{3,1}... | collective-permute-start | bytes 393224 | tf_op jit(solution)/shard_map/ppermute | solution.py:83
  56.2 11.3 %collective-permute-start.16 = (bf16[2,2,2,32,512]{4,3,1,0,2:T(8,128)(2,1)S(1)}, bf16[2,2,2,32,512]{4,3,1,0,2:T(8,128)(2,1)S(1)}, u32[]{:S(2)}, u32[]{:S(2)}) collective-permute-start(bf16[2,2,2,32,512]{4,3,1,0,2:T(8,128)(2,1)S(1)} %collective-permute-done.6), channel_id=1, source_target_pairs={{0,2},{2,4},{4,6},{6,8},{8,10},{10,12},{12,14},{14,0},{1,3},{3,5},... | collective-permute-start | bytes 786440 | tf_op jit(solution)/shard_map/ppermute | solution.py:83
  56.3 28.4 %all-to-all-start = ((bf16[16,2,32,512]{3,2,1,0:T(8,128)(2,1)}), bf16[16,2,32,512]{3,2,1,0:T(8,128)(2,1)}, u32[]{:S(2)}, u32[]{:S(2)}) async-start(bf16[16,2,32,512]{3,2,1,0:T(8,128)(2,1)} %bitcast.33), calls=%async_computation | async-start | bytes 2097152 | tf_op jit(solution)/shard_map/all_to_all | solution.py:153

commit v14 on v11

--- a/solution.py
+++ b/solution.py
@@ -81,8 +81,16 @@
     first = jnp.where(x == 0, t, other)
     second = jnp.where(x == 0, other, t)
     pair = jnp.stack([first, second], axis=2)
+    pieces = {0: pair}
     buf = jnp.zeros((nb, comps, nz, nx, width, cols), t.dtype)
-    buf = lax.dynamic_update_slice(buf, pair[:, :, None], (0, 0, z, 0, 0, 0))
+
+    def put(buf, piece, offset):
+        if hold is not None:
+            pieces[offset % nz] = piece
+            return buf
+        return lax.dynamic_update_slice(buf, piece[:, :, None], (0, 0, (z + offset) % nz, 0, 0, 0))
+
+    buf = put(buf, pair, 0)
     forward = nz // 2
     backward = nz - 1 - forward
     cur_f = pair
@@ -91,21 +99,23 @@
         if k == forward and nz % 2 == 0 and width % 2 == 0:
             half = width // 2
             if hold is not None:
-                piece = shift(cur_f, "cz", nz, 1)
-                buf = lax.dynamic_update_slice(buf, piece[:, :, None], (0, 0, (z - k) % nz, 0, 0, 0))
+                buf = put(buf, shift(cur_f, "cz", nz, 1), -k)
                 break
             a = shift(cur_f[:, :, :, :half], "cz", nz, 1)
             b = shift(cur_b[:, :, :, half:], "cz", nz, -1)
-            piece = jnp.concatenate([a, b], axis=3)
-            buf = lax.dynamic_update_slice(buf, piece[:, :, None], (0, 0, (z - k) % nz, 0, 0, 0))
+            buf = put(buf, jnp.concatenate([a, b], axis=3), -k)
             break
         if k <= backward:
             cur_b = shift(cur_b, "cz", nz, -1)
-            buf = lax.dynamic_update_slice(buf, cur_b[:, :, None], (0, 0, (z + k) % nz, 0, 0, 0))
+            buf = put(buf, cur_b, k)
         if hold is not None and k == forward - 1:
             cur_f, hold = lax.optimization_barrier((cur_f, hold))
         cur_f = shift(cur_f, "cz", nz, 1)
-        buf = lax.dynamic_update_slice(buf, cur_f[:, :, None], (0, 0, (z - k) % nz, 0, 0, 0))
+        buf = put(buf, cur_f, -k)
+    if hold is not None:
+        relative = jnp.stack([pieces[o] for o in range(nz)], axis=2)
+        twice = jnp.concatenate([relative, relative], axis=2)
+        buf = lax.dynamic_slice_in_dim(twice, (nz - z) % nz, nz, axis=2)
     return buf.reshape(nb, comps, nz * nx * width, cols), hold
 
 

time: 109 us -> 116 us (1.064)
  local copies, waits for them, and re-layouts: 12.1 us -> 19 us
  waiting for transfers between devices: 31.5 us -> 26.1 us
  other arithmetic: 0.56 us -> 3.62 us
  starting transfers between devices: 38 us -> 40.9 us
    unnamed x9 -> x20, local copies, waits for them, and re-layouts: 2.65 us -> 11.6 us
    ppermute x17, waiting for transfers between devices: 26.2 us -> 22 us  [shift(): return lax.ppermute(x, axis, [(i, (i + d) % n) for i in range(n)])]
    all_to_all x1, starting transfers between devices: 9.51 us -> 12.8 us  [shards(): lax.all_to_all(outgoing, 'row', split_axis=1, concat_axis=1, tiled=True)]
    dynamic_update_slice x13 -> x6, local copies, waits for them, and re-layouts: 2.19 us -> 0.13 us  [put(): lax.dynamic_update_slice(buf, piece[:, :, None], (0, 0, (z + offset) % nz...]
    unnamed x0 -> x2, other arithmetic: none -> 1.46 us
    slice x1, local copies, waits for them, and re-layouts: 1.27 us -> 0.08 us  [right_planar(): planar[1]]
    all_to_all x1, waiting for transfers between devices: 5.28 us -> 4.09 us  [shards(): lax.all_to_all(outgoing, 'row', split_axis=1, concat_axis=1, tiled=True)]
  transfers between devices with their start and end apart: 18 -> 18, of which waited for: 9 -> 7; matrix products, arithmetic and copies ran while one was open for 9% -> 18% of each run, Pallas kernels for 0% -> 0%
where the time goes in v14:
time: 116 us
  starting transfers between devices  40.9 us (35%)
  waiting for transfers between devices  26.1 us (22%)
  blocking collectives  20.3 us (18%)
  local copies, waits for them, and re-layouts  19 us (16%)
  matrix products  5.78 us (5%)
  other arithmetic  3.62 us (3%)
    ppermute x17, starting transfers between devices, shift(): return lax.ppermute(x, axis, [(i, (i + d) % n) for i in range(n)])  28 us
    ppermute x17, waiting for transfers between devices, shift(): return lax.ppermute(x, axis, [(i, (i + d) % n) for i in range(n)])  22 us
    all_to_all x1, blocking collectives, shards(): lax.all_to_all(leaving, 'row', split_axis=3, concat_axis=3, tiled=True)  20.3 us
    all_to_all x1, starting transfers between devices, shards(): lax.all_to_all(outgoing, 'row', split_axis=1, concat_axis=1, tiled=True)  12.8 us
    unnamed x20, local copies, waits for them, and re-layouts  11.6 us
    all_to_all x1, waiting for transfers between devices, shards(): lax.all_to_all(outgoing, 'row', split_axis=1, concat_axis=1, tiled=True)  4.09 us
  transfers between devices with their start and end apart: 18, of which 7 were waited for; matrix products, arithmetic and copies ran while one was open for 18% of the time, Pallas kernels for 0%

profile of v14, /device:TPU:1, one launch (start us, length us, event | category | flops | bytes accessed | tf_op | source)
XLA Modules:
  0.0 116.0 jit_solution(14200531149156587429)
XLA Ops:
  0.0 1.0 slice.111
  1.0 2.1 %collective-permute-start.6 = (bf16[2,2,32,512]{3,2,1,0:T(8,128)(2,1)S(1)}, bf16[2,2,32,512]{3,2,1,0:T(8,128)(2,1)S(1)}, u32[]{:S(2)}, u32[]{:S(2)}) collective-permute-start(bf16[2,2,32,512]{3,2,1,0:T(8,128)(2,1)S(1)} %slice.111), channel_id=1, source_target_pairs={{0,1},{1,0},{2,3},{3,2},{4,5},{5,4},{6,7},{7,6},{8,9},{9,8},{10,11... | collective-permute-start | bytes 393224 | tf_op jit(solution)/shard_map/ppermute | solution.py:71
  3.1 1.5 %copy.14 = bf16[64,8,2,512]{3,1,2,0:T(8,128)(2,1)S(1)} copy(bf16[64,8,2,512]{3,2,1,0:T(2,128)(2,1)} %bitcast.107) | data formatting | bytes 2097152
  4.6 0.8 collective-permute-done.6
  5.5 1.9 %collective-permute-start = (bf16[2,2,32,512]{3,2,1,0:T(8,128)(2,1)S(1)}, bf16[2,2,32,512]{3,2,1,0:T(8,128)(2,1)S(1)}, u32[]{:S(2)}, u32[]{:S(2)}) collective-permute-start(bf16[2,2,32,512]{3,2,1,0:T(8,128)(2,1)S(1)} %get-tuple-element.25), channel_id=1, source_target_pairs={{0,1},{1,0},{2,3},{3,2},{4,5},{5,4},{6,7},{7,6},{8,9},{9,8},{10,11... | collective-permute-start | bytes 393224 | tf_op jit(solution)/shard_map/ppermute | solution.py:71
  7.4 5.9 %collective-permute-start.7 = (bf16[2,2,2,32,512]{4,3,1,0,2:T(8,128)(2,1)S(1)}, bf16[2,2,2,32,512]{4,3,1,0,2:T(8,128)(2,1)S(1)}, u32[]{:S(2)}, u32[]{:S(2)}) collective-permute-start(bf16[2,2,2,32,512]{4,3,1,0,2:T(8,128)(2,1)S(1)} %pad_maximum_fusion.2), channel_id=1, source_target_pairs={{0,14},{2,0},{4,2},{6,4},{8,6},{10,8},{12,10},{14,12},{1,15},{3,1}... | collective-permute-start | bytes 786440 | tf_op jit(solution)/shard_map/ppermute | solution.py:71
  13.7 2.7 %collective-permute-start.1 = (bf16[2,2,2,32,512]{4,3,1,0,2:T(8,128)(2,1)S(1)}, bf16[2,2,2,32,512]{4,3,1,0,2:T(8,128)(2,1)S(1)}, u32[]{:S(2)}, u32[]{:S(2)}) collective-permute-start(bf16[2,2,2,32,512]{4,3,1,0,2:T(8,128)(2,1)S(1)} %pad_maximum_fusion.1), channel_id=1, source_target_pairs={{0,14},{2,0},{4,2},{6,4},{8,6},{10,8},{12,10},{14,12},{1,15},{3,1}... | collective-permute-start | bytes 786440 | tf_op jit(solution)/shard_map/ppermute | solution.py:71
  17.1 3.4 %collective-permute-start.9 = (bf16[2,2,2,32,512]{4,3,1,0,2:T(8,128)(2,1)S(1)}, bf16[2,2,2,32,512]{4,3,1,0,2:T(8,128)(2,1)S(1)}, u32[]{:S(2)}, u32[]{:S(2)}) collective-permute-start(bf16[2,2,2,32,512]{4,3,1,0,2:T(8,128)(2,1)S(1)} %collective-permute-done.7), channel_id=1, source_target_pairs={{0,14},{2,0},{4,2},{6,4},{8,6},{10,8},{12,10},{14,12},{1,15},{3,1}... | collective-permute-start | bytes 786440 | tf_op jit(solution)/shard_map/ppermute | solution.py:71
  20.6 5.3 %collective-permute-done.4 = bf16[2,2,2,32,512]{4,3,1,0,2:T(8,128)(2,1)S(1)} collective-permute-done((bf16[2,2,2,32,512]{4,3,1,0,2:T(8,128)(2,1)S(1)}, bf16[2,2,2,32,512]{4,3,1,0,2:T(8,128)(2,1)S(1)}, u32[]{:S(2)}, u32[]{:S(2)}) %collective-permute-start.4) | collective-permute-done | bytes 262176 | tf_op jit(solution)/shard_map/ppermute | solution.py:71
  25.9 2.7 %collective-permute-start.2 = (bf16[2,2,2,32,512]{4,3,1,0,2:T(8,128)(2,1)S(1)}, bf16[2,2,2,32,512]{4,3,1,0,2:T(8,128)(2,1)S(1)}, u32[]{:S(2)}, u32[]{:S(2)}) collective-permute-start(bf16[2,2,2,32,512]{4,3,1,0,2:T(8,128)(2,1)S(1)} %collective-permute-done.1), channel_id=1, source_target_pairs={{0,14},{2,0},{4,2},{6,4},{8,6},{10,8},{12,10},{14,12},{1,15},{3,1}... | collective-permute-start | bytes 786440 | tf_op jit(solution)/shard_map/ppermute | solution.py:71
  28.6 3.2 %collective-permute-start.11 = (bf16[2,2,2,32,512]{4,3,1,0,2:T(8,128)(2,1)S(1)}, bf16[2,2,2,32,512]{4,3,1,0,2:T(8,128)(2,1)S(1)}, u32[]{:S(2)}, u32[]{:S(2)}) collective-permute-start(bf16[2,2,2,32,512]{4,3,1,0,2:T(8,128)(2,1)S(1)} %collective-permute-done.9), channel_id=1, source_target_pairs={{0,14},{2,0},{4,2},{6,4},{8,6},{10,8},{12,10},{14,12},{1,15},{3,1}... | collective-permute-start | bytes 786440 | tf_op jit(solution)/shard_map/ppermute | solution.py:71
  31.9 10.9 %collective-permute-done.12 = bf16[2,2,2,32,512]{4,3,1,0,2:T(8,128)(2,1)S(1)} collective-permute-done((bf16[2,2,2,32,512]{4,3,1,0,2:T(8,128)(2,1)S(1)}, bf16[2,2,2,32,512]{4,3,1,0,2:T(8,128)(2,1)S(1)}, u32[]{:S(2)}, u32[]{:S(2)}) %collective-permute-start.12) | collective-permute-done | bytes 262176 | tf_op jit(solution)/shard_map/ppermute | solution.py:71
  42.9 2.9 %collective-permute-start.14 = (bf16[2,2,2,16,512]{4,3,1,0,2:T(8,128)(2,1)S(1)}, bf16[2,2,2,16,512]{4,3,1,0,2:T(8,128)(2,1)S(1)}, u32[]{:S(2)}, u32[]{:S(2)}) collective-permute-start(bf16[2,2,2,16,512]{4,3,1,0,2:T(8,128)(2,1)S(1)} %slice.113), channel_id=1, source_target_pairs={{0,14},{2,0},{4,2},{6,4},{8,6},{10,8},{12,10},{14,12},{1,15},{3,1}... | collective-permute-start | bytes 393224 | tf_op jit(solution)/shard_map/ppermute | solution.py:71
  45.9 2.0 %collective-permute-done.13 = bf16[2,2,2,16,512]{4,3,1,0,2:T(8,128)(2,1)S(1)} collective-permute-done((bf16[2,2,2,16,512]{4,3,1,0,2:T(8,128)(2,1)S(1)}, bf16[2,2,2,16,512]{4,3,1,0,2:T(8,128)(2,1)S(1)}, u32[]{:S(2)}, u32[]{:S(2)}) %collective-permute-start.13) | collective-permute-done | bytes 131104 | tf_op jit(solution)/shard_map/ppermute | solution.py:71
  48.3 1.3 %fusion.8 = bf16[1024,512]{1,0:T(8,128)(2,1)S(1)} fusion(bf16[512,1024]{1,0:T(8,128)(2,1)S(1)} %bitcast.108, bf16[512,512]{1,0:T(8,128)(2,1)S(1)} %bitcast.112, bf16[512,512]{1,0:T(8,128)(2,1)S(1)} %get-tuple-element.26, bf16[512,512]{1,0:T(8,128)(2,1)S(1)} %bitcast.106), kind=kOutput, calls=%fused_computation.11 | convolution fusion | flops 1082654720 | bytes 3670016 | tf_op jit(solution)/shard_map/dot_general | solution.py:15
  49.6 0.8 fusion.11
  50.4 0.8 add_convert_fusion.2
  52.0 2.9 %collective-permute-start.3 = (bf16[2,2,2,32,512]{4,3,1,0,2:T(8,128)(2,1)S(1)}, bf16[2,2,2,32,512]{4,3,1,0,2:T(8,128)(2,1)S(1)}, u32[]{:S(2)}, u32[]{:S(2)}) collective-permute-start(bf16[2,2,2,32,512]{4,3,1,0,2:T(8,128)(2,1)S(1)} %collective-permute-done.2), channel_id=1, source_target_pairs={{0,14},{2,0},{4,2},{6,4},{8,6},{10,8},{12,10},{14,12},{1,15},{3,1}... | collective-permute-start | bytes 786440 | tf_op jit(solution)/shard_map/ppermute | solution.py:71
  55.6 2.3 %collective-permute-done.15 = bf16[2,2,2,32,512]{4,3,1,0,2:T(8,128)(2,1)S(1)} collective-permute-done((bf16[2,2,2,32,512]{4,3,1,0,2:T(8,128)(2,1)S(1)}, bf16[2,2,2,32,512]{4,3,1,0,2:T(8,128)(2,1)S(1)}, u32[]{:S(2)}, u32[]{:S(2)}) %collective-permute-start.15) | collective-permute-done | bytes 262176 | tf_op jit(solution)/shard_map/ppermute | solution.py:71
  58.7 1.0 copy.9
  59.7 12.8 %all-to-all-start = ((bf16[2,16,32,512]{3,2,0,1:T(8,128)(2,1)}), bf16[2,16,32,512]{3,2,0,1:T(8,128)(2,1)S(1)}, u32[]{:S(2)}, u32[]{:S(2)}) async-start(bf16[2,16,32,512]{3,2,0,1:T(8,128)(2,1)} %copy.9), calls=%async_computation | async-start | bytes 2097152 | tf_op jit(solution)/shard_map/all_to_all | solution.py:135
  74.8 0.8 bitcast_dynamic-update-slice_fusion.2
  77.7 0.8 bitcast_dynamic-update-slice_fusion.18
  79.9 0.7 bitcast_dynamic-update-slice_fusion.5
  82.1 1.7 %constant_dynamic-slice_fusion = (bf16[1,1,8,2,32,512]{5,4,1,0,3,2:T(8,128)(2,1)S(1)}, bf16[1,1,8,2,32,512]{5,4,1,0,3,2:T(8,128)(2,1)S(1)}, bf16[1,1,8,2,32,512]...) fusion(bf16[2,2,16,2,32,512]{5,4,1,0,3,2:T(8,128)(2,1)} %bitcast_dynamic-update-slice_fusion.1, s32[]{:T(128)S(6)} %add.113, ...), kind=kLoop, calls=%fused_computation.69 | loop fusion | bytes 4194312 | tf_op jit(solution)/shard_map/slice | solution.py:20
  83.8 0.9 bitcast_negate_fusion
  84.6 0.9 bitcast_negate_fusion.1
  85.5 4.1 %all-to-all-done = bf16[2,16,32,512]{3,2,0,1:T(8,128)(2,1)S(1)} async-done(((bf16[2,16,32,512]{3,2,0,1:T(8,128)(2,1)}), bf16[2,16,32,512]{3,2,0,1:T(8,128)(2,1)S(1)}, u32[]{:S(2)}, u32[]{:S(2)}) %all-to-all-start) | async-done | bytes 1048608 | tf_op jit(solution)/shard_map/all_to_all | solution.py:135
  91.5 0.8 fusion.18
  92.5 0.8 add_convert_fusion
  93.5 20.3 %all_to_all.10 = bf16[1,512,2,16,32]{1,4,2,0,3:T(8,128)(2,1)S(1)} all-to-all(bf16[1,512,2,16,32]{1,4,2,0,3:T(8,128)(2,1)S(1)} %pad_maximum_fusion), channel_id=1, replica_groups=mesh['row'=16,'cz'=8,'cx'=2] {'row'}, dimensions={3} | all-to-all | bytes 2097152 | tf_op jit(solution)/shard_map/all_to_all | solution.py:142
  113.9 2.1 %copy.13 = bf16[1,1,1,512,2,512]{5,4,3,2,1,0:T(2,128)(2,1)} copy(bf16[1,1,1,512,2,512]{3,5,4,2,1,0:T(8,128)(2,1)S(1)} %bitcast.94) | data formatting | bytes 2097152 | tf_op jit(solution)/shard_map/reshape | solution.py:143
  (62 shorter events, 13.7 us)
Async XLA Ops:
  0.0 5.5 %copy-start.2 = (bf16[1,4,2,512,32]{3,4,2,1,0:T(8,128)(2,1)S(1)}, bf16[1,4,2,512,32]{3,4,2,1,0:T(8,128)(2,1)}, u32[]{:S(2)}) copy-start(bf16[1,4,2,512,32]{3,4,2,1,0:T(8,128)(2,1)} %param.3) | copy-start | bytes 786436
  1.0 4.5 %collective-permute-start.6 = (bf16[2,2,32,512]{3,2,1,0:T(8,128)(2,1)S(1)}, bf16[2,2,32,512]{3,2,1,0:T(8,128)(2,1)S(1)}, u32[]{:S(2)}, u32[]{:S(2)}) collective-permute-start(bf16[2,2,32,512]{3,2,1,0:T(8,128)(2,1)S(1)} %slice.111), channel_id=1, source_target_pairs={{0,1},{1,0},{2,3},{3,2},{4,5},{5,4},{6,7},{7,6},{8,9},{9,8},{10,11... | collective-permute-start | bytes 393224 | tf_op jit(solution)/shard_map/ppermute | solution.py:71
  5.5 8.1 %collective-permute-start = (bf16[2,2,32,512]{3,2,1,0:T(8,128)(2,1)S(1)}, bf16[2,2,32,512]{3,2,1,0:T(8,128)(2,1)S(1)}, u32[]{:S(2)}, u32[]{:S(2)}) collective-permute-start(bf16[2,2,32,512]{3,2,1,0:T(8,128)(2,1)S(1)} %get-tuple-element.25), channel_id=1, source_target_pairs={{0,1},{1,0},{2,3},{3,2},{4,5},{5,4},{6,7},{7,6},{8,9},{9,8},{10,11... | collective-permute-start | bytes 393224 | tf_op jit(solution)/shard_map/ppermute | solution.py:71
  7.4 9.7 %collective-permute-start.7 = (bf16[2,2,2,32,512]{4,3,1,0,2:T(8,128)(2,1)S(1)}, bf16[2,2,2,32,512]{4,3,1,0,2:T(8,128)(2,1)S(1)}, u32[]{:S(2)}, u32[]{:S(2)}) collective-permute-start(bf16[2,2,2,32,512]{4,3,1,0,2:T(8,128)(2,1)S(1)} %pad_maximum_fusion.2), channel_id=1, source_target_pairs={{0,14},{2,0},{4,2},{6,4},{8,6},{10,8},{12,10},{14,12},{1,15},{3,1}... | collective-permute-start | bytes 786440 | tf_op jit(solution)/shard_map/ppermute | solution.py:71
  13.3 7.3 %collective-permute-start.8 = (bf16[2,2,2,32,512]{4,3,1,0,2:T(8,128)(2,1)S(1)}, bf16[2,2,2,32,512]{4,3,1,0,2:T(8,128)(2,1)S(1)}, u32[]{:S(2)}, u32[]{:S(2)}) collective-permute-start(bf16[2,2,2,32,512]{4,3,1,0,2:T(8,128)(2,1)S(1)} %pad_maximum_fusion.2), channel_id=1, source_target_pairs={{0,2},{2,4},{4,6},{6,8},{8,10},{10,12},{12,14},{14,0},{1,3},{3,5},... | collective-permute-start | bytes 786440 | tf_op jit(solution)/shard_map/ppermute | solution.py:71
  13.7 12.2 %collective-permute-start.4 = (bf16[2,2,2,32,512]{4,3,1,0,2:T(8,128)(2,1)S(1)}, bf16[2,2,2,32,512]{4,3,1,0,2:T(8,128)(2,1)S(1)}, u32[]{:S(2)}, u32[]{:S(2)}) collective-permute-start(bf16[2,2,2,32,512]{4,3,1,0,2:T(8,128)(2,1)S(1)} %pad_maximum_fusion.1), channel_id=1, source_target_pairs={{0,2},{2,4},{4,6},{6,8},{8,10},{10,12},{12,14},{14,0},{1,3},{3,5},... | collective-permute-start | bytes 786440 | tf_op jit(solution)/shard_map/ppermute | solution.py:71
  13.7 12.2 %collective-permute-start.1 = (bf16[2,2,2,32,512]{4,3,1,0,2:T(8,128)(2,1)S(1)}, bf16[2,2,2,32,512]{4,3,1,0,2:T(8,128)(2,1)S(1)}, u32[]{:S(2)}, u32[]{:S(2)}) collective-permute-start(bf16[2,2,2,32,512]{4,3,1,0,2:T(8,128)(2,1)S(1)} %pad_maximum_fusion.1), channel_id=1, source_target_pairs={{0,14},{2,0},{4,2},{6,4},{8,6},{10,8},{12,10},{14,12},{1,15},{3,1}... | collective-permute-start | bytes 786440 | tf_op jit(solution)/shard_map/ppermute | solution.py:71
  17.1 11.4 %collective-permute-start.9 = (bf16[2,2,2,32,512]{4,3,1,0,2:T(8,128)(2,1)S(1)}, bf16[2,2,2,32,512]{4,3,1,0,2:T(8,128)(2,1)S(1)}, u32[]{:S(2)}, u32[]{:S(2)}) collective-permute-start(bf16[2,2,2,32,512]{4,3,1,0,2:T(8,128)(2,1)S(1)} %collective-permute-done.7), channel_id=1, source_target_pairs={{0,14},{2,0},{4,2},{6,4},{8,6},{10,8},{12,10},{14,12},{1,15},{3,1}... | collective-permute-start | bytes 786440 | tf_op jit(solution)/shard_map/ppermute | solution.py:71
  20.6 11.2 %collective-permute-start.10 = (bf16[2,2,2,32,512]{4,3,1,0,2:T(8,128)(2,1)S(1)}, bf16[2,2,2,32,512]{4,3,1,0,2:T(8,128)(2,1)S(1)}, u32[]{:S(2)}, u32[]{:S(2)}) collective-permute-start(bf16[2,2,2,32,512]{4,3,1,0,2:T(8,128)(2,1)S(1)} %collective-permute-done.8), channel_id=1, source_target_pairs={{0,2},{2,4},{4,6},{6,8},{8,10},{10,12},{12,14},{14,0},{1,3},{3,5},... | collective-permute-start | bytes 786440 | tf_op jit(solution)/shard_map/ppermute | solution.py:71
  25.9 25.2 %collective-permute-start.5 = (bf16[2,2,2,32,512]{4,3,1,0,2:T(8,128)(2,1)S(1)}, bf16[2,2,2,32,512]{4,3,1,0,2:T(8,128)(2,1)S(1)}, u32[]{:S(2)}, u32[]{:S(2)}) collective-permute-start(bf16[2,2,2,32,512]{4,3,1,0,2:T(8,128)(2,1)S(1)} %collective-permute-done.4), channel_id=1, source_target_pairs={{0,2},{2,4},{4,6},{6,8},{8,10},{10,12},{12,14},{14,0},{1,3},{3,5},... | collective-permute-start | bytes 786440 | tf_op jit(solution)/shard_map/ppermute | solution.py:71
  25.9 26.1 %collective-permute-start.2 = (bf16[2,2,2,32,512]{4,3,1,0,2:T(8,128)(2,1)S(1)}, bf16[2,2,2,32,512]{4,3,1,0,2:T(8,128)(2,1)S(1)}, u32[]{:S(2)}, u32[]{:S(2)}) collective-permute-start(bf16[2,2,2,32,512]{4,3,1,0,2:T(8,128)(2,1)S(1)} %collective-permute-done.1), channel_id=1, source_target_pairs={{0,14},{2,0},{4,2},{6,4},{8,6},{10,8},{12,10},{14,12},{1,15},{3,1}... | collective-permute-start | bytes 786440 | tf_op jit(solution)/shard_map/ppermute | solution.py:71
  28.6 14.3 %collective-permute-start.11 = (bf16[2,2,2,32,512]{4,3,1,0,2:T(8,128)(2,1)S(1)}, bf16[2,2,2,32,512]{4,3,1,0,2:T(8,128)(2,1)S(1)}, u32[]{:S(2)}, u32[]{:S(2)}) collective-permute-start(bf16[2,2,2,32,512]{4,3,1,0,2:T(8,128)(2,1)S(1)} %collective-permute-done.9), channel_id=1, source_target_pairs={{0,14},{2,0},{4,2},{6,4},{8,6},{10,8},{12,10},{14,12},{1,15},{3,1}... | collective-permute-start | bytes 786440 | tf_op jit(solution)/shard_map/ppermute | solution.py:71
  31.8 11.0 %collective-permute-start.12 = (bf16[2,2,2,32,512]{4,3,1,0,2:T(8,128)(2,1)S(1)}, bf16[2,2,2,32,512]{4,3,1,0,2:T(8,128)(2,1)S(1)}, u32[]{:S(2)}, u32[]{:S(2)}) collective-permute-start(bf16[2,2,2,32,512]{4,3,1,0,2:T(8,128)(2,1)S(1)} %collective-permute-done.10), channel_id=1, source_target_pairs={{0,2},{2,4},{4,6},{6,8},{8,10},{10,12},{12,14},{14,0},{1,3},{3,5},... | collective-permute-start | bytes 786440 | tf_op jit(solution)/shard_map/ppermute | solution.py:71
  42.8 5.1 %collective-permute-start.13 = (bf16[2,2,2,16,512]{4,3,1,0,2:T(8,128)(2,1)S(1)}, bf16[2,2,2,16,512]{4,3,1,0,2:T(8,128)(2,1)S(1)}, u32[]{:S(2)}, u32[]{:S(2)}) collective-permute-start(bf16[2,2,2,16,512]{4,3,1,0,2:T(8,128)(2,1)S(1)} %slice.112), channel_id=1, source_target_pairs={{0,2},{2,4},{4,6},{6,8},{8,10},{10,12},{12,14},{14,0},{1,3},{3,5},... | collective-permute-start | bytes 393224 | tf_op jit(solution)/shard_map/ppermute | solution.py:71
  42.9 5.0 %collective-permute-start.14 = (bf16[2,2,2,16,512]{4,3,1,0,2:T(8,128)(2,1)S(1)}, bf16[2,2,2,16,512]{4,3,1,0,2:T(8,128)(2,1)S(1)}, u32[]{:S(2)}, u32[]{:S(2)}) collective-permute-start(bf16[2,2,2,16,512]{4,3,1,0,2:T(8,128)(2,1)S(1)} %slice.113), channel_id=1, source_target_pairs={{0,14},{2,0},{4,2},{6,4},{8,6},{10,8},{12,10},{14,12},{1,15},{3,1}... | collective-permute-start | bytes 393224 | tf_op jit(solution)/shard_map/ppermute | solution.py:71
  51.2 6.8 %collective-permute-start.15 = (bf16[2,2,2,32,512]{4,3,1,0,2:T(8,128)(2,1)S(1)}, bf16[2,2,2,32,512]{4,3,1,0,2:T(8,128)(2,1)S(1)}, u32[]{:S(2)}, u32[]{:S(2)}) collective-permute-start(bf16[2,2,2,32,512]{4,3,1,0,2:T(8,128)(2,1)S(1)} %collective-permute-done.5), channel_id=1, source_target_pairs={{0,2},{2,4},{4,6},{6,8},{8,10},{10,12},{12,14},{14,0},{1,3},{3,5},... | collective-permute-start | bytes 786440 | tf_op jit(solution)/shard_map/ppermute | solution.py:71
  52.0 20.6 %collective-permute-start.3 = (bf16[2,2,2,32,512]{4,3,1,0,2:T(8,128)(2,1)S(1)}, bf16[2,2,2,32,512]{4,3,1,0,2:T(8,128)(2,1)S(1)}, u32[]{:S(2)}, u32[]{:S(2)}) collective-permute-start(bf16[2,2,2,32,512]{4,3,1,0,2:T(8,128)(2,1)S(1)} %collective-permute-done.2), channel_id=1, source_target_pairs={{0,14},{2,0},{4,2},{6,4},{8,6},{10,8},{12,10},{14,12},{1,15},{3,1}... | collective-permute-start | bytes 786440 | tf_op jit(solution)/shard_map/ppermute | solution.py:71
  57.9 15.4 %collective-permute-start.16 = (bf16[2,2,2,32,512]{4,3,1,0,2:T(8,128)(2,1)S(1)}, bf16[2,2,2,32,512]{4,3,1,0,2:T(8,128)(2,1)S(1)}, u32[]{:S(2)}, u32[]{:S(2)}) collective-permute-start(bf16[2,2,2,32,512]{4,3,1,0,2:T(8,128)(2,1)S(1)} %collective-permute-done.15), channel_id=1, source_target_pairs={{0,2},{2,4},{4,6},{6,8},{8,10},{10,12},{12,14},{14,0},{1,3},{3,5},... | collective-permute-start | bytes 786440 | tf_op jit(solution)/shard_map/ppermute | solution.py:71
  59.7 29.9 %all-to-all-start = ((bf16[2,16,32,512]{3,2,0,1:T(8,128)(2,1)}), bf16[2,16,32,512]{3,2,0,1:T(8,128)(2,1)S(1)}, u32[]{:S(2)}, u32[]{:S(2)}) async-start(bf16[2,16,32,512]{3,2,0,1:T(8,128)(2,1)} %copy.9), calls=%async_computation | async-start | bytes 2097152 | tf_op jit(solution)/shard_map/all_to_all | solution.py:135
  89.7 1.0 copy-start.1
  91.5 1.0 copy-start
